TPU v7x, 32 devices: a whole 2x2x4 slice. The times are simulated.
32 devices in a mesh: parts: 2 (over y), fsdp: 4 (over z), seq: 2 (over x), ctx: 2 (over core).
Axes of the slice: x: 2, y: 2, z: 4, core: 2. Of those that a mesh axis runs over, the one named last changes fastest.
Arguments:
- hidden_in: bfloat16 [8, 2, 96, 8192], P(('parts', 'fsdp'), 'ctx', None, 'seq'), parts along dimension 0, may hold values from -6 to 6
- weight: bfloat16 [8192, 4096], P('fsdp', 'seq'), may hold values from -0.0625 to 0.0625
- clip_upper: float32 [128, 4096], P(('parts', 'fsdp'), 'seq'), parts along dimension 0, may hold values from 0.5 to 3
- clip_lower: float32 [128, 4096], P(('parts', 'fsdp'), 'seq'), parts along dimension 0, may hold values from -0.5 to 2.5
- filters: float32 [256, 7], P('seq'), may hold values from -3 to 3
- gate: bfloat16 [8, 2, 96, 4096], P(('parts', 'fsdp'), 'ctx', None, 'seq'), parts along dimension 0, may hold values from -6 to 6
- target: bfloat16 [8, 2, 96, 4096], P(('parts', 'fsdp'), 'ctx', None, 'seq'), parts along dimension 0, may hold values from -6 to 6
Outputs:
- grad_upper: float32 [128, 4096], P(('parts', 'fsdp'), 'seq'), parts along dimension 0
- grad_lower: float32 [128, 4096], P(('parts', 'fsdp'), 'seq'), parts along dimension 0
There are 2 independent parts, one for each index of `parts`. A program takes and returns all parts, laid end to end along the dimension named above; an argument that names none is the same for every part. Nothing has to cross between parts.
All inputs are finite; a program needn't handle non-finite values.
Results may differ from a plain program's by a relative error of at most 0.0039.
Values may be sent and summed in bfloat16 or wider, within the bound.
No kernel may reach another device: no remote copies, remote signals or barrier semaphores. Data moves between devices by JAX's collectives and lax.ppermute only.
A program may use at most 128 MiB of HBM per device.

v0:
```python
import jax
import jax.numpy as jnp
from jax import lax
from jax.sharding import PartitionSpec as P

FILT = 7
CGROUP = 16


def from_behind(value, axis, by):
    devices = lax.axis_size(axis)
    pairs = [(i, i + by) for i in range(devices) if 0 <= i + by < devices]
    return lax.ppermute(value, axis, pairs)


def soft_clip(values, upper_logit, lower_logit):
    rows = values.shape[0]
    groups = upper_logit.shape[0]
    blocks = values.reshape(groups, rows // groups, values.shape[1])
    amax = jnp.max(jnp.abs(blocks), axis=1) + 1e-06
    upper = jax.nn.sigmoid(upper_logit) * amax
    lower = -jax.nn.sigmoid(lower_logit) * amax
    center = ((upper + lower) * 0.5)[:, None, :]
    radius = ((upper - lower) * 0.5)[:, None, :]
    clipped = center + radius * jnp.tanh((blocks - center) / radius)
    return clipped.reshape(rows, values.shape[1])


def fold_rows(update, init, weights, block):
    count = weights.shape[0] // block

    def advance(index, carry):
        start = index * block
        piece = lax.dynamic_slice_in_dim(weights, start, block, 0)
        return update(carry, piece, start)

    return lax.fori_loop(0, count, advance, init)


def on_device(hidden_in, weight, clip_upper, clip_lower, filters, gate, target):
    width = hidden_in.shape[-1]
    local_rows = hidden_in.reshape(-1, width)
    panel = lax.all_gather(local_rows, "seq", axis=1, tiled=True)
    length = panel.shape[0]
    columns = weight.shape[1]
    block = weight.shape[0]
    upper_all, lower_all = (
        lax.all_gather(clip_upper, "fsdp", axis=0, tiled=True),
        lax.all_gather(clip_lower, "fsdp", axis=0, tiled=True),
    )
    weights_all = lax.all_gather(weight, "fsdp", axis=0, tiled=True)
    group_rows = block // clip_upper.shape[0]
    group_count = clip_upper.shape[0]

    def add_proj(total, piece, start):
        first = start // group_rows
        upper_piece = lax.dynamic_slice_in_dim(upper_all, first, group_count, 0)
        lower_piece = lax.dynamic_slice_in_dim(lower_all, first, group_count, 0)
        quant = soft_clip(piece.astype(jnp.float32), upper_piece, lower_piece).astype(jnp.bfloat16)
        inputs = lax.dynamic_slice_in_dim(panel, start, block, 1)
        return total + jnp.dot(inputs, quant, preferred_element_type=jnp.float32)

    proj = fold_rows(
        add_proj, jnp.zeros((length, columns), jnp.float32), weights_all, block
    ).astype(jnp.bfloat16)
    taps = jnp.repeat(filters, CGROUP, axis=0).T
    pad = FILT - 1
    previous = from_behind(proj[length - pad :], "ctx", 1)
    padded = jnp.concatenate([previous, proj], axis=0).astype(jnp.float32)
    conv = jnp.zeros((length, columns), jnp.float32)
    for tap in range(FILT):
        conv = conv + taps[tap] * padded[pad - tap : pad - tap + length]
    gates = gate.reshape(length, columns).astype(jnp.float32)
    wanted = target.reshape(length, columns).astype(jnp.float32)
    total_tokens = lax.axis_size("fsdp") * lax.axis_size("ctx") * length
    scale = 1024.0 / jnp.sqrt(jnp.float32(total_tokens))
    d_conv = scale * (gates * conv - wanted) * gates
    following = from_behind(d_conv[:pad], "ctx", -1)
    padded_back = jnp.concatenate([d_conv, following], axis=0)
    d_proj = jnp.zeros((length, columns), jnp.float32)
    for tap in range(FILT):
        d_proj = d_proj + taps[tap] * padded_back[tap : tap + length]
    d_proj = d_proj.astype(jnp.bfloat16)

    def add_grad(carry, piece, start):
        first = start // group_rows
        upper_piece = lax.dynamic_slice_in_dim(upper_all, first, group_count, 0)
        lower_piece = lax.dynamic_slice_in_dim(lower_all, first, group_count, 0)
        inputs = lax.dynamic_slice_in_dim(panel, start, block, 1)
        d_piece = lax.dot_general(
            inputs, d_proj, (((0,), (0,)), ((), ())), preferred_element_type=jnp.float32
        )
        values = piece.astype(jnp.float32)
        _, pull = jax.vjp(
            lambda upper_logit, lower_logit: soft_clip(values, upper_logit, lower_logit),
            upper_piece,
            lower_piece,
        )
        grad_up, grad_low = pull(d_piece)
        return (
            lax.dynamic_update_slice_in_dim(carry[0], grad_up, first, 0),
            lax.dynamic_update_slice_in_dim(carry[1], grad_low, first, 0),
        )

    empty = jnp.zeros(upper_all.shape, jnp.float32)
    grad_up_all, grad_low_all = fold_rows(add_grad, (empty, empty), weights_all, block)
    shard_up, shard_low = (
        lax.psum_scatter(grad_up_all, "fsdp", scatter_dimension=0, tiled=True),
        lax.psum_scatter(grad_low_all, "fsdp", scatter_dimension=0, tiled=True),
    )
    grad_upper, grad_lower = lax.psum((shard_up, shard_low), "ctx")
    return (grad_upper, grad_lower)


def solution(mesh):
    return jax.shard_map(
        on_device,
        mesh=mesh,
        in_specs=(
            P(("parts", "fsdp"), "ctx", None, "seq"),
            P("fsdp", "seq"),
            P(("parts", "fsdp"), "seq"),
            P(("parts", "fsdp"), "seq"),
            P("seq", None),
            P(("parts", "fsdp"), "ctx", None, "seq"),
            P(("parts", "fsdp"), "ctx", None, "seq"),
        ),
        out_specs=(P(("parts", "fsdp"), "seq"), P(("parts", "fsdp"), "seq")),
        check_vma=False,
    )
```

profile of v0, /device:TPU:9, one launch (start us, length us, event | category | flops | bytes accessed | tf_op | source)
XLA Modules:
  0.0 842.7 jit_solution(3278080552905704007)
XLA Ops:
  9.8 13.3 %all_gather.13 = f32[64,2048]{1,0:T(8,128)S(1)} all-gather(f32[16,2048]{1,0:T(8,128)} %param.13), channel_id=1, replica_groups=mesh['parts'=2,'fsdp'=4,'seq'=2,'ctx'=2] {'fsdp'}, dimensions={0}, use_global_device_ids=true | all-gather | bytes 655360 | tf_op jit(solution)/shard_map/all_gather | solution.py:48
  23.1 13.8 %all_gather.15 = f32[64,2048]{1,0:T(8,128)S(1)} all-gather(f32[16,2048]{1,0:T(8,128)} %param.14), channel_id=1, replica_groups=mesh['parts'=2,'fsdp'=4,'seq'=2,'ctx'=2] {'fsdp'}, dimensions={0}, use_global_device_ids=true | all-gather | bytes 655360 | tf_op jit(solution)/shard_map/all_gather | solution.py:49
  37.9 560.2 %all-gather.4.cloned.1.call-done = bf16[8192,2048]{1,0:T(8,128)(2,1)} async-done(((bf16[2048,2048]{1,0:T(8,128)(2,1)}), bf16[8192,2048]{1,0:T(8,128)(2,1)}) %all-gather.4.cloned.1.call-update) | async-done | bytes 33554448 | tf_op jit(solution)/shard_map/all_gather | solution.py:51
  598.1 79.4 %while.34 = (s32[]{:T(128)}, f32[96,2048]{1,0:T(8,128)S(1)}, bf16[96,8192]{1,0:T(8,128)(2,1)}, f32[64,2048]{1,0:T(8,128)S(1)}, bf16[8192,2048]{1,0:T(8,128)(2,1)...) while((s32[]{:T(128)}, f32[96,2048]{1,0:T(8,128)S(1)}, ...), condition=%wide.region_2.3_spmd.clone, body=%wide.region_0.2_spmd.clone.sunk | while | flops 843874304 | bytes 36569464 | solution.py:37
  598.1 5.8 bitcast_reduce_fusion.3
  604.0 8.8 %fusion.54 = bf16[2048,2048]{1,0:T(8,128)(2,1)} fusion(f32[16,2048]{1,0:T(8,128)S(1)} %get-tuple-element.535, f32[16,2048]{1,0:T(8,128)S(1)} %get-tuple-element.536, bf16[8192,2048]{1,0:T(8,128)(2,1)} %get-tuple-element.569, s32[]{:T(128)S(6)} %select_n.80), kind=kLoop, calls=%fused_computation.32.clone.1 | loop fusion | flops 25165824 | bytes 17039364 | tf_op jit(solution)/shard_map/while/body/eval_jaxpr/convert_element_type | solution.py:59
  612.9 5.1 convolution_add_fusion.2
  618.1 5.7 bitcast_reduce_fusion.3
  623.9 8.8 %fusion.54 = bf16[2048,2048]{1,0:T(8,128)(2,1)} fusion(f32[16,2048]{1,0:T(8,128)S(1)} %get-tuple-element.535, f32[16,2048]{1,0:T(8,128)S(1)} %get-tuple-element.536, bf16[8192,2048]{1,0:T(8,128)(2,1)} %get-tuple-element.569, s32[]{:T(128)S(6)} %select_n.80), kind=kLoop, calls=%fused_computation.32.clone.1 | loop fusion | flops 25165824 | bytes 17039364 | tf_op jit(solution)/shard_map/while/body/eval_jaxpr/convert_element_type | solution.py:59
  632.7 5.1 convolution_add_fusion.2
  637.9 5.7 bitcast_reduce_fusion.3
  643.7 8.8 %fusion.54 = bf16[2048,2048]{1,0:T(8,128)(2,1)} fusion(f32[16,2048]{1,0:T(8,128)S(1)} %get-tuple-element.535, f32[16,2048]{1,0:T(8,128)S(1)} %get-tuple-element.536, bf16[8192,2048]{1,0:T(8,128)(2,1)} %get-tuple-element.569, s32[]{:T(128)S(6)} %select_n.80), kind=kLoop, calls=%fused_computation.32.clone.1 | loop fusion | flops 25165824 | bytes 17039364 | tf_op jit(solution)/shard_map/while/body/eval_jaxpr/convert_element_type | solution.py:59
  652.6 5.1 convolution_add_fusion.2
  657.7 5.7 bitcast_reduce_fusion.3
  663.6 8.8 %fusion.54 = bf16[2048,2048]{1,0:T(8,128)(2,1)} fusion(f32[16,2048]{1,0:T(8,128)S(1)} %get-tuple-element.535, f32[16,2048]{1,0:T(8,128)S(1)} %get-tuple-element.536, bf16[8192,2048]{1,0:T(8,128)(2,1)} %get-tuple-element.569, s32[]{:T(128)S(6)} %select_n.80), kind=kLoop, calls=%fused_computation.32.clone.1 | loop fusion | flops 25165824 | bytes 17039364 | tf_op jit(solution)/shard_map/while/body/eval_jaxpr/convert_element_type | solution.py:59
  672.4 5.1 convolution_add_fusion.2
  679.0 1.8 collective-permute-done
  681.7 2.2 collective-permute-start.1
  685.4 82.5 %while.33 = (s32[]{:T(128)}, f32[64,2048]{1,0:T(8,128)S(1)}, f32[64,2048]{1,0:T(8,128)S(1)}, bf16[96,8192]{1,0:T(8,128)(2,1)}, bf16[96,2048]{1,0:T(8,128)(2,1)S(...) while((s32[]{:T(128)}, f32[64,2048]{1,0:T(8,128)S(1)}, ...), condition=%wide.region_9.10_spmd, body=%wide.region_3.9_spmd.sunk | while | flops 886177792 | bytes 21104004 | solution.py:37
  685.5 5.7 fusion.50
  691.3 12.8 %divide_reduce_fusion.2 = (f32[16,2048]{1,0:T(8,128)S(1)}, f32[16,2048]{1,0:T(8,128)S(1)}, f32[16,2048]{1,0:T(8,128)S(1)}, f32[16,2048]{1,0:T(8,128)S(1)}) fusion(f32[16,2048]{1,0:T(8,128)S(1)} %get-tuple-element.520, f32[16,2048]{1,0:T(8,128)S(1)} %get-tuple-element.521, bf16[8192,2048]{1,0:T(8,128)(2,1)} %get-tuple-element.616, s32[]{:T(128)S(6)} %select_n.77, ...), kind=kOutput, calls=%fused_computation.10.clone.1 | convolution fusion | flops 872284160 | bytes 10093568 | tf_op jit(solution)/shard_map/while/body/eval_jaxpr/dot_general | solution.py:90
  706.3 5.7 fusion.50
  712.1 12.8 %divide_reduce_fusion.2 = (f32[16,2048]{1,0:T(8,128)S(1)}, f32[16,2048]{1,0:T(8,128)S(1)}, f32[16,2048]{1,0:T(8,128)S(1)}, f32[16,2048]{1,0:T(8,128)S(1)}) fusion(f32[16,2048]{1,0:T(8,128)S(1)} %get-tuple-element.520, f32[16,2048]{1,0:T(8,128)S(1)} %get-tuple-element.521, bf16[8192,2048]{1,0:T(8,128)(2,1)} %get-tuple-element.616, s32[]{:T(128)S(6)} %select_n.77, ...), kind=kOutput, calls=%fused_computation.10.clone.1 | convolution fusion | flops 872284160 | bytes 10093568 | tf_op jit(solution)/shard_map/while/body/eval_jaxpr/dot_general | solution.py:90
  727.1 5.7 fusion.50
  732.9 12.8 %divide_reduce_fusion.2 = (f32[16,2048]{1,0:T(8,128)S(1)}, f32[16,2048]{1,0:T(8,128)S(1)}, f32[16,2048]{1,0:T(8,128)S(1)}, f32[16,2048]{1,0:T(8,128)S(1)}) fusion(f32[16,2048]{1,0:T(8,128)S(1)} %get-tuple-element.520, f32[16,2048]{1,0:T(8,128)S(1)} %get-tuple-element.521, bf16[8192,2048]{1,0:T(8,128)(2,1)} %get-tuple-element.616, s32[]{:T(128)S(6)} %select_n.77, ...), kind=kOutput, calls=%fused_computation.10.clone.1 | convolution fusion | flops 872284160 | bytes 10093568 | tf_op jit(solution)/shard_map/while/body/eval_jaxpr/dot_general | solution.py:90
  747.9 5.7 fusion.50
  753.8 12.8 %divide_reduce_fusion.2 = (f32[16,2048]{1,0:T(8,128)S(1)}, f32[16,2048]{1,0:T(8,128)S(1)}, f32[16,2048]{1,0:T(8,128)S(1)}, f32[16,2048]{1,0:T(8,128)S(1)}) fusion(f32[16,2048]{1,0:T(8,128)S(1)} %get-tuple-element.520, f32[16,2048]{1,0:T(8,128)S(1)} %get-tuple-element.521, bf16[8192,2048]{1,0:T(8,128)(2,1)} %get-tuple-element.616, s32[]{:T(128)S(6)} %select_n.77, ...), kind=kOutput, calls=%fused_computation.10.clone.1 | convolution fusion | flops 872284160 | bytes 10093568 | tf_op jit(solution)/shard_map/while/body/eval_jaxpr/dot_general | solution.py:90
  769.3 18.2 %reduce-scatter.3.cloned.1.call-done = f32[16,2048]{1,0:T(8,128)} async-done(((f32[64,2048]{1,0:T(8,128)}), f32[16,2048]{1,0:T(8,128)}) %reduce-scatter.3.cloned.1.call-update) | async-done | bytes 131088 | tf_op jit(solution)/shard_map/reduce_scatter | solution.py:108
  787.5 22.1 %reduce-scatter.5.cloned.1.call-done = f32[16,2048]{1,0:T(8,128)} async-done(((f32[64,2048]{1,0:T(8,128)}), f32[16,2048]{1,0:T(8,128)}) %reduce-scatter.5.cloned.1.call-update) | async-done | bytes 131088 | tf_op jit(solution)/shard_map/reduce_scatter | solution.py:109
  809.6 23.4 %all-reduce.3.cloned.1.call-done = (f32[16,2048]{1,0:T(8,128)}, f32[16,2048]{1,0:T(8,128)}) async-done(((f32[16,2048]{1,0:T(8,128)}, f32[16,2048]{1,0:T(8,128)}), (f32[16,2048]{1,0:T(8,128)}, f32[16,2048]{1,0:T(8,128)})) %all-reduce.3.cloned.1.call-update) | async-done | bytes 262160 | tf_op jit(solution)/shard_map/psum | solution.py:111
  833.0 1.6 copy.29
  834.6 1.6 copy.30
  (53 shorter events, 17.4 us)
Async XLA Ops:
  7.2 30.8 %all-gather.6.cloned.1.call-start = ((), (), s32[]{:S(2)}) async-start(), calls=%async_computation.5 | async-start | bytes 2359296 | tf_op jit(solution)/shard_map/all_gather | solution.py:43
  7.9 590.2 %all-gather.4.cloned.1.call-start = ((), (), s32[]{:S(2)}) async-start(), calls=%async_computation.2 | async-start | bytes 41943040 | tf_op jit(solution)/shard_map/all_gather | solution.py:51
  8.6 778.9 %reduce-scatter.3.cloned.1.call-start = ((), (), s32[]{:S(2)}) async-start(), calls=%async_computation.3 | async-start | bytes 655360 | tf_op jit(solution)/shard_map/reduce_scatter | solution.py:108
  598.1 82.7 %copy-start.2 = (bf16[1,1,96,2048]{3,2,1,0:T(8,128)(2,1)S(1)}, bf16[1,1,96,2048]{3,2,1,0:T(8,128)(2,1)}, u32[]{:S(2)}) copy-start(bf16[1,1,96,2048]{3,2,1,0:T(8,128)(2,1)} %param.17) | copy-start | bytes 1179652
  598.1 82.7 %copy-start.3 = (bf16[1,1,96,2048]{3,2,1,0:T(8,128)(2,1)S(1)}, bf16[1,1,96,2048]{3,2,1,0:T(8,128)(2,1)}, u32[]{:S(2)}) copy-start(bf16[1,1,96,2048]{3,2,1,0:T(8,128)(2,1)} %param.16) | copy-start | bytes 1179652
  677.6 3.1 collective-permute-start
  681.7 3.0 collective-permute-start.1
  767.9 0.8 copy-start
  767.9 1.0 copy-start.1
  768.7 40.9 %reduce-scatter.5.cloned.1.call-start = ((), (), s32[]{:S(2)}) async-start(), calls=%async_computation.4 | async-start | bytes 655360 | tf_op jit(solution)/shard_map/reduce_scatter | solution.py:109
  769.3 63.7 %all-reduce.3.cloned.1.call-start = ((), (), s32[]{:S(2)}) async-start(), calls=%async_computation.6 | async-start | bytes 524288 | tf_op jit(solution)/shard_map/psum | solution.py:111
Sparse Core Ops, SparseCore 0:
  9.5 28.3 all-gather.5
  39.5 558.5 all-gather.3
  768.8 18.6 reduce-scatter.2
  789.6 19.9 reduce-scatter.4
  811.8 21.1 all-reduce.2
where the time goes:
time: 844 us; the launch traced here: 843 us
  waiting for transfers between devices  629 us (75%)
  other arithmetic  84.2 us (10%)
  matrix products  71.8 us (9%)
  blocking collectives  27.1 us (3%)
  between operations  13.9 us (2%)
  local copies, waits for them, and re-layouts  12.3 us (1%)
    all_gather x1, waiting for transfers between devices, on_device(): weights_all = lax.all_gather(weight, 'fsdp', axis=0, tiled=True)  560 us
    dot_general x4, matrix products, add_grad(): lax.dot_general(inputs, d_proj, (((0,), (0,)), ((), ())), preferred_eleme...  51.2 us
    reduce_max x8, other arithmetic, soft_clip(): amax = jnp.max(jnp.abs(blocks), axis=1) + 1e-06  45.6 us
    convert_element_type x4, other arithmetic, add_proj(): soft_clip(piece.astype(jnp.float32), upper_piece, lower_piece)  35.4 us
    psum x1, waiting for transfers between devices, on_device(): grad_upper, grad_lower = lax.psum((shard_up, shard_low), 'ctx')  23.4 us
    reduce_scatter x1, waiting for transfers between devices, on_device(): lax.psum_scatter(grad_low_all, 'fsdp', scatter_dimension=0, tiled=True)  22.1 us
    dot_general x4, matrix products, add_proj(): return total + jnp.dot(inputs, quant, preferred_element_type=jnp.float32)  20.6 us
    reduce_scatter x1, waiting for transfers between devices, on_device(): lax.psum_scatter(grad_up_all, 'fsdp', scatter_dimension=0, tiled=True)  18.2 us
  transfers between devices with their start and end apart: 7, of which 7 were waited for; matrix products, arithmetic and copies ran while one was open for 0% of the time, Pallas kernels for 0%

commit v1 on v0

v1 whole, which is shorter than its diff:
```python
import jax
import jax.numpy as jnp
from jax import lax
from jax.sharding import PartitionSpec as P

FILT = 7
CGROUP = 16


def from_behind(value, axis, by):
    devices = lax.axis_size(axis)
    pairs = [(i, i + by) for i in range(devices) if 0 <= i + by < devices]
    return lax.ppermute(value, axis, pairs)


def soft_clip(values, upper_logit, lower_logit):
    rows = values.shape[0]
    groups = upper_logit.shape[0]
    blocks = values.reshape(groups, rows // groups, values.shape[1])
    amax = jnp.max(jnp.abs(blocks), axis=1) + 1e-06
    upper = jax.nn.sigmoid(upper_logit) * amax
    lower = -jax.nn.sigmoid(lower_logit) * amax
    center = ((upper + lower) * 0.5)[:, None, :]
    radius = ((upper - lower) * 0.5)[:, None, :]
    clipped = center + radius * jnp.tanh((blocks - center) / radius)
    return clipped.reshape(rows, values.shape[1])


def on_device(hidden_in, weight, clip_upper, clip_lower, filters, gate, target):
    shards = lax.axis_size("fsdp")
    width = hidden_in.shape[-1]
    local_rows = hidden_in.reshape(-1, width)
    length = local_rows.shape[0]
    rows, columns = weight.shape
    features = lax.all_gather(local_rows, "seq", axis=1, tiled=True)
    pieces = features.reshape(length, shards, rows).transpose(1, 0, 2)
    mine = lax.all_to_all(pieces, "fsdp", 0, 0)
    inputs = mine.reshape(shards * length, rows)

    values = weight.astype(jnp.float32)
    quant = soft_clip(values, clip_upper, clip_lower).astype(jnp.bfloat16)
    partial = jnp.dot(inputs, quant, preferred_element_type=jnp.float32)
    proj = lax.psum_scatter(partial, "fsdp", scatter_dimension=0, tiled=True).astype(jnp.bfloat16)

    taps = jnp.repeat(filters, CGROUP, axis=0).T
    pad = FILT - 1
    previous = from_behind(proj[length - pad :], "ctx", 1)
    padded = jnp.concatenate([previous, proj], axis=0).astype(jnp.float32)
    conv = jnp.zeros((length, columns), jnp.float32)
    for tap in range(FILT):
        conv = conv + taps[tap] * padded[pad - tap : pad - tap + length]
    gates = gate.reshape(length, columns).astype(jnp.float32)
    wanted = target.reshape(length, columns).astype(jnp.float32)
    total_tokens = lax.axis_size("fsdp") * lax.axis_size("ctx") * length
    scale = 1024.0 / jnp.sqrt(jnp.float32(total_tokens))
    d_conv = scale * (gates * conv - wanted) * gates
    following = from_behind(d_conv[:pad], "ctx", -1)
    padded_back = jnp.concatenate([d_conv, following], axis=0)
    d_proj = jnp.zeros((length, columns), jnp.float32)
    for tap in range(FILT):
        d_proj = d_proj + taps[tap] * padded_back[tap : tap + length]
    d_proj = d_proj.astype(jnp.bfloat16)

    d_all = lax.all_gather(d_proj, "fsdp", axis=0, tiled=True)
    d_clipped = lax.dot_general(
        inputs, d_all, (((0,), (0,)), ((), ())), preferred_element_type=jnp.float32
    )
    _, pull = jax.vjp(
        lambda upper_logit, lower_logit: soft_clip(values, upper_logit, lower_logit),
        clip_upper,
        clip_lower,
    )
    grad_up, grad_low = pull(d_clipped)
    grad_upper, grad_lower = lax.psum((grad_up, grad_low), "ctx")
    return (grad_upper, grad_lower)


def solution(mesh):
    return jax.shard_map(
        on_device,
        mesh=mesh,
        in_specs=(
            P(("parts", "fsdp"), "ctx", None, "seq"),
            P("fsdp", "seq"),
            P(("parts", "fsdp"), "seq"),
            P(("parts", "fsdp"), "seq"),
            P("seq", None),
            P(("parts", "fsdp"), "ctx", None, "seq"),
            P(("parts", "fsdp"), "ctx", None, "seq"),
        ),
        out_specs=(P(("parts", "fsdp"), "seq"), P(("parts", "fsdp"), "seq")),
        check_vma=False,
    )
```

time: 844 us -> 268 us (0.32)
  waiting for transfers between devices: 629 us -> 166 us
  other arithmetic: 84.2 us -> 31.9 us
  matrix products: 71.8 us -> 24.4 us
  blocking collectives: 27.1 us -> 0 us
    all_gather x2, waiting for transfers between devices: 561 us -> 66.2 us  [the longest x1 36.2 us: on_device(): d_all = lax.all_gather(d_proj, 'fsdp', axis=0, tiled=True)]
    unnamed x5, waiting for transfers between devices: 1.83 us -> 62.3 us
    dot_general x8 -> x2, matrix products: 71.8 us -> 24.4 us  [the longest x1 15.7 us: on_device(): lax.dot_general(inputs, d_all, (((0,), (0,)), ((), ())), preferred_elemen...]
    reduce_scatter x2 -> x0, waiting for transfers between devices: 40.3 us -> none  [the longest x1 22.1 us: on_device(): lax.psum_scatter(grad_low_all, 'fsdp', scatter_dimension=0, tiled=True)]
    reduce_max x8 -> x1, other arithmetic: 45.6 us -> 5.68 us  [soft_clip(): amax = jnp.max(jnp.abs(blocks), axis=1) + 1e-06]
    all_gather x2 -> x0, blocking collectives: 27.1 us -> none  [the longest x1 13.8 us: on_device(): lax.all_gather(clip_lower, 'fsdp', axis=0, tiled=True)]
    convert_element_type x5 -> x1, other arithmetic: 35.4 us -> 8.78 us  [on_device(): quant = soft_clip(values, clip_upper, clip_lower).astype(jnp.bfloat16)]
    all_to_all x0 -> x1, waiting for transfers between devices: none -> 17.8 us  [on_device(): mine = lax.all_to_all(pieces, 'fsdp', 0, 0)]
  transfers between devices with their start and end apart: 7 -> 7, of which waited for: 7 -> 6; matrix products, arithmetic and copies ran while one was open for 0% -> 7% of each run, Pallas kernels for 0% -> 0%
where the time goes in v1:
time: 268 us; the launch traced here: 267 us
  waiting for transfers between devices  166 us (62%)
  other arithmetic  31.9 us (12%)
  matrix products  24.4 us (9%)
  local copies, waits for them, and re-layouts  20.3 us (8%)
  between operations  13.9 us (5%)
  starting transfers between devices  9.99 us (4%)
    unnamed x5, waiting for transfers between devices  62.3 us
    all_gather x1, waiting for transfers between devices, on_device(): d_all = lax.all_gather(d_proj, 'fsdp', axis=0, tiled=True)  36.2 us
    all_gather x1, waiting for transfers between devices, on_device(): features = lax.all_gather(local_rows, 'seq', axis=1, tiled=True)  30 us
    psum x1, waiting for transfers between devices, on_device(): grad_upper, grad_lower = lax.psum((grad_up, grad_low), 'ctx')  19.3 us
    all_to_all x1, waiting for transfers between devices, on_device(): mine = lax.all_to_all(pieces, 'fsdp', 0, 0)  17.8 us
    dot_general x1, matrix products, on_device(): lax.dot_general(inputs, d_all, (((0,), (0,)), ((), ())), preferred_elemen...  15.7 us
    unnamed x16, local copies, waits for them, and re-layouts  11.4 us
    convert_element_type x1, other arithmetic, on_device(): d_proj = d_proj.astype(jnp.bfloat16)  9.62 us
  transfers between devices with their start and end apart: 7, of which 6 were waited for; matrix products, arithmetic and copies ran while one was open for 7% of the time, Pallas kernels for 0%

profile of v1, /device:TPU:9, one launch (start us, length us, event | category | flops | bytes accessed | tf_op | source)
XLA Modules:
  0.0 266.8 jit_solution(9266589008034086142)
XLA Ops:
  7.2 0.7 all-gather.6.cloned.1.call-update
  7.9 30.0 %all-gather.6.cloned.1.call-done = bf16[1,1,96,8192]{3,2,1,0:T(8,128)(2,1)} async-done(((bf16[1,1,96,4096]{3,2,1,0:T(8,128)(2,1)}), bf16[1,1,96,8192]{3,2,1,0:T(8,128)(2,1)}) %all-gather.6.cloned.1.call-update) | async-done | bytes 1572880 | tf_op jit(solution)/shard_map/all_gather | solution.py:35
  37.9 2.9 %reshape.56 = bf16[96,4,2048]{2,1,0:T(4,128)(2,1)S(1)} reshape(bf16[1,1,96,8192]{3,2,1,0:T(8,128)(2,1)} %all-gather.6.cloned.1.call-done) | data formatting | bytes 3145728 | tf_op jit(solution)/shard_map/reshape | solution.py:36
  40.8 2.1 copy.18
  42.9 4.6 %all-to-all-start = ((bf16[4,96,2048]{2,1,0:T(8,128)(2,1)}), bf16[4,96,2048]{2,1,0:T(8,128)(2,1)S(1)}, u32[]{:S(2)}, u32[]{:S(2)}) async-start(bf16[4,96,2048]{2,1,0:T(8,128)(2,1)} %copy.18), calls=%async_computation | async-start | bytes 3145728 | tf_op jit(solution)/shard_map/all_to_all | solution.py:37
  47.5 5.7 %abs_reduce_fusion = f32[16,2048]{1,0:T(8,128)S(1)} fusion(bf16[2048,2048]{1,0:T(8,128)(2,1)} %param.8), kind=kLoop, calls=%fused_computation.11 | loop fusion | flops 12550144 | bytes 8519680 | tf_op jit(solution)/shard_map/reduce_max | solution.py:20
  53.2 0.8 multiply_divide_fusion
  54.0 8.8 %fusion = bf16[2048,2048]{1,0:T(8,128)(2,1)} fusion(bf16[2048,2048]{1,0:T(8,128)(2,1)} %param.8, f32[16,2048]{1,0:T(8,128)S(1)} %get-tuple-element.9, f32[16,2048]{1,0:T(8,128)S(1)} %get-tuple-element.12), kind=kLoop, calls=%fused_computation.4 | loop fusion | flops 25165824 | bytes 17039360 | tf_op jit(solution)/shard_map/convert_element_type | solution.py:41
  62.7 17.8 %all-to-all-done = bf16[4,96,2048]{2,1,0:T(8,128)(2,1)S(1)} async-done(((bf16[4,96,2048]{2,1,0:T(8,128)(2,1)}), bf16[4,96,2048]{2,1,0:T(8,128)(2,1)S(1)}, u32[]{:S(2)}, u32[]{:S(2)}) %all-to-all-start) | async-done | bytes 1572896 | tf_op jit(solution)/shard_map/all_to_all | solution.py:37
  80.5 8.7 %convolution_bitcast_fusion = f32[384,2048]{0,1:T(8,128)} fusion(bf16[2048,2048]{1,0:T(8,128)(2,1)} %fusion, bf16[384,2048]{1,0:T(8,128)(2,1)S(1)} %bitcast.73), kind=kOutput, calls=%fused_computation.13 | convolution fusion | flops 3221225472 | bytes 13107200 | tf_op jit(solution)/shard_map/dot_general | solution.py:42
  89.3 3.6 %copy.23 = f32[384,2048]{1,0:T(8,128)} copy(f32[384,2048]{0,1:T(8,128)} %convolution_bitcast_fusion) | data formatting | bytes 6291456
  93.1 0.3 reshape.53
  93.4 61.5 %reduce-scatter.4.cloned.1.call-done = f32[96,2048]{1,0:T(8,128)} async-done(((f32[384,2048]{1,0:T(8,128)}), f32[96,2048]{1,0:T(8,128)}) %reduce-scatter.4.cloned.1.call-update) | async-done | bytes 786448
  154.9 1.4 copy.24
  156.5 1.3 collective-permute-start
  157.8 0.6 fusion.26
  158.5 1.3 copy.19
  159.8 2.0 copy.17
  161.8 1.3 maximum_convert_fusion
  163.1 4.9 %convert_multiply_fusion = f32[96,2048]{0,1:T(8,128)S(1)} fusion(f32[102,2048]{0,1:T(8,128)S(1)} %maximum_convert_fusion, bf16[1,1,96,2048]{2,3,1,0:T(8,128)(2,1)S(1)} %copy.19, bf16[1,1,96,2048]{2,3,1,0:T(8,128)(2,1)} %copy.17, f32[2048]{0:T(1024)S(1)} %bitcast.79, f32[2048]{0:T(1024)} %bitcast.81, f32[2048]{0:T(1024)} %bitcast.83, f32[2048]{0:T(1024)} %bitcast.85, ...), kind=kLoop, calls=%fused_computation.14 | loop fusion | flops 3735552 | bytes 7135232 | tf_op jit(solution)/shard_map/mul | solution.py:56
  168.0 0.3 copy.20
  168.3 4.0 %collective-permute-start.1 = (f32[6,2048]{1,0:T(8,128)S(1)}, f32[6,2048]{1,0:T(8,128)S(1)}, u32[]{:S(2)}, u32[]{:S(2)}) collective-permute-start(f32[6,2048]{1,0:T(8,128)S(1)} %copy.20), channel_id=1, source_target_pairs={{1,0},{3,2},{5,4},{7,6},{9,8},{11,10},{13,12},{15,14},{17,16},{19,... | collective-permute-start | bytes 147464 | tf_op jit(solution)/shard_map/ppermute | solution.py:13
  172.4 0.7 collective-permute-done.1
  173.1 1.3 copy.21
  174.4 9.6 %fusion.6 = bf16[96,2048]{0,1:T(8,128)(2,1)S(1)} fusion(f32[6,2048]{0,1:T(8,128)} %copy.21, f32[96,2048]{0,1:T(8,128)S(1)} %convert_multiply_fusion, f32[2048]{0:T(1024)S(1)} %bitcast.80, f32[2048]{0:T(1024)} %bitcast.82, f32[2048]{0:T(1024)} %bitcast.84, f32[2048]{0:T(1024)} %bitcast.86, f32[2048]{0:T(1024)} %bitcast.88, f32[2048]{0:T(1024)} %bitcast.90, ...), kind=kLoop, calls=%fused_computation.21 | loop fusion | flops 3932160 | bytes 1286144 | tf_op jit(solution)/shard_map/convert_element_type | solution.py:62
  184.0 1.0 copy.22
  185.1 36.2 %all-gather.4.cloned.1.call-done = bf16[384,2048]{1,0:T(8,128)(2,1)} async-done(((bf16[96,2048]{1,0:T(8,128)(2,1)}), bf16[384,2048]{1,0:T(8,128)(2,1)}) %all-gather.4.cloned.1.call-update) | async-done | bytes 1572880 | tf_op jit(solution)/shard_map/all_gather | solution.py:64
  221.3 15.7 %divide_reduce_fusion = (f32[16,2048]{1,0:T(8,128)S(1)}, f32[16,2048]{1,0:T(8,128)S(1)}, f32[16,2048]{1,0:T(8,128)S(1)}, f32[16,2048]{1,0:T(8,128)S(1)}) fusion(f32[16,2048]{1,0:T(8,128)S(1)} %get-tuple-element.9, f32[16,2048]{1,0:T(8,128)S(1)} %get-tuple-element.12, bf16[2048,2048]{1,0:T(8,128)(2,1)} %param.8, f32[16,2048]{1,0:T(8,128)} %get-tuple-element.8, ...), kind=kOutput, calls=%fused_computation.12 | convolution fusion | flops 3288203264 | bytes 12451840 | tf_op jit(solution)/shard_map/dot_general | solution.py:65
  237.0 0.8 fusion.25
  237.9 19.3 %all-reduce.3.cloned.1.call-done = (f32[16,2048]{1,0:T(8,128)}, f32[16,2048]{1,0:T(8,128)}) async-done(((f32[16,2048]{1,0:T(8,128)}, f32[16,2048]{1,0:T(8,128)}), (f32[16,2048]{1,0:T(8,128)}, f32[16,2048]{1,0:T(8,128)})) %all-reduce.3.cloned.1.call-update) | async-done | bytes 262160 | tf_op jit(solution)/shard_map/psum | solution.py:74
  257.2 1.6 copy.27
  258.7 1.6 copy.28
  (20 shorter events, 0.6 us)
Async XLA Ops:
  7.2 30.8 %all-gather.6.cloned.1.call-start = ((), (), s32[]{:S(2)}) async-start(), calls=%async_computation.3 | async-start | bytes 2359296 | tf_op jit(solution)/shard_map/all_gather | solution.py:35
  7.9 45.3 %copy-start = (f32[16,2048]{1,0:T(8,128)S(1)}, f32[16,2048]{1,0:T(8,128)}, u32[]{:S(2)}) copy-start(f32[16,2048]{1,0:T(8,128)} %param.10) | copy-start | bytes 393220
  7.9 45.3 %copy-start.2 = (f32[16,2048]{1,0:T(8,128)S(1)}, f32[16,2048]{1,0:T(8,128)}, u32[]{:S(2)}) copy-start(f32[16,2048]{1,0:T(8,128)} %param.9) | copy-start | bytes 393220
  42.9 37.6 %all-to-all-start = ((bf16[4,96,2048]{2,1,0:T(8,128)(2,1)}), bf16[4,96,2048]{2,1,0:T(8,128)(2,1)S(1)}, u32[]{:S(2)}, u32[]{:S(2)}) async-start(bf16[4,96,2048]{2,1,0:T(8,128)(2,1)} %copy.18), calls=%async_computation | async-start | bytes 3145728 | tf_op jit(solution)/shard_map/all_to_all | solution.py:37
  47.5 107.4 %reduce-scatter.4.cloned.1.call-start = ((), (), s32[]{:S(2)}) async-start(), calls=%async_computation.4 | async-start | bytes 3932160
  89.3 3.7 %copy-start.4 = (f32[128,7]{0,1:T(8,128)S(1)}, f32[128,7]{0,1:T(8,128)}, u32[]{:S(2)}) copy-start(f32[128,7]{0,1:T(8,128)} %param.11) | copy-start | bytes 10756
  92.9 128.4 %all-gather.4.cloned.1.call-start = ((), (), s32[]{:S(2)}) async-start(), calls=%async_computation.2 | async-start | bytes 1966080 | tf_op jit(solution)/shard_map/all_gather | solution.py:64
  156.5 5.2 %collective-permute-start = (bf16[6,2048]{0,1:T(8,128)(2,1)S(1)}, bf16[6,2048]{0,1:T(8,128)(2,1)}, u32[]{:S(2)}, u32[]{:S(2)}) collective-permute-start(bf16[6,2048]{0,1:T(8,128)(2,1)S(1)} %slice.96), channel_id=1, source_target_pairs={{0,1},{2,3},{4,5},{6,7},{8,9},{10,11},{12,13},{14,15},{16,17},{18,... | collective-permute-start | bytes 73736 | tf_op jit(solution)/shard_map/ppermute | solution.py:13
  168.3 4.7 %collective-permute-start.1 = (f32[6,2048]{1,0:T(8,128)S(1)}, f32[6,2048]{1,0:T(8,128)S(1)}, u32[]{:S(2)}, u32[]{:S(2)}) collective-permute-start(f32[6,2048]{1,0:T(8,128)S(1)} %copy.20), channel_id=1, source_target_pairs={{1,0},{3,2},{5,4},{7,6},{9,8},{11,10},{13,12},{15,14},{17,16},{19,... | collective-permute-start | bytes 147464 | tf_op jit(solution)/shard_map/ppermute | solution.py:13
  184.0 53.0 %copy-start.1 = (f32[16,2048]{1,0:T(8,128)S(1)}, f32[16,2048]{1,0:T(8,128)}, u32[]{:S(2)}) copy-start(f32[16,2048]{1,0:T(8,128)} %param.10) | copy-start | bytes 393220
  184.0 53.0 %copy-start.3 = (f32[16,2048]{1,0:T(8,128)S(1)}, f32[16,2048]{1,0:T(8,128)}, u32[]{:S(2)}) copy-start(f32[16,2048]{1,0:T(8,128)} %param.9) | copy-start | bytes 393220
  185.0 72.1 %all-reduce.3.cloned.1.call-start = ((), (), s32[]{:S(2)}) async-start(), calls=%async_computation.5 | async-start | bytes 524288 | tf_op jit(solution)/shard_map/psum | solution.py:74
Sparse Core Ops, SparseCore 0:
  9.5 28.3 all-gather.5
  93.0 61.8 reduce-scatter.3
  185.2 36.0 all-gather.3
  238.0 19.1 all-reduce.2

commit v2 on v1

--- a/solution.py
+++ b/solution.py
@@ -26,13 +26,33 @@
     return clipped.reshape(rows, values.shape[1])
 
 
+def gather_features(local_rows):
+    devices = lax.axis_size("seq")
+    if devices != 2:
+        return lax.all_gather(local_rows, "seq", axis=1, tiled=True)
+    other = lax.ppermute(local_rows, "seq", [(0, 1), (1, 0)])
+    first = lax.axis_index("seq") == 0
+    return jnp.where(
+        first,
+        jnp.concatenate([local_rows, other], axis=1),
+        jnp.concatenate([other, local_rows], axis=1),
+    )
+
+
+def sum_over_ctx(value):
+    devices = lax.axis_size("ctx")
+    if devices != 2:
+        return lax.psum(value, "ctx")
+    return value + lax.ppermute(value, "ctx", [(0, 1), (1, 0)])
+
+
 def on_device(hidden_in, weight, clip_upper, clip_lower, filters, gate, target):
     shards = lax.axis_size("fsdp")
     width = hidden_in.shape[-1]
     local_rows = hidden_in.reshape(-1, width)
     length = local_rows.shape[0]
     rows, columns = weight.shape
-    features = lax.all_gather(local_rows, "seq", axis=1, tiled=True)
+    features = gather_features(local_rows)
     pieces = features.reshape(length, shards, rows).transpose(1, 0, 2)
     mine = lax.all_to_all(pieces, "fsdp", 0, 0)
     inputs = mine.reshape(shards * length, rows)
@@ -40,7 +60,8 @@
     values = weight.astype(jnp.float32)
     quant = soft_clip(values, clip_upper, clip_lower).astype(jnp.bfloat16)
     partial = jnp.dot(inputs, quant, preferred_element_type=jnp.float32)
-    proj = lax.psum_scatter(partial, "fsdp", scatter_dimension=0, tiled=True).astype(jnp.bfloat16)
+    received = lax.all_to_all(partial.reshape(shards, length, columns), "fsdp", 0, 0)
+    proj = jnp.sum(received, axis=0).astype(jnp.bfloat16)
 
     taps = jnp.repeat(filters, CGROUP, axis=0).T
     pad = FILT - 1
@@ -61,7 +82,8 @@
         d_proj = d_proj + taps[tap] * padded_back[tap : tap + length]
     d_proj = d_proj.astype(jnp.bfloat16)
 
-    d_all = lax.all_gather(d_proj, "fsdp", axis=0, tiled=True)
+    copies = jnp.broadcast_to(d_proj[None], (shards, length, columns))
+    d_all = lax.all_to_all(copies, "fsdp", 0, 0).reshape(shards * length, columns)
     d_clipped = lax.dot_general(
         inputs, d_all, (((0,), (0,)), ((), ())), preferred_element_type=jnp.float32
     )
@@ -71,7 +93,7 @@
         clip_lower,
     )
     grad_up, grad_low = pull(d_clipped)
-    grad_upper, grad_lower = lax.psum((grad_up, grad_low), "ctx")
+    grad_upper, grad_lower = sum_over_ctx(grad_up), sum_over_ctx(grad_low)
     return (grad_upper, grad_lower)
 
 

time: 268 us -> 217 us (0.81)
  the two profiles are of different devices: /device:TPU:9 before, /device:TPU:0 now
where the time goes in v2:
time: 217 us
  waiting for transfers between devices  141 us (65%)
  matrix products  24.5 us (11%)
  other arithmetic  21.2 us (10%)
  starting transfers between devices  18.8 us (9%)
  local copies, waits for them, and re-layouts  10.7 us (5%)
    all_to_all x1, waiting for transfers between devices, on_device(): lax.all_to_all(partial.reshape(shards, length, columns), 'fsdp', 0, 0)  67.3 us
    all_to_all x1, waiting for transfers between devices, on_device(): lax.all_to_all(copies, 'fsdp', 0, 0).reshape(shards * length, columns)  35.7 us
    all_to_all x1, waiting for transfers between devices, on_device(): mine = lax.all_to_all(pieces, 'fsdp', 0, 0)  20.1 us
    dot_general x1, matrix products, on_device(): lax.dot_general(inputs, d_all, (((0,), (0,)), ((), ())), preferred_elemen...  15.4 us
    ppermute x1, waiting for transfers between devices, gather_features(): other = lax.ppermute(local_rows, 'seq', [(0, 1), (1, 0)])  14.9 us
    dot_general x1, matrix products, on_device(): partial = jnp.dot(inputs, quant, preferred_element_type=jnp.float32)  9.07 us
    convert_element_type x1, other arithmetic, on_device(): quant = soft_clip(values, clip_upper, clip_lower).astype(jnp.bfloat16)  8.78 us
    reduce_max x1, other arithmetic, soft_clip(): amax = jnp.max(jnp.abs(blocks), axis=1) + 1e-06  5.69 us
  transfers between devices with their start and end apart: 8, of which 6 were waited for; matrix products, arithmetic and copies ran while one was open for 11% of the time, Pallas kernels for 0%

profile of v2, /device:TPU:0, one launch (start us, length us, event | category | flops | bytes accessed | tf_op | source)
XLA Modules:
  0.0 216.8 jit_solution(14906956188752368809)
XLA Ops:
  0.6 3.0 %collective-permute-start = (bf16[96,4096]{1,0:T(8,128)(2,1)}, bf16[96,4096]{1,0:T(8,128)(2,1)S(1)}, u32[]{:S(2)}, u32[]{:S(2)}) collective-permute-start(bf16[96,4096]{1,0:T(8,128)(2,1)} %bitcast.76), channel_id=1, source_target_pairs={{0,2},{2,0},{1,3},{3,1},{4,6},{6,4},{5,7},{7,5},{8,10},{10,8},{9,1... | collective-permute-start | bytes 2359304 | tf_op jit(solution)/shard_map/ppermute | solution.py:33
  3.6 2.6 %concatenate.18 = bf16[96,2,2048]{2,1,0:T(2,128)(2,1)S(1)} reshape(bf16[1,1,96,4096]{3,2,1,0:T(8,128)(2,1)} %param.7) | data formatting | bytes 1572864 | tf_op jit(solution)/shard_map/concatenate | solution.py:37
  6.2 0.2 copy.16
  6.5 14.9 %collective-permute-done = bf16[96,4096]{1,0:T(8,128)(2,1)S(1)} collective-permute-done((bf16[96,4096]{1,0:T(8,128)(2,1)}, bf16[96,4096]{1,0:T(8,128)(2,1)S(1)}, u32[]{:S(2)}, u32[]{:S(2)}) %collective-permute-start) | collective-permute-done | bytes 786464 | tf_op jit(solution)/shard_map/ppermute | solution.py:33
  21.4 1.4 fusion.4
  22.9 5.1 %all-to-all-start = ((bf16[4,96,2048]{2,1,0:T(8,128)(2,1)}), bf16[4,96,2048]{2,1,0:T(8,128)(2,1)S(1)}, u32[]{:S(2)}, u32[]{:S(2)}) async-start(bf16[4,96,2048]{2,1,0:T(8,128)(2,1)} %fusion.4), calls=%async_computation | async-start | bytes 3145728 | tf_op jit(solution)/shard_map/all_to_all | solution.py:57
  28.0 5.7 %abs_reduce_fusion = f32[16,2048]{1,0:T(8,128)S(1)} fusion(bf16[2048,2048]{1,0:T(8,128)(2,1)} %param.8), kind=kLoop, calls=%fused_computation.10 | loop fusion | flops 12550144 | bytes 8519680 | tf_op jit(solution)/shard_map/reduce_max | solution.py:20
  33.7 0.8 multiply_divide_fusion
  34.5 0.6 copy-done.4
  35.2 8.8 %fusion = bf16[2048,2048]{1,0:T(8,128)(2,1)} fusion(bf16[2048,2048]{1,0:T(8,128)(2,1)} %param.8, f32[16,2048]{1,0:T(8,128)S(1)} %get-tuple-element.7, f32[16,2048]{1,0:T(8,128)S(1)} %get-tuple-element.10), kind=kLoop, calls=%fused_computation.4 | loop fusion | flops 25165824 | bytes 17039360 | tf_op jit(solution)/shard_map/convert_element_type | solution.py:61
  44.0 20.1 %all-to-all-done = bf16[4,96,2048]{2,1,0:T(8,128)(2,1)S(1)} async-done(((bf16[4,96,2048]{2,1,0:T(8,128)(2,1)}), bf16[4,96,2048]{2,1,0:T(8,128)(2,1)S(1)}, u32[]{:S(2)}, u32[]{:S(2)}) %all-to-all-start) | async-done | bytes 1572896 | tf_op jit(solution)/shard_map/all_to_all | solution.py:57
  64.1 9.1 %fusion.2 = f32[4,96,2048]{2,1,0:T(8,128)} fusion(bf16[4,96,2048]{2,1,0:T(8,128)(2,1)S(1)} %all-to-all-done, bf16[2048,2048]{1,0:T(8,128)(2,1)} %fusion), kind=kOutput, calls=%fused_computation.12 | convolution fusion | flops 3221225472 | bytes 13107200 | tf_op jit(solution)/shard_map/dot_general | solution.py:62
  73.2 3.7 %all-to-all-start.1 = ((f32[4,96,2048]{2,1,0:T(8,128)}), f32[4,96,2048]{2,1,0:T(8,128)S(1)}, u32[]{:S(2)}, u32[]{:S(2)}) async-start(f32[4,96,2048]{2,1,0:T(8,128)} %fusion.2), calls=%async_computation.1 | async-start | bytes 6291456 | tf_op jit(solution)/shard_map/all_to_all | solution.py:63
  76.9 1.0 broadcast_in_dim.4
  77.8 1.9 reshape.65
  79.7 67.3 %all-to-all-done.1 = f32[4,96,2048]{2,1,0:T(8,128)S(1)} async-done(((f32[4,96,2048]{2,1,0:T(8,128)}), f32[4,96,2048]{2,1,0:T(8,128)S(1)}, u32[]{:S(2)}, u32[]{:S(2)}) %all-to-all-start.1) | async-done | bytes 3145760 | tf_op jit(solution)/shard_map/all_to_all | solution.py:63
  147.0 0.3 reduce_sum.43
  147.3 1.4 collective-permute-start.1
  148.7 1.2 fusion.33
  150.1 2.0 convert_multiply_fusion
  152.1 1.3 collective-permute-start.2
  153.4 1.8 collective-permute-done.2
  155.2 0.7 fusion.11
  155.9 1.3 broadcast_in_dim.5
  157.3 3.7 %all-to-all-start.2 = ((bf16[4,96,2048]{2,1,0:T(8,128)(2,1)}), bf16[4,96,2048]{2,1,0:T(8,128)(2,1)S(1)}, u32[]{:S(2)}, u32[]{:S(2)}) async-start(bf16[4,96,2048]{2,1,0:T(8,128)(2,1)} %broadcast_in_dim.5), calls=%async_computation.2 | async-start | bytes 3145728 | tf_op jit(solution)/shard_map/all_to_all | solution.py:86
  161.1 1.6 copy.20
  162.7 35.7 %all-to-all-done.2 = bf16[4,96,2048]{2,1,0:T(8,128)(2,1)S(1)} async-done(((bf16[4,96,2048]{2,1,0:T(8,128)(2,1)}), bf16[4,96,2048]{2,1,0:T(8,128)(2,1)S(1)}, u32[]{:S(2)}, u32[]{:S(2)}) %all-to-all-start.2) | async-done | bytes 1572896 | tf_op jit(solution)/shard_map/all_to_all | solution.py:86
  198.4 15.4 %divide_reduce_fusion = (f32[16,2048]{1,0:T(8,128)S(1)}, f32[16,2048]{1,0:T(8,128)S(1)}, f32[16,2048]{1,0:T(8,128)S(1)}, f32[16,2048]{1,0:T(8,128)S(1)}) fusion(f32[16,2048]{1,0:T(8,128)S(1)} %copy-done.5, f32[16,2048]{1,0:T(8,128)S(1)} %copy-done.7, bf16[2048,2048]{1,0:T(8,128)(2,1)} %param.8, f32[16,2048]{1,0:T(8,128)S(1)} %copy-done.12, ...), kind=kOutput, calls=%fused_computation.11 | convolution fusion | flops 3288203264 | bytes 12451840 | tf_op jit(solution)/shard_map/dot_general | solution.py:87
  214.1 0.5 collective-permute-start.3
  214.6 0.8 collective-permute-done.4
  215.4 0.7 add.93
  216.1 0.7 add.92
  (35 shorter events, 0.5 us)
Async XLA Ops:
  0.6 20.8 %collective-permute-start = (bf16[96,4096]{1,0:T(8,128)(2,1)}, bf16[96,4096]{1,0:T(8,128)(2,1)S(1)}, u32[]{:S(2)}, u32[]{:S(2)}) collective-permute-start(bf16[96,4096]{1,0:T(8,128)(2,1)} %bitcast.76), channel_id=1, source_target_pairs={{0,2},{2,0},{1,3},{3,1},{4,6},{6,4},{5,7},{7,5},{8,10},{10,8},{9,1... | collective-permute-start | bytes 2359304 | tf_op jit(solution)/shard_map/ppermute | solution.py:33
  6.5 27.2 %copy-start.8 = (f32[16,2048]{1,0:T(8,128)S(1)}, f32[16,2048]{1,0:T(8,128)}, u32[]{:S(2)}) copy-start(f32[16,2048]{1,0:T(8,128)} %param.10) | copy-start | bytes 393220
  6.5 27.2 %copy-start.10 = (f32[16,2048]{1,0:T(8,128)S(1)}, f32[16,2048]{1,0:T(8,128)}, u32[]{:S(2)}) copy-start(f32[16,2048]{1,0:T(8,128)} %param.9) | copy-start | bytes 393220
  22.9 41.2 %all-to-all-start = ((bf16[4,96,2048]{2,1,0:T(8,128)(2,1)}), bf16[4,96,2048]{2,1,0:T(8,128)(2,1)S(1)}, u32[]{:S(2)}, u32[]{:S(2)}) async-start(bf16[4,96,2048]{2,1,0:T(8,128)(2,1)} %fusion.4), calls=%async_computation | async-start | bytes 3145728 | tf_op jit(solution)/shard_map/all_to_all | solution.py:57
  33.7 0.8 copy-start.2
  34.5 0.6 copy-start.4
  34.5 0.7 copy-start.6
  44.0 32.9 %copy-start.13 = (f32[128,7]{0,1:T(8,128)S(1)}, f32[128,7]{0,1:T(8,128)}, u32[]{:S(2)}) copy-start(f32[128,7]{0,1:T(8,128)} %param.11) | copy-start | bytes 10756
  64.1 9.1 %copy-start = (bf16[4,96,2048]{2,1,0:T(8,128)(2,1)}, bf16[4,96,2048]{2,1,0:T(8,128)(2,1)S(1)}, u32[]{:S(2)}) copy-start(bf16[4,96,2048]{2,1,0:T(8,128)(2,1)S(1)} %all-to-all-done) | copy-start | bytes 4718596
  73.2 73.8 %all-to-all-start.1 = ((f32[4,96,2048]{2,1,0:T(8,128)}), f32[4,96,2048]{2,1,0:T(8,128)S(1)}, u32[]{:S(2)}, u32[]{:S(2)}) async-start(f32[4,96,2048]{2,1,0:T(8,128)} %fusion.2), calls=%async_computation.1 | async-start | bytes 6291456 | tf_op jit(solution)/shard_map/all_to_all | solution.py:63
  147.3 13.8 %copy-start.1 = (bf16[4,96,2048]{2,1,0:T(8,128)(2,1)S(1)}, bf16[4,96,2048]{2,1,0:T(8,128)(2,1)}, u32[]{:S(2)}) copy-start(bf16[4,96,2048]{2,1,0:T(8,128)(2,1)} %copy-done) | copy-start | bytes 4718596
  147.3 2.7 %collective-permute-start.1 = (bf16[6,2048]{1,0:T(8,128)(2,1)S(1)}, bf16[6,2048]{1,0:T(8,128)(2,1)S(1)}, u32[]{:S(2)}, u32[]{:S(2)}) collective-permute-start(bf16[6,2048]{1,0:T(8,128)(2,1)S(1)} %slice.96), channel_id=1, source_target_pairs={{0,1},{2,3},{4,5},{6,7},{8,9},{10,11},{12,13},{14,15},{16,17},{18,... | collective-permute-start | bytes 73736 | tf_op jit(solution)/shard_map/ppermute | solution.py:13
  150.1 48.3 %copy-start.5 = (f32[16,2048]{1,0:T(8,128)S(1)}, f32[16,2048]{1,0:T(8,128)}, u32[]{:S(2)}) copy-start(f32[16,2048]{1,0:T(8,128)} %copy-done.4) | copy-start | bytes 393220
  150.1 48.3 %copy-start.7 = (f32[16,2048]{1,0:T(8,128)S(1)}, f32[16,2048]{1,0:T(8,128)}, u32[]{:S(2)}) copy-start(f32[16,2048]{1,0:T(8,128)} %copy-done.6) | copy-start | bytes 393220
  150.1 48.3 %copy-start.12 = (f32[16,2048]{1,0:T(8,128)S(1)}, f32[16,2048]{1,0:T(8,128)}, u32[]{:S(2)}) copy-start(f32[16,2048]{1,0:T(8,128)} %get-tuple-element.6) | copy-start | bytes 393220
  152.1 3.1 %collective-permute-start.2 = (f32[6,2048]{1,0:T(8,128)S(1)}, f32[6,2048]{1,0:T(8,128)S(1)}, u32[]{:S(2)}, u32[]{:S(2)}) collective-permute-start(f32[6,2048]{1,0:T(8,128)S(1)} %slice.110), channel_id=1, source_target_pairs={{1,0},{3,2},{5,4},{7,6},{9,8},{11,10},{13,12},{15,14},{17,16},{19,... | collective-permute-start | bytes 147464 | tf_op jit(solution)/shard_map/ppermute | solution.py:13
  157.3 41.1 %all-to-all-start.2 = ((bf16[4,96,2048]{2,1,0:T(8,128)(2,1)}), bf16[4,96,2048]{2,1,0:T(8,128)(2,1)S(1)}, u32[]{:S(2)}, u32[]{:S(2)}) async-start(bf16[4,96,2048]{2,1,0:T(8,128)(2,1)} %broadcast_in_dim.5), calls=%async_computation.2 | async-start | bytes 3145728 | tf_op jit(solution)/shard_map/all_to_all | solution.py:86
  198.4 15.4 %copy-start.3 = (f32[16,2048]{1,0:T(8,128)S(1)}, f32[16,2048]{1,0:T(8,128)}, u32[]{:S(2)}) copy-start(f32[16,2048]{1,0:T(8,128)} %copy-done.2) | copy-start | bytes 393220
  198.4 15.4 %copy-start.9 = (f32[16,2048]{1,0:T(8,128)S(1)}, f32[16,2048]{1,0:T(8,128)}, u32[]{:S(2)}) copy-start(f32[16,2048]{1,0:T(8,128)} %param.10) | copy-start | bytes 393220
  198.4 15.4 %copy-start.11 = (f32[16,2048]{1,0:T(8,128)S(1)}, f32[16,2048]{1,0:T(8,128)}, u32[]{:S(2)}) copy-start(f32[16,2048]{1,0:T(8,128)} %param.9) | copy-start | bytes 393220
  214.0 1.4 collective-permute-start.4
  214.1 2.0 collective-permute-start.3

commit v3 on v2

--- a/solution.py
+++ b/solution.py
@@ -46,6 +46,48 @@
     return value + lax.ppermute(value, "ctx", [(0, 1), (1, 0)])
 
 
+def line_reduce_scatter(partial_for, axis):
+    devices = lax.axis_size(axis)
+    me = lax.axis_index(axis)
+    right = left = None
+    for step in range(1, devices):
+        term = partial_for(jnp.minimum(me + devices - step, devices - 1))
+        if right is not None:
+            term = right + term
+        pairs = [(i, i + 1) for i in range(0, min(step - 1, devices - 2) + 1)]
+        right = lax.ppermute(term, axis, pairs)
+        term = partial_for(jnp.maximum(me - devices + step, 0))
+        if left is not None:
+            term = left + term
+        pairs = [(i, i - 1) for i in range(max(devices - step, 1), devices)]
+        left = lax.ppermute(term, axis, pairs)
+    own = partial_for(me)
+    if right is None:
+        return own
+    return own + right + left
+
+
+def line_all_gather(value, axis):
+    devices = lax.axis_size(axis)
+    me = lax.axis_index(axis)
+    gathered = jnp.zeros((devices,) + value.shape, value.dtype)
+    gathered = lax.dynamic_update_index_in_dim(gathered, value, me, 0)
+    right = left = value
+
+    def place(gathered, block, origin):
+        valid = (origin >= 0) & (origin < devices)
+        at = jnp.clip(origin, 0, devices - 1)
+        held = lax.dynamic_index_in_dim(gathered, at, 0, keepdims=False)
+        return lax.dynamic_update_index_in_dim(gathered, jnp.where(valid, block, held), at, 0)
+
+    for step in range(1, devices):
+        right = lax.ppermute(right, axis, [(i, i + 1) for i in range(step - 1, devices - 1)])
+        left = lax.ppermute(left, axis, [(i, i - 1) for i in range(1, devices - step + 1)])
+        gathered = place(gathered, right, me - step)
+        gathered = place(gathered, left, me + step)
+    return gathered
+
+
 def on_device(hidden_in, weight, clip_upper, clip_lower, filters, gate, target):
     shards = lax.axis_size("fsdp")
     width = hidden_in.shape[-1]
@@ -59,9 +101,12 @@
 
     values = weight.astype(jnp.float32)
     quant = soft_clip(values, clip_upper, clip_lower).astype(jnp.bfloat16)
-    partial = jnp.dot(inputs, quant, preferred_element_type=jnp.float32)
-    received = lax.all_to_all(partial.reshape(shards, length, columns), "fsdp", 0, 0)
-    proj = jnp.sum(received, axis=0).astype(jnp.bfloat16)
+
+    def partial_for(chunk):
+        block = lax.dynamic_index_in_dim(mine, chunk, 0, keepdims=False)
+        return jnp.dot(block, quant, preferred_element_type=jnp.float32)
+
+    proj = line_reduce_scatter(partial_for, "fsdp").astype(jnp.bfloat16)
 
     taps = jnp.repeat(filters, CGROUP, axis=0).T
     pad = FILT - 1
@@ -82,8 +127,7 @@
         d_proj = d_proj + taps[tap] * padded_back[tap : tap + length]
     d_proj = d_proj.astype(jnp.bfloat16)
 
-    copies = jnp.broadcast_to(d_proj[None], (shards, length, columns))
-    d_all = lax.all_to_all(copies, "fsdp", 0, 0).reshape(shards * length, columns)
+    d_all = line_all_gather(d_proj, "fsdp").reshape(shards * length, columns)
     d_clipped = lax.dot_general(
         inputs, d_all, (((0,), (0,)), ((), ())), preferred_element_type=jnp.float32
     )

time: 217 us -> 214 us (0.986)
  the two profiles are of different devices: /device:TPU:0 before, /device:TPU:9 now
where the time goes in v3:
time: 214 us; the launch traced here: 210 us
  waiting for transfers between devices  92.1 us (43%)
  matrix products  43.4 us (20%)
  starting transfers between devices  38.9 us (18%)
  other arithmetic  26.3 us (12%)
  local copies, waits for them, and re-layouts  7.76 us (4%)
    dot_general x7, matrix products, partial_for(): return jnp.dot(block, quant, preferred_element_type=jnp.float32)  28.5 us
    ppermute x3, waiting for transfers between devices, line_reduce_scatter(): right = lax.ppermute(term, axis, pairs)  28 us
    all_to_all x1, waiting for transfers between devices, on_device(): mine = lax.all_to_all(pieces, 'fsdp', 0, 0)  16.8 us
    dot_general x1, matrix products, on_device(): lax.dot_general(inputs, d_all, (((0,), (0,)), ((), ())), preferred_elemen...  15 us
    ppermute x1, waiting for transfers between devices, gather_features(): other = lax.ppermute(local_rows, 'seq', [(0, 1), (1, 0)])  14.8 us
    ppermute x3, starting transfers between devices, line_all_gather(): lax.ppermute(left, axis, [(i, i - 1) for i in range(1, devices - step + 1)])  11.5 us
    ppermute x3, waiting for transfers between devices, line_reduce_scatter(): left = lax.ppermute(term, axis, pairs)  9.32 us
    ppermute x3, waiting for transfers between devices, line_all_gather(): lax.ppermute(left, axis, [(i, i - 1) for i in range(1, devices - step + 1)])  9.21 us
  transfers between devices with their start and end apart: 18, of which 14 were waited for; matrix products, arithmetic and copies ran while one was open for 22% of the time, Pallas kernels for 0%

profile of v3, /device:TPU:9, one launch (start us, length us, event | category | flops | bytes accessed | tf_op | source)
XLA Modules:
  0.0 209.7 jit_solution(3510488818582670542)
XLA Ops:
  1.9 2.6 %concatenate.18 = bf16[96,2,2048]{2,1,0:T(2,128)(2,1)S(1)} reshape(bf16[1,1,96,4096]{3,2,1,0:T(8,128)(2,1)} %param.7) | data formatting | bytes 1572864 | tf_op jit(solution)/shard_map/concatenate | solution.py:37
  4.5 14.8 %collective-permute-done = bf16[96,4096]{1,0:T(8,128)(2,1)S(1)} collective-permute-done((bf16[96,4096]{1,0:T(8,128)(2,1)}, bf16[96,4096]{1,0:T(8,128)(2,1)S(1)}, u32[]{:S(2)}, u32[]{:S(2)}) %collective-permute-start) | collective-permute-done | bytes 786464 | tf_op jit(solution)/shard_map/ppermute | solution.py:33
  19.9 2.9 %fusion.2 = bf16[4,96,2048]{2,0,1:T(4,128)(2,1)S(1)} fusion(bf16[96,2,2048]{2,1,0:T(2,128)(2,1)S(1)} %concatenate.19, bf16[96,2,2048]{2,1,0:T(2,128)(2,1)S(1)} %concatenate.18, pred[]{:T(512)S(6)} %eq.3), kind=kLoop, calls=%fused_computation.20 | loop fusion | flops 7077888 | bytes 3145729 | tf_op jit(solution)/shard_map/transpose | solution.py:98
  22.8 2.1 copy.14
  24.9 4.8 %all-to-all-start = ((bf16[4,96,2048]{2,1,0:T(8,128)(2,1)}), bf16[4,96,2048]{2,1,0:T(8,128)(2,1)S(1)}, u32[]{:S(2)}, u32[]{:S(2)}) async-start(bf16[4,96,2048]{2,1,0:T(8,128)(2,1)} %copy.14), calls=%async_computation | async-start | bytes 3145728 | tf_op jit(solution)/shard_map/all_to_all | solution.py:99
  29.6 5.7 %abs_reduce_fusion = f32[16,2048]{1,0:T(8,128)S(1)} fusion(bf16[2048,2048]{1,0:T(8,128)(2,1)} %param.8), kind=kLoop, calls=%fused_computation.10 | loop fusion | flops 12550144 | bytes 8519680 | tf_op jit(solution)/shard_map/reduce_max | solution.py:20
  36.1 8.8 %fusion = bf16[2048,2048]{1,0:T(8,128)(2,1)} fusion(bf16[2048,2048]{1,0:T(8,128)(2,1)} %param.8, f32[16,2048]{1,0:T(8,128)S(1)} %get-tuple-element.7, f32[16,2048]{1,0:T(8,128)S(1)} %get-tuple-element.12), kind=kLoop, calls=%fused_computation.4 | loop fusion | flops 25165824 | bytes 17039360 | tf_op jit(solution)/shard_map/convert_element_type | solution.py:103
  45.0 16.8 %all-to-all-done = bf16[4,96,2048]{2,1,0:T(8,128)(2,1)S(1)} async-done(((bf16[4,96,2048]{2,1,0:T(8,128)(2,1)}), bf16[4,96,2048]{2,1,0:T(8,128)(2,1)S(1)}, u32[]{:S(2)}, u32[]{:S(2)}) %all-to-all-start) | async-done | bytes 1572896 | tf_op jit(solution)/shard_map/all_to_all | solution.py:99
  61.8 5.8 %fusion.37 = f32[96,2048]{1,0:T(8,128)} fusion(bf16[2048,2048]{1,0:T(8,128)(2,1)} %fusion, bf16[4,96,2048]{2,1,0:T(8,128)(2,1)S(1)} %all-to-all-done, s32[]{:T(128)S(6)} %select_n.80), kind=kOutput, calls=%fused_computation.83 | convolution fusion | flops 805306368 | bytes 9568260 | tf_op jit(solution)/shard_map/dot_general | solution.py:107
  68.9 4.8 %fusion.32 = f32[96,2048]{1,0:T(8,128)S(1)} fusion(bf16[2048,2048]{1,0:T(8,128)(2,1)} %fusion, bf16[4,96,2048]{2,1,0:T(8,128)(2,1)S(1)} %all-to-all-done, s32[]{:T(128)S(6)} %max.22), kind=kOutput, calls=%fused_computation.78 | convolution fusion | flops 805306368 | bytes 9568260 | tf_op jit(solution)/shard_map/dot_general | solution.py:107
  74.6 15.2 %collective-permute-done.1 = f32[96,2048]{1,0:T(8,128)} collective-permute-done((f32[96,2048]{1,0:T(8,128)}, f32[96,2048]{1,0:T(8,128)}, u32[]{:S(2)}, u32[]{:S(2)}) %collective-permute-start.1) | collective-permute-done | bytes 786464 | tf_op jit(solution)/shard_map/ppermute | solution.py:58
  89.9 5.1 %convolution_add_fusion.1 = f32[96,2048]{1,0:T(8,128)S(1)} fusion(f32[96,2048]{1,0:T(8,128)} %collective-permute-done.1, bf16[2048,2048]{1,0:T(8,128)(2,1)} %fusion, bf16[4,96,2048]{2,1,0:T(8,128)(2,1)S(1)} %all-to-all-done, s32[]{:T(128)S(6)} %select_n.81), kind=kOutput, calls=%fused_computation.13 | convolution fusion | flops 805502976 | bytes 10354692 | tf_op jit(solution)/shard_map/dot_general | solution.py:107
  95.0 2.2 %collective-permute-start.2 = (f32[96,2048]{1,0:T(8,128)S(1)}, f32[96,2048]{1,0:T(8,128)S(1)}, u32[]{:S(2)}, u32[]{:S(2)}) collective-permute-start(f32[96,2048]{1,0:T(8,128)S(1)} %convolution_add_fusion.1), channel_id=1, source_target_pairs={{0,4},{4,8},{1,5},{5,9},{2,6},{6,10},{3,7},{7,11},{16,20},{20,24},... | collective-permute-start | bytes 2359304 | tf_op jit(solution)/shard_map/ppermute | solution.py:58
  97.2 4.9 %convolution_add_fusion = f32[96,2048]{1,0:T(8,128)S(1)} fusion(f32[96,2048]{1,0:T(8,128)S(1)} %collective-permute-done.4, bf16[2048,2048]{1,0:T(8,128)(2,1)} %fusion, bf16[4,96,2048]{2,1,0:T(8,128)(2,1)S(1)} %all-to-all-done, s32[]{:T(128)S(6)} %max.23), kind=kOutput, calls=%fused_computation.12 | convolution fusion | flops 805502976 | bytes 10354692 | tf_op jit(solution)/shard_map/dot_general | solution.py:107
  106.4 7.7 %collective-permute-done.2 = f32[96,2048]{1,0:T(8,128)S(1)} collective-permute-done((f32[96,2048]{1,0:T(8,128)S(1)}, f32[96,2048]{1,0:T(8,128)S(1)}, u32[]{:S(2)}, u32[]{:S(2)}) %collective-permute-start.2) | collective-permute-done | bytes 786464 | tf_op jit(solution)/shard_map/ppermute | solution.py:58
  115.1 2.2 %collective-permute-start.3 = (f32[96,2048]{1,0:T(8,128)}, f32[96,2048]{1,0:T(8,128)}, u32[]{:S(2)}, u32[]{:S(2)}) collective-permute-start(f32[96,2048]{1,0:T(8,128)} %add.166), channel_id=1, source_target_pairs={{0,4},{4,8},{8,12},{1,5},{5,9},{9,13},{2,6},{6,10},{10,14},{3,7},{... | collective-permute-start | bytes 2359304 | tf_op jit(solution)/shard_map/ppermute | solution.py:58
  117.3 3.6 %collective-permute-done.5 = f32[96,2048]{1,0:T(8,128)S(1)} collective-permute-done((f32[96,2048]{1,0:T(8,128)S(1)}, f32[96,2048]{1,0:T(8,128)S(1)}, u32[]{:S(2)}, u32[]{:S(2)}) %collective-permute-start.5) | collective-permute-done | bytes 786464 | tf_op jit(solution)/shard_map/ppermute | solution.py:63
  123.4 4.8 %fusion.39 = f32[96,2048]{1,0:T(8,128)S(1)} fusion(bf16[2048,2048]{1,0:T(8,128)(2,1)} %fusion, bf16[4,96,2048]{2,1,0:T(8,128)(2,1)S(1)} %all-to-all-done, s32[]{:T(128)S(6)} %select_n.79), kind=kOutput, calls=%fused_computation.85 | convolution fusion | flops 805306368 | bytes 9568260 | tf_op jit(solution)/shard_map/dot_general | solution.py:107
  128.2 5.1 %collective-permute-done.3 = f32[96,2048]{1,0:T(8,128)} collective-permute-done((f32[96,2048]{1,0:T(8,128)}, f32[96,2048]{1,0:T(8,128)}, u32[]{:S(2)}, u32[]{:S(2)}) %collective-permute-start.3) | collective-permute-done | bytes 786464 | tf_op jit(solution)/shard_map/ppermute | solution.py:58
  133.3 5.7 %collective-permute-done.6 = f32[96,2048]{1,0:T(8,128)} collective-permute-done((f32[96,2048]{1,0:T(8,128)S(1)}, f32[96,2048]{1,0:T(8,128)}, u32[]{:S(2)}, u32[]{:S(2)}) %collective-permute-start.6) | collective-permute-done | bytes 786464 | tf_op jit(solution)/shard_map/ppermute | solution.py:63
  141.9 4.6 %collective-permute-done.7 = bf16[6,2048]{1,0:T(8,128)(2,1)S(1)} collective-permute-done((bf16[6,2048]{1,0:T(8,128)(2,1)S(1)}, bf16[6,2048]{1,0:T(8,128)(2,1)S(1)}, u32[]{:S(2)}, u32[]{:S(2)}) %collective-permute-start.7) | collective-permute-done | bytes 24608 | tf_op jit(solution)/shard_map/ppermute | solution.py:13
  147.4 2.1 collective-permute-start.8
  155.6 4.0 %collective-permute-start.10 = (bf16[96,2048]{1,0:T(8,128)(2,1)}, bf16[96,2048]{1,0:T(8,128)(2,1)S(1)}, u32[]{:S(2)}, u32[]{:S(2)}) collective-permute-start(bf16[96,2048]{1,0:T(8,128)(2,1)} %get-tuple-element.9), channel_id=1, source_target_pairs={{4,0},{8,4},{12,8},{5,1},{9,5},{13,9},{6,2},{10,6},{14,10},{7,3},{... | collective-permute-start | bytes 1179656 | tf_op jit(solution)/shard_map/ppermute | solution.py:85
  159.7 4.9 %collective-permute-done.9 = bf16[96,2048]{1,0:T(8,128)(2,1)} collective-permute-done((bf16[96,2048]{1,0:T(8,128)(2,1)}, bf16[96,2048]{1,0:T(8,128)(2,1)}, u32[]{:S(2)}, u32[]{:S(2)}) %collective-permute-start.9) | collective-permute-done | bytes 393248 | tf_op jit(solution)/shard_map/ppermute | solution.py:84
  164.6 2.2 %collective-permute-start.11 = (bf16[96,2048]{1,0:T(8,128)(2,1)}, bf16[96,2048]{1,0:T(8,128)(2,1)S(1)}, u32[]{:S(2)}, u32[]{:S(2)}) collective-permute-start(bf16[96,2048]{1,0:T(8,128)(2,1)} %collective-permute-done.9), channel_id=1, source_target_pairs={{4,8},{8,12},{5,9},{9,13},{6,10},{10,14},{7,11},{11,15},{20,24},{2... | collective-permute-start | bytes 1179656 | tf_op jit(solution)/shard_map/ppermute | solution.py:84
  168.0 3.7 %collective-permute-start.12 = (bf16[96,2048]{1,0:T(8,128)(2,1)S(1)}, bf16[96,2048]{1,0:T(8,128)(2,1)S(1)}, u32[]{:S(2)}, u32[]{:S(2)}) collective-permute-start(bf16[96,2048]{1,0:T(8,128)(2,1)S(1)} %collective-permute-done.10), channel_id=1, source_target_pairs={{4,0},{8,4},{5,1},{9,5},{6,2},{10,6},{7,3},{11,7},{20,16},{24,20},... | collective-permute-start | bytes 1179656 | tf_op jit(solution)/shard_map/ppermute | solution.py:85
  171.9 2.8 %collective-permute-done.11 = bf16[96,2048]{1,0:T(8,128)(2,1)S(1)} collective-permute-done((bf16[96,2048]{1,0:T(8,128)(2,1)}, bf16[96,2048]{1,0:T(8,128)(2,1)S(1)}, u32[]{:S(2)}, u32[]{:S(2)}) %collective-permute-start.11) | collective-permute-done | bytes 393248 | tf_op jit(solution)/shard_map/ppermute | solution.py:84
  175.5 3.8 %collective-permute-done.12 = bf16[96,2048]{1,0:T(8,128)(2,1)S(1)} collective-permute-done((bf16[96,2048]{1,0:T(8,128)(2,1)S(1)}, bf16[96,2048]{1,0:T(8,128)(2,1)S(1)}, u32[]{:S(2)}, u32[]{:S(2)}) %collective-permute-start.12) | collective-permute-done | bytes 393248 | tf_op jit(solution)/shard_map/ppermute | solution.py:85
  179.3 3.7 %collective-permute-start.14 = (bf16[96,2048]{1,0:T(8,128)(2,1)S(1)}, bf16[96,2048]{1,0:T(8,128)(2,1)S(1)}, u32[]{:S(2)}, u32[]{:S(2)}) collective-permute-start(bf16[96,2048]{1,0:T(8,128)(2,1)S(1)} %collective-permute-done.12), channel_id=1, source_target_pairs={{4,0},{5,1},{6,2},{7,3},{20,16},{21,17},{22,18},{23,19}} | collective-permute-start | bytes 1179656 | tf_op jit(solution)/shard_map/ppermute | solution.py:85
  183.3 5.4 %collective-permute-done.14 = bf16[96,2048]{1,0:T(8,128)(2,1)S(1)} collective-permute-done((bf16[96,2048]{1,0:T(8,128)(2,1)S(1)}, bf16[96,2048]{1,0:T(8,128)(2,1)S(1)}, u32[]{:S(2)}, u32[]{:S(2)}) %collective-permute-start.14) | collective-permute-done | bytes 393248 | tf_op jit(solution)/shard_map/ppermute | solution.py:85
  188.9 15.0 %divide_reduce_fusion = (f32[16,2048]{1,0:T(8,128)S(1)}, f32[16,2048]{1,0:T(8,128)S(1)}, f32[16,2048]{1,0:T(8,128)S(1)}, f32[16,2048]{1,0:T(8,128)S(1)}) fusion(f32[16,2048]{1,0:T(8,128)S(1)} %get-tuple-element.7, f32[16,2048]{1,0:T(8,128)S(1)} %get-tuple-element.12, bf16[2048,2048]{1,0:T(8,128)(2,1)} %param.8, f32[16,2048]{1,0:T(8,128)S(1)} %copy-done.7, ...), kind=kOutput, calls=%fused_computation.11 | convolution fusion | flops 3288203264 | bytes 12451840 | tf_op jit(solution)/shard_map/dot_general | solution.py:131
  204.0 3.4 %collective-permute-start.16 = (f32[16,2048]{1,0:T(8,128)S(1)}, f32[16,2048]{1,0:T(8,128)S(1)}, u32[]{:S(2)}, u32[]{:S(2)}) collective-permute-start(f32[16,2048]{1,0:T(8,128)S(1)} %get-tuple-element.10), channel_id=1, source_target_pairs={{0,1},{1,0},{2,3},{3,2},{4,5},{5,4},{6,7},{7,6},{8,9},{9,8},{10,11... | collective-permute-start | bytes 393224 | tf_op jit(solution)/shard_map/ppermute | solution.py:46
  (70 shorter events, 27.4 us)
Async XLA Ops:
  0.6 18.7 %collective-permute-start = (bf16[96,4096]{1,0:T(8,128)(2,1)}, bf16[96,4096]{1,0:T(8,128)(2,1)S(1)}, u32[]{:S(2)}, u32[]{:S(2)}) collective-permute-start(bf16[96,4096]{1,0:T(8,128)(2,1)} %bitcast.135), channel_id=1, source_target_pairs={{0,2},{2,0},{1,3},{3,1},{4,6},{6,4},{5,7},{7,5},{8,10},{10,8},{9,1... | collective-permute-start | bytes 2359304 | tf_op jit(solution)/shard_map/ppermute | solution.py:33
  24.9 36.9 %all-to-all-start = ((bf16[4,96,2048]{2,1,0:T(8,128)(2,1)}), bf16[4,96,2048]{2,1,0:T(8,128)(2,1)S(1)}, u32[]{:S(2)}, u32[]{:S(2)}) async-start(bf16[4,96,2048]{2,1,0:T(8,128)(2,1)} %copy.14), calls=%async_computation | async-start | bytes 3145728 | tf_op jit(solution)/shard_map/all_to_all | solution.py:99
  29.6 5.7 %copy-start.1 = (f32[16,2048]{1,0:T(8,128)S(1)}, f32[16,2048]{1,0:T(8,128)}, u32[]{:S(2)}) copy-start(f32[16,2048]{1,0:T(8,128)} %param.10) | copy-start | bytes 393220
  29.6 5.7 %copy-start.3 = (f32[16,2048]{1,0:T(8,128)S(1)}, f32[16,2048]{1,0:T(8,128)}, u32[]{:S(2)}) copy-start(f32[16,2048]{1,0:T(8,128)} %param.9) | copy-start | bytes 393220
  67.6 22.3 %collective-permute-start.1 = (f32[96,2048]{1,0:T(8,128)}, f32[96,2048]{1,0:T(8,128)}, u32[]{:S(2)}, u32[]{:S(2)}) collective-permute-start(f32[96,2048]{1,0:T(8,128)} %fusion.37), channel_id=1, source_target_pairs={{0,4},{1,5},{2,6},{3,7},{16,20},{17,21},{18,22},{19,23}} | collective-permute-start | bytes 2359304 | tf_op jit(solution)/shard_map/ppermute | solution.py:58
  73.7 23.5 %collective-permute-start.4 = (f32[96,2048]{1,0:T(8,128)S(1)}, f32[96,2048]{1,0:T(8,128)S(1)}, u32[]{:S(2)}, u32[]{:S(2)}) collective-permute-start(f32[96,2048]{1,0:T(8,128)S(1)} %fusion.32), channel_id=1, source_target_pairs={{12,8},{13,9},{14,10},{15,11},{28,24},{29,25},{30,26},{31,27}} | collective-permute-start | bytes 2359304 | tf_op jit(solution)/shard_map/ppermute | solution.py:63
  89.9 13.5 %slice-start = ((s8[8388608]{0:T(1024)(128)(4,1)}), s8[4194304]{0:T(1024)(128)(4,1)S(1)}, s32[]{:S(2)}) async-start(s8[8388608]{0:T(1024)(128)(4,1)} %bitcast.130), calls=%async_computation.1 | async-start | bytes 8388608
  95.0 8.4 %slice-start.1 = ((s8[8388608]{0:T(1024)(128)(4,1)}), s8[4194304]{0:T(1024)(128)(4,1)S(1)}, s32[]{:S(2)}) async-start(s8[8388608]{0:T(1024)(128)(4,1)} %bitcast.130), calls=%async_computation.2 | async-start | bytes 8388608
  95.0 19.1 %collective-permute-start.2 = (f32[96,2048]{1,0:T(8,128)S(1)}, f32[96,2048]{1,0:T(8,128)S(1)}, u32[]{:S(2)}, u32[]{:S(2)}) collective-permute-start(f32[96,2048]{1,0:T(8,128)S(1)} %convolution_add_fusion.1), channel_id=1, source_target_pairs={{0,4},{4,8},{1,5},{5,9},{2,6},{6,10},{3,7},{7,11},{16,20},{20,24},... | collective-permute-start | bytes 2359304 | tf_op jit(solution)/shard_map/ppermute | solution.py:58
  102.1 18.8 %collective-permute-start.5 = (f32[96,2048]{1,0:T(8,128)S(1)}, f32[96,2048]{1,0:T(8,128)S(1)}, u32[]{:S(2)}, u32[]{:S(2)}) collective-permute-start(f32[96,2048]{1,0:T(8,128)S(1)} %convolution_add_fusion), channel_id=1, source_target_pairs={{8,4},{12,8},{9,5},{13,9},{10,6},{14,10},{11,7},{15,11},{24,20},{2... | collective-permute-start | bytes 2359304 | tf_op jit(solution)/shard_map/ppermute | solution.py:63
  106.4 16.5 %copy-start.8 = (f32[128,7]{0,1:T(8,128)S(1)}, f32[128,7]{0,1:T(8,128)}, u32[]{:S(2)}) copy-start(f32[128,7]{0,1:T(8,128)} %param.11) | copy-start | bytes 10756
  115.1 18.2 %collective-permute-start.3 = (f32[96,2048]{1,0:T(8,128)}, f32[96,2048]{1,0:T(8,128)}, u32[]{:S(2)}, u32[]{:S(2)}) collective-permute-start(f32[96,2048]{1,0:T(8,128)} %add.166), channel_id=1, source_target_pairs={{0,4},{4,8},{8,12},{1,5},{5,9},{9,13},{2,6},{6,10},{10,14},{3,7},{... | collective-permute-start | bytes 2359304 | tf_op jit(solution)/shard_map/ppermute | solution.py:58
  121.0 18.0 %collective-permute-start.6 = (f32[96,2048]{1,0:T(8,128)S(1)}, f32[96,2048]{1,0:T(8,128)}, u32[]{:S(2)}, u32[]{:S(2)}) collective-permute-start(f32[96,2048]{1,0:T(8,128)S(1)} %add.172), channel_id=1, source_target_pairs={{4,0},{8,4},{12,8},{5,1},{9,5},{13,9},{6,2},{10,6},{14,10},{7,3},{... | collective-permute-start | bytes 2359304 | tf_op jit(solution)/shard_map/ppermute | solution.py:63
  128.2 18.4 %copy-start.5 = (bf16[1,1,96,2048]{3,2,1,0:T(8,128)(2,1)S(1)}, bf16[1,1,96,2048]{3,2,1,0:T(8,128)(2,1)}, u32[]{:S(2)}) copy-start(bf16[1,1,96,2048]{3,2,1,0:T(8,128)(2,1)} %param.13) | copy-start | bytes 1179652
  128.2 18.4 %copy-start.6 = (bf16[1,1,96,2048]{3,2,1,0:T(8,128)(2,1)S(1)}, bf16[1,1,96,2048]{3,2,1,0:T(8,128)(2,1)}, u32[]{:S(2)}) copy-start(bf16[1,1,96,2048]{3,2,1,0:T(8,128)(2,1)} %param.12) | copy-start | bytes 1179652
  140.6 5.9 %collective-permute-start.7 = (bf16[6,2048]{1,0:T(8,128)(2,1)S(1)}, bf16[6,2048]{1,0:T(8,128)(2,1)S(1)}, u32[]{:S(2)}, u32[]{:S(2)}) collective-permute-start(bf16[6,2048]{1,0:T(8,128)(2,1)S(1)} %slice.96), channel_id=1, source_target_pairs={{0,1},{2,3},{4,5},{6,7},{8,9},{10,11},{12,13},{14,15},{16,17},{18,... | collective-permute-start | bytes 73736 | tf_op jit(solution)/shard_map/ppermute | solution.py:13
  147.4 3.0 %collective-permute-start.8 = (f32[6,2048]{1,0:T(8,128)S(1)}, f32[6,2048]{1,0:T(8,128)S(1)}, u32[]{:S(2)}, u32[]{:S(2)}) collective-permute-start(f32[6,2048]{1,0:T(8,128)S(1)} %slice.110), channel_id=1, source_target_pairs={{1,0},{3,2},{5,4},{7,6},{9,8},{11,10},{13,12},{15,14},{17,16},{19,... | collective-permute-start | bytes 147464 | tf_op jit(solution)/shard_map/ppermute | solution.py:13
  152.0 12.5 %collective-permute-start.9 = (bf16[96,2048]{1,0:T(8,128)(2,1)}, bf16[96,2048]{1,0:T(8,128)(2,1)}, u32[]{:S(2)}, u32[]{:S(2)}) collective-permute-start(bf16[96,2048]{1,0:T(8,128)(2,1)} %get-tuple-element.9), channel_id=1, source_target_pairs={{0,4},{4,8},{8,12},{1,5},{5,9},{9,13},{2,6},{6,10},{10,14},{3,7},{... | collective-permute-start | bytes 1179656 | tf_op jit(solution)/shard_map/ppermute | solution.py:84
  155.6 12.4 %collective-permute-start.10 = (bf16[96,2048]{1,0:T(8,128)(2,1)}, bf16[96,2048]{1,0:T(8,128)(2,1)S(1)}, u32[]{:S(2)}, u32[]{:S(2)}) collective-permute-start(bf16[96,2048]{1,0:T(8,128)(2,1)} %get-tuple-element.9), channel_id=1, source_target_pairs={{4,0},{8,4},{12,8},{5,1},{9,5},{13,9},{6,2},{10,6},{14,10},{7,3},{... | collective-permute-start | bytes 1179656 | tf_op jit(solution)/shard_map/ppermute | solution.py:85
  164.6 10.1 %collective-permute-start.11 = (bf16[96,2048]{1,0:T(8,128)(2,1)}, bf16[96,2048]{1,0:T(8,128)(2,1)S(1)}, u32[]{:S(2)}, u32[]{:S(2)}) collective-permute-start(bf16[96,2048]{1,0:T(8,128)(2,1)} %collective-permute-done.9), channel_id=1, source_target_pairs={{4,8},{8,12},{5,9},{9,13},{6,10},{10,14},{7,11},{11,15},{20,24},{2... | collective-permute-start | bytes 1179656 | tf_op jit(solution)/shard_map/ppermute | solution.py:84
  168.0 11.3 %collective-permute-start.12 = (bf16[96,2048]{1,0:T(8,128)(2,1)S(1)}, bf16[96,2048]{1,0:T(8,128)(2,1)S(1)}, u32[]{:S(2)}, u32[]{:S(2)}) collective-permute-start(bf16[96,2048]{1,0:T(8,128)(2,1)S(1)} %collective-permute-done.10), channel_id=1, source_target_pairs={{4,0},{8,4},{5,1},{9,5},{6,2},{10,6},{7,3},{11,7},{20,16},{24,20},... | collective-permute-start | bytes 1179656 | tf_op jit(solution)/shard_map/ppermute | solution.py:85
  174.7 8.5 %collective-permute-start.13 = (bf16[96,2048]{1,0:T(8,128)(2,1)S(1)}, bf16[96,2048]{1,0:T(8,128)(2,1)S(1)}, u32[]{:S(2)}, u32[]{:S(2)}) collective-permute-start(bf16[96,2048]{1,0:T(8,128)(2,1)S(1)} %collective-permute-done.11), channel_id=1, source_target_pairs={{8,12},{9,13},{10,14},{11,15},{24,28},{25,29},{26,30},{27,31}} | collective-permute-start | bytes 1179656 | tf_op jit(solution)/shard_map/ppermute | solution.py:84
  175.5 13.4 %copy-start = (bf16[2048,384]{1,0:T(8,128)(2,1)S(1)}, bf16[2048,384]{1,0:T(8,128)(2,1)}, u32[]{:S(2)}) copy-start(bf16[2048,384]{1,0:T(8,128)(2,1)} %copy.15) | copy-start | bytes 4718596
  175.5 13.4 %copy-start.7 = (f32[16,2048]{1,0:T(8,128)S(1)}, f32[16,2048]{1,0:T(8,128)}, u32[]{:S(2)}) copy-start(f32[16,2048]{1,0:T(8,128)} %get-tuple-element.6) | copy-start | bytes 393220
  179.3 9.4 %collective-permute-start.14 = (bf16[96,2048]{1,0:T(8,128)(2,1)S(1)}, bf16[96,2048]{1,0:T(8,128)(2,1)S(1)}, u32[]{:S(2)}, u32[]{:S(2)}) collective-permute-start(bf16[96,2048]{1,0:T(8,128)(2,1)S(1)} %collective-permute-done.12), channel_id=1, source_target_pairs={{4,0},{5,1},{6,2},{7,3},{20,16},{21,17},{22,18},{23,19}} | collective-permute-start | bytes 1179656 | tf_op jit(solution)/shard_map/ppermute | solution.py:85
  188.8 15.0 %copy-start.2 = (f32[16,2048]{1,0:T(8,128)S(1)}, f32[16,2048]{1,0:T(8,128)}, u32[]{:S(2)}) copy-start(f32[16,2048]{1,0:T(8,128)} %param.10) | copy-start | bytes 393220
  188.9 15.0 %copy-start.4 = (f32[16,2048]{1,0:T(8,128)S(1)}, f32[16,2048]{1,0:T(8,128)}, u32[]{:S(2)}) copy-start(f32[16,2048]{1,0:T(8,128)} %param.9) | copy-start | bytes 393220
  204.0 4.4 %collective-permute-start.16 = (f32[16,2048]{1,0:T(8,128)S(1)}, f32[16,2048]{1,0:T(8,128)S(1)}, u32[]{:S(2)}, u32[]{:S(2)}) collective-permute-start(f32[16,2048]{1,0:T(8,128)S(1)} %get-tuple-element.10), channel_id=1, source_target_pairs={{0,1},{1,0},{2,3},{3,2},{4,5},{5,4},{6,7},{7,6},{8,9},{9,8},{10,11... | collective-permute-start | bytes 393224 | tf_op jit(solution)/shard_map/ppermute | solution.py:46
  207.4 1.7 collective-permute-start.15

commit v4 on v2

--- a/solution.py
+++ b/solution.py
@@ -59,9 +59,12 @@
 
     values = weight.astype(jnp.float32)
     quant = soft_clip(values, clip_upper, clip_lower).astype(jnp.bfloat16)
-    partial = jnp.dot(inputs, quant, preferred_element_type=jnp.float32)
-    received = lax.all_to_all(partial.reshape(shards, length, columns), "fsdp", 0, 0)
-    proj = jnp.sum(received, axis=0).astype(jnp.bfloat16)
+    partial = jnp.dot(inputs, quant, preferred_element_type=jnp.float32).reshape(shards, length, columns)
+    me = lax.axis_index("fsdp")
+    received = lax.all_to_all(partial.astype(jnp.float16), "fsdp", 0, 0).astype(jnp.float32)
+    others = jnp.where((jnp.arange(shards) == me)[:, None, None], 0.0, received)
+    own = lax.dynamic_index_in_dim(partial, me, 0, keepdims=False)
+    proj = (own + jnp.sum(others, axis=0)).astype(jnp.bfloat16)
 
     taps = jnp.repeat(filters, CGROUP, axis=0).T
     pad = FILT - 1

time: 217 us -> 184 us (0.85)
  waiting for transfers between devices: 141 us -> 108 us
    all_to_all x1, waiting for transfers between devices: 67.3 us -> 33.6 us  [on_device(): lax.all_to_all(partial.astype(jnp.float16), 'fsdp', 0, 0)]
  transfers between devices with their start and end apart: 8 -> 8, of which waited for: 6 -> 6; matrix products, arithmetic and copies ran while one was open for 11% -> 13% of each run, Pallas kernels for 0% -> 0%
where the time goes in v4:
time: 184 us
  waiting for transfers between devices  108 us (59%)
  matrix products  23.8 us (13%)
  other arithmetic  22.6 us (12%)
  starting transfers between devices  18.6 us (10%)
  local copies, waits for them, and re-layouts  9.93 us (5%)
    all_to_all x1, waiting for transfers between devices, on_device(): lax.all_to_all(copies, 'fsdp', 0, 0).reshape(shards * length, columns)  35.8 us
    all_to_all x1, waiting for transfers between devices, on_device(): lax.all_to_all(partial.astype(jnp.float16), 'fsdp', 0, 0)  33.6 us
    all_to_all x1, waiting for transfers between devices, on_device(): mine = lax.all_to_all(pieces, 'fsdp', 0, 0)  20.8 us
    dot_general x1, matrix products, on_device(): lax.dot_general(inputs, d_all, (((0,), (0,)), ((), ())), preferred_elemen...  15.4 us
    ppermute x1, waiting for transfers between devices, gather_features(): other = lax.ppermute(local_rows, 'seq', [(0, 1), (1, 0)])  14.9 us
    convert_element_type x1, other arithmetic, on_device(): quant = soft_clip(values, clip_upper, clip_lower).astype(jnp.bfloat16)  8.76 us
    dot_general x1, matrix products, on_device(): jnp.dot(inputs, quant, preferred_element_type=jnp.float32)  8.41 us
    reduce_max x1, other arithmetic, soft_clip(): amax = jnp.max(jnp.abs(blocks), axis=1) + 1e-06  5.68 us
  transfers between devices with their start and end apart: 8, of which 6 were waited for; matrix products, arithmetic and copies ran while one was open for 13% of the time, Pallas kernels for 0%

profile of v4, /device:TPU:0, one launch (start us, length us, event | category | flops | bytes accessed | tf_op | source)
XLA Modules:
  0.0 183.5 jit_solution(13415507235052593007)
XLA Ops:
  0.6 3.0 %collective-permute-start = (bf16[96,4096]{1,0:T(8,128)(2,1)}, bf16[96,4096]{1,0:T(8,128)(2,1)S(1)}, u32[]{:S(2)}, u32[]{:S(2)}) collective-permute-start(bf16[96,4096]{1,0:T(8,128)(2,1)} %bitcast.82), channel_id=1, source_target_pairs={{0,2},{2,0},{1,3},{3,1},{4,6},{6,4},{5,7},{7,5},{8,10},{10,8},{9,1... | collective-permute-start | bytes 2359304 | tf_op jit(solution)/shard_map/ppermute | solution.py:33
  3.6 2.6 %concatenate.18 = bf16[96,2,2048]{2,1,0:T(2,128)(2,1)S(1)} reshape(bf16[1,1,96,4096]{3,2,1,0:T(8,128)(2,1)} %param.7) | data formatting | bytes 1572864 | tf_op jit(solution)/shard_map/concatenate | solution.py:37
  6.2 0.2 copy.16
  6.5 14.9 %collective-permute-done = bf16[96,4096]{1,0:T(8,128)(2,1)S(1)} collective-permute-done((bf16[96,4096]{1,0:T(8,128)(2,1)}, bf16[96,4096]{1,0:T(8,128)(2,1)S(1)}, u32[]{:S(2)}, u32[]{:S(2)}) %collective-permute-start) | collective-permute-done | bytes 786464 | tf_op jit(solution)/shard_map/ppermute | solution.py:33
  21.4 1.5 fusion.4
  22.9 5.1 %all-to-all-start = ((bf16[4,96,2048]{2,1,0:T(8,128)(2,1)}), bf16[4,96,2048]{2,1,0:T(8,128)(2,1)S(1)}, u32[]{:S(2)}, u32[]{:S(2)}) async-start(bf16[4,96,2048]{2,1,0:T(8,128)(2,1)} %fusion.4), calls=%async_computation | async-start | bytes 3145728 | tf_op jit(solution)/shard_map/all_to_all | solution.py:57
  28.0 5.7 %abs_reduce_fusion = f32[16,2048]{1,0:T(8,128)S(1)} fusion(bf16[2048,2048]{1,0:T(8,128)(2,1)} %param.8), kind=kLoop, calls=%fused_computation.10 | loop fusion | flops 12550144 | bytes 8519680 | tf_op jit(solution)/shard_map/reduce_max | solution.py:20
  33.7 0.8 multiply_divide_fusion
  34.5 8.8 %fusion = bf16[2048,2048]{1,0:T(8,128)(2,1)} fusion(bf16[2048,2048]{1,0:T(8,128)(2,1)} %param.8, f32[16,2048]{1,0:T(8,128)S(1)} %get-tuple-element.7, f32[16,2048]{1,0:T(8,128)S(1)} %get-tuple-element.10), kind=kLoop, calls=%fused_computation.4 | loop fusion | flops 25165824 | bytes 17039360 | tf_op jit(solution)/shard_map/convert_element_type | solution.py:61
  43.3 20.8 %all-to-all-done = bf16[4,96,2048]{2,1,0:T(8,128)(2,1)S(1)} async-done(((bf16[4,96,2048]{2,1,0:T(8,128)(2,1)}), bf16[4,96,2048]{2,1,0:T(8,128)(2,1)S(1)}, u32[]{:S(2)}, u32[]{:S(2)}) %all-to-all-start) | async-done | bytes 1572896 | tf_op jit(solution)/shard_map/all_to_all | solution.py:57
  64.1 8.4 %fusion.35 = (f16[4,96,2048]{2,1,0:T(8,128)(2,1)}, f32[4,96,2048]{2,1,0:T(8,128)}) fusion(bf16[4,96,2048]{2,1,0:T(8,128)(2,1)S(1)} %all-to-all-done, bf16[2048,2048]{1,0:T(8,128)(2,1)} %fusion), kind=kOutput, calls=%fused_computation.80 | convolution fusion | flops 3222011904 | bytes 14680064 | tf_op jit(solution)/shard_map/dot_general | solution.py:62
  72.5 3.6 %all-to-all-start.1 = ((f16[4,96,2048]{2,1,0:T(8,128)(2,1)}), f16[4,96,2048]{2,1,0:T(8,128)(2,1)S(1)}, u32[]{:S(2)}, u32[]{:S(2)}) async-start(f16[4,96,2048]{2,1,0:T(8,128)(2,1)} %get-tuple-element.18), calls=%async_computation.1 | async-start | bytes 3145728 | tf_op jit(solution)/shard_map/all_to_all | solution.py:64
  76.1 1.0 broadcast_in_dim.16
  77.1 1.9 %reshape.69 = f32[2048,7]{0,1:T(8,128)} reshape(f32[128,16,7]{1,0,2:T(8,128)} %broadcast_in_dim.16) | data formatting | bytes 114688 | tf_op jit(solution)/shard_map/reshape | solution.py:69
  79.0 33.6 %all-to-all-done.1 = f16[4,96,2048]{2,1,0:T(8,128)(2,1)S(1)} async-done(((f16[4,96,2048]{2,1,0:T(8,128)(2,1)}), f16[4,96,2048]{2,1,0:T(8,128)(2,1)S(1)}, u32[]{:S(2)}, u32[]{:S(2)}) %all-to-all-start.1) | async-done | bytes 1572896 | tf_op jit(solution)/shard_map/all_to_all | solution.py:64
  112.5 0.5 select_reduce_fusion
  113.0 1.2 fusion.31
  114.3 1.3 collective-permute-start.1
  115.6 1.2 fusion.34
  116.9 1.9 %convert_multiply_fusion = f32[96,2048]{1,0:T(8,128)S(1)} fusion(f32[102,2048]{1,0:T(8,128)S(1)} %maximum_convert_fusion, bf16[1,1,96,2048]{3,2,1,0:T(8,128)(2,1)} %param.13, bf16[1,1,96,2048]{3,2,1,0:T(8,128)(2,1)} %param.12, f32[2048]{0:T(1024)S(1)} %bitcast.87, f32[2048]{0:T(1024)S(1)} %bitcast.89, f32[2048]{0:T(1024)S(1)} %bitcast.91, ...), kind=kLoop, calls=%fused_computation.22 | loop fusion | flops 3735552 | bytes 7135232 | tf_op jit(solution)/shard_map/mul | solution.py:80
  118.9 1.3 collective-permute-start.2
  120.2 1.8 %collective-permute-done.2 = f32[6,2048]{1,0:T(8,128)S(1)} collective-permute-done((f32[6,2048]{1,0:T(8,128)S(1)}, f32[6,2048]{1,0:T(8,128)S(1)}, u32[]{:S(2)}, u32[]{:S(2)}) %collective-permute-start.2) | collective-permute-done | bytes 49184 | tf_op jit(solution)/shard_map/ppermute | solution.py:13
  122.0 0.7 fusion.11
  122.7 1.4 broadcast_in_dim.30
  124.1 3.7 %all-to-all-start.2 = ((bf16[4,96,2048]{2,1,0:T(8,128)(2,1)}), bf16[4,96,2048]{2,1,0:T(8,128)(2,1)S(1)}, u32[]{:S(2)}, u32[]{:S(2)}) async-start(bf16[4,96,2048]{2,1,0:T(8,128)(2,1)} %broadcast_in_dim.30), calls=%async_computation.2 | async-start | bytes 3145728 | tf_op jit(solution)/shard_map/all_to_all | solution.py:89
  127.8 1.6 copy.20
  129.4 35.8 %all-to-all-done.2 = bf16[4,96,2048]{2,1,0:T(8,128)(2,1)S(1)} async-done(((bf16[4,96,2048]{2,1,0:T(8,128)(2,1)}), bf16[4,96,2048]{2,1,0:T(8,128)(2,1)S(1)}, u32[]{:S(2)}, u32[]{:S(2)}) %all-to-all-start.2) | async-done | bytes 1572896 | tf_op jit(solution)/shard_map/all_to_all | solution.py:89
  165.2 15.4 %divide_reduce_fusion = (f32[16,2048]{1,0:T(8,128)S(1)}, f32[16,2048]{1,0:T(8,128)S(1)}, f32[16,2048]{1,0:T(8,128)S(1)}, f32[16,2048]{1,0:T(8,128)S(1)}) fusion(f32[16,2048]{1,0:T(8,128)S(1)} %get-tuple-element.7, f32[16,2048]{1,0:T(8,128)S(1)} %get-tuple-element.10, bf16[2048,2048]{1,0:T(8,128)(2,1)} %param.8, f32[16,2048]{1,0:T(8,128)} %get-tuple-element.6, ...), kind=kOutput, calls=%fused_computation.11 | convolution fusion | flops 3288203264 | bytes 12451840 | tf_op jit(solution)/shard_map/dot_general | solution.py:90
  180.8 0.5 collective-permute-start.3
  181.3 0.8 collective-permute-done.4
  182.2 0.7 add.102
  182.8 0.7 add.101
  (19 shorter events, 0.4 us)
Async XLA Ops:
  0.6 20.8 %collective-permute-start = (bf16[96,4096]{1,0:T(8,128)(2,1)}, bf16[96,4096]{1,0:T(8,128)(2,1)S(1)}, u32[]{:S(2)}, u32[]{:S(2)}) collective-permute-start(bf16[96,4096]{1,0:T(8,128)(2,1)} %bitcast.82), channel_id=1, source_target_pairs={{0,2},{2,0},{1,3},{3,1},{4,6},{6,4},{5,7},{7,5},{8,10},{10,8},{9,1... | collective-permute-start | bytes 2359304 | tf_op jit(solution)/shard_map/ppermute | solution.py:33
  6.5 27.2 %copy-start = (f32[16,2048]{1,0:T(8,128)S(1)}, f32[16,2048]{1,0:T(8,128)}, u32[]{:S(2)}) copy-start(f32[16,2048]{1,0:T(8,128)} %param.10) | copy-start | bytes 393220
  6.5 27.2 %copy-start.2 = (f32[16,2048]{1,0:T(8,128)S(1)}, f32[16,2048]{1,0:T(8,128)}, u32[]{:S(2)}) copy-start(f32[16,2048]{1,0:T(8,128)} %param.9) | copy-start | bytes 393220
  22.9 41.2 %all-to-all-start = ((bf16[4,96,2048]{2,1,0:T(8,128)(2,1)}), bf16[4,96,2048]{2,1,0:T(8,128)(2,1)S(1)}, u32[]{:S(2)}, u32[]{:S(2)}) async-start(bf16[4,96,2048]{2,1,0:T(8,128)(2,1)} %fusion.4), calls=%async_computation | async-start | bytes 3145728 | tf_op jit(solution)/shard_map/all_to_all | solution.py:57
  43.3 32.8 %copy-start.4 = (f32[128,7]{0,1:T(8,128)S(1)}, f32[128,7]{0,1:T(8,128)}, u32[]{:S(2)}) copy-start(f32[128,7]{0,1:T(8,128)} %param.11) | copy-start | bytes 10756
  72.5 40.0 %all-to-all-start.1 = ((f16[4,96,2048]{2,1,0:T(8,128)(2,1)}), f16[4,96,2048]{2,1,0:T(8,128)(2,1)S(1)}, u32[]{:S(2)}, u32[]{:S(2)}) async-start(f16[4,96,2048]{2,1,0:T(8,128)(2,1)} %get-tuple-element.18), calls=%async_computation.1 | async-start | bytes 3145728 | tf_op jit(solution)/shard_map/all_to_all | solution.py:64
  114.3 2.5 %collective-permute-start.1 = (bf16[6,2048]{1,0:T(8,128)(2,1)S(1)}, bf16[6,2048]{1,0:T(8,128)(2,1)S(1)}, u32[]{:S(2)}, u32[]{:S(2)}) collective-permute-start(bf16[6,2048]{1,0:T(8,128)(2,1)S(1)} %slice.96), channel_id=1, source_target_pairs={{0,1},{2,3},{4,5},{6,7},{8,9},{10,11},{12,13},{14,15},{16,17},{18,... | collective-permute-start | bytes 73736 | tf_op jit(solution)/shard_map/ppermute | solution.py:13
  118.9 3.1 %collective-permute-start.2 = (f32[6,2048]{1,0:T(8,128)S(1)}, f32[6,2048]{1,0:T(8,128)S(1)}, u32[]{:S(2)}, u32[]{:S(2)}) collective-permute-start(f32[6,2048]{1,0:T(8,128)S(1)} %slice.110), channel_id=1, source_target_pairs={{1,0},{3,2},{5,4},{7,6},{9,8},{11,10},{13,12},{15,14},{17,16},{19,... | collective-permute-start | bytes 147464 | tf_op jit(solution)/shard_map/ppermute | solution.py:13
  124.1 41.1 %all-to-all-start.2 = ((bf16[4,96,2048]{2,1,0:T(8,128)(2,1)}), bf16[4,96,2048]{2,1,0:T(8,128)(2,1)S(1)}, u32[]{:S(2)}, u32[]{:S(2)}) async-start(bf16[4,96,2048]{2,1,0:T(8,128)(2,1)} %broadcast_in_dim.30), calls=%async_computation.2 | async-start | bytes 3145728 | tf_op jit(solution)/shard_map/all_to_all | solution.py:89
  165.2 15.4 %copy-start.1 = (f32[16,2048]{1,0:T(8,128)S(1)}, f32[16,2048]{1,0:T(8,128)}, u32[]{:S(2)}) copy-start(f32[16,2048]{1,0:T(8,128)} %param.10) | copy-start | bytes 393220
  165.2 15.4 %copy-start.3 = (f32[16,2048]{1,0:T(8,128)S(1)}, f32[16,2048]{1,0:T(8,128)}, u32[]{:S(2)}) copy-start(f32[16,2048]{1,0:T(8,128)} %param.9) | copy-start | bytes 393220
  180.7 1.4 collective-permute-start.4
  180.8 2.0 %collective-permute-start.3 = (f32[16,2048]{1,0:T(8,128)S(1)}, f32[16,2048]{1,0:T(8,128)S(1)}, u32[]{:S(2)}, u32[]{:S(2)}) collective-permute-start(f32[16,2048]{1,0:T(8,128)S(1)} %get-tuple-element.9), channel_id=1, source_target_pairs={{0,1},{1,0},{2,3},{3,2},{4,5},{5,4},{6,7},{7,6},{8,9},{9,8},{10,11... | collective-permute-start | bytes 393224 | tf_op jit(solution)/shard_map/ppermute | solution.py:46

commit v5 on v4

--- a/solution.py
+++ b/solution.py
@@ -53,12 +53,13 @@
     length = local_rows.shape[0]
     rows, columns = weight.shape
     features = gather_features(local_rows)
+    values = weight.astype(jnp.float32)
+    quant = soft_clip(values, clip_upper, clip_lower).astype(jnp.bfloat16)
+    features, quant = lax.optimization_barrier((features, quant))
     pieces = features.reshape(length, shards, rows).transpose(1, 0, 2)
     mine = lax.all_to_all(pieces, "fsdp", 0, 0)
     inputs = mine.reshape(shards * length, rows)
 
-    values = weight.astype(jnp.float32)
-    quant = soft_clip(values, clip_upper, clip_lower).astype(jnp.bfloat16)
     partial = jnp.dot(inputs, quant, preferred_element_type=jnp.float32).reshape(shards, length, columns)
     me = lax.axis_index("fsdp")
     received = lax.all_to_all(partial.astype(jnp.float16), "fsdp", 0, 0).astype(jnp.float32)

time: 184 us -> 178 us (0.967)
  blocking collectives: 0 us -> 41.3 us
  waiting for transfers between devices: 108 us -> 76.9 us
  starting transfers between devices: 18.6 us -> 13.6 us
  other arithmetic: 22.6 us -> 18.4 us
  local copies, waits for them, and re-layouts: 9.93 us -> 6.02 us
  matrix products: 23.8 us -> 20.4 us
    all_to_all x0 -> x1, blocking collectives: none -> 41.3 us  [on_device(): mine = lax.all_to_all(pieces, 'fsdp', 0, 0)]
    all_to_all x1 -> x0, waiting for transfers between devices: 20.8 us -> none  [on_device(): mine = lax.all_to_all(pieces, 'fsdp', 0, 0)]
    ppermute x1, waiting for transfers between devices: 14.9 us -> 4.55 us  [gather_features(): other = lax.ppermute(local_rows, 'seq', [(0, 1), (1, 0)])]
    all_to_all x1 -> x0, starting transfers between devices: 5.12 us -> none  [on_device(): mine = lax.all_to_all(pieces, 'fsdp', 0, 0)]
    dot_general x1, matrix products: 8.41 us -> 5.06 us  [on_device(): jnp.dot(inputs, quant, preferred_element_type=jnp.float32)]
    convert_element_type x1, other arithmetic: 8.76 us -> 5.6 us  [on_device(): quant = soft_clip(values, clip_upper, clip_lower).astype(jnp.bfloat16)]
    concatenate x3 -> x0, local copies, waits for them, and re-layouts: 2.88 us -> none  [gather_features(): jnp.concatenate([local_rows, other], axis=1)]
  transfers between devices with their start and end apart: 8 -> 7, of which waited for: 6 -> 6; matrix products, arithmetic and copies ran while one was open for 13% -> 10% of each run, Pallas kernels for 0% -> 0%
where the time goes in v5:
time: 178 us; the launch traced here: 177 us
  waiting for transfers between devices  76.9 us (43%)
  blocking collectives  41.3 us (23%)
  matrix products  20.4 us (11%)
  other arithmetic  18.4 us (10%)
  starting transfers between devices  13.6 us (8%)
  local copies, waits for them, and re-layouts  6.02 us (3%)
    all_to_all x1, blocking collectives, on_device(): mine = lax.all_to_all(pieces, 'fsdp', 0, 0)  41.3 us
    all_to_all x1, waiting for transfers between devices, on_device(): lax.all_to_all(copies, 'fsdp', 0, 0).reshape(shards * length, columns)  35.8 us
    all_to_all x1, waiting for transfers between devices, on_device(): lax.all_to_all(partial.astype(jnp.float16), 'fsdp', 0, 0)  33.1 us
    dot_general x1, matrix products, on_device(): lax.dot_general(inputs, d_all, (((0,), (0,)), ((), ())), preferred_elemen...  15.4 us
    reduce_max x1, other arithmetic, soft_clip(): amax = jnp.max(jnp.abs(blocks), axis=1) + 1e-06  5.9 us
    convert_element_type x1, other arithmetic, on_device(): quant = soft_clip(values, clip_upper, clip_lower).astype(jnp.bfloat16)  5.6 us
    dot_general x1, matrix products, on_device(): jnp.dot(inputs, quant, preferred_element_type=jnp.float32)  5.06 us
    ppermute x1, waiting for transfers between devices, gather_features(): other = lax.ppermute(local_rows, 'seq', [(0, 1), (1, 0)])  4.55 us
  transfers between devices with their start and end apart: 7, of which 6 were waited for; matrix products, arithmetic and copies ran while one was open for 10% of the time, Pallas kernels for 0%

profile of v5, /device:TPU:0, one launch (start us, length us, event | category | flops | bytes accessed | tf_op | source)
XLA Modules:
  0.0 177.4 jit_solution(15087268211872718716)
XLA Ops:
  0.6 3.0 %collective-permute-start = (bf16[96,4096]{1,0:T(8,128)(2,1)}, bf16[96,4096]{1,0:T(8,128)(2,1)S(1)}, u32[]{:S(2)}, u32[]{:S(2)}) collective-permute-start(bf16[96,4096]{1,0:T(8,128)(2,1)} %bitcast.82), channel_id=1, source_target_pairs={{0,2},{2,0},{1,3},{3,1},{4,6},{6,4},{5,7},{7,5},{8,10},{10,8},{9,1... | collective-permute-start | bytes 2359304 | tf_op jit(solution)/shard_map/ppermute | solution.py:33
  3.6 5.9 %abs_reduce_fusion = f32[16,2048]{1,0:T(8,128)S(1)} fusion(bf16[2048,2048]{1,0:T(8,128)(2,1)} %param.8), kind=kLoop, calls=%fused_computation.10 | loop fusion | flops 12550144 | bytes 8519680 | tf_op jit(solution)/shard_map/reduce_max | solution.py:20
  9.6 1.7 multiply_divide_fusion
  11.2 5.6 %fusion = bf16[2048,2048]{1,0:T(8,128)(2,1)} fusion(bf16[2048,2048]{1,0:T(8,128)(2,1)S(1)} %copy-done, f32[16,2048]{1,0:T(8,128)S(1)} %get-tuple-element.11, f32[16,2048]{1,0:T(8,128)S(1)} %get-tuple-element.14), kind=kLoop, calls=%fused_computation.4 | loop fusion | flops 25165824 | bytes 17039360 | tf_op jit(solution)/shard_map/convert_element_type | solution.py:57
  16.8 4.6 %collective-permute-done = bf16[96,4096]{1,0:T(8,128)(2,1)S(1)} collective-permute-done((bf16[96,4096]{1,0:T(8,128)(2,1)}, bf16[96,4096]{1,0:T(8,128)(2,1)S(1)}, u32[]{:S(2)}, u32[]{:S(2)}) %collective-permute-start) | collective-permute-done | bytes 786464 | tf_op jit(solution)/shard_map/ppermute | solution.py:33
  21.4 0.4 maximum_select_fusion
  21.8 0.1 copy.17
  21.9 41.3 %all_to_all.15 = bf16[4,96,2048]{2,1,0:T(8,128)(2,1)S(1)} all-to-all(bf16[4,96,2048]{2,1,0:T(8,128)(2,1)S(1)} %bitcast.78), channel_id=1, replica_groups=mesh['parts'=2,'fsdp'=4,'seq'=2,'ctx'=2] {'fsdp'}, dimensions={0} | all-to-all | bytes 3145728 | tf_op jit(solution)/shard_map/all_to_all | solution.py:60
  63.2 5.1 %fusion.34 = (f16[4,96,2048]{2,1,0:T(8,128)(2,1)}, f32[4,96,2048]{2,1,0:T(8,128)}) fusion(bf16[4,96,2048]{2,1,0:T(8,128)(2,1)S(1)} %all_to_all.15, bf16[2048,2048]{1,0:T(8,128)(2,1)S(1)} %copy-done.1), kind=kOutput, calls=%fused_computation.79 | convolution fusion | flops 3222011904 | bytes 14680064 | tf_op jit(solution)/shard_map/dot_general | solution.py:63
  68.2 3.7 %all-to-all-start.1 = ((f16[4,96,2048]{2,1,0:T(8,128)(2,1)}), f16[4,96,2048]{2,1,0:T(8,128)(2,1)S(1)}, u32[]{:S(2)}, u32[]{:S(2)}) async-start(f16[4,96,2048]{2,1,0:T(8,128)(2,1)} %get-tuple-element.22), calls=%async_computation.1 | async-start | bytes 3145728 | tf_op jit(solution)/shard_map/all_to_all | solution.py:65
  71.9 1.0 broadcast_in_dim.16
  72.9 1.9 %reshape.67 = f32[2048,7]{0,1:T(8,128)} reshape(f32[128,16,7]{1,0,2:T(8,128)} %broadcast_in_dim.16) | data formatting | bytes 114688 | tf_op jit(solution)/shard_map/reshape | solution.py:70
  74.8 33.1 %all-to-all-done.1 = f16[4,96,2048]{2,1,0:T(8,128)(2,1)S(1)} async-done(((f16[4,96,2048]{2,1,0:T(8,128)(2,1)}), f16[4,96,2048]{2,1,0:T(8,128)(2,1)S(1)}, u32[]{:S(2)}, u32[]{:S(2)}) %all-to-all-start.1) | async-done | bytes 1572896 | tf_op jit(solution)/shard_map/all_to_all | solution.py:65
  107.9 0.5 select_reduce_fusion
  108.4 1.2 fusion.30
  109.7 1.3 collective-permute-start.1
  111.0 0.8 collective-permute-done.1
  111.8 0.1 maximum_convert_fusion
  112.0 0.8 convert_multiply_fusion
  112.8 1.3 collective-permute-start.2
  114.1 1.8 %collective-permute-done.2 = f32[6,2048]{1,0:T(8,128)S(1)} collective-permute-done((f32[6,2048]{1,0:T(8,128)S(1)}, f32[6,2048]{1,0:T(8,128)S(1)}, u32[]{:S(2)}, u32[]{:S(2)}) %collective-permute-start.2) | collective-permute-done | bytes 49184 | tf_op jit(solution)/shard_map/ppermute | solution.py:13
  115.9 0.7 fusion.10
  116.6 1.4 broadcast_in_dim.30
  118.0 3.7 %all-to-all-start.2 = ((bf16[4,96,2048]{2,1,0:T(8,128)(2,1)}), bf16[4,96,2048]{2,1,0:T(8,128)(2,1)S(1)}, u32[]{:S(2)}, u32[]{:S(2)}) async-start(bf16[4,96,2048]{2,1,0:T(8,128)(2,1)} %broadcast_in_dim.30), calls=%async_computation.2 | async-start | bytes 3145728 | tf_op jit(solution)/shard_map/all_to_all | solution.py:90
  121.7 1.6 copy.14
  123.3 35.8 %all-to-all-done.2 = bf16[4,96,2048]{2,1,0:T(8,128)(2,1)S(1)} async-done(((bf16[4,96,2048]{2,1,0:T(8,128)(2,1)}), bf16[4,96,2048]{2,1,0:T(8,128)(2,1)S(1)}, u32[]{:S(2)}, u32[]{:S(2)}) %all-to-all-start.2) | async-done | bytes 1572896 | tf_op jit(solution)/shard_map/all_to_all | solution.py:90
  159.1 15.4 %divide_reduce_fusion = (f32[16,2048]{1,0:T(8,128)S(1)}, f32[16,2048]{1,0:T(8,128)S(1)}, f32[16,2048]{1,0:T(8,128)S(1)}, f32[16,2048]{1,0:T(8,128)S(1)}) fusion(f32[16,2048]{1,0:T(8,128)S(1)} %get-tuple-element.11, f32[16,2048]{1,0:T(8,128)S(1)} %get-tuple-element.14, bf16[2048,2048]{1,0:T(8,128)(2,1)} %param.8, f32[16,2048]{1,0:T(8,128)} %get-tuple-element.10, ...), kind=kOutput, calls=%fused_computation.11 | convolution fusion | flops 3288203264 | bytes 12451840 | tf_op jit(solution)/shard_map/dot_general | solution.py:91
  174.5 0.1 fusion.32
  174.7 0.5 collective-permute-start.3
  175.2 0.8 collective-permute-done.4
  176.0 0.7 add.102
  176.7 0.7 add.101
  (26 shorter events, 0.2 us)
Async XLA Ops:
  0.6 20.8 %collective-permute-start = (bf16[96,4096]{1,0:T(8,128)(2,1)}, bf16[96,4096]{1,0:T(8,128)(2,1)S(1)}, u32[]{:S(2)}, u32[]{:S(2)}) collective-permute-start(bf16[96,4096]{1,0:T(8,128)(2,1)} %bitcast.82), channel_id=1, source_target_pairs={{0,2},{2,0},{1,3},{3,1},{4,6},{6,4},{5,7},{7,5},{8,10},{10,8},{9,1... | collective-permute-start | bytes 2359304 | tf_op jit(solution)/shard_map/ppermute | solution.py:33
  3.6 5.9 %copy-start.3 = (f32[16,2048]{1,0:T(8,128)S(1)}, f32[16,2048]{1,0:T(8,128)}, u32[]{:S(2)}) copy-start(f32[16,2048]{1,0:T(8,128)} %param.10) | copy-start | bytes 393220
  3.6 7.6 %copy-start = (bf16[2048,2048]{1,0:T(8,128)(2,1)S(1)}, bf16[2048,2048]{1,0:T(8,128)(2,1)}, u32[]{:S(2)}) copy-start(bf16[2048,2048]{1,0:T(8,128)(2,1)} %param.8) | copy-start | bytes 25165828
  11.2 10.2 %copy-start.2 = (bf16[1,1,96,4096]{3,2,1,0:T(8,128)(2,1)S(1)}, bf16[1,1,96,4096]{3,2,1,0:T(8,128)(2,1)}, u32[]{:S(2)}) copy-start(bf16[1,1,96,4096]{3,2,1,0:T(8,128)(2,1)} %param.7) | copy-start | bytes 2359300
  21.4 41.8 %copy-start.1 = (bf16[2048,2048]{1,0:T(8,128)(2,1)S(1)}, bf16[2048,2048]{1,0:T(8,128)(2,1)}, u32[]{:S(2)}) copy-start(bf16[2048,2048]{1,0:T(8,128)(2,1)} %fusion) | copy-start | bytes 25165828
  68.2 3.7 %copy-start.9 = (f32[128,7]{0,1:T(8,128)S(1)}, f32[128,7]{0,1:T(8,128)}, u32[]{:S(2)}) copy-start(f32[128,7]{0,1:T(8,128)} %param.11) | copy-start | bytes 10756
  68.2 39.7 %all-to-all-start.1 = ((f16[4,96,2048]{2,1,0:T(8,128)(2,1)}), f16[4,96,2048]{2,1,0:T(8,128)(2,1)S(1)}, u32[]{:S(2)}, u32[]{:S(2)}) async-start(f16[4,96,2048]{2,1,0:T(8,128)(2,1)} %get-tuple-element.22), calls=%async_computation.1 | async-start | bytes 3145728 | tf_op jit(solution)/shard_map/all_to_all | solution.py:65
  107.9 3.1 %copy-start.8 = (f32[2048,7]{0,1:T(8,128)S(1)}, f32[2048,7]{0,1:T(8,128)}, u32[]{:S(2)}) copy-start(f32[2048,7]{0,1:T(8,128)} %reshape.67) | copy-start | bytes 172036
  107.9 4.0 %copy-start.6 = (bf16[1,1,96,2048]{3,2,1,0:T(8,128)(2,1)S(1)}, bf16[1,1,96,2048]{3,2,1,0:T(8,128)(2,1)}, u32[]{:S(2)}) copy-start(bf16[1,1,96,2048]{3,2,1,0:T(8,128)(2,1)} %param.13) | copy-start | bytes 1179652
  107.9 4.0 %copy-start.7 = (bf16[1,1,96,2048]{3,2,1,0:T(8,128)(2,1)S(1)}, bf16[1,1,96,2048]{3,2,1,0:T(8,128)(2,1)}, u32[]{:S(2)}) copy-start(bf16[1,1,96,2048]{3,2,1,0:T(8,128)(2,1)} %param.12) | copy-start | bytes 1179652
  109.7 2.1 %collective-permute-start.1 = (bf16[6,2048]{1,0:T(8,128)(2,1)S(1)}, bf16[6,2048]{1,0:T(8,128)(2,1)S(1)}, u32[]{:S(2)}, u32[]{:S(2)}) collective-permute-start(bf16[6,2048]{1,0:T(8,128)(2,1)S(1)} %slice.96), channel_id=1, source_target_pairs={{0,1},{2,3},{4,5},{6,7},{8,9},{10,11},{12,13},{14,15},{16,17},{18,... | collective-permute-start | bytes 73736 | tf_op jit(solution)/shard_map/ppermute | solution.py:13
  112.8 3.1 %collective-permute-start.2 = (f32[6,2048]{1,0:T(8,128)S(1)}, f32[6,2048]{1,0:T(8,128)S(1)}, u32[]{:S(2)}, u32[]{:S(2)}) collective-permute-start(f32[6,2048]{1,0:T(8,128)S(1)} %slice.110), channel_id=1, source_target_pairs={{1,0},{3,2},{5,4},{7,6},{9,8},{11,10},{13,12},{15,14},{17,16},{19,... | collective-permute-start | bytes 147464 | tf_op jit(solution)/shard_map/ppermute | solution.py:13
  118.0 41.1 %all-to-all-start.2 = ((bf16[4,96,2048]{2,1,0:T(8,128)(2,1)}), bf16[4,96,2048]{2,1,0:T(8,128)(2,1)S(1)}, u32[]{:S(2)}, u32[]{:S(2)}) async-start(bf16[4,96,2048]{2,1,0:T(8,128)(2,1)} %broadcast_in_dim.30), calls=%async_computation.2 | async-start | bytes 3145728 | tf_op jit(solution)/shard_map/all_to_all | solution.py:90
  159.1 15.4 %copy-start.4 = (f32[16,2048]{1,0:T(8,128)S(1)}, f32[16,2048]{1,0:T(8,128)}, u32[]{:S(2)}) copy-start(f32[16,2048]{1,0:T(8,128)} %param.10) | copy-start | bytes 393220
  159.1 15.4 %copy-start.5 = (f32[16,2048]{1,0:T(8,128)S(1)}, f32[16,2048]{1,0:T(8,128)}, u32[]{:S(2)}) copy-start(f32[16,2048]{1,0:T(8,128)} %param.9) | copy-start | bytes 393220
  174.6 1.4 collective-permute-start.4
  174.7 2.0 %collective-permute-start.3 = (f32[16,2048]{1,0:T(8,128)S(1)}, f32[16,2048]{1,0:T(8,128)S(1)}, u32[]{:S(2)}, u32[]{:S(2)}) collective-permute-start(f32[16,2048]{1,0:T(8,128)S(1)} %get-tuple-element.13), channel_id=1, source_target_pairs={{0,1},{1,0},{2,3},{3,2},{4,5},{5,4},{6,7},{7,6},{8,9},{9,8},{10,11... | collective-permute-start | bytes 393224 | tf_op jit(solution)/shard_map/ppermute | solution.py:46

commit v6 on v4

--- a/solution.py
+++ b/solution.py
@@ -46,37 +46,22 @@
     return value + lax.ppermute(value, "ctx", [(0, 1), (1, 0)])
 
 
-def on_device(hidden_in, weight, clip_upper, clip_lower, filters, gate, target):
-    shards = lax.axis_size("fsdp")
-    width = hidden_in.shape[-1]
-    local_rows = hidden_in.reshape(-1, width)
-    length = local_rows.shape[0]
-    rows, columns = weight.shape
-    features = gather_features(local_rows)
-    pieces = features.reshape(length, shards, rows).transpose(1, 0, 2)
-    mine = lax.all_to_all(pieces, "fsdp", 0, 0)
-    inputs = mine.reshape(shards * length, rows)
-
-    values = weight.astype(jnp.float32)
-    quant = soft_clip(values, clip_upper, clip_lower).astype(jnp.bfloat16)
+def column_stream(inputs, quant, values, clip_upper, clip_lower, taps, gates, wanted, scale, me, shards, length):
+    columns = quant.shape[1]
     partial = jnp.dot(inputs, quant, preferred_element_type=jnp.float32).reshape(shards, length, columns)
-    me = lax.axis_index("fsdp")
     received = lax.all_to_all(partial.astype(jnp.float16), "fsdp", 0, 0).astype(jnp.float32)
     others = jnp.where((jnp.arange(shards) == me)[:, None, None], 0.0, received)
     own = lax.dynamic_index_in_dim(partial, me, 0, keepdims=False)
     proj = (own + jnp.sum(others, axis=0)).astype(jnp.bfloat16)
 
-    taps = jnp.repeat(filters, CGROUP, axis=0).T
     pad = FILT - 1
     previous = from_behind(proj[length - pad :], "ctx", 1)
     padded = jnp.concatenate([previous, proj], axis=0).astype(jnp.float32)
     conv = jnp.zeros((length, columns), jnp.float32)
     for tap in range(FILT):
         conv = conv + taps[tap] * padded[pad - tap : pad - tap + length]
-    gates = gate.reshape(length, columns).astype(jnp.float32)
-    wanted = target.reshape(length, columns).astype(jnp.float32)
-    total_tokens = lax.axis_size("fsdp") * lax.axis_size("ctx") * length
-    scale = 1024.0 / jnp.sqrt(jnp.float32(total_tokens))
+    gates = gates.astype(jnp.float32)
+    wanted = wanted.astype(jnp.float32)
     d_conv = scale * (gates * conv - wanted) * gates
     following = from_behind(d_conv[:pad], "ctx", -1)
     padded_back = jnp.concatenate([d_conv, following], axis=0)
@@ -95,7 +80,42 @@
         clip_upper,
         clip_lower,
     )
-    grad_up, grad_low = pull(d_clipped)
+    return pull(d_clipped)
+
+
+def on_device(hidden_in, weight, clip_upper, clip_lower, filters, gate, target):
+    shards = lax.axis_size("fsdp")
+    width = hidden_in.shape[-1]
+    local_rows = hidden_in.reshape(-1, width)
+    length = local_rows.shape[0]
+    rows, columns = weight.shape
+    features = gather_features(local_rows)
+    values = weight.astype(jnp.float32)
+    quant = soft_clip(values, clip_upper, clip_lower).astype(jnp.bfloat16)
+    features, quant = lax.optimization_barrier((features, quant))
+    pieces = features.reshape(length, shards, rows).transpose(1, 0, 2)
+    mine = lax.all_to_all(pieces, "fsdp", 0, 0)
+    inputs = mine.reshape(shards * length, rows)
+
+    taps_all = jnp.repeat(filters, CGROUP, axis=0).T
+    gates_all = gate.reshape(length, columns)
+    wanted_all = target.reshape(length, columns)
+    total_tokens = lax.axis_size("fsdp") * lax.axis_size("ctx") * length
+    scale = 1024.0 / jnp.sqrt(jnp.float32(total_tokens))
+    me = lax.axis_index("fsdp")
+    streams = 2 if columns % (2 * 128) == 0 else 1
+    width_of = columns // streams
+    ups, lows = [], []
+    for stream in range(streams):
+        cols = slice(stream * width_of, (stream + 1) * width_of)
+        grad_up, grad_low = column_stream(
+            inputs, quant[:, cols], values[:, cols], clip_upper[:, cols], clip_lower[:, cols],
+            taps_all[:, cols], gates_all[:, cols], wanted_all[:, cols], scale, me, shards, length,
+        )
+        ups.append(grad_up)
+        lows.append(grad_low)
+    grad_up = jnp.concatenate(ups, axis=1)
+    grad_low = jnp.concatenate(lows, axis=1)
     grad_upper, grad_lower = sum_over_ctx(grad_up), sum_over_ctx(grad_low)
     return (grad_upper, grad_lower)
 

time: 184 us -> 191 us (1.038)
  waiting for transfers between devices: 108 us -> 48.3 us
  blocking collectives: 0 us -> 41 us
  other arithmetic: 22.6 us -> 36.9 us
  matrix products: 23.8 us -> 30.8 us
  starting transfers between devices: 18.6 us -> 24.6 us
  local copies, waits for them, and re-layouts: 9.93 us -> 7.2 us
    all_to_all x3 -> x4, waiting for transfers between devices: 90.2 us -> 37 us  [the longest x2 30.5 us: column_stream(): lax.all_to_all(partial.astype(jnp.float16), 'fsdp', 0, 0)]
    all_to_all x0 -> x1, blocking collectives: none -> 41 us  [on_device(): mine = lax.all_to_all(pieces, 'fsdp', 0, 0)]
    convert_element_type x3 -> x7, other arithmetic: 2.05 us -> 14.1 us  [the longest x1 11.2 us: on_device(): values = weight.astype(jnp.float32)]
    reduce_max x1 -> x2, other arithmetic: 5.68 us -> 12.9 us  [soft_clip(): amax = jnp.max(jnp.abs(blocks), axis=1) + 1e-06]
    dot_general x2 -> x4, matrix products: 23.8 us -> 30.8 us  [the longest x2 22.1 us: column_stream(): lax.dot_general(inputs, d_all, (((0,), (0,)), ((), ())), preferred_elemen...]
    ppermute x1, waiting for transfers between devices: 14.9 us -> 7.94 us  [gather_features(): other = lax.ppermute(local_rows, 'seq', [(0, 1), (1, 0)])]
    convert_element_type x1, other arithmetic: 8.76 us -> 3.73 us  [on_device(): quant = soft_clip(values, clip_upper, clip_lower).astype(jnp.bfloat16)]
    ppermute x2 -> x4, starting transfers between devices: 2.58 us -> 6.12 us  [from_behind(): return lax.ppermute(value, axis, pairs)]
  transfers between devices with their start and end apart: 8 -> 11, of which waited for: 6 -> 8; matrix products, arithmetic and copies ran while one was open for 13% -> 26% of each run, Pallas kernels for 0% -> 0%
where the time goes in v6:
time: 191 us; the launch traced here: 190 us
  waiting for transfers between devices  48.3 us (25%)
  blocking collectives  41 us (21%)
  other arithmetic  36.9 us (19%)
  matrix products  30.8 us (16%)
  starting transfers between devices  24.6 us (13%)
  local copies, waits for them, and re-layouts  7.2 us (4%)
    all_to_all x1, blocking collectives, on_device(): mine = lax.all_to_all(pieces, 'fsdp', 0, 0)  41 us
    all_to_all x2, waiting for transfers between devices, column_stream(): lax.all_to_all(partial.astype(jnp.float16), 'fsdp', 0, 0)  30.5 us
    dot_general x2, matrix products, column_stream(): lax.dot_general(inputs, d_all, (((0,), (0,)), ((), ())), preferred_elemen...  22.1 us
    reduce_max x2, other arithmetic, soft_clip(): amax = jnp.max(jnp.abs(blocks), axis=1) + 1e-06  12.9 us
    convert_element_type x1, other arithmetic, on_device(): values = weight.astype(jnp.float32)  11.2 us
    dot_general x2, matrix products, column_stream(): jnp.dot(inputs, quant, preferred_element_type=jnp.float32)  8.64 us
    ppermute x1, waiting for transfers between devices, gather_features(): other = lax.ppermute(local_rows, 'seq', [(0, 1), (1, 0)])  7.94 us
    all_to_all x2, starting transfers between devices, column_stream(): lax.all_to_all(copies, 'fsdp', 0, 0).reshape(shards * length, columns)  7.69 us
  transfers between devices with their start and end apart: 11, of which 8 were waited for; matrix products, arithmetic and copies ran while one was open for 26% of the time, Pallas kernels for 0%

profile of v6, /device:TPU:0, one launch (start us, length us, event | category | flops | bytes accessed | tf_op | source)
XLA Modules:
  0.0 189.9 jit_solution(8979097081942138328)
XLA Ops:
  0.7 3.0 %collective-permute-start = (bf16[96,4096]{1,0:T(8,128)(2,1)}, bf16[96,4096]{1,0:T(8,128)(2,1)S(1)}, u32[]{:S(2)}, u32[]{:S(2)}) collective-permute-start(bf16[96,4096]{1,0:T(8,128)(2,1)} %bitcast.115), channel_id=1, source_target_pairs={{0,2},{2,0},{1,3},{3,1},{4,6},{6,4},{5,7},{7,5},{8,10},{10,8},{9,1... | collective-permute-start | bytes 2359304 | tf_op jit(solution)/shard_map/ppermute | solution.py:33
  3.7 5.9 %bitcast_reduce_fusion = f32[16,2048]{1,0:T(8,128)S(1)} fusion(bf16[2048,2048]{1,0:T(8,128)(2,1)} %param.8), kind=kLoop, calls=%fused_computation.6 | loop fusion | flops 12550144 | bytes 8519680 | tf_op jit(solution)/shard_map/reduce_max | solution.py:20
  9.7 3.7 %fusion = bf16[2048,2048]{1,0:T(8,128)(2,1)S(1)} fusion(f32[16,2048]{1,0:T(8,128)S(1)} %get-tuple-element.26, f32[16,2048]{1,0:T(8,128)S(1)} %get-tuple-element.25, bf16[2048,2048]{1,0:T(8,128)(2,1)S(1)} %copy-done), kind=kLoop, calls=%fused_computation.4 | loop fusion | flops 25165824 | bytes 17039360 | tf_op jit(solution)/shard_map/convert_element_type | solution.py:94
  13.5 7.9 %collective-permute-done = bf16[96,4096]{1,0:T(8,128)(2,1)S(1)} collective-permute-done((bf16[96,4096]{1,0:T(8,128)(2,1)}, bf16[96,4096]{1,0:T(8,128)(2,1)S(1)}, u32[]{:S(2)}, u32[]{:S(2)}) %collective-permute-start) | collective-permute-done | bytes 786464 | tf_op jit(solution)/shard_map/ppermute | solution.py:33
  21.9 41.0 %all_to_all.25 = bf16[4,96,2048]{2,1,0:T(8,128)(2,1)S(1)} all-to-all(bf16[4,96,2048]{2,1,0:T(8,128)(2,1)S(1)} %bitcast.110), channel_id=1, replica_groups=mesh['parts'=2,'fsdp'=4,'seq'=2,'ctx'=2] {'fsdp'}, dimensions={0} | all-to-all | bytes 3145728 | tf_op jit(solution)/shard_map/all_to_all | solution.py:97
  62.9 3.3 %fusion.70 = (f16[4,96,1024]{2,1,0:T(8,128)(2,1)}, f32[4,96,1024]{2,1,0:T(8,128)}) fusion(bf16[4,96,2048]{2,1,0:T(8,128)(2,1)S(1)} %all_to_all.25, bf16[2048,2048]{1,0:T(8,128)(2,1)S(1)} %fusion), kind=kOutput, calls=%fused_computation.161 | convolution fusion | flops 1611005952 | bytes 8126464 | tf_op jit(solution)/shard_map/dot_general | solution.py:51
  66.2 3.6 %all-to-all-start.3 = ((f16[4,96,1024]{2,1,0:T(8,128)(2,1)}), f16[4,96,1024]{2,1,0:T(8,128)(2,1)S(1)}, u32[]{:S(2)}, u32[]{:S(2)}) async-start(f16[4,96,1024]{2,1,0:T(8,128)(2,1)} %get-tuple-element.54), calls=%async_computation.3 | async-start | bytes 1572864 | tf_op jit(solution)/shard_map/all_to_all | solution.py:52
  69.8 5.4 %fusion.69 = (f16[4,96,1024]{2,1,0:T(8,128)(2,1)}, f32[4,96,1024]{2,1,0:T(8,128)}) fusion(bf16[4,96,2048]{2,1,0:T(8,128)(2,1)S(1)} %all_to_all.25, bf16[2048,2048]{1,0:T(8,128)(2,1)} %copy-done.1), kind=kOutput, calls=%fused_computation.160 | convolution fusion | flops 1611005952 | bytes 8126464 | tf_op jit(solution)/shard_map/dot_general | solution.py:51
  75.2 13.8 %all-to-all-done.3 = f16[4,96,1024]{2,1,0:T(8,128)(2,1)S(1)} async-done(((f16[4,96,1024]{2,1,0:T(8,128)(2,1)}), f16[4,96,1024]{2,1,0:T(8,128)(2,1)S(1)}, u32[]{:S(2)}, u32[]{:S(2)}) %all-to-all-start.3) | async-done | bytes 786464 | tf_op jit(solution)/shard_map/all_to_all | solution.py:52
  89.0 3.5 %all-to-all-start.1 = ((f16[4,96,1024]{2,1,0:T(8,128)(2,1)}), f16[4,96,1024]{2,1,0:T(8,128)(2,1)S(1)}, u32[]{:S(2)}, u32[]{:S(2)}) async-start(f16[4,96,1024]{2,1,0:T(8,128)(2,1)} %get-tuple-element.52), calls=%async_computation.1 | async-start | bytes 1572864 | tf_op jit(solution)/shard_map/all_to_all | solution.py:52
  93.4 1.9 reshape.100
  95.3 16.7 %all-to-all-done.1 = f16[4,96,1024]{2,1,0:T(8,128)(2,1)S(1)} async-done(((f16[4,96,1024]{2,1,0:T(8,128)(2,1)}), f16[4,96,1024]{2,1,0:T(8,128)(2,1)S(1)}, u32[]{:S(2)}, u32[]{:S(2)}) %all-to-all-start.1) | async-done | bytes 786464 | tf_op jit(solution)/shard_map/all_to_all | solution.py:52
  112.6 1.0 fusion.60
  113.6 1.3 collective-permute-start.3
  114.9 1.2 fusion.68
  116.2 1.4 convert_multiply_fusion
  117.7 1.3 collective-permute-start.4
  119.0 1.8 collective-permute-done.4
  121.1 1.0 broadcast_in_dim.43
  122.1 3.5 %all-to-all-start.4 = ((bf16[4,96,1024]{2,1,0:T(8,128)(2,1)}), bf16[4,96,1024]{2,1,0:T(8,128)(2,1)S(1)}, u32[]{:S(2)}, u32[]{:S(2)}) async-start(bf16[4,96,1024]{2,1,0:T(8,128)(2,1)} %broadcast_in_dim.43), calls=%async_computation.4 | async-start | bytes 1572864 | tf_op jit(solution)/shard_map/all_to_all | solution.py:74
  125.6 1.0 fusion.61
  126.7 2.1 %collective-permute-start.1 = (bf16[6,1024]{1,0:T(8,128)(2,1)S(1)}, bf16[6,1024]{1,0:T(8,128)(2,1)S(1)}, u32[]{:S(2)}, u32[]{:S(2)}) collective-permute-start(bf16[6,1024]{1,0:T(8,128)(2,1)S(1)} %slice.256), channel_id=1, source_target_pairs={{0,1},{2,3},{4,5},{6,7},{8,9},{10,11},{12,13},{14,15},{16,17},{18,... | collective-permute-start | bytes 36872 | tf_op jit(solution)/shard_map/ppermute | solution.py:13
  129.6 1.4 convert_multiply_fusion.2
  131.1 1.5 collective-permute-start.2
  132.6 11.2 %convert_element_type.48 = f32[2048,2048]{1,0:T(8,128)} convert(bf16[2048,2048]{1,0:T(8,128)(2,1)} %param.8) | non-fusion elementwise | flops 4194304 | bytes 25165824 | tf_op jit(solution)/shard_map/convert_element_type | solution.py:93
  144.1 2.2 %all-to-all-done.4 = bf16[4,96,1024]{2,1,0:T(8,128)(2,1)S(1)} async-done(((bf16[4,96,1024]{2,1,0:T(8,128)(2,1)}), bf16[4,96,1024]{2,1,0:T(8,128)(2,1)S(1)}, u32[]{:S(2)}, u32[]{:S(2)}) %all-to-all-start.4) | async-done | bytes 786464 | tf_op jit(solution)/shard_map/all_to_all | solution.py:74
  146.3 1.1 broadcast_in_dim.42
  147.4 4.2 %all-to-all-start.2 = ((bf16[4,96,1024]{2,1,0:T(8,128)(2,1)}), bf16[4,96,1024]{2,1,0:T(8,128)(2,1)}, u32[]{:S(2)}, u32[]{:S(2)}) async-start(bf16[4,96,1024]{2,1,0:T(8,128)(2,1)} %broadcast_in_dim.42), calls=%async_computation.2 | async-start | bytes 1572864 | tf_op jit(solution)/shard_map/all_to_all | solution.py:74
  151.6 7.0 %abs_reduce_fusion.1 = (f32[16,1024]{1,0:T(8,128)S(1)}, f32[16,1024]{1,0:T(8,128)S(1)}) fusion(f32[2048,2048]{1,0:T(8,128)} %convert_element_type.48), kind=kLoop, calls=%fused_computation.16 | loop fusion | flops 8355840 | bytes 16908288 | tf_op jit(solution)/shard_map/jvp()/reduce_max | solution.py:20
  160.4 6.8 %fusion.71 = f32[16,128,1024]{2,1,0:T(8,128)} fusion(bf16[16,128,384]{2,1,0:T(8,128)(2,1)S(1)} %bitcast.112, bf16[384,1024,1]{1,0,2:T(8,128)(2,1)} %bitcast.114), kind=kOutput, calls=%fused_computation.162 | convolution fusion | flops 1610612736 | bytes 10747904 | tf_op jit(solution)/shard_map/dot_general | solution.py:75
  167.1 4.4 %all-to-all-done.2 = bf16[4,96,1024]{2,1,0:T(8,128)(2,1)} async-done(((bf16[4,96,1024]{2,1,0:T(8,128)(2,1)}), bf16[4,96,1024]{2,1,0:T(8,128)(2,1)}, u32[]{:S(2)}, u32[]{:S(2)}) %all-to-all-start.2) | async-done | bytes 786464 | tf_op jit(solution)/shard_map/all_to_all | solution.py:74
  171.6 15.4 %divide_reduce_fusion.1 = (f32[16,1024]{1,0:T(8,128)S(1)}, f32[16,1024]{1,0:T(8,128)S(1)}, f32[16,1024]{1,0:T(8,128)S(1)}, f32[16,1024]{1,0:T(8,128)S(1)}, f32[1...) fusion(f32[16,1024]{1,0:T(8,128)S(1)} %copy-done.13, ...), kind=kOutput, calls=%fused_computation.19 | convolution fusion | flops 1673396224 | bytes 28442624 | tf_op jit(solution)/shard_map/dot_general | solution.py:75
  (58 shorter events, 8.3 us)
Async XLA Ops:
  0.6 9.0 %copy-start.3 = (f32[16,2048]{1,0:T(8,128)S(1)}, f32[16,2048]{1,0:T(8,128)}, u32[]{:S(2)}) copy-start(f32[16,2048]{1,0:T(8,128)} %param.10) | copy-start | bytes 393220
  0.6 8.9 %copy-start.5 = (f32[16,2048]{1,0:T(8,128)S(1)}, f32[16,2048]{1,0:T(8,128)}, u32[]{:S(2)}) copy-start(f32[16,2048]{1,0:T(8,128)} %param.9) | copy-start | bytes 393220
  0.7 20.8 %collective-permute-start = (bf16[96,4096]{1,0:T(8,128)(2,1)}, bf16[96,4096]{1,0:T(8,128)(2,1)S(1)}, u32[]{:S(2)}, u32[]{:S(2)}) collective-permute-start(bf16[96,4096]{1,0:T(8,128)(2,1)} %bitcast.115), channel_id=1, source_target_pairs={{0,2},{2,0},{1,3},{3,1},{4,6},{6,4},{5,7},{7,5},{8,10},{10,8},{9,1... | collective-permute-start | bytes 2359304 | tf_op jit(solution)/shard_map/ppermute | solution.py:33
  3.7 6.0 %copy-start = (bf16[2048,2048]{1,0:T(8,128)(2,1)S(1)}, bf16[2048,2048]{1,0:T(8,128)(2,1)}, u32[]{:S(2)}) copy-start(bf16[2048,2048]{1,0:T(8,128)(2,1)} %param.8) | copy-start | bytes 25165828
  9.7 11.7 %copy-start.7 = (bf16[1,1,96,4096]{3,2,1,0:T(8,128)(2,1)S(1)}, bf16[1,1,96,4096]{3,2,1,0:T(8,128)(2,1)}, u32[]{:S(2)}) copy-start(bf16[1,1,96,4096]{3,2,1,0:T(8,128)(2,1)} %param.7) | copy-start | bytes 2359300
  13.5 52.7 %copy-start.1 = (bf16[2048,2048]{1,0:T(8,128)(2,1)}, bf16[2048,2048]{1,0:T(8,128)(2,1)S(1)}, u32[]{:S(2)}) copy-start(bf16[2048,2048]{1,0:T(8,128)(2,1)S(1)} %fusion) | copy-start | bytes 25165828
  66.2 26.3 %copy-start.14 = (f32[128,7]{0,1:T(8,128)S(1)}, f32[128,7]{0,1:T(8,128)}, u32[]{:S(2)}) copy-start(f32[128,7]{0,1:T(8,128)} %param.11) | copy-start | bytes 10756
  66.2 22.8 %all-to-all-start.3 = ((f16[4,96,1024]{2,1,0:T(8,128)(2,1)}), f16[4,96,1024]{2,1,0:T(8,128)(2,1)S(1)}, u32[]{:S(2)}, u32[]{:S(2)}) async-start(f16[4,96,1024]{2,1,0:T(8,128)(2,1)} %get-tuple-element.54), calls=%async_computation.3 | async-start | bytes 1572864 | tf_op jit(solution)/shard_map/all_to_all | solution.py:52
  89.0 23.1 %all-to-all-start.1 = ((f16[4,96,1024]{2,1,0:T(8,128)(2,1)}), f16[4,96,1024]{2,1,0:T(8,128)(2,1)S(1)}, u32[]{:S(2)}, u32[]{:S(2)}) async-start(f16[4,96,1024]{2,1,0:T(8,128)(2,1)} %get-tuple-element.52), calls=%async_computation.1 | async-start | bytes 1572864 | tf_op jit(solution)/shard_map/all_to_all | solution.py:52
  113.6 2.5 %collective-permute-start.3 = (bf16[6,1024]{1,0:T(8,128)(2,1)S(1)}, bf16[6,1024]{1,0:T(8,128)(2,1)S(1)}, u32[]{:S(2)}, u32[]{:S(2)}) collective-permute-start(bf16[6,1024]{1,0:T(8,128)(2,1)S(1)} %slice.285), channel_id=1, source_target_pairs={{0,1},{2,3},{4,5},{6,7},{8,9},{10,11},{12,13},{14,15},{16,17},{18,... | collective-permute-start | bytes 36872 | tf_op jit(solution)/shard_map/ppermute | solution.py:13
  117.7 3.1 %collective-permute-start.4 = (f32[6,1024]{1,0:T(8,128)S(1)}, f32[6,1024]{1,0:T(8,128)S(1)}, u32[]{:S(2)}, u32[]{:S(2)}) collective-permute-start(f32[6,1024]{1,0:T(8,128)S(1)} %slice.300), channel_id=1, source_target_pairs={{1,0},{3,2},{5,4},{7,6},{9,8},{11,10},{13,12},{15,14},{17,16},{19,... | collective-permute-start | bytes 73736 | tf_op jit(solution)/shard_map/ppermute | solution.py:13
  122.1 24.2 %all-to-all-start.4 = ((bf16[4,96,1024]{2,1,0:T(8,128)(2,1)}), bf16[4,96,1024]{2,1,0:T(8,128)(2,1)S(1)}, u32[]{:S(2)}, u32[]{:S(2)}) async-start(bf16[4,96,1024]{2,1,0:T(8,128)(2,1)} %broadcast_in_dim.43), calls=%async_computation.4 | async-start | bytes 1572864 | tf_op jit(solution)/shard_map/all_to_all | solution.py:74
  126.7 2.9 %collective-permute-start.1 = (bf16[6,1024]{1,0:T(8,128)(2,1)S(1)}, bf16[6,1024]{1,0:T(8,128)(2,1)S(1)}, u32[]{:S(2)}, u32[]{:S(2)}) collective-permute-start(bf16[6,1024]{1,0:T(8,128)(2,1)S(1)} %slice.256), channel_id=1, source_target_pairs={{0,1},{2,3},{4,5},{6,7},{8,9},{10,11},{12,13},{14,15},{16,17},{18,... | collective-permute-start | bytes 36872 | tf_op jit(solution)/shard_map/ppermute | solution.py:13
  131.1 12.7 %collective-permute-start.2 = (f32[6,1024]{1,0:T(8,128)S(1)}, f32[6,1024]{1,0:T(8,128)S(1)}, u32[]{:S(2)}, u32[]{:S(2)}) collective-permute-start(f32[6,1024]{1,0:T(8,128)S(1)} %slice.271), channel_id=1, source_target_pairs={{1,0},{3,2},{5,4},{7,6},{9,8},{11,10},{13,12},{15,14},{17,16},{19,... | collective-permute-start | bytes 73736 | tf_op jit(solution)/shard_map/ppermute | solution.py:13
  146.3 12.3 %copy-start.2 = (bf16[4,96,1024]{2,1,0:T(8,128)(2,1)}, bf16[4,96,1024]{2,1,0:T(8,128)(2,1)S(1)}, u32[]{:S(2)}) copy-start(bf16[4,96,1024]{2,1,0:T(8,128)(2,1)S(1)} %all-to-all-done.4) | copy-start | bytes 2359300
  147.4 24.1 %all-to-all-start.2 = ((bf16[4,96,1024]{2,1,0:T(8,128)(2,1)}), bf16[4,96,1024]{2,1,0:T(8,128)(2,1)}, u32[]{:S(2)}, u32[]{:S(2)}) async-start(bf16[4,96,1024]{2,1,0:T(8,128)(2,1)} %broadcast_in_dim.42), calls=%async_computation.2 | async-start | bytes 1572864 | tf_op jit(solution)/shard_map/all_to_all | solution.py:74
  151.6 7.0 %copy-start.4 = (f32[16,2048]{1,0:T(8,128)S(1)}, f32[16,2048]{1,0:T(8,128)}, u32[]{:S(2)}) copy-start(f32[16,2048]{1,0:T(8,128)} %param.10) | copy-start | bytes 393220
  151.6 7.0 %copy-start.6 = (f32[16,2048]{1,0:T(8,128)S(1)}, f32[16,2048]{1,0:T(8,128)}, u32[]{:S(2)}) copy-start(f32[16,2048]{1,0:T(8,128)} %param.9) | copy-start | bytes 393220
  160.3 11.2 %copy-start.8 = (f32[16,1024]{1,0:T(8,128)S(1)}, f32[16,1024]{1,0:T(8,128)}, u32[]{:S(2)}) copy-start(f32[16,1024]{1,0:T(8,128)} %get-tuple-element.21) | copy-start | bytes 196612
  160.3 11.2 %copy-start.9 = (f32[16,1024]{1,0:T(8,128)S(1)}, f32[16,1024]{1,0:T(8,128)}, u32[]{:S(2)}) copy-start(f32[16,1024]{1,0:T(8,128)} %get-tuple-element.22) | copy-start | bytes 196612
  160.3 11.2 %copy-start.10 = (f32[16,1024]{1,0:T(8,128)S(1)}, f32[16,1024]{1,0:T(8,128)}, u32[]{:S(2)}) copy-start(f32[16,1024]{1,0:T(8,128)} %get-tuple-element.31) | copy-start | bytes 196612
  160.3 11.2 %copy-start.11 = (f32[16,1024]{1,0:T(8,128)S(1)}, f32[16,1024]{1,0:T(8,128)}, u32[]{:S(2)}) copy-start(f32[16,1024]{1,0:T(8,128)} %get-tuple-element.35) | copy-start | bytes 196612
  160.3 11.2 %copy-start.12 = (f32[16,1024]{1,0:T(8,128)S(1)}, f32[16,1024]{1,0:T(8,128)}, u32[]{:S(2)}) copy-start(f32[16,1024]{1,0:T(8,128)} %get-tuple-element.36) | copy-start | bytes 196612
  160.4 11.2 %copy-start.13 = (f32[16,1024]{1,0:T(8,128)S(1)}, f32[16,1024]{1,0:T(8,128)}, u32[]{:S(2)}) copy-start(f32[16,1024]{1,0:T(8,128)} %get-tuple-element.37) | copy-start | bytes 196612
  187.1 1.4 collective-permute-start.5
  187.2 2.0 %collective-permute-start.6 = (f32[16,2048]{1,0:T(8,128)S(1)}, f32[16,2048]{1,0:T(8,128)S(1)}, u32[]{:S(2)}, u32[]{:S(2)}) collective-permute-start(f32[16,2048]{1,0:T(8,128)S(1)} %pad_maximum_fusion.3), channel_id=1, source_target_pairs={{0,1},{1,0},{2,3},{3,2},{4,5},{5,4},{6,7},{7,6},{8,9},{9,8},{10,11... | collective-permute-start | bytes 393224 | tf_op jit(solution)/shard_map/ppermute | solution.py:46

commit v7 on v6

--- a/solution.py
+++ b/solution.py
@@ -26,6 +26,28 @@
     return clipped.reshape(rows, values.shape[1])
 
 
+def clip_factors(values, upper_logit, lower_logit):
+    rows, columns = values.shape
+    groups = upper_logit.shape[0]
+    blocks = values.reshape(groups, rows // groups, columns)
+    amax = jnp.max(jnp.abs(blocks), axis=1) + 1e-06
+    up = jax.nn.sigmoid(upper_logit)
+    low = jax.nn.sigmoid(lower_logit)
+    upper = up * amax
+    lower = -low * amax
+    center = ((upper + lower) * 0.5)[:, None, :]
+    radius = ((upper - lower) * 0.5)[:, None, :]
+    z = (blocks - center) / radius
+    t = jnp.tanh(z)
+    square = t * t
+    slope = t - (1.0 - square) * z
+    toward_upper = (square + slope).reshape(rows, columns)
+    toward_lower = (square - slope).reshape(rows, columns)
+    scale_upper = 0.5 * up * (1.0 - up) * amax
+    scale_lower = -0.5 * low * (1.0 - low) * amax
+    return toward_upper, toward_lower, scale_upper, scale_lower
+
+
 def gather_features(local_rows):
     devices = lax.axis_size("seq")
     if devices != 2:
@@ -46,7 +68,7 @@
     return value + lax.ppermute(value, "ctx", [(0, 1), (1, 0)])
 
 
-def column_stream(inputs, quant, values, clip_upper, clip_lower, taps, gates, wanted, scale, me, shards, length):
+def column_stream(inputs, quant, factors, taps, gates, wanted, scale, me, shards, length):
     columns = quant.shape[1]
     partial = jnp.dot(inputs, quant, preferred_element_type=jnp.float32).reshape(shards, length, columns)
     received = lax.all_to_all(partial.astype(jnp.float16), "fsdp", 0, 0).astype(jnp.float32)
@@ -75,12 +97,12 @@
     d_clipped = lax.dot_general(
         inputs, d_all, (((0,), (0,)), ((), ())), preferred_element_type=jnp.float32
     )
-    _, pull = jax.vjp(
-        lambda upper_logit, lower_logit: soft_clip(values, upper_logit, lower_logit),
-        clip_upper,
-        clip_lower,
-    )
-    return pull(d_clipped)
+    toward_upper, toward_lower, scale_upper, scale_lower = factors
+    groups = scale_upper.shape[0]
+    grouped = d_clipped.reshape(groups, -1, columns)
+    grad_up = jnp.sum(grouped * toward_upper.reshape(groups, -1, columns), axis=1) * scale_upper
+    grad_low = jnp.sum(grouped * toward_lower.reshape(groups, -1, columns), axis=1) * scale_lower
+    return grad_up, grad_low
 
 
 def on_device(hidden_in, weight, clip_upper, clip_lower, filters, gate, target):
@@ -97,6 +119,7 @@
     mine = lax.all_to_all(pieces, "fsdp", 0, 0)
     inputs = mine.reshape(shards * length, rows)
 
+    factors = clip_factors(values, clip_upper, clip_lower)
     taps_all = jnp.repeat(filters, CGROUP, axis=0).T
     gates_all = gate.reshape(length, columns)
     wanted_all = target.reshape(length, columns)
@@ -109,7 +132,7 @@
     for stream in range(streams):
         cols = slice(stream * width_of, (stream + 1) * width_of)
         grad_up, grad_low = column_stream(
-            inputs, quant[:, cols], values[:, cols], clip_upper[:, cols], clip_lower[:, cols],
+            inputs, quant[:, cols], [factor[:, cols] for factor in factors],
             taps_all[:, cols], gates_all[:, cols], wanted_all[:, cols], scale, me, shards, length,
         )
         ups.append(grad_up)

time: 191 us -> 191 us (level)
  the two profiles are of different devices: /device:TPU:0 before, /device:TPU:9 now
where the time goes in v7:
time: 191 us; the launch traced here: 189 us
  blocking collectives  39 us (20%)
  starting transfers between devices  36 us (19%)
  waiting for transfers between devices  31.5 us (16%)
  other arithmetic  28 us (15%)
  local copies, waits for them, and re-layouts  27.6 us (14%)
  matrix products  26.2 us (14%)
    all_to_all x1, blocking collectives, on_device(): mine = lax.all_to_all(pieces, 'fsdp', 0, 0)  39 us
    all_to_all x2, waiting for transfers between devices, column_stream(): lax.all_to_all(partial.astype(jnp.float16), 'fsdp', 0, 0)  23.6 us
    slice x2, local copies, waits for them, and re-layouts, on_device(): factor[:, cols]  21.6 us
    dot_general x2, matrix products, column_stream(): lax.dot_general(inputs, d_all, (((0,), (0,)), ((), ())), preferred_elemen...  17.6 us
    add x1, other arithmetic, clip_factors(): toward_upper = (square + slope).reshape(rows, columns)  14.9 us
    all_to_all x2, starting transfers between devices, column_stream(): lax.all_to_all(copies, 'fsdp', 0, 0).reshape(shards * length, columns)  13.4 us
    all_to_all x2, starting transfers between devices, column_stream(): lax.all_to_all(partial.astype(jnp.float16), 'fsdp', 0, 0)  13 us
    dot_general x2, matrix products, column_stream(): jnp.dot(inputs, quant, preferred_element_type=jnp.float32)  8.64 us
  transfers between devices with their start and end apart: 11, of which 5 were waited for; matrix products, arithmetic and copies ran while one was open for 35% of the time, Pallas kernels for 0%

profile of v7, /device:TPU:9, one launch (start us, length us, event | category | flops | bytes accessed | tf_op | source)
XLA Modules:
  0.0 189.2 jit_solution(12046216035762157201)
XLA Ops:
  0.7 1.3 collective-permute-start
  1.9 5.9 %bitcast_reduce_fusion = f32[16,2048]{1,0:T(8,128)S(1)} fusion(bf16[2048,2048]{1,0:T(8,128)(2,1)} %param.8), kind=kLoop, calls=%fused_computation.6 | loop fusion | flops 12550144 | bytes 8519680 | tf_op jit(solution)/shard_map/reduce_max | solution.py:20
  8.0 14.9 %multiply_add_fusion = (f32[2048,2048]{1,0:T(8,128)}, f32[2048,2048]{1,0:T(8,128)}, bf16[2048,2048]{1,0:T(8,128)(2,1)}) fusion(f32[16,2048]{1,0:T(8,128)S(1)} %get-tuple-element.20, f32[16,2048]{1,0:T(8,128)S(1)} %get-tuple-element.19, bf16[2048,2048]{1,0:T(8,128)(2,1)S(1)} %copy-done), kind=kLoop, calls=%fused_computation.9 | loop fusion | flops 50331648 | bytes 50593792 | tf_op jit(solution)/shard_map/add | solution.py:44
  23.4 39.0 %all_to_all.25 = bf16[4,96,2048]{2,1,0:T(8,128)(2,1)S(1)} all-to-all(bf16[4,96,2048]{2,1,0:T(8,128)(2,1)S(1)} %bitcast.98), channel_id=1, replica_groups=mesh['parts'=2,'fsdp'=4,'seq'=2,'ctx'=2] {'fsdp'}, dimensions={0} | all-to-all | bytes 3145728 | tf_op jit(solution)/shard_map/all_to_all | solution.py:119
  62.4 3.3 %fusion.67 = (f16[4,96,1024]{2,1,0:T(8,128)(2,1)}, f32[4,96,1024]{2,1,0:T(8,128)}) fusion(bf16[4,96,2048]{2,1,0:T(8,128)(2,1)S(1)} %all_to_all.25, bf16[2048,2048]{1,0:T(8,128)(2,1)S(1)} %copy-done.1), kind=kOutput, calls=%fused_computation.139 | convolution fusion | flops 1611005952 | bytes 8126464 | tf_op jit(solution)/shard_map/dot_general | solution.py:73
  65.7 5.5 %all-to-all-start.3 = ((f16[4,96,1024]{2,1,0:T(8,128)(2,1)}), f16[4,96,1024]{2,1,0:T(8,128)(2,1)S(1)}, u32[]{:S(2)}, u32[]{:S(2)}) async-start(f16[4,96,1024]{2,1,0:T(8,128)(2,1)} %get-tuple-element.43), calls=%async_computation.3 | async-start | bytes 1572864 | tf_op jit(solution)/shard_map/all_to_all | solution.py:74
  71.2 5.3 %fusion.66 = (f16[4,96,1024]{2,1,0:T(8,128)(2,1)}, f32[4,96,1024]{2,1,0:T(8,128)}) fusion(bf16[4,96,2048]{2,1,0:T(8,128)(2,1)S(1)} %all_to_all.25, bf16[2048,2048]{1,0:T(8,128)(2,1)} %get-tuple-element.5), kind=kOutput, calls=%fused_computation.138 | convolution fusion | flops 1611005952 | bytes 8126464 | tf_op jit(solution)/shard_map/dot_general | solution.py:73
  76.5 10.2 %all-to-all-done.3 = f16[4,96,1024]{2,1,0:T(8,128)(2,1)S(1)} async-done(((f16[4,96,1024]{2,1,0:T(8,128)(2,1)}), f16[4,96,1024]{2,1,0:T(8,128)(2,1)S(1)}, u32[]{:S(2)}, u32[]{:S(2)}) %all-to-all-start.3) | async-done | bytes 786464 | tf_op jit(solution)/shard_map/all_to_all | solution.py:74
  86.7 7.5 %all-to-all-start.1 = ((f16[4,96,1024]{2,1,0:T(8,128)(2,1)}), f16[4,96,1024]{2,1,0:T(8,128)(2,1)S(1)}, u32[]{:S(2)}, u32[]{:S(2)}) async-start(f16[4,96,1024]{2,1,0:T(8,128)(2,1)} %get-tuple-element.41), calls=%async_computation.1 | async-start | bytes 1572864 | tf_op jit(solution)/shard_map/all_to_all | solution.py:74
  94.2 1.0 broadcast_in_dim.22
  95.2 1.3 reshape.75
  96.5 13.4 %all-to-all-done.1 = f16[4,96,1024]{2,1,0:T(8,128)(2,1)S(1)} async-done(((f16[4,96,1024]{2,1,0:T(8,128)(2,1)}), f16[4,96,1024]{2,1,0:T(8,128)(2,1)S(1)}, u32[]{:S(2)}, u32[]{:S(2)}) %all-to-all-start.1) | async-done | bytes 786464 | tf_op jit(solution)/shard_map/all_to_all | solution.py:74
  110.5 1.0 fusion.59
  111.5 1.3 collective-permute-start.3
  112.8 1.0 fusion.60
  113.9 1.3 collective-permute-start.1
  115.2 0.7 collective-permute-done.3
  115.9 1.4 convert_multiply_fusion
  117.4 3.6 %collective-permute-start.4 = (f32[6,1024]{1,0:T(8,128)S(1)}, f32[6,1024]{1,0:T(8,128)S(1)}, u32[]{:S(2)}, u32[]{:S(2)}) collective-permute-start(f32[6,1024]{1,0:T(8,128)S(1)} %slice.309), channel_id=1, source_target_pairs={{1,0},{3,2},{5,4},{7,6},{9,8},{11,10},{13,12},{15,14},{17,16},{19,... | collective-permute-start | bytes 73736 | tf_op jit(solution)/shard_map/ppermute | solution.py:13
  122.1 1.3 collective-permute-start.2
  123.8 1.0 broadcast_in_dim.41
  124.8 6.5 %all-to-all-start.4 = ((bf16[4,96,1024]{2,1,0:T(8,128)(2,1)}), bf16[4,96,1024]{2,1,0:T(8,128)(2,1)S(1)}, u32[]{:S(2)}, u32[]{:S(2)}) async-start(bf16[4,96,1024]{2,1,0:T(8,128)(2,1)} %broadcast_in_dim.41), calls=%async_computation.4 | async-start | bytes 1572864 | tf_op jit(solution)/shard_map/all_to_all | solution.py:96
  131.2 10.8 %fusion.63 = (f32[2048,1024]{1,0:T(8,128)}, f32[2048,1024]{1,0:T(8,128)}) fusion(f32[2048,2048]{1,0:T(8,128)} %get-tuple-element.16), kind=kLoop, calls=%fused_computation.135 | loop fusion | bytes 33554432 | tf_op jit(solution)/shard_map/slice | solution.py:135
  142.4 6.4 %all-to-all-done.4 = bf16[4,96,1024]{2,1,0:T(8,128)(2,1)S(1)} async-done(((bf16[4,96,1024]{2,1,0:T(8,128)(2,1)}), bf16[4,96,1024]{2,1,0:T(8,128)(2,1)S(1)}, u32[]{:S(2)}, u32[]{:S(2)}) %all-to-all-start.4) | async-done | bytes 786464 | tf_op jit(solution)/shard_map/all_to_all | solution.py:96
  148.7 1.1 broadcast_in_dim.40
  149.8 7.0 %all-to-all-start.2 = ((bf16[4,96,1024]{2,1,0:T(8,128)(2,1)}), bf16[4,96,1024]{2,1,0:T(8,128)(2,1)}, u32[]{:S(2)}, u32[]{:S(2)}) async-start(bf16[4,96,1024]{2,1,0:T(8,128)(2,1)} %broadcast_in_dim.40), calls=%async_computation.2 | async-start | bytes 1572864 | tf_op jit(solution)/shard_map/all_to_all | solution.py:96
  156.8 10.8 %fusion.64 = (f32[2048,1024]{1,0:T(8,128)}, f32[2048,1024]{1,0:T(8,128)}) fusion(f32[2048,2048]{1,0:T(8,128)} %get-tuple-element.17), kind=kLoop, calls=%fused_computation.136 | loop fusion | bytes 33554432 | tf_op jit(solution)/shard_map/slice | solution.py:135
  167.6 0.9 copy.14
  168.5 8.8 %multiply_reduce_fusion = (f32[16,1024]{1,0:T(8,128)S(1)}, f32[16,1024]{1,0:T(8,128)S(1)}) fusion(f32[2048,1024]{1,0:T(8,128)} %get-tuple-element.15, f32[2048,1024]{1,0:T(8,128)} %get-tuple-element.13, bf16[16,128,384]{2,1,0:T(8,128)(2,1)S(1)} %bitcast.95, bf16[384,1024,1]{1,0,2:T(8,128)(2,1)} %bitcast.100), kind=kOutput, calls=%fused_computation.10 | convolution fusion | flops 1618968576 | bytes 19267584 | tf_op jit(solution)/shard_map/dot_general | solution.py:97
  177.3 8.8 %multiply_reduce_fusion.1 = (f32[16,1024]{1,0:T(8,128)S(1)}, f32[16,1024]{1,0:T(8,128)S(1)}) fusion(f32[2048,1024]{1,0:T(8,128)} %get-tuple-element.14, f32[2048,1024]{1,0:T(8,128)} %get-tuple-element.12, bf16[16,128,384]{2,1,0:T(8,128)(2,1)S(1)} %bitcast.96, bf16[384,1024,1]{1,0,2:T(8,128)(2,1)} %bitcast.21), kind=kOutput, calls=%fused_computation.11 | convolution fusion | flops 1618968576 | bytes 19267584 | tf_op jit(solution)/shard_map/dot_general | solution.py:97
  186.1 0.7 collective-permute-start.6
  187.0 0.9 collective-permute-done.6
  (45 shorter events, 4.6 us)
Async XLA Ops:
  0.6 7.2 %copy-start.7 = (f32[16,2048]{1,0:T(8,128)S(1)}, f32[16,2048]{1,0:T(8,128)}, u32[]{:S(2)}) copy-start(f32[16,2048]{1,0:T(8,128)} %param.10) | copy-start | bytes 393220
  0.6 7.2 %copy-start.6 = (f32[16,2048]{1,0:T(8,128)S(1)}, f32[16,2048]{1,0:T(8,128)}, u32[]{:S(2)}) copy-start(f32[16,2048]{1,0:T(8,128)} %param.9) | copy-start | bytes 393220
  0.7 22.3 %collective-permute-start = (bf16[96,4096]{1,0:T(8,128)(2,1)}, bf16[96,4096]{1,0:T(8,128)(2,1)S(1)}, u32[]{:S(2)}, u32[]{:S(2)}) collective-permute-start(bf16[96,4096]{1,0:T(8,128)(2,1)} %bitcast.101), channel_id=1, source_target_pairs={{0,2},{2,0},{1,3},{3,1},{4,6},{6,4},{5,7},{7,5},{8,10},{10,8},{9,1... | collective-permute-start | bytes 2359304 | tf_op jit(solution)/shard_map/ppermute | solution.py:55
  1.9 6.1 %copy-start = (bf16[2048,2048]{1,0:T(8,128)(2,1)S(1)}, bf16[2048,2048]{1,0:T(8,128)(2,1)}, u32[]{:S(2)}) copy-start(bf16[2048,2048]{1,0:T(8,128)(2,1)} %param.8) | copy-start | bytes 25165828
  8.0 14.9 %copy-start.3 = (bf16[1,1,96,4096]{3,2,1,0:T(8,128)(2,1)S(1)}, bf16[1,1,96,4096]{3,2,1,0:T(8,128)(2,1)}, u32[]{:S(2)}) copy-start(bf16[1,1,96,4096]{3,2,1,0:T(8,128)(2,1)} %param.7) | copy-start | bytes 2359300
  22.9 39.5 %copy-start.1 = (bf16[2048,2048]{1,0:T(8,128)(2,1)S(1)}, bf16[2048,2048]{1,0:T(8,128)(2,1)}, u32[]{:S(2)}) copy-start(bf16[2048,2048]{1,0:T(8,128)(2,1)} %get-tuple-element.5) | copy-start | bytes 25165828
  65.7 28.5 %copy-start.8 = (f32[128,7]{0,1:T(8,128)S(1)}, f32[128,7]{0,1:T(8,128)}, u32[]{:S(2)}) copy-start(f32[128,7]{0,1:T(8,128)} %param.11) | copy-start | bytes 10756
  65.7 21.0 %all-to-all-start.3 = ((f16[4,96,1024]{2,1,0:T(8,128)(2,1)}), f16[4,96,1024]{2,1,0:T(8,128)(2,1)S(1)}, u32[]{:S(2)}, u32[]{:S(2)}) async-start(f16[4,96,1024]{2,1,0:T(8,128)(2,1)} %get-tuple-element.43), calls=%async_computation.3 | async-start | bytes 1572864 | tf_op jit(solution)/shard_map/all_to_all | solution.py:74
  86.7 23.2 %all-to-all-start.1 = ((f16[4,96,1024]{2,1,0:T(8,128)(2,1)}), f16[4,96,1024]{2,1,0:T(8,128)(2,1)S(1)}, u32[]{:S(2)}, u32[]{:S(2)}) async-start(f16[4,96,1024]{2,1,0:T(8,128)(2,1)} %get-tuple-element.41), calls=%async_computation.1 | async-start | bytes 1572864 | tf_op jit(solution)/shard_map/all_to_all | solution.py:74
  109.9 11.1 %copy-start.4 = (bf16[1,1,96,2048]{3,2,1,0:T(8,128)(2,1)S(1)}, bf16[1,1,96,2048]{3,2,1,0:T(8,128)(2,1)}, u32[]{:S(2)}) copy-start(bf16[1,1,96,2048]{3,2,1,0:T(8,128)(2,1)} %param.13) | copy-start | bytes 1179652
  109.9 11.2 %copy-start.5 = (bf16[1,1,96,2048]{3,2,1,0:T(8,128)(2,1)S(1)}, bf16[1,1,96,2048]{3,2,1,0:T(8,128)(2,1)}, u32[]{:S(2)}) copy-start(bf16[1,1,96,2048]{3,2,1,0:T(8,128)(2,1)} %param.12) | copy-start | bytes 1179652
  111.5 4.3 %collective-permute-start.3 = (bf16[6,1024]{1,0:T(8,128)(2,1)S(1)}, bf16[6,1024]{1,0:T(8,128)(2,1)S(1)}, u32[]{:S(2)}, u32[]{:S(2)}) collective-permute-start(bf16[6,1024]{1,0:T(8,128)(2,1)S(1)} %slice.294), channel_id=1, source_target_pairs={{0,1},{2,3},{4,5},{6,7},{8,9},{10,11},{12,13},{14,15},{16,17},{18,... | collective-permute-start | bytes 36872 | tf_op jit(solution)/shard_map/ppermute | solution.py:13
  113.9 7.1 %collective-permute-start.1 = (bf16[6,1024]{1,0:T(8,128)(2,1)S(1)}, bf16[6,1024]{1,0:T(8,128)(2,1)S(1)}, u32[]{:S(2)}, u32[]{:S(2)}) collective-permute-start(bf16[6,1024]{1,0:T(8,128)(2,1)S(1)} %slice.264), channel_id=1, source_target_pairs={{0,1},{2,3},{4,5},{6,7},{8,9},{10,11},{12,13},{14,15},{16,17},{18,... | collective-permute-start | bytes 36872 | tf_op jit(solution)/shard_map/ppermute | solution.py:13
  117.4 6.0 %collective-permute-start.4 = (f32[6,1024]{1,0:T(8,128)S(1)}, f32[6,1024]{1,0:T(8,128)S(1)}, u32[]{:S(2)}, u32[]{:S(2)}) collective-permute-start(f32[6,1024]{1,0:T(8,128)S(1)} %slice.309), channel_id=1, source_target_pairs={{1,0},{3,2},{5,4},{7,6},{9,8},{11,10},{13,12},{15,14},{17,16},{19,... | collective-permute-start | bytes 73736 | tf_op jit(solution)/shard_map/ppermute | solution.py:13
  122.1 19.9 %collective-permute-start.2 = (f32[6,1024]{1,0:T(8,128)}, f32[6,1024]{1,0:T(8,128)S(1)}, u32[]{:S(2)}, u32[]{:S(2)}) collective-permute-start(f32[6,1024]{1,0:T(8,128)} %slice.279), channel_id=1, source_target_pairs={{1,0},{3,2},{5,4},{7,6},{9,8},{11,10},{13,12},{15,14},{17,16},{19,... | collective-permute-start | bytes 73736 | tf_op jit(solution)/shard_map/ppermute | solution.py:13
  124.8 24.0 %all-to-all-start.4 = ((bf16[4,96,1024]{2,1,0:T(8,128)(2,1)}), bf16[4,96,1024]{2,1,0:T(8,128)(2,1)S(1)}, u32[]{:S(2)}, u32[]{:S(2)}) async-start(bf16[4,96,1024]{2,1,0:T(8,128)(2,1)} %broadcast_in_dim.41), calls=%async_computation.4 | async-start | bytes 1572864 | tf_op jit(solution)/shard_map/all_to_all | solution.py:96
  148.7 18.9 %copy-start.2 = (bf16[4,96,1024]{2,1,0:T(8,128)(2,1)}, bf16[4,96,1024]{2,1,0:T(8,128)(2,1)S(1)}, u32[]{:S(2)}) copy-start(bf16[4,96,1024]{2,1,0:T(8,128)(2,1)S(1)} %all-to-all-done.4) | copy-start | bytes 2359300
  149.8 27.5 %all-to-all-start.2 = ((bf16[4,96,1024]{2,1,0:T(8,128)(2,1)}), bf16[4,96,1024]{2,1,0:T(8,128)(2,1)}, u32[]{:S(2)}, u32[]{:S(2)}) async-start(bf16[4,96,1024]{2,1,0:T(8,128)(2,1)} %broadcast_in_dim.40), calls=%async_computation.2 | async-start | bytes 1572864 | tf_op jit(solution)/shard_map/all_to_all | solution.py:96
  186.1 1.7 collective-permute-start.6
  186.9 1.6 collective-permute-start.5

commit v8 on v5

--- a/solution.py
+++ b/solution.py
@@ -39,6 +39,31 @@
     )
 
 
+def rows_of_block(local_rows, shards, rows):
+    devices = lax.axis_size("seq")
+    length = local_rows.shape[0]
+    if devices != 2 or length % 2:
+        features = gather_features(local_rows)
+        pieces = features.reshape(length, shards, rows).transpose(1, 0, 2)
+        return lax.all_to_all(pieces, "fsdp", 0, 0)
+    half = length // 2
+    first = lax.axis_index("seq") == 0
+    wanted_by_other = lax.dynamic_slice_in_dim(local_rows, jnp.where(first, half, 0), half, 0)
+    kept = lax.dynamic_slice_in_dim(local_rows, jnp.where(first, 0, half), half, 0)
+    other = lax.ppermute(wanted_by_other, "seq", [(0, 1), (1, 0)])
+    features = jnp.where(
+        first, jnp.concatenate([kept, other], axis=1), jnp.concatenate([other, kept], axis=1)
+    )
+    pieces = features.reshape(half, shards, rows).transpose(1, 0, 2)
+    own_half = lax.all_to_all(pieces, "fsdp", 0, 0)
+    other_half = lax.ppermute(own_half, "seq", [(0, 1), (1, 0)])
+    return jnp.where(
+        first,
+        jnp.concatenate([own_half, other_half], axis=1),
+        jnp.concatenate([other_half, own_half], axis=1),
+    )
+
+
 def sum_over_ctx(value):
     devices = lax.axis_size("ctx")
     if devices != 2:
@@ -52,12 +77,10 @@
     local_rows = hidden_in.reshape(-1, width)
     length = local_rows.shape[0]
     rows, columns = weight.shape
-    features = gather_features(local_rows)
     values = weight.astype(jnp.float32)
     quant = soft_clip(values, clip_upper, clip_lower).astype(jnp.bfloat16)
-    features, quant = lax.optimization_barrier((features, quant))
-    pieces = features.reshape(length, shards, rows).transpose(1, 0, 2)
-    mine = lax.all_to_all(pieces, "fsdp", 0, 0)
+    mine = rows_of_block(local_rows, shards, rows)
+    mine, quant = lax.optimization_barrier((mine, quant))
     inputs = mine.reshape(shards * length, rows)
 
     partial = jnp.dot(inputs, quant, preferred_element_type=jnp.float32).reshape(shards, length, columns)

time: 178 us -> 173 us (0.972)
  blocking collectives: 41.3 us -> 24.2 us
  waiting for transfers between devices: 76.9 us -> 84.2 us
  local copies, waits for them, and re-layouts: 6.02 us -> 8.07 us
    all_to_all x1, blocking collectives: 41.3 us -> 24.2 us  [rows_of_block(): own_half = lax.all_to_all(pieces, 'fsdp', 0, 0)]
    ppermute x1 -> x2, waiting for transfers between devices: 4.55 us -> 12.8 us  [the longest x1 8.83 us: rows_of_block(): other = lax.ppermute(wanted_by_other, 'seq', [(0, 1), (1, 0)])]
    ppermute x1 -> x2, starting transfers between devices: 3 us -> 4.49 us  [the longest x1 3 us: rows_of_block(): other = lax.ppermute(wanted_by_other, 'seq', [(0, 1), (1, 0)])]
  transfers between devices with their start and end apart: 7 -> 8, of which waited for: 6 -> 7; matrix products, arithmetic and copies ran while one was open for 10% -> 10% of each run, Pallas kernels for 0% -> 0%
where the time goes in v8:
time: 173 us; the launch traced here: 172 us
  waiting for transfers between devices  84.2 us (49%)
  blocking collectives  24.2 us (14%)
  matrix products  20.5 us (12%)
  other arithmetic  19.4 us (11%)
  starting transfers between devices  15.1 us (9%)
  local copies, waits for them, and re-layouts  8.07 us (5%)
    all_to_all x1, waiting for transfers between devices, on_device(): lax.all_to_all(copies, 'fsdp', 0, 0).reshape(shards * length, columns)  35.8 us
    all_to_all x1, waiting for transfers between devices, on_device(): lax.all_to_all(partial.astype(jnp.float16), 'fsdp', 0, 0)  32.2 us
    all_to_all x1, blocking collectives, rows_of_block(): own_half = lax.all_to_all(pieces, 'fsdp', 0, 0)  24.2 us
    dot_general x1, matrix products, on_device(): lax.dot_general(inputs, d_all, (((0,), (0,)), ((), ())), preferred_elemen...  15.4 us
    ppermute x1, waiting for transfers between devices, rows_of_block(): other = lax.ppermute(wanted_by_other, 'seq', [(0, 1), (1, 0)])  8.83 us
    convert_element_type x1, other arithmetic, on_device(): quant = soft_clip(values, clip_upper, clip_lower).astype(jnp.bfloat16)  6.06 us
    reduce_max x1, other arithmetic, soft_clip(): amax = jnp.max(jnp.abs(blocks), axis=1) + 1e-06  5.71 us
    dot_general x1, matrix products, on_device(): jnp.dot(inputs, quant, preferred_element_type=jnp.float32)  5.08 us
  transfers between devices with their start and end apart: 8, of which 7 were waited for; matrix products, arithmetic and copies ran while one was open for 10% of the time, Pallas kernels for 0%

profile of v8, /device:TPU:0, one launch (start us, length us, event | category | flops | bytes accessed | tf_op | source)
XLA Modules:
  0.0 172.3 jit_solution(18301838742981634633)
XLA Ops:
  0.6 1.2 constant_dynamic-slice_fusion
  1.8 3.0 %collective-permute-start = (bf16[48,4096]{1,0:T(8,128)(2,1)S(1)}, bf16[48,4096]{1,0:T(8,128)(2,1)S(1)}, u32[]{:S(2)}, u32[]{:S(2)}) collective-permute-start(bf16[48,4096]{1,0:T(8,128)(2,1)S(1)} %get-tuple-element.13), channel_id=1, source_target_pairs={{0,2},{2,0},{1,3},{3,1},{4,6},{6,4},{5,7},{7,5},{8,10},{10,8},{9,1... | collective-permute-start | bytes 1179656 | tf_op jit(solution)/shard_map/ppermute | solution.py:53
  5.1 8.8 %collective-permute-done = bf16[48,4096]{1,0:T(8,128)(2,1)S(1)} collective-permute-done((bf16[48,4096]{1,0:T(8,128)(2,1)S(1)}, bf16[48,4096]{1,0:T(8,128)(2,1)S(1)}, u32[]{:S(2)}, u32[]{:S(2)}) %collective-permute-start) | collective-permute-done | bytes 393248 | tf_op jit(solution)/shard_map/ppermute | solution.py:53
  14.2 1.4 fusion.30
  16.1 24.2 %all_to_all.15 = bf16[4,48,2048]{2,1,0:T(8,128)(2,1)S(1)} all-to-all(bf16[4,48,2048]{2,1,0:T(8,128)(2,1)S(1)} %copy.15), channel_id=1, replica_groups=mesh['parts'=2,'fsdp'=4,'seq'=2,'ctx'=2] {'fsdp'}, dimensions={0} | all-to-all | bytes 1572864 | tf_op jit(solution)/shard_map/all_to_all | solution.py:58
  40.2 1.5 collective-permute-start.1
  41.7 5.7 %abs_reduce_fusion = f32[16,2048]{1,0:T(8,128)S(1)} fusion(bf16[2048,2048]{1,0:T(8,128)(2,1)} %param.8), kind=kLoop, calls=%fused_computation.10 | loop fusion | flops 12550144 | bytes 8519680 | tf_op jit(solution)/shard_map/reduce_max | solution.py:20
  47.5 0.8 multiply_divide_fusion
  48.2 6.1 %fusion = bf16[2048,2048]{1,0:T(8,128)(2,1)S(1)} fusion(bf16[2048,2048]{1,0:T(8,128)(2,1)} %param.8, f32[16,2048]{1,0:T(8,128)S(1)} %get-tuple-element.11, f32[16,2048]{1,0:T(8,128)S(1)} %get-tuple-element.16), kind=kLoop, calls=%fused_computation.4 | loop fusion | flops 25165824 | bytes 17039360 | tf_op jit(solution)/shard_map/convert_element_type | solution.py:81
  54.3 4.0 %collective-permute-done.1 = bf16[4,48,2048]{2,1,0:T(8,128)(2,1)S(1)} collective-permute-done((bf16[4,48,2048]{2,1,0:T(8,128)(2,1)S(1)}, bf16[4,48,2048]{2,1,0:T(8,128)(2,1)S(1)}, u32[]{:S(2)}, u32[]{:S(2)}) %collective-permute-start.1) | collective-permute-done | bytes 786464 | tf_op jit(solution)/shard_map/ppermute | solution.py:59
  58.3 0.6 maximum_select_fusion
  58.9 5.1 %fusion.35 = (f16[4,96,2048]{2,1,0:T(8,128)(2,1)}, f32[4,96,2048]{2,1,0:T(8,128)}) fusion(bf16[4,96,2048]{2,1,0:T(8,128)(2,1)S(1)} %maximum_select_fusion, bf16[2048,2048]{1,0:T(8,128)(2,1)S(1)} %fusion), kind=kOutput, calls=%fused_computation.82 | convolution fusion | flops 3222011904 | bytes 14680064 | tf_op jit(solution)/shard_map/dot_general | solution.py:86
  64.0 3.7 %all-to-all-start.1 = ((f16[4,96,2048]{2,1,0:T(8,128)(2,1)}), f16[4,96,2048]{2,1,0:T(8,128)(2,1)S(1)}, u32[]{:S(2)}, u32[]{:S(2)}) async-start(f16[4,96,2048]{2,1,0:T(8,128)(2,1)} %get-tuple-element.24), calls=%async_computation.1 | async-start | bytes 3145728 | tf_op jit(solution)/shard_map/all_to_all | solution.py:88
  67.7 1.0 broadcast_in_dim.16
  68.7 1.9 %reshape.69 = f32[2048,7]{0,1:T(8,128)} reshape(f32[128,16,7]{1,0,2:T(8,128)} %broadcast_in_dim.16) | data formatting | bytes 114688 | tf_op jit(solution)/shard_map/reshape | solution.py:93
  70.6 32.2 %all-to-all-done.1 = f16[4,96,2048]{2,1,0:T(8,128)(2,1)S(1)} async-done(((f16[4,96,2048]{2,1,0:T(8,128)(2,1)}), f16[4,96,2048]{2,1,0:T(8,128)(2,1)S(1)}, u32[]{:S(2)}, u32[]{:S(2)}) %all-to-all-start.1) | async-done | bytes 1572896 | tf_op jit(solution)/shard_map/all_to_all | solution.py:88
  103.3 1.2 fusion.31
  104.6 1.3 collective-permute-start.2
  105.9 0.8 collective-permute-done.2
  106.8 0.8 convert_multiply_fusion
  107.6 1.3 collective-permute-start.3
  108.9 1.8 %collective-permute-done.3 = f32[6,2048]{1,0:T(8,128)S(1)} collective-permute-done((f32[6,2048]{1,0:T(8,128)S(1)}, f32[6,2048]{1,0:T(8,128)S(1)}, u32[]{:S(2)}, u32[]{:S(2)}) %collective-permute-start.3) | collective-permute-done | bytes 49184 | tf_op jit(solution)/shard_map/ppermute | solution.py:13
  110.8 0.7 fusion.10
  111.5 1.4 broadcast_in_dim.30
  112.8 3.7 %all-to-all-start.2 = ((bf16[4,96,2048]{2,1,0:T(8,128)(2,1)}), bf16[4,96,2048]{2,1,0:T(8,128)(2,1)S(1)}, u32[]{:S(2)}, u32[]{:S(2)}) async-start(bf16[4,96,2048]{2,1,0:T(8,128)(2,1)} %broadcast_in_dim.30), calls=%async_computation.2 | async-start | bytes 3145728 | tf_op jit(solution)/shard_map/all_to_all | solution.py:113
  116.6 1.6 copy.17
  118.2 35.8 %all-to-all-done.2 = bf16[4,96,2048]{2,1,0:T(8,128)(2,1)S(1)} async-done(((bf16[4,96,2048]{2,1,0:T(8,128)(2,1)}), bf16[4,96,2048]{2,1,0:T(8,128)(2,1)S(1)}, u32[]{:S(2)}, u32[]{:S(2)}) %all-to-all-start.2) | async-done | bytes 1572896 | tf_op jit(solution)/shard_map/all_to_all | solution.py:113
  153.9 15.4 %divide_reduce_fusion = (f32[16,2048]{1,0:T(8,128)S(1)}, f32[16,2048]{1,0:T(8,128)S(1)}, f32[16,2048]{1,0:T(8,128)S(1)}, f32[16,2048]{1,0:T(8,128)S(1)}) fusion(f32[16,2048]{1,0:T(8,128)S(1)} %get-tuple-element.11, f32[16,2048]{1,0:T(8,128)S(1)} %get-tuple-element.16, bf16[2048,2048]{1,0:T(8,128)(2,1)} %param.8, f32[16,2048]{1,0:T(8,128)} %get-tuple-element.10, ...), kind=kOutput, calls=%fused_computation.11 | convolution fusion | flops 3288203264 | bytes 12451840 | tf_op jit(solution)/shard_map/dot_general | solution.py:114
  169.6 0.5 collective-permute-start.4
  170.1 0.8 collective-permute-done.5
  170.9 0.7 add.104
  171.6 0.7 add.103
  (28 shorter events, 1.9 us)
Async XLA Ops:
  1.8 12.1 %collective-permute-start = (bf16[48,4096]{1,0:T(8,128)(2,1)S(1)}, bf16[48,4096]{1,0:T(8,128)(2,1)S(1)}, u32[]{:S(2)}, u32[]{:S(2)}) collective-permute-start(bf16[48,4096]{1,0:T(8,128)(2,1)S(1)} %get-tuple-element.13), channel_id=1, source_target_pairs={{0,2},{2,0},{1,3},{3,1},{4,6},{6,4},{5,7},{7,5},{8,10},{10,8},{9,1... | collective-permute-start | bytes 1179656 | tf_op jit(solution)/shard_map/ppermute | solution.py:53
  40.2 7.2 %copy-start = (f32[16,2048]{1,0:T(8,128)S(1)}, f32[16,2048]{1,0:T(8,128)}, u32[]{:S(2)}) copy-start(f32[16,2048]{1,0:T(8,128)} %param.10) | copy-start | bytes 393220
  40.2 7.2 %copy-start.2 = (f32[16,2048]{1,0:T(8,128)S(1)}, f32[16,2048]{1,0:T(8,128)}, u32[]{:S(2)}) copy-start(f32[16,2048]{1,0:T(8,128)} %param.9) | copy-start | bytes 393220
  40.2 18.1 %collective-permute-start.1 = (bf16[4,48,2048]{2,1,0:T(8,128)(2,1)S(1)}, bf16[4,48,2048]{2,1,0:T(8,128)(2,1)S(1)}, u32[]{:S(2)}, u32[]{:S(2)}) collective-permute-start(bf16[4,48,2048]{2,1,0:T(8,128)(2,1)S(1)} %all_to_all.15), channel_id=1, source_target_pairs={{0,2},{2,0},{1,3},{3,1},{4,6},{6,4},{5,7},{7,5},{8,10},{10,8},{9,1... | collective-permute-start | bytes 2359304 | tf_op jit(solution)/shard_map/ppermute | solution.py:59
  64.0 3.7 %copy-start.7 = (f32[128,7]{0,1:T(8,128)S(1)}, f32[128,7]{0,1:T(8,128)}, u32[]{:S(2)}) copy-start(f32[128,7]{0,1:T(8,128)} %param.11) | copy-start | bytes 10756
  64.0 38.8 %all-to-all-start.1 = ((f16[4,96,2048]{2,1,0:T(8,128)(2,1)}), f16[4,96,2048]{2,1,0:T(8,128)(2,1)S(1)}, u32[]{:S(2)}, u32[]{:S(2)}) async-start(f16[4,96,2048]{2,1,0:T(8,128)(2,1)} %get-tuple-element.24), calls=%async_computation.1 | async-start | bytes 3145728 | tf_op jit(solution)/shard_map/all_to_all | solution.py:88
  102.8 3.1 %copy-start.6 = (f32[2048,7]{0,1:T(8,128)S(1)}, f32[2048,7]{0,1:T(8,128)}, u32[]{:S(2)}) copy-start(f32[2048,7]{0,1:T(8,128)} %reshape.69) | copy-start | bytes 172036
  102.8 4.0 %copy-start.4 = (bf16[1,1,96,2048]{3,2,1,0:T(8,128)(2,1)S(1)}, bf16[1,1,96,2048]{3,2,1,0:T(8,128)(2,1)}, u32[]{:S(2)}) copy-start(bf16[1,1,96,2048]{3,2,1,0:T(8,128)(2,1)} %param.13) | copy-start | bytes 1179652
  102.8 4.0 %copy-start.5 = (bf16[1,1,96,2048]{3,2,1,0:T(8,128)(2,1)S(1)}, bf16[1,1,96,2048]{3,2,1,0:T(8,128)(2,1)}, u32[]{:S(2)}) copy-start(bf16[1,1,96,2048]{3,2,1,0:T(8,128)(2,1)} %param.12) | copy-start | bytes 1179652
  104.6 2.1 %collective-permute-start.2 = (bf16[6,2048]{1,0:T(8,128)(2,1)S(1)}, bf16[6,2048]{1,0:T(8,128)(2,1)S(1)}, u32[]{:S(2)}, u32[]{:S(2)}) collective-permute-start(bf16[6,2048]{1,0:T(8,128)(2,1)S(1)} %slice.96), channel_id=1, source_target_pairs={{0,1},{2,3},{4,5},{6,7},{8,9},{10,11},{12,13},{14,15},{16,17},{18,... | collective-permute-start | bytes 73736 | tf_op jit(solution)/shard_map/ppermute | solution.py:13
  107.6 3.1 %collective-permute-start.3 = (f32[6,2048]{1,0:T(8,128)S(1)}, f32[6,2048]{1,0:T(8,128)S(1)}, u32[]{:S(2)}, u32[]{:S(2)}) collective-permute-start(f32[6,2048]{1,0:T(8,128)S(1)} %slice.110), channel_id=1, source_target_pairs={{1,0},{3,2},{5,4},{7,6},{9,8},{11,10},{13,12},{15,14},{17,16},{19,... | collective-permute-start | bytes 147464 | tf_op jit(solution)/shard_map/ppermute | solution.py:13
  112.8 41.1 %all-to-all-start.2 = ((bf16[4,96,2048]{2,1,0:T(8,128)(2,1)}), bf16[4,96,2048]{2,1,0:T(8,128)(2,1)S(1)}, u32[]{:S(2)}, u32[]{:S(2)}) async-start(bf16[4,96,2048]{2,1,0:T(8,128)(2,1)} %broadcast_in_dim.30), calls=%async_computation.2 | async-start | bytes 3145728 | tf_op jit(solution)/shard_map/all_to_all | solution.py:113
  153.9 15.4 %copy-start.1 = (f32[16,2048]{1,0:T(8,128)S(1)}, f32[16,2048]{1,0:T(8,128)}, u32[]{:S(2)}) copy-start(f32[16,2048]{1,0:T(8,128)} %param.10) | copy-start | bytes 393220
  153.9 15.4 %copy-start.3 = (f32[16,2048]{1,0:T(8,128)S(1)}, f32[16,2048]{1,0:T(8,128)}, u32[]{:S(2)}) copy-start(f32[16,2048]{1,0:T(8,128)} %param.9) | copy-start | bytes 393220
  169.5 1.4 collective-permute-start.5
  169.6 2.0 %collective-permute-start.4 = (f32[16,2048]{1,0:T(8,128)S(1)}, f32[16,2048]{1,0:T(8,128)S(1)}, u32[]{:S(2)}, u32[]{:S(2)}) collective-permute-start(f32[16,2048]{1,0:T(8,128)S(1)} %get-tuple-element.15), channel_id=1, source_target_pairs={{0,1},{1,0},{2,3},{3,2},{4,5},{5,4},{6,7},{7,6},{8,9},{9,8},{10,11... | collective-permute-start | bytes 393224 | tf_op jit(solution)/shard_map/ppermute | solution.py:71

commit v9 on v8

--- a/solution.py
+++ b/solution.py
@@ -13,7 +13,7 @@
     return lax.ppermute(value, axis, pairs)
 
 
-def soft_clip(values, upper_logit, lower_logit):
+def clip_bounds(values, upper_logit, lower_logit):
     rows = values.shape[0]
     groups = upper_logit.shape[0]
     blocks = values.reshape(groups, rows // groups, values.shape[1])
@@ -22,8 +22,29 @@
     lower = -jax.nn.sigmoid(lower_logit) * amax
     center = ((upper + lower) * 0.5)[:, None, :]
     radius = ((upper - lower) * 0.5)[:, None, :]
-    clipped = center + radius * jnp.tanh((blocks - center) / radius)
-    return clipped.reshape(rows, values.shape[1])
+    return blocks, amax, center, radius
+
+
+def soft_clip(values, upper_logit, lower_logit):
+    blocks, _, center, radius = clip_bounds(values, upper_logit, lower_logit)
+    clipped = center + radius * jnp.tanh((blocks - center) * (1.0 / radius))
+    return clipped.reshape(values.shape)
+
+
+def soft_clip_grads(values, upper_logit, lower_logit, d_clipped):
+    blocks, amax, center, radius = clip_bounds(values, upper_logit, lower_logit)
+    z = (blocks - center) * (1.0 / radius)
+    t = jnp.tanh(z)
+    square = t * t
+    slope = t - (1.0 - square) * z
+    grouped = d_clipped.reshape(blocks.shape)
+    toward_upper = jnp.sum(grouped * (square + slope), axis=1)
+    toward_lower = jnp.sum(grouped * (square - slope), axis=1)
+    up = jax.nn.sigmoid(upper_logit)
+    low = jax.nn.sigmoid(lower_logit)
+    grad_up = toward_upper * (0.5 * up * (1.0 - up) * amax)
+    grad_low = toward_lower * (-0.5 * low * (1.0 - low) * amax)
+    return grad_up, grad_low
 
 
 def gather_features(local_rows):
@@ -114,12 +135,7 @@
     d_clipped = lax.dot_general(
         inputs, d_all, (((0,), (0,)), ((), ())), preferred_element_type=jnp.float32
     )
-    _, pull = jax.vjp(
-        lambda upper_logit, lower_logit: soft_clip(values, upper_logit, lower_logit),
-        clip_upper,
-        clip_lower,
-    )
-    grad_up, grad_low = pull(d_clipped)
+    grad_up, grad_low = soft_clip_grads(values, clip_upper, clip_lower, d_clipped)
     grad_upper, grad_lower = sum_over_ctx(grad_up), sum_over_ctx(grad_low)
     return (grad_upper, grad_lower)
 

time: 173 us -> 171 us (0.988)
  matrix products: 20.5 us -> 18.5 us
    dot_general x1, matrix products: 15.4 us -> 13.4 us  [on_device(): lax.dot_general(inputs, d_all, (((0,), (0,)), ((), ())), preferred_elemen...]
where the time goes in v9:
time: 171 us; the launch traced here: 170 us
  waiting for transfers between devices  84.9 us (50%)
  blocking collectives  24.2 us (14%)
  other arithmetic  18.7 us (11%)
  matrix products  18.5 us (11%)
  starting transfers between devices  15.1 us (9%)
  local copies, waits for them, and re-layouts  8.04 us (5%)
    all_to_all x1, waiting for transfers between devices, on_device(): lax.all_to_all(copies, 'fsdp', 0, 0).reshape(shards * length, columns)  35.8 us
    all_to_all x1, waiting for transfers between devices, on_device(): lax.all_to_all(partial.astype(jnp.float16), 'fsdp', 0, 0)  32.2 us
    all_to_all x1, blocking collectives, rows_of_block(): own_half = lax.all_to_all(pieces, 'fsdp', 0, 0)  24.2 us
    dot_general x1, matrix products, on_device(): lax.dot_general(inputs, d_all, (((0,), (0,)), ((), ())), preferred_elemen...  13.4 us
    ppermute x1, waiting for transfers between devices, rows_of_block(): other = lax.ppermute(wanted_by_other, 'seq', [(0, 1), (1, 0)])  8.83 us
    convert_element_type x1, other arithmetic, on_device(): quant = soft_clip(values, clip_upper, clip_lower).astype(jnp.bfloat16)  6.03 us
    reduce_max x1, other arithmetic, clip_bounds(): amax = jnp.max(jnp.abs(blocks), axis=1) + 1e-06  5.71 us
    dot_general x1, matrix products, on_device(): jnp.dot(inputs, quant, preferred_element_type=jnp.float32)  5.13 us
  transfers between devices with their start and end apart: 8, of which 7 were waited for; matrix products, arithmetic and copies ran while one was open for 10% of the time, Pallas kernels for 0%

profile of v9, /device:TPU:0, one launch (start us, length us, event | category | flops | bytes accessed | tf_op | source)
XLA Modules:
  0.0 170.2 jit_solution(18229072685609722713)
XLA Ops:
  0.6 1.2 constant_dynamic-slice_fusion
  1.8 3.0 %collective-permute-start = (bf16[48,4096]{1,0:T(8,128)(2,1)S(1)}, bf16[48,4096]{1,0:T(8,128)(2,1)S(1)}, u32[]{:S(2)}, u32[]{:S(2)}) collective-permute-start(bf16[48,4096]{1,0:T(8,128)(2,1)S(1)} %get-tuple-element.11), channel_id=1, source_target_pairs={{0,2},{2,0},{1,3},{3,1},{4,6},{6,4},{5,7},{7,5},{8,10},{10,8},{9,1... | collective-permute-start | bytes 1179656 | tf_op jit(solution)/shard_map/ppermute | solution.py:74
  5.1 8.8 %collective-permute-done = bf16[48,4096]{1,0:T(8,128)(2,1)S(1)} collective-permute-done((bf16[48,4096]{1,0:T(8,128)(2,1)S(1)}, bf16[48,4096]{1,0:T(8,128)(2,1)S(1)}, u32[]{:S(2)}, u32[]{:S(2)}) %collective-permute-start) | collective-permute-done | bytes 393248 | tf_op jit(solution)/shard_map/ppermute | solution.py:74
  14.2 1.4 fusion.32
  16.1 24.2 %all_to_all.15 = bf16[4,48,2048]{2,1,0:T(8,128)(2,1)S(1)} all-to-all(bf16[4,48,2048]{2,1,0:T(8,128)(2,1)S(1)} %copy.15), channel_id=1, replica_groups=mesh['parts'=2,'fsdp'=4,'seq'=2,'ctx'=2] {'fsdp'}, dimensions={0} | all-to-all | bytes 1572864 | tf_op jit(solution)/shard_map/all_to_all | solution.py:79
  40.2 1.5 collective-permute-start.1
  41.7 5.7 %abs_reduce_fusion = f32[16,2048]{1,0:T(8,128)S(1)} fusion(bf16[2048,2048]{1,0:T(8,128)(2,1)} %param.8), kind=kLoop, calls=%fused_computation.10 | loop fusion | flops 12550144 | bytes 8519680 | tf_op jit(solution)/shard_map/reduce_max | solution.py:20
  47.6 6.0 %fusion.3 = bf16[2048,2048]{1,0:T(8,128)(2,1)S(1)} fusion(bf16[2048,2048]{1,0:T(8,128)(2,1)} %param.8, f32[16,2048]{1,0:T(8,128)S(1)} %get-tuple-element.8, f32[16,2048]{1,0:T(8,128)S(1)} %get-tuple-element.9, f32[16,2048]{1,0:T(8,128)S(1)} %get-tuple-element.12), kind=kLoop, calls=%fused_computation.5 | loop fusion | flops 25165824 | bytes 17170432 | tf_op jit(solution)/shard_map/convert_element_type | solution.py:102
  53.6 4.7 %collective-permute-done.1 = bf16[4,48,2048]{2,1,0:T(8,128)(2,1)S(1)} collective-permute-done((bf16[4,48,2048]{2,1,0:T(8,128)(2,1)S(1)}, bf16[4,48,2048]{2,1,0:T(8,128)(2,1)S(1)}, u32[]{:S(2)}, u32[]{:S(2)}) %collective-permute-start.1) | collective-permute-done | bytes 786464 | tf_op jit(solution)/shard_map/ppermute | solution.py:80
  58.3 0.6 maximum_select_fusion
  58.9 5.1 %fusion.35 = (f16[4,96,2048]{2,1,0:T(8,128)(2,1)}, f32[4,96,2048]{2,1,0:T(8,128)}) fusion(bf16[4,96,2048]{2,1,0:T(8,128)(2,1)S(1)} %maximum_select_fusion, bf16[2048,2048]{1,0:T(8,128)(2,1)S(1)} %fusion.3), kind=kOutput, calls=%fused_computation.78 | convolution fusion | flops 3222011904 | bytes 14680064 | tf_op jit(solution)/shard_map/dot_general | solution.py:107
  64.0 3.7 %all-to-all-start.1 = ((f16[4,96,2048]{2,1,0:T(8,128)(2,1)}), f16[4,96,2048]{2,1,0:T(8,128)(2,1)S(1)}, u32[]{:S(2)}, u32[]{:S(2)}) async-start(f16[4,96,2048]{2,1,0:T(8,128)(2,1)} %get-tuple-element.22), calls=%async_computation.1 | async-start | bytes 3145728 | tf_op jit(solution)/shard_map/all_to_all | solution.py:109
  67.8 0.9 broadcast_in_dim.16
  68.7 1.9 %reshape.54 = f32[2048,7]{0,1:T(8,128)} reshape(f32[128,16,7]{1,0,2:T(8,128)} %broadcast_in_dim.16) | data formatting | bytes 114688 | tf_op jit(solution)/shard_map/reshape | solution.py:114
  70.6 32.2 %all-to-all-done.1 = f16[4,96,2048]{2,1,0:T(8,128)(2,1)S(1)} async-done(((f16[4,96,2048]{2,1,0:T(8,128)(2,1)}), f16[4,96,2048]{2,1,0:T(8,128)(2,1)S(1)}, u32[]{:S(2)}, u32[]{:S(2)}) %all-to-all-start.1) | async-done | bytes 1572896 | tf_op jit(solution)/shard_map/all_to_all | solution.py:109
  102.8 0.5 select_reduce_fusion
  103.3 1.2 fusion.33
  104.6 1.3 collective-permute-start.2
  106.0 0.8 collective-permute-done.2
  106.9 0.8 convert_multiply_fusion
  107.7 1.3 collective-permute-start.3
  109.0 1.8 %collective-permute-done.3 = f32[6,2048]{1,0:T(8,128)S(1)} collective-permute-done((f32[6,2048]{1,0:T(8,128)S(1)}, f32[6,2048]{1,0:T(8,128)S(1)}, u32[]{:S(2)}, u32[]{:S(2)}) %collective-permute-start.3) | collective-permute-done | bytes 49184 | tf_op jit(solution)/shard_map/ppermute | solution.py:13
  110.8 0.7 fusion.12
  111.5 1.3 broadcast_in_dim.29
  112.9 3.7 %all-to-all-start.2 = ((bf16[4,96,2048]{2,1,0:T(8,128)(2,1)}), bf16[4,96,2048]{2,1,0:T(8,128)(2,1)S(1)}, u32[]{:S(2)}, u32[]{:S(2)}) async-start(bf16[4,96,2048]{2,1,0:T(8,128)(2,1)} %broadcast_in_dim.29), calls=%async_computation.2 | async-start | bytes 3145728 | tf_op jit(solution)/shard_map/all_to_all | solution.py:134
  116.6 1.6 copy.17
  118.2 35.8 %all-to-all-done.2 = bf16[4,96,2048]{2,1,0:T(8,128)(2,1)S(1)} async-done(((bf16[4,96,2048]{2,1,0:T(8,128)(2,1)}), bf16[4,96,2048]{2,1,0:T(8,128)(2,1)S(1)}, u32[]{:S(2)}, u32[]{:S(2)}) %all-to-all-start.2) | async-done | bytes 1572896 | tf_op jit(solution)/shard_map/all_to_all | solution.py:134
  154.0 13.4 %multiply_reduce_fusion = (f32[16,2048]{1,0:T(8,128)S(1)}, f32[16,2048]{1,0:T(8,128)S(1)}) fusion(bf16[2048,2048]{1,0:T(8,128)(2,1)} %param.8, f32[16,2048]{1,0:T(8,128)S(1)} %get-tuple-element.8, f32[16,2048]{1,0:T(8,128)S(1)} %get-tuple-element.12, bf16[16,128,384]{2,1,0:T(8,128)(2,1)} %bitcast.64, bf16[384,2048,1]{1,0,2:T(8,128)(2,1)S(1)} %bitcast.63), kind=kOutput, calls=%fused_computation.6 | convolution fusion | flops 3275685888 | bytes 12058624 | tf_op jit(solution)/shard_map/dot_general | solution.py:135
  167.6 0.5 collective-permute-start.4
  168.1 0.8 collective-permute-done.5
  168.9 0.7 add.106
  169.6 0.7 add.105
  (28 shorter events, 1.5 us)
Async XLA Ops:
  1.8 12.1 %collective-permute-start = (bf16[48,4096]{1,0:T(8,128)(2,1)S(1)}, bf16[48,4096]{1,0:T(8,128)(2,1)S(1)}, u32[]{:S(2)}, u32[]{:S(2)}) collective-permute-start(bf16[48,4096]{1,0:T(8,128)(2,1)S(1)} %get-tuple-element.11), channel_id=1, source_target_pairs={{0,2},{2,0},{1,3},{3,1},{4,6},{6,4},{5,7},{7,5},{8,10},{10,8},{9,1... | collective-permute-start | bytes 1179656 | tf_op jit(solution)/shard_map/ppermute | solution.py:74
  40.2 7.2 %copy-start = (f32[16,2048]{1,0:T(8,128)S(1)}, f32[16,2048]{1,0:T(8,128)}, u32[]{:S(2)}) copy-start(f32[16,2048]{1,0:T(8,128)} %param.10) | copy-start | bytes 393220
  40.2 7.2 %copy-start.2 = (f32[16,2048]{1,0:T(8,128)S(1)}, f32[16,2048]{1,0:T(8,128)}, u32[]{:S(2)}) copy-start(f32[16,2048]{1,0:T(8,128)} %param.9) | copy-start | bytes 393220
  40.2 18.1 %collective-permute-start.1 = (bf16[4,48,2048]{2,1,0:T(8,128)(2,1)S(1)}, bf16[4,48,2048]{2,1,0:T(8,128)(2,1)S(1)}, u32[]{:S(2)}, u32[]{:S(2)}) collective-permute-start(bf16[4,48,2048]{2,1,0:T(8,128)(2,1)S(1)} %all_to_all.15), channel_id=1, source_target_pairs={{0,2},{2,0},{1,3},{3,1},{4,6},{6,4},{5,7},{7,5},{8,10},{10,8},{9,1... | collective-permute-start | bytes 2359304 | tf_op jit(solution)/shard_map/ppermute | solution.py:80
  64.0 3.7 %copy-start.7 = (f32[128,7]{0,1:T(8,128)S(1)}, f32[128,7]{0,1:T(8,128)}, u32[]{:S(2)}) copy-start(f32[128,7]{0,1:T(8,128)} %param.11) | copy-start | bytes 10756
  64.0 38.8 %all-to-all-start.1 = ((f16[4,96,2048]{2,1,0:T(8,128)(2,1)}), f16[4,96,2048]{2,1,0:T(8,128)(2,1)S(1)}, u32[]{:S(2)}, u32[]{:S(2)}) async-start(f16[4,96,2048]{2,1,0:T(8,128)(2,1)} %get-tuple-element.22), calls=%async_computation.1 | async-start | bytes 3145728 | tf_op jit(solution)/shard_map/all_to_all | solution.py:109
  102.8 3.1 %copy-start.6 = (f32[2048,7]{0,1:T(8,128)S(1)}, f32[2048,7]{0,1:T(8,128)}, u32[]{:S(2)}) copy-start(f32[2048,7]{0,1:T(8,128)} %reshape.54) | copy-start | bytes 172036
  102.8 4.0 %copy-start.4 = (bf16[1,1,96,2048]{3,2,1,0:T(8,128)(2,1)S(1)}, bf16[1,1,96,2048]{3,2,1,0:T(8,128)(2,1)}, u32[]{:S(2)}) copy-start(bf16[1,1,96,2048]{3,2,1,0:T(8,128)(2,1)} %param.13) | copy-start | bytes 1179652
  102.8 4.0 %copy-start.5 = (bf16[1,1,96,2048]{3,2,1,0:T(8,128)(2,1)S(1)}, bf16[1,1,96,2048]{3,2,1,0:T(8,128)(2,1)}, u32[]{:S(2)}) copy-start(bf16[1,1,96,2048]{3,2,1,0:T(8,128)(2,1)} %param.12) | copy-start | bytes 1179652
  104.6 2.1 %collective-permute-start.2 = (bf16[6,2048]{1,0:T(8,128)(2,1)S(1)}, bf16[6,2048]{1,0:T(8,128)(2,1)S(1)}, u32[]{:S(2)}, u32[]{:S(2)}) collective-permute-start(bf16[6,2048]{1,0:T(8,128)(2,1)S(1)} %slice.96), channel_id=1, source_target_pairs={{0,1},{2,3},{4,5},{6,7},{8,9},{10,11},{12,13},{14,15},{16,17},{18,... | collective-permute-start | bytes 73736 | tf_op jit(solution)/shard_map/ppermute | solution.py:13
  107.7 3.1 %collective-permute-start.3 = (f32[6,2048]{1,0:T(8,128)S(1)}, f32[6,2048]{1,0:T(8,128)S(1)}, u32[]{:S(2)}, u32[]{:S(2)}) collective-permute-start(f32[6,2048]{1,0:T(8,128)S(1)} %slice.110), channel_id=1, source_target_pairs={{1,0},{3,2},{5,4},{7,6},{9,8},{11,10},{13,12},{15,14},{17,16},{19,... | collective-permute-start | bytes 147464 | tf_op jit(solution)/shard_map/ppermute | solution.py:13
  112.9 41.1 %all-to-all-start.2 = ((bf16[4,96,2048]{2,1,0:T(8,128)(2,1)}), bf16[4,96,2048]{2,1,0:T(8,128)(2,1)S(1)}, u32[]{:S(2)}, u32[]{:S(2)}) async-start(bf16[4,96,2048]{2,1,0:T(8,128)(2,1)} %broadcast_in_dim.29), calls=%async_computation.2 | async-start | bytes 3145728 | tf_op jit(solution)/shard_map/all_to_all | solution.py:134
  154.0 13.4 %copy-start.1 = (f32[16,2048]{1,0:T(8,128)S(1)}, f32[16,2048]{1,0:T(8,128)}, u32[]{:S(2)}) copy-start(f32[16,2048]{1,0:T(8,128)} %param.10) | copy-start | bytes 393220
  154.0 13.4 %copy-start.3 = (f32[16,2048]{1,0:T(8,128)S(1)}, f32[16,2048]{1,0:T(8,128)}, u32[]{:S(2)}) copy-start(f32[16,2048]{1,0:T(8,128)} %param.9) | copy-start | bytes 393220
  167.5 1.4 collective-permute-start.5
  167.6 2.0 %collective-permute-start.4 = (f32[16,2048]{1,0:T(8,128)S(1)}, f32[16,2048]{1,0:T(8,128)S(1)}, u32[]{:S(2)}, u32[]{:S(2)}) collective-permute-start(f32[16,2048]{1,0:T(8,128)S(1)} %get-tuple-element.14), channel_id=1, source_target_pairs={{0,1},{1,0},{2,3},{3,2},{4,5},{5,4},{6,7},{7,6},{8,9},{9,8},{10,11... | collective-permute-start | bytes 393224 | tf_op jit(solution)/shard_map/ppermute | solution.py:92

commit v10 on v9

--- a/solution.py
+++ b/solution.py
@@ -60,29 +60,35 @@
     )
 
 
-def rows_of_block(local_rows, shards, rows):
+def rows_of_block(local_rows, shards, rows, quant):
     devices = lax.axis_size("seq")
     length = local_rows.shape[0]
     if devices != 2 or length % 2:
-        features = gather_features(local_rows)
+        features, quant = lax.optimization_barrier((gather_features(local_rows), quant))
         pieces = features.reshape(length, shards, rows).transpose(1, 0, 2)
-        return lax.all_to_all(pieces, "fsdp", 0, 0)
+        return [(lax.all_to_all(pieces, "fsdp", 0, 0), 0)], quant
     half = length // 2
     first = lax.axis_index("seq") == 0
     wanted_by_other = lax.dynamic_slice_in_dim(local_rows, jnp.where(first, half, 0), half, 0)
     kept = lax.dynamic_slice_in_dim(local_rows, jnp.where(first, 0, half), half, 0)
     other = lax.ppermute(wanted_by_other, "seq", [(0, 1), (1, 0)])
+    other, quant = lax.optimization_barrier((other, quant))
     features = jnp.where(
         first, jnp.concatenate([kept, other], axis=1), jnp.concatenate([other, kept], axis=1)
     )
     pieces = features.reshape(half, shards, rows).transpose(1, 0, 2)
     own_half = lax.all_to_all(pieces, "fsdp", 0, 0)
     other_half = lax.ppermute(own_half, "seq", [(0, 1), (1, 0)])
-    return jnp.where(
-        first,
-        jnp.concatenate([own_half, other_half], axis=1),
-        jnp.concatenate([other_half, own_half], axis=1),
-    )
+    own_at = jnp.where(first, 0, half)
+    return [(own_half, own_at), (other_half, half - own_at)], quant
+
+
+def reduce_partial(partial, me):
+    shards = partial.shape[0]
+    received = lax.all_to_all(partial.astype(jnp.float16), "fsdp", 0, 0).astype(jnp.float32)
+    others = jnp.where((jnp.arange(shards) == me)[:, None, None], 0.0, received)
+    own = lax.dynamic_index_in_dim(partial, me, 0, keepdims=False)
+    return own + jnp.sum(others, axis=0)
 
 
 def sum_over_ctx(value):
@@ -100,16 +106,18 @@
     rows, columns = weight.shape
     values = weight.astype(jnp.float32)
     quant = soft_clip(values, clip_upper, clip_lower).astype(jnp.bfloat16)
-    mine = rows_of_block(local_rows, shards, rows)
-    mine, quant = lax.optimization_barrier((mine, quant))
+    pieces, quant = rows_of_block(local_rows, shards, rows, quant)
+    me = lax.axis_index("fsdp")
+    proj = jnp.zeros((length, columns), jnp.float32)
+    mine = jnp.zeros((shards, length, rows), local_rows.dtype)
+    for piece, at in pieces:
+        count = piece.shape[1]
+        flat = piece.reshape(shards * count, rows)
+        partial = jnp.dot(flat, quant, preferred_element_type=jnp.float32).reshape(shards, count, columns)
+        proj = lax.dynamic_update_slice_in_dim(proj, reduce_partial(partial, me), at, 0)
+        mine = lax.dynamic_update_slice_in_dim(mine, piece, at, 1)
+    proj = proj.astype(jnp.bfloat16)
     inputs = mine.reshape(shards * length, rows)
-
-    partial = jnp.dot(inputs, quant, preferred_element_type=jnp.float32).reshape(shards, length, columns)
-    me = lax.axis_index("fsdp")
-    received = lax.all_to_all(partial.astype(jnp.float16), "fsdp", 0, 0).astype(jnp.float32)
-    others = jnp.where((jnp.arange(shards) == me)[:, None, None], 0.0, received)
-    own = lax.dynamic_index_in_dim(partial, me, 0, keepdims=False)
-    proj = (own + jnp.sum(others, axis=0)).astype(jnp.bfloat16)
 
     taps = jnp.repeat(filters, CGROUP, axis=0).T
     pad = FILT - 1

time: 171 us -> 161 us (0.942)
  waiting for transfers between devices: 84.9 us -> 67.9 us
  matrix products: 18.5 us -> 21.9 us
  starting transfers between devices: 15.1 us -> 18.3 us
    all_to_all x1 -> x2, waiting for transfers between devices: 32.2 us -> 18.4 us  [reduce_partial(): lax.all_to_all(partial.astype(jnp.float16), 'fsdp', 0, 0)]
    ppermute x1, waiting for transfers between devices: 8.83 us -> 0.01 us  [rows_of_block(): other = lax.ppermute(wanted_by_other, 'seq', [(0, 1), (1, 0)])]
    ppermute x1, waiting for transfers between devices: 4.68 us -> 10.6 us  [rows_of_block(): other_half = lax.ppermute(own_half, 'seq', [(0, 1), (1, 0)])]
    dot_general x1 -> x2, matrix products: 5.13 us -> 9.88 us  [on_device(): jnp.dot(flat, quant, preferred_element_type=jnp.float32)]
    all_to_all x1 -> x2, starting transfers between devices: 3.69 us -> 7.12 us  [reduce_partial(): lax.all_to_all(partial.astype(jnp.float16), 'fsdp', 0, 0)]
    dynamic_update_slice x0 -> x2, other arithmetic: none -> 2.09 us  [on_device(): lax.dynamic_update_slice_in_dim(proj, reduce_partial(partial, me), at, 0)]
  transfers between devices with their start and end apart: 8 -> 9, of which waited for: 7 -> 6; matrix products, arithmetic and copies ran while one was open for 10% -> 17% of each run, Pallas kernels for 0% -> 0%
where the time goes in v10:
time: 161 us
  waiting for transfers between devices  67.9 us (42%)
  blocking collectives  24.5 us (15%)
  matrix products  21.9 us (14%)
  other arithmetic  18.7 us (12%)
  starting transfers between devices  18.3 us (11%)
  local copies, waits for them, and re-layouts  8.33 us (5%)
    all_to_all x1, waiting for transfers between devices, on_device(): lax.all_to_all(copies, 'fsdp', 0, 0).reshape(shards * length, columns)  36.2 us
    all_to_all x1, blocking collectives, rows_of_block(): own_half = lax.all_to_all(pieces, 'fsdp', 0, 0)  24.5 us
    all_to_all x2, waiting for transfers between devices, reduce_partial(): lax.all_to_all(partial.astype(jnp.float16), 'fsdp', 0, 0)  18.4 us
    dot_general x1, matrix products, on_device(): lax.dot_general(inputs, d_all, (((0,), (0,)), ((), ())), preferred_elemen...  12 us
    ppermute x1, waiting for transfers between devices, rows_of_block(): other_half = lax.ppermute(own_half, 'seq', [(0, 1), (1, 0)])  10.6 us
    dot_general x2, matrix products, on_device(): jnp.dot(flat, quant, preferred_element_type=jnp.float32)  9.88 us
    all_to_all x2, starting transfers between devices, reduce_partial(): lax.all_to_all(partial.astype(jnp.float16), 'fsdp', 0, 0)  7.12 us
    convert_element_type x1, other arithmetic, on_device(): quant = soft_clip(values, clip_upper, clip_lower).astype(jnp.bfloat16)  6.03 us
  transfers between devices with their start and end apart: 9, of which 6 were waited for; matrix products, arithmetic and copies ran while one was open for 17% of the time, Pallas kernels for 0%

profile of v10, /device:TPU:0, one launch (start us, length us, event | category | flops | bytes accessed | tf_op | source)
XLA Modules:
  0.0 160.6 jit_solution(13892062096658383696)
XLA Ops:
  0.7 1.2 constant_dynamic-slice_fusion
  1.9 3.0 %collective-permute-start = (bf16[48,4096]{1,0:T(8,128)(2,1)S(1)}, bf16[48,4096]{1,0:T(8,128)(2,1)S(1)}, u32[]{:S(2)}, u32[]{:S(2)}) collective-permute-start(bf16[48,4096]{1,0:T(8,128)(2,1)S(1)} %get-tuple-element.13), channel_id=1, source_target_pairs={{0,2},{2,0},{1,3},{3,1},{4,6},{6,4},{5,7},{7,5},{8,10},{10,8},{9,1... | collective-permute-start | bytes 1179656 | tf_op jit(solution)/shard_map/ppermute | solution.py:74
  4.9 5.7 %abs_reduce_fusion = f32[16,2048]{1,0:T(8,128)S(1)} fusion(bf16[2048,2048]{1,0:T(8,128)(2,1)} %param.8), kind=kLoop, calls=%fused_computation.10 | loop fusion | flops 12550144 | bytes 8519680 | tf_op jit(solution)/shard_map/reduce_max | solution.py:20
  11.1 6.0 %fusion.3 = bf16[2048,2048]{1,0:T(8,128)(2,1)S(1)} fusion(bf16[2048,2048]{1,0:T(8,128)(2,1)} %param.8, f32[16,2048]{1,0:T(8,128)S(1)} %get-tuple-element.10, f32[16,2048]{1,0:T(8,128)S(1)} %get-tuple-element.11, f32[16,2048]{1,0:T(8,128)S(1)} %get-tuple-element.14), kind=kLoop, calls=%fused_computation.5 | loop fusion | flops 25165824 | bytes 17170432 | tf_op jit(solution)/shard_map/convert_element_type | solution.py:108
  17.4 24.5 %all_to_all.20 = bf16[4,48,2048]{2,1,0:T(8,128)(2,1)S(1)} all-to-all(bf16[4,48,2048]{2,1,0:T(8,128)(2,1)S(1)} %fusion.34), channel_id=1, replica_groups=mesh['parts'=2,'fsdp'=4,'seq'=2,'ctx'=2] {'fsdp'}, dimensions={0} | all-to-all | bytes 1572864 | tf_op jit(solution)/shard_map/all_to_all | solution.py:80
  41.9 0.5 collective-permute-start.1
  42.4 3.3 %fusion.39 = (f16[4,48,2048]{2,1,0:T(8,128)(2,1)}, f32[4,48,2048]{2,1,0:T(8,128)}) fusion(bf16[4,48,2048]{2,1,0:T(8,128)(2,1)S(1)} %all_to_all.20, bf16[2048,2048]{1,0:T(8,128)(2,1)S(1)} %fusion.3), kind=kOutput, calls=%fused_computation.86 | convolution fusion | flops 1611005952 | bytes 11534336 | tf_op jit(solution)/shard_map/dot_general | solution.py:116
  45.7 3.6 %all-to-all-start.1 = ((f16[4,48,2048]{2,1,0:T(8,128)(2,1)}), f16[4,48,2048]{2,1,0:T(8,128)(2,1)S(1)}, u32[]{:S(2)}, u32[]{:S(2)}) async-start(f16[4,48,2048]{2,1,0:T(8,128)(2,1)} %get-tuple-element.26), calls=%async_computation.1 | async-start | bytes 1572864 | tf_op jit(solution)/shard_map/all_to_all | solution.py:88
  49.4 10.6 %collective-permute-done.1 = bf16[4,48,2048]{2,1,0:T(8,128)(2,1)S(1)} collective-permute-done((bf16[4,48,2048]{2,1,0:T(8,128)(2,1)S(1)}, bf16[4,48,2048]{2,1,0:T(8,128)(2,1)S(1)}, u32[]{:S(2)}, u32[]{:S(2)}) %collective-permute-start.1) | collective-permute-done | bytes 786464 | tf_op jit(solution)/shard_map/ppermute | solution.py:81
  59.9 6.6 %fusion.38 = (f16[4,48,2048]{2,1,0:T(8,128)(2,1)}, f32[4,48,2048]{2,1,0:T(8,128)}) fusion(bf16[4,48,2048]{2,1,0:T(8,128)(2,1)S(1)} %collective-permute-done.1, bf16[2048,2048]{1,0:T(8,128)(2,1)} %copy-done), kind=kOutput, calls=%fused_computation.85 | convolution fusion | flops 1611005952 | bytes 11534336 | tf_op jit(solution)/shard_map/dot_general | solution.py:116
  66.5 1.7 %all-to-all-done.1 = f16[4,48,2048]{2,1,0:T(8,128)(2,1)S(1)} async-done(((f16[4,48,2048]{2,1,0:T(8,128)(2,1)}), f16[4,48,2048]{2,1,0:T(8,128)(2,1)S(1)}, u32[]{:S(2)}, u32[]{:S(2)}) %all-to-all-start.1) | async-done | bytes 786464 | tf_op jit(solution)/shard_map/all_to_all | solution.py:88
  68.2 3.5 %all-to-all-start.2 = ((f16[4,48,2048]{2,1,0:T(8,128)(2,1)}), f16[4,48,2048]{2,1,0:T(8,128)(2,1)S(1)}, u32[]{:S(2)}, u32[]{:S(2)}) async-start(f16[4,48,2048]{2,1,0:T(8,128)(2,1)} %get-tuple-element.24), calls=%async_computation.2 | async-start | bytes 1572864 | tf_op jit(solution)/shard_map/all_to_all | solution.py:88
  71.7 1.0 broadcast_in_dim.38
  72.7 1.9 %reshape.59 = f32[2048,7]{0,1:T(8,128)} reshape(f32[128,16,7]{1,0,2:T(8,128)} %broadcast_in_dim.38) | data formatting | bytes 114688 | tf_op jit(solution)/shard_map/reshape | solution.py:122
  74.6 16.7 %all-to-all-done.2 = f16[4,48,2048]{2,1,0:T(8,128)(2,1)S(1)} async-done(((f16[4,48,2048]{2,1,0:T(8,128)(2,1)}), f16[4,48,2048]{2,1,0:T(8,128)(2,1)S(1)}, u32[]{:S(2)}, u32[]{:S(2)}) %all-to-all-start.2) | async-done | bytes 786464 | tf_op jit(solution)/shard_map/all_to_all | solution.py:88
  91.8 1.0 fusion.36
  92.9 1.0 fusion.35
  93.9 1.3 collective-permute-start.2
  95.2 1.2 fusion.37
  96.6 1.9 %convert_multiply_fusion = f32[96,2048]{1,0:T(8,128)S(1)} fusion(f32[102,2048]{1,0:T(8,128)S(1)} %maximum_convert_fusion, bf16[1,1,96,2048]{3,2,1,0:T(8,128)(2,1)} %param.13, bf16[1,1,96,2048]{3,2,1,0:T(8,128)(2,1)} %param.12, f32[2048]{0:T(1024)S(1)} %bitcast.82, f32[2048]{0:T(1024)S(1)} %bitcast.84, f32[2048]{0:T(1024)S(1)} %bitcast.86, ...), kind=kLoop, calls=%fused_computation.23 | loop fusion | flops 3735552 | bytes 7135232 | tf_op jit(solution)/shard_map/mul | solution.py:133
  98.5 1.3 collective-permute-start.3
  99.8 1.8 %collective-permute-done.3 = f32[6,2048]{1,0:T(8,128)S(1)} collective-permute-done((f32[6,2048]{1,0:T(8,128)S(1)}, f32[6,2048]{1,0:T(8,128)S(1)}, u32[]{:S(2)}, u32[]{:S(2)}) %collective-permute-start.3) | collective-permute-done | bytes 49184 | tf_op jit(solution)/shard_map/ppermute | solution.py:13
  101.6 0.7 fusion.14
  102.3 1.3 broadcast_in_dim.42
  103.7 4.5 %all-to-all-start.3 = ((bf16[4,96,2048]{2,1,0:T(8,128)(2,1)}), bf16[4,96,2048]{2,1,0:T(8,128)(2,1)}, u32[]{:S(2)}, u32[]{:S(2)}) async-start(bf16[4,96,2048]{2,1,0:T(8,128)(2,1)} %broadcast_in_dim.42), calls=%async_computation.3 | async-start | bytes 3145728 | tf_op jit(solution)/shard_map/all_to_all | solution.py:142
  108.6 0.9 copy.20
  109.4 36.2 %all-to-all-done.3 = bf16[4,96,2048]{2,1,0:T(8,128)(2,1)} async-done(((bf16[4,96,2048]{2,1,0:T(8,128)(2,1)}), bf16[4,96,2048]{2,1,0:T(8,128)(2,1)}, u32[]{:S(2)}, u32[]{:S(2)}) %all-to-all-start.3) | async-done | bytes 1572896 | tf_op jit(solution)/shard_map/all_to_all | solution.py:142
  145.7 12.0 %multiply_reduce_fusion = (f32[16,2048]{1,0:T(8,128)S(1)}, f32[16,2048]{1,0:T(8,128)S(1)}) fusion(bf16[2048,2048]{1,0:T(8,128)(2,1)} %param.8, f32[16,2048]{1,0:T(8,128)S(1)} %get-tuple-element.10, f32[16,2048]{1,0:T(8,128)S(1)} %get-tuple-element.14, bf16[16,128,384]{2,1,0:T(8,128)(2,1)S(1)} %bitcast.76, bf16[384,2048,1]{1,0,2:T(8,128)(2,1)} %bitcast.23), kind=kOutput, calls=%fused_computation.6 | convolution fusion | flops 3275685888 | bytes 12058624 | tf_op jit(solution)/shard_map/dot_general | solution.py:143
  157.9 0.5 collective-permute-start.4
  158.4 0.8 collective-permute-done.5
  159.3 0.7 add.119
  159.9 0.7 add.118
  (31 shorter events, 1.9 us)
Async XLA Ops:
  0.6 10.4 %copy-start.1 = (f32[16,2048]{1,0:T(8,128)S(1)}, f32[16,2048]{1,0:T(8,128)}, u32[]{:S(2)}) copy-start(f32[16,2048]{1,0:T(8,128)} %param.10) | copy-start | bytes 393220
  0.6 10.4 %copy-start.3 = (f32[16,2048]{1,0:T(8,128)S(1)}, f32[16,2048]{1,0:T(8,128)}, u32[]{:S(2)}) copy-start(f32[16,2048]{1,0:T(8,128)} %param.9) | copy-start | bytes 393220
  1.9 15.3 %collective-permute-start = (bf16[48,4096]{1,0:T(8,128)(2,1)S(1)}, bf16[48,4096]{1,0:T(8,128)(2,1)S(1)}, u32[]{:S(2)}, u32[]{:S(2)}) collective-permute-start(bf16[48,4096]{1,0:T(8,128)(2,1)S(1)} %get-tuple-element.13), channel_id=1, source_target_pairs={{0,2},{2,0},{1,3},{3,1},{4,6},{6,4},{5,7},{7,5},{8,10},{10,8},{9,1... | collective-permute-start | bytes 1179656 | tf_op jit(solution)/shard_map/ppermute | solution.py:74
  17.2 25.2 %copy-start = (bf16[2048,2048]{1,0:T(8,128)(2,1)}, bf16[2048,2048]{1,0:T(8,128)(2,1)S(1)}, u32[]{:S(2)}) copy-start(bf16[2048,2048]{1,0:T(8,128)(2,1)S(1)} %fusion.3) | copy-start | bytes 25165828
  41.9 18.1 %collective-permute-start.1 = (bf16[4,48,2048]{2,1,0:T(8,128)(2,1)S(1)}, bf16[4,48,2048]{2,1,0:T(8,128)(2,1)S(1)}, u32[]{:S(2)}, u32[]{:S(2)}) collective-permute-start(bf16[4,48,2048]{2,1,0:T(8,128)(2,1)S(1)} %all_to_all.20), channel_id=1, source_target_pairs={{0,2},{2,0},{1,3},{3,1},{4,6},{6,4},{5,7},{7,5},{8,10},{10,8},{9,1... | collective-permute-start | bytes 2359304 | tf_op jit(solution)/shard_map/ppermute | solution.py:81
  45.7 26.0 %copy-start.5 = (f32[128,7]{0,1:T(8,128)S(1)}, f32[128,7]{0,1:T(8,128)}, u32[]{:S(2)}) copy-start(f32[128,7]{0,1:T(8,128)} %param.11) | copy-start | bytes 10756
  45.7 22.5 %all-to-all-start.1 = ((f16[4,48,2048]{2,1,0:T(8,128)(2,1)}), f16[4,48,2048]{2,1,0:T(8,128)(2,1)S(1)}, u32[]{:S(2)}, u32[]{:S(2)}) async-start(f16[4,48,2048]{2,1,0:T(8,128)(2,1)} %get-tuple-element.26), calls=%async_computation.1 | async-start | bytes 1572864 | tf_op jit(solution)/shard_map/all_to_all | solution.py:88
  68.2 23.1 %all-to-all-start.2 = ((f16[4,48,2048]{2,1,0:T(8,128)(2,1)}), f16[4,48,2048]{2,1,0:T(8,128)(2,1)S(1)}, u32[]{:S(2)}, u32[]{:S(2)}) async-start(f16[4,48,2048]{2,1,0:T(8,128)(2,1)} %get-tuple-element.24), calls=%async_computation.2 | async-start | bytes 1572864 | tf_op jit(solution)/shard_map/all_to_all | solution.py:88
  93.9 2.5 %collective-permute-start.2 = (bf16[6,2048]{1,0:T(8,128)(2,1)S(1)}, bf16[6,2048]{1,0:T(8,128)(2,1)S(1)}, u32[]{:S(2)}, u32[]{:S(2)}) collective-permute-start(bf16[6,2048]{1,0:T(8,128)(2,1)S(1)} %slice.96), channel_id=1, source_target_pairs={{0,1},{2,3},{4,5},{6,7},{8,9},{10,11},{12,13},{14,15},{16,17},{18,... | collective-permute-start | bytes 73736 | tf_op jit(solution)/shard_map/ppermute | solution.py:13
  98.5 3.1 %collective-permute-start.3 = (f32[6,2048]{1,0:T(8,128)S(1)}, f32[6,2048]{1,0:T(8,128)S(1)}, u32[]{:S(2)}, u32[]{:S(2)}) collective-permute-start(f32[6,2048]{1,0:T(8,128)S(1)} %slice.110), channel_id=1, source_target_pairs={{1,0},{3,2},{5,4},{7,6},{9,8},{11,10},{13,12},{15,14},{17,16},{19,... | collective-permute-start | bytes 147464 | tf_op jit(solution)/shard_map/ppermute | solution.py:13
  103.7 42.0 %all-to-all-start.3 = ((bf16[4,96,2048]{2,1,0:T(8,128)(2,1)}), bf16[4,96,2048]{2,1,0:T(8,128)(2,1)}, u32[]{:S(2)}, u32[]{:S(2)}) async-start(bf16[4,96,2048]{2,1,0:T(8,128)(2,1)} %broadcast_in_dim.42), calls=%async_computation.3 | async-start | bytes 3145728 | tf_op jit(solution)/shard_map/all_to_all | solution.py:142
  145.7 12.1 %copy-start.2 = (f32[16,2048]{1,0:T(8,128)S(1)}, f32[16,2048]{1,0:T(8,128)}, u32[]{:S(2)}) copy-start(f32[16,2048]{1,0:T(8,128)} %param.10) | copy-start | bytes 393220
  145.7 12.1 %copy-start.4 = (f32[16,2048]{1,0:T(8,128)S(1)}, f32[16,2048]{1,0:T(8,128)}, u32[]{:S(2)}) copy-start(f32[16,2048]{1,0:T(8,128)} %param.9) | copy-start | bytes 393220
  157.9 1.4 collective-permute-start.5
  157.9 2.0 %collective-permute-start.4 = (f32[16,2048]{1,0:T(8,128)S(1)}, f32[16,2048]{1,0:T(8,128)S(1)}, u32[]{:S(2)}, u32[]{:S(2)}) collective-permute-start(f32[16,2048]{1,0:T(8,128)S(1)} %get-tuple-element.16), channel_id=1, source_target_pairs={{0,1},{1,0},{2,3},{3,2},{4,5},{5,4},{6,7},{7,6},{8,9},{9,8},{10,11... | collective-permute-start | bytes 393224 | tf_op jit(solution)/shard_map/ppermute | solution.py:98

commit v11 on v10

--- a/solution.py
+++ b/solution.py
@@ -17,7 +17,7 @@
     rows = values.shape[0]
     groups = upper_logit.shape[0]
     blocks = values.reshape(groups, rows // groups, values.shape[1])
-    amax = jnp.max(jnp.abs(blocks), axis=1) + 1e-06
+    amax = jnp.max(jnp.abs(blocks.astype(jnp.bfloat16)), axis=1).astype(jnp.float32) + 1e-06
     upper = jax.nn.sigmoid(upper_logit) * amax
     lower = -jax.nn.sigmoid(lower_logit) * amax
     center = ((upper + lower) * 0.5)[:, None, :]
@@ -122,20 +122,24 @@
     taps = jnp.repeat(filters, CGROUP, axis=0).T
     pad = FILT - 1
     previous = from_behind(proj[length - pad :], "ctx", 1)
-    padded = jnp.concatenate([previous, proj], axis=0).astype(jnp.float32)
-    conv = jnp.zeros((length, columns), jnp.float32)
+    upcoming = from_behind(proj[:pad], "ctx", -1)
+    gates_in = gate.reshape(length, columns)
+    wanted_in = target.reshape(length, columns)
+    gates_next = from_behind(gates_in[:pad], "ctx", -1)
+    wanted_next = from_behind(wanted_in[:pad], "ctx", -1)
+    padded = jnp.concatenate([previous, proj, upcoming], axis=0).astype(jnp.float32)
+    extent = length + pad
+    conv = jnp.zeros((extent, columns), jnp.float32)
     for tap in range(FILT):
-        conv = conv + taps[tap] * padded[pad - tap : pad - tap + length]
-    gates = gate.reshape(length, columns).astype(jnp.float32)
-    wanted = target.reshape(length, columns).astype(jnp.float32)
+        conv = conv + taps[tap] * padded[pad - tap : pad - tap + extent]
+    gates = jnp.concatenate([gates_in, gates_next], axis=0).astype(jnp.float32)
+    wanted = jnp.concatenate([wanted_in, wanted_next], axis=0).astype(jnp.float32)
     total_tokens = lax.axis_size("fsdp") * lax.axis_size("ctx") * length
     scale = 1024.0 / jnp.sqrt(jnp.float32(total_tokens))
     d_conv = scale * (gates * conv - wanted) * gates
-    following = from_behind(d_conv[:pad], "ctx", -1)
-    padded_back = jnp.concatenate([d_conv, following], axis=0)
     d_proj = jnp.zeros((length, columns), jnp.float32)
     for tap in range(FILT):
-        d_proj = d_proj + taps[tap] * padded_back[tap : tap + length]
+        d_proj = d_proj + taps[tap] * d_conv[tap : tap + length]
     d_proj = d_proj.astype(jnp.bfloat16)
 
     copies = jnp.broadcast_to(d_proj[None], (shards, length, columns))

time: 161 us -> 160 us (level)
  waiting for transfers between devices: 67.9 us -> 63.1 us
  starting transfers between devices: 18.3 us -> 20.9 us
    all_to_all x2, waiting for transfers between devices: 18.4 us -> 13.7 us  [reduce_partial(): lax.all_to_all(partial.astype(jnp.float16), 'fsdp', 0, 0)]
    ppermute x2 -> x4, starting transfers between devices: 2.58 us -> 5.14 us  [from_behind(): return lax.ppermute(value, axis, pairs)]
  transfers between devices with their start and end apart: 9 -> 11, of which waited for: 6 -> 6; matrix products, arithmetic and copies ran while one was open for 17% -> 20% of each run, Pallas kernels for 0% -> 0%
where the time goes in v11:
time: 160 us; the launch traced here: 159 us
  waiting for transfers between devices  63.1 us (39%)
  blocking collectives  24.5 us (15%)
  matrix products  21.9 us (14%)
  starting transfers between devices  20.9 us (13%)
  other arithmetic  18.8 us (12%)
  local copies, waits for them, and re-layouts  9.27 us (6%)
    all_to_all x1, waiting for transfers between devices, on_device(): lax.all_to_all(copies, 'fsdp', 0, 0).reshape(shards * length, columns)  36.2 us
    all_to_all x1, blocking collectives, rows_of_block(): own_half = lax.all_to_all(pieces, 'fsdp', 0, 0)  24.5 us
    all_to_all x2, waiting for transfers between devices, reduce_partial(): lax.all_to_all(partial.astype(jnp.float16), 'fsdp', 0, 0)  13.7 us
    dot_general x1, matrix products, on_device(): lax.dot_general(inputs, d_all, (((0,), (0,)), ((), ())), preferred_elemen...  12.1 us
    ppermute x1, waiting for transfers between devices, rows_of_block(): other_half = lax.ppermute(own_half, 'seq', [(0, 1), (1, 0)])  10.6 us
    dot_general x2, matrix products, on_device(): jnp.dot(flat, quant, preferred_element_type=jnp.float32)  9.89 us
    all_to_all x2, starting transfers between devices, reduce_partial(): lax.all_to_all(partial.astype(jnp.float16), 'fsdp', 0, 0)  7.12 us
    convert_element_type x1, other arithmetic, on_device(): quant = soft_clip(values, clip_upper, clip_lower).astype(jnp.bfloat16)  6.03 us
  transfers between devices with their start and end apart: 11, of which 6 were waited for; matrix products, arithmetic and copies ran while one was open for 20% of the time, Pallas kernels for 0%

profile of v11, /device:TPU:0, one launch (start us, length us, event | category | flops | bytes accessed | tf_op | source)
XLA Modules:
  0.0 159.4 jit_solution(10979927713092960791)
XLA Ops:
  0.7 1.2 constant_dynamic-slice_fusion
  1.9 3.0 %collective-permute-start = (bf16[48,4096]{1,0:T(8,128)(2,1)S(1)}, bf16[48,4096]{1,0:T(8,128)(2,1)S(1)}, u32[]{:S(2)}, u32[]{:S(2)}) collective-permute-start(bf16[48,4096]{1,0:T(8,128)(2,1)S(1)} %get-tuple-element.13), channel_id=1, source_target_pairs={{0,2},{2,0},{1,3},{3,1},{4,6},{6,4},{5,7},{7,5},{8,10},{10,8},{9,1... | collective-permute-start | bytes 1179656 | tf_op jit(solution)/shard_map/ppermute | solution.py:74
  4.9 5.7 %abs_reduce_fusion = bf16[16,2048]{1,0:T(8,128)(2,1)S(1)} fusion(bf16[2048,2048]{1,0:T(8,128)(2,1)} %param.8), kind=kLoop, calls=%fused_computation.15 | loop fusion | flops 16744448 | bytes 8454144 | tf_op jit(solution)/shard_map/reduce_max | solution.py:20
  11.1 6.0 %fusion.3 = bf16[2048,2048]{1,0:T(8,128)(2,1)S(1)} fusion(bf16[2048,2048]{1,0:T(8,128)(2,1)} %param.8, f32[16,2048]{1,0:T(8,128)S(1)} %get-tuple-element.10, f32[16,2048]{1,0:T(8,128)S(1)} %get-tuple-element.11, f32[16,2048]{1,0:T(8,128)S(1)} %get-tuple-element.16), kind=kLoop, calls=%fused_computation.5 | loop fusion | flops 25165824 | bytes 17170432 | tf_op jit(solution)/shard_map/convert_element_type | solution.py:108
  17.4 24.5 %all_to_all.20 = bf16[4,48,2048]{2,1,0:T(8,128)(2,1)S(1)} all-to-all(bf16[4,48,2048]{2,1,0:T(8,128)(2,1)S(1)} %fusion.23), channel_id=1, replica_groups=mesh['parts'=2,'fsdp'=4,'seq'=2,'ctx'=2] {'fsdp'}, dimensions={0} | all-to-all | bytes 1572864 | tf_op jit(solution)/shard_map/all_to_all | solution.py:80
  42.4 3.3 %fusion.30 = (f16[4,48,2048]{2,1,0:T(8,128)(2,1)}, f32[4,48,2048]{2,1,0:T(8,128)}) fusion(bf16[4,48,2048]{2,1,0:T(8,128)(2,1)S(1)} %all_to_all.20, bf16[2048,2048]{1,0:T(8,128)(2,1)S(1)} %fusion.3), kind=kOutput, calls=%fused_computation.77 | convolution fusion | flops 1611005952 | bytes 11534336 | tf_op jit(solution)/shard_map/dot_general | solution.py:116
  45.7 3.6 %all-to-all-start.1 = ((f16[4,48,2048]{2,1,0:T(8,128)(2,1)}), f16[4,48,2048]{2,1,0:T(8,128)(2,1)S(1)}, u32[]{:S(2)}, u32[]{:S(2)}) async-start(f16[4,48,2048]{2,1,0:T(8,128)(2,1)} %get-tuple-element.28), calls=%async_computation.1 | async-start | bytes 1572864 | tf_op jit(solution)/shard_map/all_to_all | solution.py:88
  49.4 10.6 %collective-permute-done.1 = bf16[4,48,2048]{2,1,0:T(8,128)(2,1)S(1)} collective-permute-done((bf16[4,48,2048]{2,1,0:T(8,128)(2,1)S(1)}, bf16[4,48,2048]{2,1,0:T(8,128)(2,1)S(1)}, u32[]{:S(2)}, u32[]{:S(2)}) %collective-permute-start.1) | collective-permute-done | bytes 786464 | tf_op jit(solution)/shard_map/ppermute | solution.py:81
  59.9 6.6 %fusion.29 = (f16[4,48,2048]{2,1,0:T(8,128)(2,1)}, f32[4,48,2048]{2,1,0:T(8,128)}) fusion(bf16[4,48,2048]{2,1,0:T(8,128)(2,1)S(1)} %collective-permute-done.1, bf16[2048,2048]{1,0:T(8,128)(2,1)} %copy-done), kind=kOutput, calls=%fused_computation.76 | convolution fusion | flops 1611005952 | bytes 11534336 | tf_op jit(solution)/shard_map/dot_general | solution.py:116
  66.5 1.7 %all-to-all-done.1 = f16[4,48,2048]{2,1,0:T(8,128)(2,1)S(1)} async-done(((f16[4,48,2048]{2,1,0:T(8,128)(2,1)}), f16[4,48,2048]{2,1,0:T(8,128)(2,1)S(1)}, u32[]{:S(2)}, u32[]{:S(2)}) %all-to-all-start.1) | async-done | bytes 786464 | tf_op jit(solution)/shard_map/all_to_all | solution.py:88
  68.2 3.5 %all-to-all-start.2 = ((f16[4,48,2048]{2,1,0:T(8,128)(2,1)}), f16[4,48,2048]{2,1,0:T(8,128)(2,1)S(1)}, u32[]{:S(2)}, u32[]{:S(2)}) async-start(f16[4,48,2048]{2,1,0:T(8,128)(2,1)} %get-tuple-element.26), calls=%async_computation.2 | async-start | bytes 1572864 | tf_op jit(solution)/shard_map/all_to_all | solution.py:88
  71.7 1.4 slice_bitcast_fusion.1
  73.1 1.3 collective-permute-start.2
  74.4 1.4 slice_bitcast_fusion
  75.8 1.3 collective-permute-start.5
  77.1 1.0 broadcast_in_dim.38
  78.0 1.3 reshape.61
  79.3 12.0 %all-to-all-done.2 = f16[4,48,2048]{2,1,0:T(8,128)(2,1)S(1)} async-done(((f16[4,48,2048]{2,1,0:T(8,128)(2,1)}), f16[4,48,2048]{2,1,0:T(8,128)(2,1)S(1)}, u32[]{:S(2)}, u32[]{:S(2)}) %all-to-all-start.2) | async-done | bytes 786464 | tf_op jit(solution)/shard_map/all_to_all | solution.py:88
  91.8 1.0 fusion.25
  92.9 1.0 fusion.24
  93.9 1.3 collective-permute-start.3
  95.2 1.3 collective-permute-start.4
  96.6 1.7 %collective-permute-done.4 = bf16[6,2048]{1,0:T(8,128)(2,1)S(1)} collective-permute-done((bf16[6,2048]{1,0:T(8,128)(2,1)S(1)}, bf16[6,2048]{1,0:T(8,128)(2,1)S(1)}, u32[]{:S(2)}, u32[]{:S(2)}) %collective-permute-start.4) | collective-permute-done | bytes 24608 | tf_op jit(solution)/shard_map/ppermute | solution.py:13
  98.5 2.0 %convert_multiply_fusion = f32[102,2048]{1,0:T(8,128)S(1)} fusion(f32[108,2048]{1,0:T(8,128)S(1)} %maximum_convert_fusion, bf16[6,2048]{1,0:T(8,128)(2,1)} %collective-permute-done.2, bf16[96,2048]{1,0:T(8,128)(2,1)} %bitcast.78, bf16[6,2048]{1,0:T(8,128)(2,1)} %collective-permute-done.5, bf16[96,2048]{1,0:T(8,128)(2,1)} %bitcast.79, f32[2048]{0:T(1024)S(1)} %bitcast.84, ...), kind=kLoop, calls=%fused_computation.18 | loop fusion | flops 5222400 | bytes 7577600 | tf_op jit(solution)/shard_map/mul | solution.py:139
  101.2 1.3 broadcast_in_dim.42
  102.5 4.5 %all-to-all-start.3 = ((bf16[4,96,2048]{2,1,0:T(8,128)(2,1)}), bf16[4,96,2048]{2,1,0:T(8,128)(2,1)}, u32[]{:S(2)}, u32[]{:S(2)}) async-start(bf16[4,96,2048]{2,1,0:T(8,128)(2,1)} %broadcast_in_dim.42), calls=%async_computation.3 | async-start | bytes 3145728 | tf_op jit(solution)/shard_map/all_to_all | solution.py:146
  107.4 0.9 copy.20
  108.2 36.2 %all-to-all-done.3 = bf16[4,96,2048]{2,1,0:T(8,128)(2,1)} async-done(((bf16[4,96,2048]{2,1,0:T(8,128)(2,1)}), bf16[4,96,2048]{2,1,0:T(8,128)(2,1)}, u32[]{:S(2)}, u32[]{:S(2)}) %all-to-all-start.3) | async-done | bytes 1572896 | tf_op jit(solution)/shard_map/all_to_all | solution.py:146
  144.5 12.1 %multiply_reduce_fusion = (f32[16,2048]{1,0:T(8,128)S(1)}, f32[16,2048]{1,0:T(8,128)S(1)}) fusion(bf16[2048,2048]{1,0:T(8,128)(2,1)} %param.8, f32[16,2048]{1,0:T(8,128)S(1)} %get-tuple-element.10, f32[16,2048]{1,0:T(8,128)S(1)} %get-tuple-element.16, bf16[16,128,384]{2,1,0:T(8,128)(2,1)S(1)} %bitcast.76, bf16[384,2048,1]{1,0,2:T(8,128)(2,1)} %bitcast.25), kind=kOutput, calls=%fused_computation.6 | convolution fusion | flops 3275685888 | bytes 12058624 | tf_op jit(solution)/shard_map/dot_general | solution.py:147
  157.2 0.8 collective-permute-done.7
  158.1 0.7 add.119
  158.8 0.7 add.118
  (36 shorter events, 3.6 us)
Async XLA Ops:
  0.6 10.4 %copy-start.1 = (f32[16,2048]{1,0:T(8,128)S(1)}, f32[16,2048]{1,0:T(8,128)}, u32[]{:S(2)}) copy-start(f32[16,2048]{1,0:T(8,128)} %param.10) | copy-start | bytes 393220
  0.6 10.4 %copy-start.3 = (f32[16,2048]{1,0:T(8,128)S(1)}, f32[16,2048]{1,0:T(8,128)}, u32[]{:S(2)}) copy-start(f32[16,2048]{1,0:T(8,128)} %param.9) | copy-start | bytes 393220
  1.9 15.3 %collective-permute-start = (bf16[48,4096]{1,0:T(8,128)(2,1)S(1)}, bf16[48,4096]{1,0:T(8,128)(2,1)S(1)}, u32[]{:S(2)}, u32[]{:S(2)}) collective-permute-start(bf16[48,4096]{1,0:T(8,128)(2,1)S(1)} %get-tuple-element.13), channel_id=1, source_target_pairs={{0,2},{2,0},{1,3},{3,1},{4,6},{6,4},{5,7},{7,5},{8,10},{10,8},{9,1... | collective-permute-start | bytes 1179656 | tf_op jit(solution)/shard_map/ppermute | solution.py:74
  17.2 25.2 %copy-start = (bf16[2048,2048]{1,0:T(8,128)(2,1)}, bf16[2048,2048]{1,0:T(8,128)(2,1)S(1)}, u32[]{:S(2)}) copy-start(bf16[2048,2048]{1,0:T(8,128)(2,1)S(1)} %fusion.3) | copy-start | bytes 25165828
  41.9 18.1 %collective-permute-start.1 = (bf16[4,48,2048]{2,1,0:T(8,128)(2,1)S(1)}, bf16[4,48,2048]{2,1,0:T(8,128)(2,1)S(1)}, u32[]{:S(2)}, u32[]{:S(2)}) collective-permute-start(bf16[4,48,2048]{2,1,0:T(8,128)(2,1)S(1)} %all_to_all.20), channel_id=1, source_target_pairs={{0,2},{2,0},{1,3},{3,1},{4,6},{6,4},{5,7},{7,5},{8,10},{10,8},{9,1... | collective-permute-start | bytes 2359304 | tf_op jit(solution)/shard_map/ppermute | solution.py:81
  45.7 31.3 %copy-start.5 = (f32[128,7]{0,1:T(8,128)S(1)}, f32[128,7]{0,1:T(8,128)}, u32[]{:S(2)}) copy-start(f32[128,7]{0,1:T(8,128)} %param.11) | copy-start | bytes 10756
  45.7 22.5 %all-to-all-start.1 = ((f16[4,48,2048]{2,1,0:T(8,128)(2,1)}), f16[4,48,2048]{2,1,0:T(8,128)(2,1)S(1)}, u32[]{:S(2)}, u32[]{:S(2)}) async-start(f16[4,48,2048]{2,1,0:T(8,128)(2,1)} %get-tuple-element.28), calls=%async_computation.1 | async-start | bytes 1572864 | tf_op jit(solution)/shard_map/all_to_all | solution.py:88
  68.2 23.1 %all-to-all-start.2 = ((f16[4,48,2048]{2,1,0:T(8,128)(2,1)}), f16[4,48,2048]{2,1,0:T(8,128)(2,1)S(1)}, u32[]{:S(2)}, u32[]{:S(2)}) async-start(f16[4,48,2048]{2,1,0:T(8,128)(2,1)} %get-tuple-element.26), calls=%async_computation.2 | async-start | bytes 1572864 | tf_op jit(solution)/shard_map/all_to_all | solution.py:88
  73.1 25.4 %collective-permute-start.2 = (bf16[6,2048]{1,0:T(8,128)(2,1)}, bf16[6,2048]{1,0:T(8,128)(2,1)}, u32[]{:S(2)}, u32[]{:S(2)}) collective-permute-start(bf16[6,2048]{1,0:T(8,128)(2,1)} %slice_bitcast_fusion.1), channel_id=1, source_target_pairs={{1,0},{3,2},{5,4},{7,6},{9,8},{11,10},{13,12},{15,14},{17,16},{19,... | collective-permute-start | bytes 73736 | tf_op jit(solution)/shard_map/ppermute | solution.py:13
  75.8 22.7 %collective-permute-start.5 = (bf16[6,2048]{1,0:T(8,128)(2,1)}, bf16[6,2048]{1,0:T(8,128)(2,1)}, u32[]{:S(2)}, u32[]{:S(2)}) collective-permute-start(bf16[6,2048]{1,0:T(8,128)(2,1)} %slice_bitcast_fusion), channel_id=1, source_target_pairs={{1,0},{3,2},{5,4},{7,6},{9,8},{11,10},{13,12},{15,14},{17,16},{19,... | collective-permute-start | bytes 73736 | tf_op jit(solution)/shard_map/ppermute | solution.py:13
  93.9 2.7 %collective-permute-start.3 = (bf16[6,2048]{1,0:T(8,128)(2,1)S(1)}, bf16[6,2048]{1,0:T(8,128)(2,1)S(1)}, u32[]{:S(2)}, u32[]{:S(2)}) collective-permute-start(bf16[6,2048]{1,0:T(8,128)(2,1)S(1)} %get-tuple-element.14), channel_id=1, source_target_pairs={{0,1},{2,3},{4,5},{6,7},{8,9},{10,11},{12,13},{14,15},{16,17},{18,... | collective-permute-start | bytes 73736 | tf_op jit(solution)/shard_map/ppermute | solution.py:13
  95.2 3.1 %collective-permute-start.4 = (bf16[6,2048]{1,0:T(8,128)(2,1)S(1)}, bf16[6,2048]{1,0:T(8,128)(2,1)S(1)}, u32[]{:S(2)}, u32[]{:S(2)}) collective-permute-start(bf16[6,2048]{1,0:T(8,128)(2,1)S(1)} %get-tuple-element.15), channel_id=1, source_target_pairs={{1,0},{3,2},{5,4},{7,6},{9,8},{11,10},{13,12},{15,14},{17,16},{19,... | collective-permute-start | bytes 73736 | tf_op jit(solution)/shard_map/ppermute | solution.py:13
  102.5 42.0 %all-to-all-start.3 = ((bf16[4,96,2048]{2,1,0:T(8,128)(2,1)}), bf16[4,96,2048]{2,1,0:T(8,128)(2,1)}, u32[]{:S(2)}, u32[]{:S(2)}) async-start(bf16[4,96,2048]{2,1,0:T(8,128)(2,1)} %broadcast_in_dim.42), calls=%async_computation.3 | async-start | bytes 3145728 | tf_op jit(solution)/shard_map/all_to_all | solution.py:146
  144.5 12.1 %copy-start.2 = (f32[16,2048]{1,0:T(8,128)S(1)}, f32[16,2048]{1,0:T(8,128)}, u32[]{:S(2)}) copy-start(f32[16,2048]{1,0:T(8,128)} %param.10) | copy-start | bytes 393220
  144.5 12.1 %copy-start.4 = (f32[16,2048]{1,0:T(8,128)S(1)}, f32[16,2048]{1,0:T(8,128)}, u32[]{:S(2)}) copy-start(f32[16,2048]{1,0:T(8,128)} %param.9) | copy-start | bytes 393220
  156.7 1.4 collective-permute-start.7
  156.7 2.0 %collective-permute-start.6 = (f32[16,2048]{1,0:T(8,128)S(1)}, f32[16,2048]{1,0:T(8,128)S(1)}, u32[]{:S(2)}, u32[]{:S(2)}) collective-permute-start(f32[16,2048]{1,0:T(8,128)S(1)} %get-tuple-element.18), channel_id=1, source_target_pairs={{0,1},{1,0},{2,3},{3,2},{4,5},{5,4},{6,7},{7,6},{8,9},{9,8},{10,11... | collective-permute-start | bytes 393224 | tf_op jit(solution)/shard_map/ppermute | solution.py:98

commit v12 on v11

--- a/solution.py
+++ b/solution.py
@@ -27,8 +27,12 @@
 
 def soft_clip(values, upper_logit, lower_logit):
     blocks, _, center, radius = clip_bounds(values, upper_logit, lower_logit)
+    return clip_with(blocks, center, radius)
+
+
+def clip_with(blocks, center, radius):
     clipped = center + radius * jnp.tanh((blocks - center) * (1.0 / radius))
-    return clipped.reshape(values.shape)
+    return clipped.reshape(-1, blocks.shape[2])
 
 
 def soft_clip_grads(values, upper_logit, lower_logit, d_clipped):
@@ -60,11 +64,12 @@
     )
 
 
-def rows_of_block(local_rows, shards, rows, quant):
+def rows_of_block(local_rows, shards, rows, blocks, bounds):
     devices = lax.axis_size("seq")
     length = local_rows.shape[0]
     if devices != 2 or length % 2:
-        features, quant = lax.optimization_barrier((gather_features(local_rows), quant))
+        features, bounds = lax.optimization_barrier((gather_features(local_rows), bounds))
+        quant = clip_with(blocks, *bounds).astype(jnp.bfloat16)
         pieces = features.reshape(length, shards, rows).transpose(1, 0, 2)
         return [(lax.all_to_all(pieces, "fsdp", 0, 0), 0)], quant
     half = length // 2
@@ -72,12 +77,14 @@
     wanted_by_other = lax.dynamic_slice_in_dim(local_rows, jnp.where(first, half, 0), half, 0)
     kept = lax.dynamic_slice_in_dim(local_rows, jnp.where(first, 0, half), half, 0)
     other = lax.ppermute(wanted_by_other, "seq", [(0, 1), (1, 0)])
-    other, quant = lax.optimization_barrier((other, quant))
+    other, bounds = lax.optimization_barrier((other, bounds))
+    quant = clip_with(blocks, *bounds).astype(jnp.bfloat16)
     features = jnp.where(
         first, jnp.concatenate([kept, other], axis=1), jnp.concatenate([other, kept], axis=1)
     )
     pieces = features.reshape(half, shards, rows).transpose(1, 0, 2)
     own_half = lax.all_to_all(pieces, "fsdp", 0, 0)
+    own_half, quant = lax.optimization_barrier((own_half, quant))
     other_half = lax.ppermute(own_half, "seq", [(0, 1), (1, 0)])
     own_at = jnp.where(first, 0, half)
     return [(own_half, own_at), (other_half, half - own_at)], quant
@@ -105,8 +112,8 @@
     length = local_rows.shape[0]
     rows, columns = weight.shape
     values = weight.astype(jnp.float32)
-    quant = soft_clip(values, clip_upper, clip_lower).astype(jnp.bfloat16)
-    pieces, quant = rows_of_block(local_rows, shards, rows, quant)
+    blocks, _, center, radius = clip_bounds(values, clip_upper, clip_lower)
+    pieces, quant = rows_of_block(local_rows, shards, rows, blocks, (center, radius))
     me = lax.axis_index("fsdp")
     proj = jnp.zeros((length, columns), jnp.float32)
     mine = jnp.zeros((shards, length, rows), local_rows.dtype)

time: 160 us -> 163 us (1.019)
  blocking collectives: 24.5 us -> 0 us
  waiting for transfers between devices: 63.1 us -> 76.2 us
  starting transfers between devices: 20.9 us -> 27 us
  other arithmetic: 18.8 us -> 23.2 us
  matrix products: 21.9 us -> 25.3 us
    all_to_all x1 -> x0, blocking collectives: 24.5 us -> none  [rows_of_block(): own_half = lax.all_to_all(pieces, 'fsdp', 0, 0)]
    all_to_all x0 -> x1, waiting for transfers between devices: none -> 10.4 us  [rows_of_block(): own_half = lax.all_to_all(pieces, 'fsdp', 0, 0)]
    all_to_all x0 -> x1, starting transfers between devices: none -> 5.12 us  [rows_of_block(): own_half = lax.all_to_all(pieces, 'fsdp', 0, 0)]
    all_to_all x2, waiting for transfers between devices: 13.7 us -> 17.9 us  [reduce_partial(): lax.all_to_all(partial.astype(jnp.float16), 'fsdp', 0, 0)]
    ppermute x1, waiting for transfers between devices: 10.6 us -> 6.77 us  [rows_of_block(): other_half = lax.ppermute(own_half, 'seq', [(0, 1), (1, 0)])]
    dot_general x2, matrix products: 9.89 us -> 13.2 us  [on_device(): jnp.dot(flat, quant, preferred_element_type=jnp.float32)]
    convert_element_type x1, other arithmetic: 6.03 us -> 8.79 us  [rows_of_block(): quant = clip_with(blocks, *bounds).astype(jnp.bfloat16)]
    ppermute x1, waiting for transfers between devices: 0.01 us -> 2.22 us  [rows_of_block(): other = lax.ppermute(wanted_by_other, 'seq', [(0, 1), (1, 0)])]
  transfers between devices with their start and end apart: 11 -> 12, of which waited for: 6 -> 8; matrix products, arithmetic and copies ran while one was open for 20% -> 24% of each run, Pallas kernels for 0% -> 0%
where the time goes in v12:
time: 163 us; the launch traced here: 162 us
  waiting for transfers between devices  76.2 us (47%)
  starting transfers between devices  27 us (17%)
  matrix products  25.3 us (16%)
  other arithmetic  23.2 us (14%)
  local copies, waits for them, and re-layouts  9.25 us (6%)
    all_to_all x1, waiting for transfers between devices, on_device(): lax.all_to_all(copies, 'fsdp', 0, 0).reshape(shards * length, columns)  36.2 us
    all_to_all x2, waiting for transfers between devices, reduce_partial(): lax.all_to_all(partial.astype(jnp.float16), 'fsdp', 0, 0)  17.9 us
    dot_general x2, matrix products, on_device(): jnp.dot(flat, quant, preferred_element_type=jnp.float32)  13.2 us
    dot_general x1, matrix products, on_device(): lax.dot_general(inputs, d_all, (((0,), (0,)), ((), ())), preferred_elemen...  12.1 us
    all_to_all x1, waiting for transfers between devices, rows_of_block(): own_half = lax.all_to_all(pieces, 'fsdp', 0, 0)  10.4 us
    convert_element_type x1, other arithmetic, rows_of_block(): quant = clip_with(blocks, *bounds).astype(jnp.bfloat16)  8.79 us
    all_to_all x2, starting transfers between devices, reduce_partial(): lax.all_to_all(partial.astype(jnp.float16), 'fsdp', 0, 0)  7.12 us
    ppermute x1, waiting for transfers between devices, rows_of_block(): other_half = lax.ppermute(own_half, 'seq', [(0, 1), (1, 0)])  6.77 us
  transfers between devices with their start and end apart: 12, of which 8 were waited for; matrix products, arithmetic and copies ran while one was open for 24% of the time, Pallas kernels for 0%

profile of v12, /device:TPU:0, one launch (start us, length us, event | category | flops | bytes accessed | tf_op | source)
XLA Modules:
  0.0 161.7 jit_solution(974304499320655424)
XLA Ops:
  0.7 1.2 constant_dynamic-slice_fusion
  1.9 3.0 %collective-permute-start = (bf16[48,4096]{1,0:T(8,128)(2,1)S(1)}, bf16[48,4096]{1,0:T(8,128)(2,1)S(1)}, u32[]{:S(2)}, u32[]{:S(2)}) collective-permute-start(bf16[48,4096]{1,0:T(8,128)(2,1)S(1)} %get-tuple-element.17), channel_id=1, source_target_pairs={{0,2},{2,0},{1,3},{3,1},{4,6},{6,4},{5,7},{7,5},{8,10},{10,8},{9,1... | collective-permute-start | bytes 1179656 | tf_op jit(solution)/shard_map/ppermute | solution.py:79
  4.9 5.7 %abs_reduce_fusion = bf16[16,2048]{1,0:T(8,128)(2,1)S(1)} fusion(bf16[2048,2048]{1,0:T(8,128)(2,1)} %param.8), kind=kLoop, calls=%fused_computation.15 | loop fusion | flops 16744448 | bytes 8454144 | tf_op jit(solution)/shard_map/reduce_max | solution.py:20
  11.8 2.2 %collective-permute-done = bf16[48,4096]{1,0:T(8,128)(2,1)S(1)} collective-permute-done((bf16[48,4096]{1,0:T(8,128)(2,1)S(1)}, bf16[48,4096]{1,0:T(8,128)(2,1)S(1)}, u32[]{:S(2)}, u32[]{:S(2)}) %collective-permute-start) | collective-permute-done | bytes 393248 | tf_op jit(solution)/shard_map/ppermute | solution.py:79
  14.0 1.1 fusion.23
  15.1 5.1 %all-to-all-start = ((bf16[4,48,2048]{2,1,0:T(8,128)(2,1)}), bf16[4,48,2048]{2,1,0:T(8,128)(2,1)S(1)}, u32[]{:S(2)}, u32[]{:S(2)}) async-start(bf16[4,48,2048]{2,1,0:T(8,128)(2,1)} %fusion.23), calls=%async_computation | async-start | bytes 1572864 | tf_op jit(solution)/shard_map/all_to_all | solution.py:86
  20.3 8.8 %fusion.3 = bf16[2048,2048]{1,0:T(8,128)(2,1)} fusion(bf16[2048,2048]{1,0:T(8,128)(2,1)} %param.8, f32[16,2048]{1,0:T(8,128)S(1)} %divide_bitcast_fusion, f32[16,2048]{1,0:T(8,128)S(1)} %bitcast.85, f32[16,2048]{1,0:T(8,128)S(1)} %get-tuple-element.22), kind=kLoop, calls=%fused_computation.5 | loop fusion | flops 25165824 | bytes 17170432 | tf_op jit(solution)/shard_map/convert_element_type | solution.py:81
  29.1 10.4 %all-to-all-done = bf16[4,48,2048]{2,1,0:T(8,128)(2,1)S(1)} async-done(((bf16[4,48,2048]{2,1,0:T(8,128)(2,1)}), bf16[4,48,2048]{2,1,0:T(8,128)(2,1)S(1)}, u32[]{:S(2)}, u32[]{:S(2)}) %all-to-all-start) | async-done | bytes 786464 | tf_op jit(solution)/shard_map/all_to_all | solution.py:86
  39.5 1.5 collective-permute-start.1
  41.0 6.6 %fusion.31 = (f16[4,48,2048]{2,1,0:T(8,128)(2,1)}, f32[4,48,2048]{2,1,0:T(8,128)}) fusion(bf16[4,48,2048]{2,1,0:T(8,128)(2,1)S(1)} %all-to-all-done, bf16[2048,2048]{1,0:T(8,128)(2,1)} %fusion.3), kind=kOutput, calls=%fused_computation.79 | convolution fusion | flops 1611005952 | bytes 11534336 | tf_op jit(solution)/shard_map/dot_general | solution.py:123
  47.6 3.6 %all-to-all-start.1 = ((f16[4,48,2048]{2,1,0:T(8,128)(2,1)}), f16[4,48,2048]{2,1,0:T(8,128)(2,1)S(1)}, u32[]{:S(2)}, u32[]{:S(2)}) async-start(f16[4,48,2048]{2,1,0:T(8,128)(2,1)} %get-tuple-element.34), calls=%async_computation.1 | async-start | bytes 1572864 | tf_op jit(solution)/shard_map/all_to_all | solution.py:95
  51.2 6.8 %collective-permute-done.1 = bf16[4,48,2048]{2,1,0:T(8,128)(2,1)S(1)} collective-permute-done((bf16[4,48,2048]{2,1,0:T(8,128)(2,1)S(1)}, bf16[4,48,2048]{2,1,0:T(8,128)(2,1)S(1)}, u32[]{:S(2)}, u32[]{:S(2)}) %collective-permute-start.1) | collective-permute-done | bytes 786464 | tf_op jit(solution)/shard_map/ppermute | solution.py:88
  58.0 6.6 %fusion.30 = (f16[4,48,2048]{2,1,0:T(8,128)(2,1)}, f32[4,48,2048]{2,1,0:T(8,128)}) fusion(bf16[4,48,2048]{2,1,0:T(8,128)(2,1)S(1)} %collective-permute-done.1, bf16[2048,2048]{1,0:T(8,128)(2,1)} %fusion.3), kind=kOutput, calls=%fused_computation.78 | convolution fusion | flops 1611005952 | bytes 11534336 | tf_op jit(solution)/shard_map/dot_general | solution.py:123
  64.6 6.0 %all-to-all-done.1 = f16[4,48,2048]{2,1,0:T(8,128)(2,1)S(1)} async-done(((f16[4,48,2048]{2,1,0:T(8,128)(2,1)}), f16[4,48,2048]{2,1,0:T(8,128)(2,1)S(1)}, u32[]{:S(2)}, u32[]{:S(2)}) %all-to-all-start.1) | async-done | bytes 786464 | tf_op jit(solution)/shard_map/all_to_all | solution.py:95
  70.5 3.5 %all-to-all-start.2 = ((f16[4,48,2048]{2,1,0:T(8,128)(2,1)}), f16[4,48,2048]{2,1,0:T(8,128)(2,1)S(1)}, u32[]{:S(2)}, u32[]{:S(2)}) async-start(f16[4,48,2048]{2,1,0:T(8,128)(2,1)} %get-tuple-element.32), calls=%async_computation.2 | async-start | bytes 1572864 | tf_op jit(solution)/shard_map/all_to_all | solution.py:95
  74.0 1.4 slice_bitcast_fusion.1
  75.4 1.3 collective-permute-start.2
  76.7 1.4 slice_bitcast_fusion
  78.0 1.3 collective-permute-start.5
  79.3 1.0 broadcast_in_dim.44
  80.3 1.3 reshape.60
  81.6 12.0 %all-to-all-done.2 = f16[4,48,2048]{2,1,0:T(8,128)(2,1)S(1)} async-done(((f16[4,48,2048]{2,1,0:T(8,128)(2,1)}), f16[4,48,2048]{2,1,0:T(8,128)(2,1)S(1)}, u32[]{:S(2)}, u32[]{:S(2)}) %all-to-all-start.2) | async-done | bytes 786464 | tf_op jit(solution)/shard_map/all_to_all | solution.py:95
  94.1 1.0 fusion.25
  95.2 1.0 fusion.24
  96.2 1.3 collective-permute-start.3
  97.5 1.3 collective-permute-start.4
  98.9 1.7 %collective-permute-done.4 = bf16[6,2048]{1,0:T(8,128)(2,1)S(1)} collective-permute-done((bf16[6,2048]{1,0:T(8,128)(2,1)S(1)}, bf16[6,2048]{1,0:T(8,128)(2,1)S(1)}, u32[]{:S(2)}, u32[]{:S(2)}) %collective-permute-start.4) | collective-permute-done | bytes 24608 | tf_op jit(solution)/shard_map/ppermute | solution.py:13
  100.8 2.0 %convert_multiply_fusion = f32[102,2048]{1,0:T(8,128)S(1)} fusion(f32[108,2048]{1,0:T(8,128)S(1)} %maximum_convert_fusion, bf16[6,2048]{1,0:T(8,128)(2,1)} %collective-permute-done.2, bf16[96,2048]{1,0:T(8,128)(2,1)} %bitcast.86, bf16[6,2048]{1,0:T(8,128)(2,1)} %collective-permute-done.5, bf16[96,2048]{1,0:T(8,128)(2,1)} %bitcast.87, f32[2048]{0:T(1024)S(1)} %bitcast.92, ...), kind=kLoop, calls=%fused_computation.18 | loop fusion | flops 5222400 | bytes 7577600 | tf_op jit(solution)/shard_map/mul | solution.py:146
  103.4 1.3 broadcast_in_dim.48
  104.8 4.5 %all-to-all-start.3 = ((bf16[4,96,2048]{2,1,0:T(8,128)(2,1)}), bf16[4,96,2048]{2,1,0:T(8,128)(2,1)}, u32[]{:S(2)}, u32[]{:S(2)}) async-start(bf16[4,96,2048]{2,1,0:T(8,128)(2,1)} %broadcast_in_dim.48), calls=%async_computation.3 | async-start | bytes 3145728 | tf_op jit(solution)/shard_map/all_to_all | solution.py:153
  110.5 36.2 %all-to-all-done.3 = bf16[4,96,2048]{2,1,0:T(8,128)(2,1)} async-done(((bf16[4,96,2048]{2,1,0:T(8,128)(2,1)}), bf16[4,96,2048]{2,1,0:T(8,128)(2,1)}, u32[]{:S(2)}, u32[]{:S(2)}) %all-to-all-start.3) | async-done | bytes 1572896 | tf_op jit(solution)/shard_map/all_to_all | solution.py:153
  146.8 12.1 %multiply_reduce_fusion = (f32[16,2048]{1,0:T(8,128)S(1)}, f32[16,2048]{1,0:T(8,128)S(1)}) fusion(bf16[2048,2048]{1,0:T(8,128)(2,1)} %param.8, f32[16,2048]{1,0:T(8,128)} %get-tuple-element.20, f32[16,2048]{1,0:T(8,128)S(1)} %get-tuple-element.22, bf16[16,128,384]{2,1,0:T(8,128)(2,1)S(1)} %bitcast.83, bf16[384,2048,1]{1,0,2:T(8,128)(2,1)} %bitcast.30), kind=kOutput, calls=%fused_computation.6 | convolution fusion | flops 3275685888 | bytes 12058624 | tf_op jit(solution)/shard_map/dot_general | solution.py:154
  (34 shorter events, 6.6 us)
Async XLA Ops:
  0.6 10.4 %copy-start.1 = (f32[16,2048]{1,0:T(8,128)S(1)}, f32[16,2048]{1,0:T(8,128)}, u32[]{:S(2)}) copy-start(f32[16,2048]{1,0:T(8,128)} %param.10) | copy-start | bytes 393220
  0.6 10.4 %copy-start = (f32[16,2048]{1,0:T(8,128)S(1)}, f32[16,2048]{1,0:T(8,128)}, u32[]{:S(2)}) copy-start(f32[16,2048]{1,0:T(8,128)} %param.9) | copy-start | bytes 393220
  1.9 12.1 %collective-permute-start = (bf16[48,4096]{1,0:T(8,128)(2,1)S(1)}, bf16[48,4096]{1,0:T(8,128)(2,1)S(1)}, u32[]{:S(2)}, u32[]{:S(2)}) collective-permute-start(bf16[48,4096]{1,0:T(8,128)(2,1)S(1)} %get-tuple-element.17), channel_id=1, source_target_pairs={{0,2},{2,0},{1,3},{3,1},{4,6},{6,4},{5,7},{7,5},{8,10},{10,8},{9,1... | collective-permute-start | bytes 1179656 | tf_op jit(solution)/shard_map/ppermute | solution.py:79
  15.1 24.4 %all-to-all-start = ((bf16[4,48,2048]{2,1,0:T(8,128)(2,1)}), bf16[4,48,2048]{2,1,0:T(8,128)(2,1)S(1)}, u32[]{:S(2)}, u32[]{:S(2)}) async-start(bf16[4,48,2048]{2,1,0:T(8,128)(2,1)} %fusion.23), calls=%async_computation | async-start | bytes 1572864 | tf_op jit(solution)/shard_map/all_to_all | solution.py:86
  39.5 18.5 %collective-permute-start.1 = (bf16[4,48,2048]{2,1,0:T(8,128)(2,1)S(1)}, bf16[4,48,2048]{2,1,0:T(8,128)(2,1)S(1)}, u32[]{:S(2)}, u32[]{:S(2)}) collective-permute-start(bf16[4,48,2048]{2,1,0:T(8,128)(2,1)S(1)} %all-to-all-done), channel_id=1, source_target_pairs={{0,2},{2,0},{1,3},{3,1},{4,6},{6,4},{5,7},{7,5},{8,10},{10,8},{9,1... | collective-permute-start | bytes 2359304 | tf_op jit(solution)/shard_map/ppermute | solution.py:88
  47.6 31.8 %copy-start.3 = (f32[128,7]{0,1:T(8,128)S(1)}, f32[128,7]{0,1:T(8,128)}, u32[]{:S(2)}) copy-start(f32[128,7]{0,1:T(8,128)} %param.11) | copy-start | bytes 10756
  47.6 22.9 %all-to-all-start.1 = ((f16[4,48,2048]{2,1,0:T(8,128)(2,1)}), f16[4,48,2048]{2,1,0:T(8,128)(2,1)S(1)}, u32[]{:S(2)}, u32[]{:S(2)}) async-start(f16[4,48,2048]{2,1,0:T(8,128)(2,1)} %get-tuple-element.34), calls=%async_computation.1 | async-start | bytes 1572864 | tf_op jit(solution)/shard_map/all_to_all | solution.py:95
  70.5 23.1 %all-to-all-start.2 = ((f16[4,48,2048]{2,1,0:T(8,128)(2,1)}), f16[4,48,2048]{2,1,0:T(8,128)(2,1)S(1)}, u32[]{:S(2)}, u32[]{:S(2)}) async-start(f16[4,48,2048]{2,1,0:T(8,128)(2,1)} %get-tuple-element.32), calls=%async_computation.2 | async-start | bytes 1572864 | tf_op jit(solution)/shard_map/all_to_all | solution.py:95
  75.4 25.4 %collective-permute-start.2 = (bf16[6,2048]{1,0:T(8,128)(2,1)}, bf16[6,2048]{1,0:T(8,128)(2,1)}, u32[]{:S(2)}, u32[]{:S(2)}) collective-permute-start(bf16[6,2048]{1,0:T(8,128)(2,1)} %slice_bitcast_fusion.1), channel_id=1, source_target_pairs={{1,0},{3,2},{5,4},{7,6},{9,8},{11,10},{13,12},{15,14},{17,16},{19,... | collective-permute-start | bytes 73736 | tf_op jit(solution)/shard_map/ppermute | solution.py:13
  78.0 22.7 %collective-permute-start.5 = (bf16[6,2048]{1,0:T(8,128)(2,1)}, bf16[6,2048]{1,0:T(8,128)(2,1)}, u32[]{:S(2)}, u32[]{:S(2)}) collective-permute-start(bf16[6,2048]{1,0:T(8,128)(2,1)} %slice_bitcast_fusion), channel_id=1, source_target_pairs={{1,0},{3,2},{5,4},{7,6},{9,8},{11,10},{13,12},{15,14},{17,16},{19,... | collective-permute-start | bytes 73736 | tf_op jit(solution)/shard_map/ppermute | solution.py:13
  96.2 2.7 %collective-permute-start.3 = (bf16[6,2048]{1,0:T(8,128)(2,1)S(1)}, bf16[6,2048]{1,0:T(8,128)(2,1)S(1)}, u32[]{:S(2)}, u32[]{:S(2)}) collective-permute-start(bf16[6,2048]{1,0:T(8,128)(2,1)S(1)} %get-tuple-element.18), channel_id=1, source_target_pairs={{0,1},{2,3},{4,5},{6,7},{8,9},{10,11},{12,13},{14,15},{16,17},{18,... | collective-permute-start | bytes 73736 | tf_op jit(solution)/shard_map/ppermute | solution.py:13
  97.5 3.1 %collective-permute-start.4 = (bf16[6,2048]{1,0:T(8,128)(2,1)S(1)}, bf16[6,2048]{1,0:T(8,128)(2,1)S(1)}, u32[]{:S(2)}, u32[]{:S(2)}) collective-permute-start(bf16[6,2048]{1,0:T(8,128)(2,1)S(1)} %get-tuple-element.19), channel_id=1, source_target_pairs={{1,0},{3,2},{5,4},{7,6},{9,8},{11,10},{13,12},{15,14},{17,16},{19,... | collective-permute-start | bytes 73736 | tf_op jit(solution)/shard_map/ppermute | solution.py:13
  104.8 42.0 %all-to-all-start.3 = ((bf16[4,96,2048]{2,1,0:T(8,128)(2,1)}), bf16[4,96,2048]{2,1,0:T(8,128)(2,1)}, u32[]{:S(2)}, u32[]{:S(2)}) async-start(bf16[4,96,2048]{2,1,0:T(8,128)(2,1)} %broadcast_in_dim.48), calls=%async_computation.3 | async-start | bytes 3145728 | tf_op jit(solution)/shard_map/all_to_all | solution.py:153
  146.8 12.1 %copy-start.2 = (f32[16,2048]{1,0:T(8,128)S(1)}, f32[16,2048]{1,0:T(8,128)}, u32[]{:S(2)}) copy-start(f32[16,2048]{1,0:T(8,128)} %param.10) | copy-start | bytes 393220
  159.0 1.4 collective-permute-start.7
  159.1 2.0 %collective-permute-start.6 = (f32[16,2048]{1,0:T(8,128)S(1)}, f32[16,2048]{1,0:T(8,128)S(1)}, u32[]{:S(2)}, u32[]{:S(2)}) collective-permute-start(f32[16,2048]{1,0:T(8,128)S(1)} %get-tuple-element.24), channel_id=1, source_target_pairs={{0,1},{1,0},{2,3},{3,2},{4,5},{5,4},{6,7},{7,6},{8,9},{9,8},{10,11... | collective-permute-start | bytes 393224 | tf_op jit(solution)/shard_map/ppermute | solution.py:105

commit v13 on v11

--- a/solution.py
+++ b/solution.py
@@ -31,19 +31,22 @@
     return clipped.reshape(values.shape)
 
 
-def soft_clip_grads(values, upper_logit, lower_logit, d_clipped):
+def clip_factors(values, upper_logit, lower_logit):
     blocks, amax, center, radius = clip_bounds(values, upper_logit, lower_logit)
     z = (blocks - center) * (1.0 / radius)
     t = jnp.tanh(z)
     square = t * t
     slope = t - (1.0 - square) * z
-    grouped = d_clipped.reshape(blocks.shape)
-    toward_upper = jnp.sum(grouped * (square + slope), axis=1)
-    toward_lower = jnp.sum(grouped * (square - slope), axis=1)
     up = jax.nn.sigmoid(upper_logit)
     low = jax.nn.sigmoid(lower_logit)
-    grad_up = toward_upper * (0.5 * up * (1.0 - up) * amax)
-    grad_low = toward_lower * (-0.5 * low * (1.0 - low) * amax)
+    return square + slope, square - slope, 0.5 * up * (1.0 - up) * amax, -0.5 * low * (1.0 - low) * amax
+
+
+def soft_clip_grads(factors, d_clipped):
+    toward_upper, toward_lower, scale_upper, scale_lower = factors
+    grouped = d_clipped.reshape(toward_upper.shape)
+    grad_up = jnp.sum(grouped * toward_upper, axis=1) * scale_upper
+    grad_low = jnp.sum(grouped * toward_lower, axis=1) * scale_lower
     return grad_up, grad_low
 
 
@@ -144,10 +147,12 @@
 
     copies = jnp.broadcast_to(d_proj[None], (shards, length, columns))
     d_all = lax.all_to_all(copies, "fsdp", 0, 0).reshape(shards * length, columns)
+    factors = clip_factors(values, clip_upper, clip_lower)
+    d_all, factors = lax.optimization_barrier((d_all, factors))
     d_clipped = lax.dot_general(
         inputs, d_all, (((0,), (0,)), ((), ())), preferred_element_type=jnp.float32
     )
-    grad_up, grad_low = soft_clip_grads(values, clip_upper, clip_lower, d_clipped)
+    grad_up, grad_low = soft_clip_grads(factors, d_clipped)
     grad_upper, grad_lower = sum_over_ctx(grad_up), sum_over_ctx(grad_low)
     return (grad_upper, grad_lower)
 

time: 160 us -> 162 us (1.012)
  waiting for transfers between devices: 63.1 us -> 41.8 us
  other arithmetic: 18.8 us -> 34.5 us
  local copies, waits for them, and re-layouts: 9.27 us -> 15.7 us
  matrix products: 21.9 us -> 23.7 us
    all_to_all x1, waiting for transfers between devices: 36.2 us -> 16.8 us  [on_device(): lax.all_to_all(copies, 'fsdp', 0, 0).reshape(shards * length, columns)]
    sub x0 -> x1, other arithmetic: none -> 15.1 us  [clip_factors(): square - slope]
    dot_general x1, matrix products: 12.1 us -> 13.8 us  [on_device(): lax.dot_general(inputs, d_all, (((0,), (0,)), ((), ())), preferred_elemen...]
    dynamic_update_slice x2, local copies, waits for them, and re-layouts: 0.15 us -> 1.87 us  [on_device(): mine = lax.dynamic_update_slice_in_dim(mine, piece, at, 1)]
    dot_general x1, local copies, waits for them, and re-layouts: 0.87 us -> 2.57 us  [on_device(): lax.dot_general(inputs, d_all, (((0,), (0,)), ((), ())), preferred_elemen...]
  transfers between devices with their start and end apart: 11 -> 11, of which waited for: 6 -> 6; matrix products, arithmetic and copies ran while one was open for 20% -> 33% of each run, Pallas kernels for 0% -> 0%
where the time goes in v13:
time: 162 us; the launch traced here: 161 us
  waiting for transfers between devices  41.8 us (26%)
  other arithmetic  34.5 us (21%)
  blocking collectives  24.5 us (15%)
  matrix products  23.7 us (15%)
  starting transfers between devices  20.2 us (12%)
  local copies, waits for them, and re-layouts  15.7 us (10%)
    all_to_all x1, blocking collectives, rows_of_block(): own_half = lax.all_to_all(pieces, 'fsdp', 0, 0)  24.5 us
    all_to_all x1, waiting for transfers between devices, on_device(): lax.all_to_all(copies, 'fsdp', 0, 0).reshape(shards * length, columns)  16.8 us
    sub x1, other arithmetic, clip_factors(): square - slope  15.1 us
    dot_general x1, matrix products, on_device(): lax.dot_general(inputs, d_all, (((0,), (0,)), ((), ())), preferred_elemen...  13.8 us
    all_to_all x2, waiting for transfers between devices, reduce_partial(): lax.all_to_all(partial.astype(jnp.float16), 'fsdp', 0, 0)  13.1 us
    ppermute x1, waiting for transfers between devices, rows_of_block(): other_half = lax.ppermute(own_half, 'seq', [(0, 1), (1, 0)])  10.6 us
    dot_general x2, matrix products, on_device(): jnp.dot(flat, quant, preferred_element_type=jnp.float32)  9.9 us
    all_to_all x2, starting transfers between devices, reduce_partial(): lax.all_to_all(partial.astype(jnp.float16), 'fsdp', 0, 0)  7.12 us
  transfers between devices with their start and end apart: 11, of which 6 were waited for; matrix products, arithmetic and copies ran while one was open for 33% of the time, Pallas kernels for 0%

profile of v13, /device:TPU:0, one launch (start us, length us, event | category | flops | bytes accessed | tf_op | source)
XLA Modules:
  0.0 161.3 jit_solution(567795244479927281)
XLA Ops:
  0.7 1.2 constant_dynamic-slice_fusion
  1.9 3.0 %collective-permute-start = (bf16[48,4096]{1,0:T(8,128)(2,1)S(1)}, bf16[48,4096]{1,0:T(8,128)(2,1)S(1)}, u32[]{:S(2)}, u32[]{:S(2)}) collective-permute-start(bf16[48,4096]{1,0:T(8,128)(2,1)S(1)} %get-tuple-element.25), channel_id=1, source_target_pairs={{0,2},{2,0},{1,3},{3,1},{4,6},{6,4},{5,7},{7,5},{8,10},{10,8},{9,1... | collective-permute-start | bytes 1179656 | tf_op jit(solution)/shard_map/ppermute | solution.py:77
  4.9 5.7 %abs_reduce_fusion = bf16[16,2048]{1,0:T(8,128)(2,1)S(1)} fusion(bf16[2048,2048]{1,0:T(8,128)(2,1)} %param.8), kind=kLoop, calls=%fused_computation.17 | loop fusion | flops 16744448 | bytes 8454144 | tf_op jit(solution)/shard_map/reduce_max | solution.py:20
  11.8 6.0 %fusion.3 = bf16[2048,2048]{1,0:T(8,128)(2,1)S(1)} fusion(f32[16,2048]{1,0:T(8,128)S(1)} %get-tuple-element.20, f32[16,2048]{1,0:T(8,128)S(1)} %get-tuple-element.21, f32[16,2048]{1,0:T(8,128)S(1)} %get-tuple-element.28, bf16[2048,2048]{1,0:T(8,128)(2,1)} %param.8), kind=kLoop, calls=%fused_computation.5 | loop fusion | flops 25165824 | bytes 17170432 | tf_op jit(solution)/shard_map/convert_element_type | solution.py:111
  18.0 24.5 %all_to_all.20 = bf16[4,48,2048]{2,1,0:T(8,128)(2,1)S(1)} all-to-all(bf16[4,48,2048]{2,1,0:T(8,128)(2,1)S(1)} %fusion.27), channel_id=1, replica_groups=mesh['parts'=2,'fsdp'=4,'seq'=2,'ctx'=2] {'fsdp'}, dimensions={0} | all-to-all | bytes 1572864 | tf_op jit(solution)/shard_map/all_to_all | solution.py:83
  43.1 3.3 %fusion.34 = (f16[4,48,2048]{2,1,0:T(8,128)(2,1)}, f32[4,48,2048]{2,1,0:T(8,128)}) fusion(bf16[4,48,2048]{2,1,0:T(8,128)(2,1)S(1)} %all_to_all.20, bf16[2048,2048]{1,0:T(8,128)(2,1)S(1)} %fusion.3), kind=kOutput, calls=%fused_computation.81 | convolution fusion | flops 1611005952 | bytes 11534336 | tf_op jit(solution)/shard_map/dot_general | solution.py:119
  46.4 3.6 %all-to-all-start.1 = ((f16[4,48,2048]{2,1,0:T(8,128)(2,1)}), f16[4,48,2048]{2,1,0:T(8,128)(2,1)S(1)}, u32[]{:S(2)}, u32[]{:S(2)}) async-start(f16[4,48,2048]{2,1,0:T(8,128)(2,1)} %get-tuple-element.40), calls=%async_computation.1 | async-start | bytes 1572864 | tf_op jit(solution)/shard_map/all_to_all | solution.py:91
  50.0 10.6 %collective-permute-done.1 = bf16[4,48,2048]{2,1,0:T(8,128)(2,1)S(1)} collective-permute-done((bf16[4,48,2048]{2,1,0:T(8,128)(2,1)S(1)}, bf16[4,48,2048]{2,1,0:T(8,128)(2,1)S(1)}, u32[]{:S(2)}, u32[]{:S(2)}) %collective-permute-start.1) | collective-permute-done | bytes 786464 | tf_op jit(solution)/shard_map/ppermute | solution.py:84
  60.6 6.6 %fusion.33 = (f16[4,48,2048]{2,1,0:T(8,128)(2,1)}, f32[4,48,2048]{2,1,0:T(8,128)}) fusion(bf16[4,48,2048]{2,1,0:T(8,128)(2,1)S(1)} %collective-permute-done.1, bf16[2048,2048]{1,0:T(8,128)(2,1)} %copy-done), kind=kOutput, calls=%fused_computation.80 | convolution fusion | flops 1611005952 | bytes 11534336 | tf_op jit(solution)/shard_map/dot_general | solution.py:119
  67.2 1.7 %all-to-all-done.1 = f16[4,48,2048]{2,1,0:T(8,128)(2,1)S(1)} async-done(((f16[4,48,2048]{2,1,0:T(8,128)(2,1)}), f16[4,48,2048]{2,1,0:T(8,128)(2,1)S(1)}, u32[]{:S(2)}, u32[]{:S(2)}) %all-to-all-start.1) | async-done | bytes 786464 | tf_op jit(solution)/shard_map/all_to_all | solution.py:91
  68.9 3.5 %all-to-all-start.2 = ((f16[4,48,2048]{2,1,0:T(8,128)(2,1)}), f16[4,48,2048]{2,1,0:T(8,128)(2,1)S(1)}, u32[]{:S(2)}, u32[]{:S(2)}) async-start(f16[4,48,2048]{2,1,0:T(8,128)(2,1)} %get-tuple-element.38), calls=%async_computation.2 | async-start | bytes 1572864 | tf_op jit(solution)/shard_map/all_to_all | solution.py:91
  72.4 1.4 slice_bitcast_fusion
  73.8 1.3 collective-permute-start.5
  75.0 1.4 slice_bitcast_fusion.1
  76.4 1.3 collective-permute-start.2
  77.7 1.0 broadcast_in_dim.38
  78.7 1.9 %reshape.61 = f32[2048,7]{0,1:T(8,128)} reshape(f32[128,16,7]{1,0,2:T(8,128)} %broadcast_in_dim.38) | data formatting | bytes 114688 | tf_op jit(solution)/shard_map/reshape | solution.py:125
  80.6 11.4 %all-to-all-done.2 = f16[4,48,2048]{2,1,0:T(8,128)(2,1)S(1)} async-done(((f16[4,48,2048]{2,1,0:T(8,128)(2,1)}), f16[4,48,2048]{2,1,0:T(8,128)(2,1)S(1)}, u32[]{:S(2)}, u32[]{:S(2)}) %all-to-all-start.2) | async-done | bytes 786464 | tf_op jit(solution)/shard_map/all_to_all | solution.py:91
  92.5 1.0 fusion.29
  93.5 1.0 fusion.28
  94.6 1.3 collective-permute-start.3
  95.9 1.3 collective-permute-start.4
  97.2 1.2 fusion.32
  99.2 2.0 %convert_multiply_fusion = f32[102,2048]{1,0:T(8,128)S(1)} fusion(f32[108,2048]{1,0:T(8,128)S(1)} %maximum_convert_fusion, bf16[6,2048]{1,0:T(8,128)(2,1)} %collective-permute-done.2, bf16[96,2048]{1,0:T(8,128)(2,1)} %bitcast.80, bf16[6,2048]{1,0:T(8,128)(2,1)} %collective-permute-done.5, bf16[96,2048]{1,0:T(8,128)(2,1)} %bitcast.81, f32[2048]{0:T(1024)S(1)} %bitcast.86, ...), kind=kLoop, calls=%fused_computation.22 | loop fusion | flops 5222400 | bytes 7577600 | tf_op jit(solution)/shard_map/mul | solution.py:142
  101.8 1.3 broadcast_in_dim.42
  103.2 3.7 %all-to-all-start.3 = ((bf16[4,96,2048]{2,1,0:T(8,128)(2,1)}), bf16[4,96,2048]{2,1,0:T(8,128)(2,1)S(1)}, u32[]{:S(2)}, u32[]{:S(2)}) async-start(bf16[4,96,2048]{2,1,0:T(8,128)(2,1)} %broadcast_in_dim.42), calls=%async_computation.3 | async-start | bytes 3145728 | tf_op jit(solution)/shard_map/all_to_all | solution.py:149
  106.9 15.1 %fusion.4 = (f32[16,128,2048]{2,1,0:T(8,128)}, f32[16,128,2048]{2,1,0:T(8,128)}) fusion(f32[16,2048]{1,0:T(8,128)S(1)} %get-tuple-element.20, f32[16,2048]{1,0:T(8,128)S(1)} %get-tuple-element.28, bf16[2048,2048]{1,0:T(8,128)(2,1)} %param.8), kind=kLoop, calls=%fused_computation.11 | loop fusion | flops 37748736 | bytes 42205184 | tf_op jit(solution)/shard_map/sub | solution.py:42
  122.0 1.4 broadcast_in_dim.37
  123.4 1.0 constant_dynamic-update-slice_fusion.1
  125.3 2.6 %copy.20 = bf16[2048,384]{1,0:T(8,128)(2,1)} copy(bf16[2048,384]{0,1:T(8,128)(2,1)} %bitcast.7) | data formatting | bytes 3145728 | tf_op jit(solution)/shard_map/dot_general | solution.py:152
  127.8 16.8 %all-to-all-done.3 = bf16[4,96,2048]{2,1,0:T(8,128)(2,1)S(1)} async-done(((bf16[4,96,2048]{2,1,0:T(8,128)(2,1)}), bf16[4,96,2048]{2,1,0:T(8,128)(2,1)S(1)}, u32[]{:S(2)}, u32[]{:S(2)}) %all-to-all-start.3) | async-done | bytes 1572896 | tf_op jit(solution)/shard_map/all_to_all | solution.py:149
  144.7 13.8 %multiply_reduce_fusion = (f32[16,2048]{1,0:T(8,128)S(1)}, f32[16,2048]{1,0:T(8,128)S(1)}) fusion(f32[16,128,2048]{2,1,0:T(8,128)} %get-tuple-element.14, f32[16,128,2048]{2,1,0:T(8,128)} %get-tuple-element.12, bf16[16,128,384]{2,1,0:T(8,128)(2,1)} %bitcast.78, bf16[384,2048]{1,0:T(8,128)(2,1)S(1)} %bitcast.77), kind=kOutput, calls=%fused_computation.6 | convolution fusion | flops 3237937152 | bytes 36962304 | tf_op jit(solution)/shard_map/dot_general | solution.py:152
  (36 shorter events, 7.5 us)
Async XLA Ops:
  0.6 10.4 %copy-start.2 = (f32[16,2048]{1,0:T(8,128)S(1)}, f32[16,2048]{1,0:T(8,128)}, u32[]{:S(2)}) copy-start(f32[16,2048]{1,0:T(8,128)} %param.10) | copy-start | bytes 393220
  0.6 10.4 %copy-start.3 = (f32[16,2048]{1,0:T(8,128)S(1)}, f32[16,2048]{1,0:T(8,128)}, u32[]{:S(2)}) copy-start(f32[16,2048]{1,0:T(8,128)} %param.9) | copy-start | bytes 393220
  1.9 16.0 %collective-permute-start = (bf16[48,4096]{1,0:T(8,128)(2,1)S(1)}, bf16[48,4096]{1,0:T(8,128)(2,1)S(1)}, u32[]{:S(2)}, u32[]{:S(2)}) collective-permute-start(bf16[48,4096]{1,0:T(8,128)(2,1)S(1)} %get-tuple-element.25), channel_id=1, source_target_pairs={{0,2},{2,0},{1,3},{3,1},{4,6},{6,4},{5,7},{7,5},{8,10},{10,8},{9,1... | collective-permute-start | bytes 1179656 | tf_op jit(solution)/shard_map/ppermute | solution.py:77
  17.9 25.2 %copy-start = (bf16[2048,2048]{1,0:T(8,128)(2,1)}, bf16[2048,2048]{1,0:T(8,128)(2,1)S(1)}, u32[]{:S(2)}) copy-start(bf16[2048,2048]{1,0:T(8,128)(2,1)S(1)} %fusion.3) | copy-start | bytes 25165828
  42.5 18.1 %collective-permute-start.1 = (bf16[4,48,2048]{2,1,0:T(8,128)(2,1)S(1)}, bf16[4,48,2048]{2,1,0:T(8,128)(2,1)S(1)}, u32[]{:S(2)}, u32[]{:S(2)}) collective-permute-start(bf16[4,48,2048]{2,1,0:T(8,128)(2,1)S(1)} %all_to_all.20), channel_id=1, source_target_pairs={{0,2},{2,0},{1,3},{3,1},{4,6},{6,4},{5,7},{7,5},{8,10},{10,8},{9,1... | collective-permute-start | bytes 2359304 | tf_op jit(solution)/shard_map/ppermute | solution.py:84
  46.4 31.3 %copy-start.4 = (f32[128,7]{0,1:T(8,128)S(1)}, f32[128,7]{0,1:T(8,128)}, u32[]{:S(2)}) copy-start(f32[128,7]{0,1:T(8,128)} %param.11) | copy-start | bytes 10756
  46.4 22.5 %all-to-all-start.1 = ((f16[4,48,2048]{2,1,0:T(8,128)(2,1)}), f16[4,48,2048]{2,1,0:T(8,128)(2,1)S(1)}, u32[]{:S(2)}, u32[]{:S(2)}) async-start(f16[4,48,2048]{2,1,0:T(8,128)(2,1)} %get-tuple-element.40), calls=%async_computation.1 | async-start | bytes 1572864 | tf_op jit(solution)/shard_map/all_to_all | solution.py:91
  68.9 23.1 %all-to-all-start.2 = ((f16[4,48,2048]{2,1,0:T(8,128)(2,1)}), f16[4,48,2048]{2,1,0:T(8,128)(2,1)S(1)}, u32[]{:S(2)}, u32[]{:S(2)}) async-start(f16[4,48,2048]{2,1,0:T(8,128)(2,1)} %get-tuple-element.38), calls=%async_computation.2 | async-start | bytes 1572864 | tf_op jit(solution)/shard_map/all_to_all | solution.py:91
  73.8 25.4 %collective-permute-start.5 = (bf16[6,2048]{1,0:T(8,128)(2,1)}, bf16[6,2048]{1,0:T(8,128)(2,1)}, u32[]{:S(2)}, u32[]{:S(2)}) collective-permute-start(bf16[6,2048]{1,0:T(8,128)(2,1)} %slice_bitcast_fusion), channel_id=1, source_target_pairs={{1,0},{3,2},{5,4},{7,6},{9,8},{11,10},{13,12},{15,14},{17,16},{19,... | collective-permute-start | bytes 73736 | tf_op jit(solution)/shard_map/ppermute | solution.py:13
  76.4 22.7 %collective-permute-start.2 = (bf16[6,2048]{1,0:T(8,128)(2,1)}, bf16[6,2048]{1,0:T(8,128)(2,1)}, u32[]{:S(2)}, u32[]{:S(2)}) collective-permute-start(bf16[6,2048]{1,0:T(8,128)(2,1)} %slice_bitcast_fusion.1), channel_id=1, source_target_pairs={{1,0},{3,2},{5,4},{7,6},{9,8},{11,10},{13,12},{15,14},{17,16},{19,... | collective-permute-start | bytes 73736 | tf_op jit(solution)/shard_map/ppermute | solution.py:13
  94.6 3.8 %collective-permute-start.3 = (bf16[6,2048]{1,0:T(8,128)(2,1)S(1)}, bf16[6,2048]{1,0:T(8,128)(2,1)S(1)}, u32[]{:S(2)}, u32[]{:S(2)}) collective-permute-start(bf16[6,2048]{1,0:T(8,128)(2,1)S(1)} %get-tuple-element.26), channel_id=1, source_target_pairs={{0,1},{2,3},{4,5},{6,7},{8,9},{10,11},{12,13},{14,15},{16,17},{18,... | collective-permute-start | bytes 73736 | tf_op jit(solution)/shard_map/ppermute | solution.py:13
  95.9 3.1 %collective-permute-start.4 = (bf16[6,2048]{1,0:T(8,128)(2,1)S(1)}, bf16[6,2048]{1,0:T(8,128)(2,1)S(1)}, u32[]{:S(2)}, u32[]{:S(2)}) collective-permute-start(bf16[6,2048]{1,0:T(8,128)(2,1)S(1)} %get-tuple-element.27), channel_id=1, source_target_pairs={{1,0},{3,2},{5,4},{7,6},{9,8},{11,10},{13,12},{15,14},{17,16},{19,... | collective-permute-start | bytes 73736 | tf_op jit(solution)/shard_map/ppermute | solution.py:13
  103.2 41.5 %all-to-all-start.3 = ((bf16[4,96,2048]{2,1,0:T(8,128)(2,1)}), bf16[4,96,2048]{2,1,0:T(8,128)(2,1)S(1)}, u32[]{:S(2)}, u32[]{:S(2)}) async-start(bf16[4,96,2048]{2,1,0:T(8,128)(2,1)} %broadcast_in_dim.42), calls=%async_computation.3 | async-start | bytes 3145728 | tf_op jit(solution)/shard_map/all_to_all | solution.py:149
  144.7 13.9 %copy-start.1 = (f32[16,2048]{1,0:T(8,128)S(1)}, f32[16,2048]{1,0:T(8,128)}, u32[]{:S(2)}) copy-start(f32[16,2048]{1,0:T(8,128)} %get-tuple-element.13) | copy-start | bytes 393220
  158.6 1.4 collective-permute-start.6
  158.7 2.0 %collective-permute-start.7 = (f32[16,2048]{1,0:T(8,128)S(1)}, f32[16,2048]{1,0:T(8,128)S(1)}, u32[]{:S(2)}, u32[]{:S(2)}) collective-permute-start(f32[16,2048]{1,0:T(8,128)S(1)} %mul.283), channel_id=1, source_target_pairs={{0,1},{1,0},{2,3},{3,2},{4,5},{5,4},{6,7},{7,6},{8,9},{9,8},{10,11... | collective-permute-start | bytes 393224 | tf_op jit(solution)/shard_map/ppermute | solution.py:101

commit v14 on v11

--- a/solution.py
+++ b/solution.py
@@ -91,6 +91,17 @@
     return own + jnp.sum(others, axis=0)
 
 
+def ring_gather(value, axis):
+    devices = lax.axis_size(axis)
+    me = lax.axis_index(axis)
+    gathered = jnp.zeros((devices,) + value.shape, value.dtype)
+    gathered = lax.dynamic_update_index_in_dim(gathered, value, me, 0)
+    for shift in range(1, devices):
+        block = lax.ppermute(value, axis, [(i, (i + shift) % devices) for i in range(devices)])
+        gathered = lax.dynamic_update_index_in_dim(gathered, block, (me + devices - shift) % devices, 0)
+    return gathered
+
+
 def sum_over_ctx(value):
     devices = lax.axis_size("ctx")
     if devices != 2:
@@ -142,8 +153,7 @@
         d_proj = d_proj + taps[tap] * d_conv[tap : tap + length]
     d_proj = d_proj.astype(jnp.bfloat16)
 
-    copies = jnp.broadcast_to(d_proj[None], (shards, length, columns))
-    d_all = lax.all_to_all(copies, "fsdp", 0, 0).reshape(shards * length, columns)
+    d_all = ring_gather(d_proj, "fsdp").reshape(shards * length, columns)
     d_clipped = lax.dot_general(
         inputs, d_all, (((0,), (0,)), ((), ())), preferred_element_type=jnp.float32
     )

time: 160 us -> 155 us (0.969)
  the two profiles are of different devices: /device:TPU:0 before, /device:TPU:9 now
where the time goes in v14:
time: 155 us; the launch traced here: 154 us
  waiting for transfers between devices  46.5 us (30%)
  starting transfers between devices  32 us (21%)
  matrix products  21.9 us (14%)
  blocking collectives  21.8 us (14%)
  other arithmetic  19.5 us (13%)
  local copies, waits for them, and re-layouts  11.4 us (7%)
    ppermute x3, waiting for transfers between devices, ring_gather(): lax.ppermute(value, axis, [(i, (i + shift) % devices) for i in range(devi...  31.3 us
    all_to_all x1, blocking collectives, rows_of_block(): own_half = lax.all_to_all(pieces, 'fsdp', 0, 0)  21.8 us
    all_to_all x2, starting transfers between devices, reduce_partial(): lax.all_to_all(partial.astype(jnp.float16), 'fsdp', 0, 0)  13 us
    dot_general x1, matrix products, on_device(): lax.dot_general(inputs, d_all, (((0,), (0,)), ((), ())), preferred_elemen...  12 us
    ppermute x4, starting transfers between devices, from_behind(): return lax.ppermute(value, axis, pairs)  11.7 us
    dot_general x2, matrix products, on_device(): jnp.dot(flat, quant, preferred_element_type=jnp.float32)  9.88 us
    ppermute x1, waiting for transfers between devices, rows_of_block(): other_half = lax.ppermute(own_half, 'seq', [(0, 1), (1, 0)])  7.74 us
    convert_element_type x1, other arithmetic, on_device(): quant = soft_clip(values, clip_upper, clip_lower).astype(jnp.bfloat16)  6.03 us
  transfers between devices with their start and end apart: 13, of which 8 were waited for; matrix products, arithmetic and copies ran while one was open for 22% of the time, Pallas kernels for 0%

profile of v14, /device:TPU:9, one launch (start us, length us, event | category | flops | bytes accessed | tf_op | source)
XLA Modules:
  0.0 154.2 jit_solution(8128559062966863991)
XLA Ops:
  0.7 1.2 constant_dynamic-slice_fusion
  1.9 1.3 collective-permute-start
  3.2 5.7 %abs_reduce_fusion = bf16[16,2048]{1,0:T(8,128)(2,1)S(1)} fusion(bf16[2048,2048]{1,0:T(8,128)(2,1)} %param.8), kind=kLoop, calls=%fused_computation.15 | loop fusion | flops 16744448 | bytes 8454144 | tf_op jit(solution)/shard_map/reduce_max | solution.py:20
  9.4 6.0 %fusion.3 = bf16[2048,2048]{1,0:T(8,128)(2,1)S(1)} fusion(bf16[2048,2048]{1,0:T(8,128)(2,1)} %param.8, f32[16,2048]{1,0:T(8,128)S(1)} %get-tuple-element.12, f32[16,2048]{1,0:T(8,128)S(1)} %get-tuple-element.13, f32[16,2048]{1,0:T(8,128)S(1)} %get-tuple-element.18), kind=kLoop, calls=%fused_computation.5 | loop fusion | flops 25165824 | bytes 17170432 | tf_op jit(solution)/shard_map/convert_element_type | solution.py:119
  15.6 21.8 %all_to_all.15 = bf16[4,48,2048]{2,1,0:T(8,128)(2,1)S(1)} all-to-all(bf16[4,48,2048]{2,1,0:T(8,128)(2,1)S(1)} %fusion.23), channel_id=1, replica_groups=mesh['parts'=2,'fsdp'=4,'seq'=2,'ctx'=2] {'fsdp'}, dimensions={0} | all-to-all | bytes 1572864 | tf_op jit(solution)/shard_map/all_to_all | solution.py:80
  37.7 3.3 %fusion.31 = (f16[4,48,2048]{2,1,0:T(8,128)(2,1)}, f32[4,48,2048]{2,1,0:T(8,128)}) fusion(bf16[4,48,2048]{2,1,0:T(8,128)(2,1)S(1)} %all_to_all.15, bf16[2048,2048]{1,0:T(8,128)(2,1)S(1)} %fusion.3), kind=kOutput, calls=%fused_computation.81 | convolution fusion | flops 1611005952 | bytes 11534336 | tf_op jit(solution)/shard_map/dot_general | solution.py:127
  41.1 5.5 %all-to-all-start.1 = ((f16[4,48,2048]{2,1,0:T(8,128)(2,1)}), f16[4,48,2048]{2,1,0:T(8,128)(2,1)S(1)}, u32[]{:S(2)}, u32[]{:S(2)}) async-start(f16[4,48,2048]{2,1,0:T(8,128)(2,1)} %get-tuple-element.30), calls=%async_computation.1 | async-start | bytes 1572864 | tf_op jit(solution)/shard_map/all_to_all | solution.py:88
  46.5 7.7 %collective-permute-done.1 = bf16[4,48,2048]{2,1,0:T(8,128)(2,1)S(1)} collective-permute-done((bf16[4,48,2048]{2,1,0:T(8,128)(2,1)S(1)}, bf16[4,48,2048]{2,1,0:T(8,128)(2,1)S(1)}, u32[]{:S(2)}, u32[]{:S(2)}) %collective-permute-start.1) | collective-permute-done | bytes 786464 | tf_op jit(solution)/shard_map/ppermute | solution.py:81
  54.3 6.6 %fusion.30 = (f16[4,48,2048]{2,1,0:T(8,128)(2,1)}, f32[4,48,2048]{2,1,0:T(8,128)}) fusion(bf16[4,48,2048]{2,1,0:T(8,128)(2,1)S(1)} %collective-permute-done.1, bf16[2048,2048]{1,0:T(8,128)(2,1)} %copy-done), kind=kOutput, calls=%fused_computation.80 | convolution fusion | flops 1611005952 | bytes 11534336 | tf_op jit(solution)/shard_map/dot_general | solution.py:127
  60.8 1.2 all-to-all-done.1
  62.1 7.5 %all-to-all-start.2 = ((f16[4,48,2048]{2,1,0:T(8,128)(2,1)}), f16[4,48,2048]{2,1,0:T(8,128)(2,1)S(1)}, u32[]{:S(2)}, u32[]{:S(2)}) async-start(f16[4,48,2048]{2,1,0:T(8,128)(2,1)} %get-tuple-element.28), calls=%async_computation.2 | async-start | bytes 1572864 | tf_op jit(solution)/shard_map/all_to_all | solution.py:88
  69.6 1.4 slice_bitcast_fusion.1
  71.0 4.2 %collective-permute-start.2 = (bf16[6,2048]{1,0:T(8,128)(2,1)}, bf16[6,2048]{1,0:T(8,128)(2,1)}, u32[]{:S(2)}, u32[]{:S(2)}) collective-permute-start(bf16[6,2048]{1,0:T(8,128)(2,1)} %slice_bitcast_fusion.1), channel_id=1, source_target_pairs={{1,0},{3,2},{5,4},{7,6},{9,8},{11,10},{13,12},{15,14},{17,16},{19,... | collective-permute-start | bytes 73736 | tf_op jit(solution)/shard_map/ppermute | solution.py:13
  75.2 1.4 slice_bitcast_fusion
  76.6 1.9 %collective-permute-start.5 = (bf16[6,2048]{1,0:T(8,128)(2,1)}, bf16[6,2048]{1,0:T(8,128)(2,1)}, u32[]{:S(2)}, u32[]{:S(2)}) collective-permute-start(bf16[6,2048]{1,0:T(8,128)(2,1)} %slice_bitcast_fusion), channel_id=1, source_target_pairs={{1,0},{3,2},{5,4},{7,6},{9,8},{11,10},{13,12},{15,14},{17,16},{19,... | collective-permute-start | bytes 73736 | tf_op jit(solution)/shard_map/ppermute | solution.py:13
  78.5 1.0 broadcast_in_dim.41
  79.4 1.3 reshape.60
  80.7 4.6 %all-to-all-done.2 = f16[4,48,2048]{2,1,0:T(8,128)(2,1)S(1)} async-done(((f16[4,48,2048]{2,1,0:T(8,128)(2,1)}), f16[4,48,2048]{2,1,0:T(8,128)(2,1)S(1)}, u32[]{:S(2)}, u32[]{:S(2)}) %all-to-all-start.2) | async-done | bytes 786464 | tf_op jit(solution)/shard_map/all_to_all | solution.py:88
  85.8 1.0 fusion.25
  86.9 1.0 fusion.24
  87.9 1.3 collective-permute-start.3
  89.2 4.3 %collective-permute-start.4 = (bf16[6,2048]{1,0:T(8,128)(2,1)S(1)}, bf16[6,2048]{1,0:T(8,128)(2,1)S(1)}, u32[]{:S(2)}, u32[]{:S(2)}) collective-permute-start(bf16[6,2048]{1,0:T(8,128)(2,1)S(1)} %get-tuple-element.17), channel_id=1, source_target_pairs={{1,0},{3,2},{5,4},{7,6},{9,8},{11,10},{13,12},{15,14},{17,16},{19,... | collective-permute-start | bytes 73736 | tf_op jit(solution)/shard_map/ppermute | solution.py:13
  94.5 2.0 %convert_multiply_fusion = f32[102,2048]{1,0:T(8,128)S(1)} fusion(f32[108,2048]{1,0:T(8,128)S(1)} %maximum_convert_fusion, bf16[6,2048]{1,0:T(8,128)(2,1)} %collective-permute-done.2, bf16[96,2048]{1,0:T(8,128)(2,1)} %bitcast.87, bf16[6,2048]{1,0:T(8,128)(2,1)} %collective-permute-done.5, bf16[96,2048]{1,0:T(8,128)(2,1)} %bitcast.88, f32[2048]{0:T(1024)S(1)} %bitcast.93, ...), kind=kLoop, calls=%fused_computation.18 | loop fusion | flops 5222400 | bytes 7577600 | tf_op jit(solution)/shard_map/mul | solution.py:150
  96.7 1.4 bitcast_dynamic-update-slice_fusion.3
  98.1 1.2 collective-permute-start.6
  100.6 4.0 %collective-permute-start.7 = (bf16[96,2048]{1,0:T(8,128)(2,1)}, bf16[96,2048]{1,0:T(8,128)(2,1)S(1)}, u32[]{:S(2)}, u32[]{:S(2)}) collective-permute-start(bf16[96,2048]{1,0:T(8,128)(2,1)} %get-tuple-element.11), channel_id=1, source_target_pairs={{0,8},{4,12},{8,0},{12,4},{1,9},{5,13},{9,1},{13,5},{2,10},{6,14},... | collective-permute-start | bytes 1179656 | tf_op jit(solution)/shard_map/ppermute | solution.py:100
  104.5 6.1 %collective-permute-done.6 = bf16[96,2048]{1,0:T(8,128)(2,1)} collective-permute-done((bf16[96,2048]{1,0:T(8,128)(2,1)}, bf16[96,2048]{1,0:T(8,128)(2,1)}, u32[]{:S(2)}, u32[]{:S(2)}) %collective-permute-start.6) | collective-permute-done | bytes 393248 | tf_op jit(solution)/shard_map/ppermute | solution.py:100
  110.7 1.8 %bitcast_dynamic-update-slice_fusion.2 = bf16[4,96,2048]{2,1,0:T(8,128)(2,1)} fusion(bf16[4,96,2048]{2,1,0:T(8,128)(2,1)} %copy-done.1, s32[]{:T(128)S(6)} %select_n.72, bf16[96,2048]{1,0:T(8,128)(2,1)} %collective-permute-done.6), kind=kLoop, calls=%fused_computation.55 | loop fusion | bytes 786436 | tf_op jit(solution)/shard_map/jit(dynamic_update_index_in_dim)/dynamic_update_slice | solution.py:101
  112.4 20.6 %collective-permute-done.7 = bf16[96,2048]{1,0:T(8,128)(2,1)S(1)} collective-permute-done((bf16[96,2048]{1,0:T(8,128)(2,1)}, bf16[96,2048]{1,0:T(8,128)(2,1)S(1)}, u32[]{:S(2)}, u32[]{:S(2)}) %collective-permute-start.7) | collective-permute-done | bytes 393248 | tf_op jit(solution)/shard_map/ppermute | solution.py:100
  133.8 4.5 %collective-permute-done.8 = bf16[96,2048]{1,0:T(8,128)(2,1)S(1)} collective-permute-done((bf16[96,2048]{1,0:T(8,128)(2,1)}, bf16[96,2048]{1,0:T(8,128)(2,1)S(1)}, u32[]{:S(2)}, u32[]{:S(2)}) %collective-permute-start.8) | collective-permute-done | bytes 393248 | tf_op jit(solution)/shard_map/ppermute | solution.py:100
  139.1 12.0 %multiply_reduce_fusion = (f32[16,2048]{1,0:T(8,128)S(1)}, f32[16,2048]{1,0:T(8,128)S(1)}) fusion(bf16[2048,2048]{1,0:T(8,128)(2,1)} %param.8, f32[16,2048]{1,0:T(8,128)S(1)} %get-tuple-element.12, f32[16,2048]{1,0:T(8,128)S(1)} %get-tuple-element.18, bf16[16,128,384]{2,1,0:T(8,128)(2,1)S(1)} %bitcast.84, bf16[384,2048,1]{1,0,2:T(8,128)(2,1)} %bitcast.85), kind=kOutput, calls=%fused_computation.6 | convolution fusion | flops 3275685888 | bytes 12058624 | tf_op jit(solution)/shard_map/dot_general | solution.py:157
  151.9 0.9 collective-permute-done.10
  (45 shorter events, 7.4 us)
Async XLA Ops:
  0.6 8.6 %copy-start.2 = (f32[16,2048]{1,0:T(8,128)S(1)}, f32[16,2048]{1,0:T(8,128)}, u32[]{:S(2)}) copy-start(f32[16,2048]{1,0:T(8,128)} %param.10) | copy-start | bytes 393220
  0.6 8.6 %copy-start.4 = (f32[16,2048]{1,0:T(8,128)S(1)}, f32[16,2048]{1,0:T(8,128)}, u32[]{:S(2)}) copy-start(f32[16,2048]{1,0:T(8,128)} %param.9) | copy-start | bytes 393220
  1.9 13.6 %collective-permute-start = (bf16[48,4096]{1,0:T(8,128)(2,1)S(1)}, bf16[48,4096]{1,0:T(8,128)(2,1)S(1)}, u32[]{:S(2)}, u32[]{:S(2)}) collective-permute-start(bf16[48,4096]{1,0:T(8,128)(2,1)S(1)} %get-tuple-element.15), channel_id=1, source_target_pairs={{0,2},{2,0},{1,3},{3,1},{4,6},{6,4},{5,7},{7,5},{8,10},{10,8},{9,1... | collective-permute-start | bytes 1179656 | tf_op jit(solution)/shard_map/ppermute | solution.py:74
  15.5 22.3 %copy-start = (bf16[2048,2048]{1,0:T(8,128)(2,1)}, bf16[2048,2048]{1,0:T(8,128)(2,1)S(1)}, u32[]{:S(2)}) copy-start(bf16[2048,2048]{1,0:T(8,128)(2,1)S(1)} %fusion.3) | copy-start | bytes 25165828
  37.5 16.8 %collective-permute-start.1 = (bf16[4,48,2048]{2,1,0:T(8,128)(2,1)S(1)}, bf16[4,48,2048]{2,1,0:T(8,128)(2,1)S(1)}, u32[]{:S(2)}, u32[]{:S(2)}) collective-permute-start(bf16[4,48,2048]{2,1,0:T(8,128)(2,1)S(1)} %all_to_all.15), channel_id=1, source_target_pairs={{0,2},{2,0},{1,3},{3,1},{4,6},{6,4},{5,7},{7,5},{8,10},{10,8},{9,1... | collective-permute-start | bytes 2359304 | tf_op jit(solution)/shard_map/ppermute | solution.py:81
  41.1 37.4 %copy-start.6 = (f32[128,7]{0,1:T(8,128)S(1)}, f32[128,7]{0,1:T(8,128)}, u32[]{:S(2)}) copy-start(f32[128,7]{0,1:T(8,128)} %param.11) | copy-start | bytes 10756
  41.1 21.0 %all-to-all-start.1 = ((f16[4,48,2048]{2,1,0:T(8,128)(2,1)}), f16[4,48,2048]{2,1,0:T(8,128)(2,1)S(1)}, u32[]{:S(2)}, u32[]{:S(2)}) async-start(f16[4,48,2048]{2,1,0:T(8,128)(2,1)} %get-tuple-element.30), calls=%async_computation.1 | async-start | bytes 1572864 | tf_op jit(solution)/shard_map/all_to_all | solution.py:88
  62.1 23.2 %all-to-all-start.2 = ((f16[4,48,2048]{2,1,0:T(8,128)(2,1)}), f16[4,48,2048]{2,1,0:T(8,128)(2,1)S(1)}, u32[]{:S(2)}, u32[]{:S(2)}) async-start(f16[4,48,2048]{2,1,0:T(8,128)(2,1)} %get-tuple-element.28), calls=%async_computation.2 | async-start | bytes 1572864 | tf_op jit(solution)/shard_map/all_to_all | solution.py:88
  71.0 23.5 %collective-permute-start.2 = (bf16[6,2048]{1,0:T(8,128)(2,1)}, bf16[6,2048]{1,0:T(8,128)(2,1)}, u32[]{:S(2)}, u32[]{:S(2)}) collective-permute-start(bf16[6,2048]{1,0:T(8,128)(2,1)} %slice_bitcast_fusion.1), channel_id=1, source_target_pairs={{1,0},{3,2},{5,4},{7,6},{9,8},{11,10},{13,12},{15,14},{17,16},{19,... | collective-permute-start | bytes 73736 | tf_op jit(solution)/shard_map/ppermute | solution.py:13
  76.6 17.9 %collective-permute-start.5 = (bf16[6,2048]{1,0:T(8,128)(2,1)}, bf16[6,2048]{1,0:T(8,128)(2,1)}, u32[]{:S(2)}, u32[]{:S(2)}) collective-permute-start(bf16[6,2048]{1,0:T(8,128)(2,1)} %slice_bitcast_fusion), channel_id=1, source_target_pairs={{1,0},{3,2},{5,4},{7,6},{9,8},{11,10},{13,12},{15,14},{17,16},{19,... | collective-permute-start | bytes 73736 | tf_op jit(solution)/shard_map/ppermute | solution.py:13
  87.9 5.7 %collective-permute-start.3 = (bf16[6,2048]{1,0:T(8,128)(2,1)S(1)}, bf16[6,2048]{1,0:T(8,128)(2,1)S(1)}, u32[]{:S(2)}, u32[]{:S(2)}) collective-permute-start(bf16[6,2048]{1,0:T(8,128)(2,1)S(1)} %get-tuple-element.16), channel_id=1, source_target_pairs={{0,1},{2,3},{4,5},{6,7},{8,9},{10,11},{12,13},{14,15},{16,17},{18,... | collective-permute-start | bytes 73736 | tf_op jit(solution)/shard_map/ppermute | solution.py:13
  89.2 5.1 %collective-permute-start.4 = (bf16[6,2048]{1,0:T(8,128)(2,1)S(1)}, bf16[6,2048]{1,0:T(8,128)(2,1)S(1)}, u32[]{:S(2)}, u32[]{:S(2)}) collective-permute-start(bf16[6,2048]{1,0:T(8,128)(2,1)S(1)} %get-tuple-element.17), channel_id=1, source_target_pairs={{1,0},{3,2},{5,4},{7,6},{9,8},{11,10},{13,12},{15,14},{17,16},{19,... | collective-permute-start | bytes 73736 | tf_op jit(solution)/shard_map/ppermute | solution.py:13
  98.1 1.5 copy-start.1
  98.1 12.5 %collective-permute-start.6 = (bf16[96,2048]{1,0:T(8,128)(2,1)}, bf16[96,2048]{1,0:T(8,128)(2,1)}, u32[]{:S(2)}, u32[]{:S(2)}) collective-permute-start(bf16[96,2048]{1,0:T(8,128)(2,1)} %get-tuple-element.11), channel_id=1, source_target_pairs={{0,4},{4,8},{8,12},{12,0},{1,5},{5,9},{9,13},{13,1},{2,6},{6,10},{... | collective-permute-start | bytes 1179656 | tf_op jit(solution)/shard_map/ppermute | solution.py:100
  100.6 32.5 %collective-permute-start.7 = (bf16[96,2048]{1,0:T(8,128)(2,1)}, bf16[96,2048]{1,0:T(8,128)(2,1)S(1)}, u32[]{:S(2)}, u32[]{:S(2)}) collective-permute-start(bf16[96,2048]{1,0:T(8,128)(2,1)} %get-tuple-element.11), channel_id=1, source_target_pairs={{0,8},{4,12},{8,0},{12,4},{1,9},{5,13},{9,1},{13,5},{2,10},{6,14},... | collective-permute-start | bytes 1179656 | tf_op jit(solution)/shard_map/ppermute | solution.py:100
  104.5 33.8 %collective-permute-start.8 = (bf16[96,2048]{1,0:T(8,128)(2,1)}, bf16[96,2048]{1,0:T(8,128)(2,1)S(1)}, u32[]{:S(2)}, u32[]{:S(2)}) collective-permute-start(bf16[96,2048]{1,0:T(8,128)(2,1)} %get-tuple-element.11), channel_id=1, source_target_pairs={{0,12},{4,0},{8,4},{12,8},{1,13},{5,1},{9,5},{13,9},{2,14},{6,2},{... | collective-permute-start | bytes 1179656 | tf_op jit(solution)/shard_map/ppermute | solution.py:100
  139.1 12.1 %copy-start.3 = (f32[16,2048]{1,0:T(8,128)S(1)}, f32[16,2048]{1,0:T(8,128)}, u32[]{:S(2)}) copy-start(f32[16,2048]{1,0:T(8,128)} %param.10) | copy-start | bytes 393220
  139.1 12.1 %copy-start.5 = (f32[16,2048]{1,0:T(8,128)S(1)}, f32[16,2048]{1,0:T(8,128)}, u32[]{:S(2)}) copy-start(f32[16,2048]{1,0:T(8,128)} %param.9) | copy-start | bytes 393220
  151.3 1.5 collective-permute-start.10
  151.9 1.7 %collective-permute-start.9 = (f32[16,2048]{1,0:T(8,128)S(1)}, f32[16,2048]{1,0:T(8,128)S(1)}, u32[]{:S(2)}, u32[]{:S(2)}) collective-permute-start(f32[16,2048]{1,0:T(8,128)S(1)} %get-tuple-element.20), channel_id=1, source_target_pairs={{0,1},{1,0},{2,3},{3,2},{4,5},{5,4},{6,7},{7,6},{8,9},{9,8},{10,11... | collective-permute-start | bytes 393224 | tf_op jit(solution)/shard_map/ppermute | solution.py:109

commit v15 on v14

--- a/solution.py
+++ b/solution.py
@@ -77,7 +77,7 @@
         first, jnp.concatenate([kept, other], axis=1), jnp.concatenate([other, kept], axis=1)
     )
     pieces = features.reshape(half, shards, rows).transpose(1, 0, 2)
-    own_half = lax.all_to_all(pieces, "fsdp", 0, 0)
+    own_half = ring_all_to_all(pieces, "fsdp")
     other_half = lax.ppermute(own_half, "seq", [(0, 1), (1, 0)])
     own_at = jnp.where(first, 0, half)
     return [(own_half, own_at), (other_half, half - own_at)], quant
@@ -85,7 +85,7 @@
 
 def reduce_partial(partial, me):
     shards = partial.shape[0]
-    received = lax.all_to_all(partial.astype(jnp.float16), "fsdp", 0, 0).astype(jnp.float32)
+    received = ring_all_to_all(partial.astype(jnp.float16), "fsdp").astype(jnp.float32)
     others = jnp.where((jnp.arange(shards) == me)[:, None, None], 0.0, received)
     own = lax.dynamic_index_in_dim(partial, me, 0, keepdims=False)
     return own + jnp.sum(others, axis=0)
@@ -100,6 +100,20 @@
         block = lax.ppermute(value, axis, [(i, (i + shift) % devices) for i in range(devices)])
         gathered = lax.dynamic_update_index_in_dim(gathered, block, (me + devices - shift) % devices, 0)
     return gathered
+
+
+def ring_all_to_all(pieces, axis):
+    devices = lax.axis_size(axis)
+    me = lax.axis_index(axis)
+    received = jnp.zeros_like(pieces)
+    received = lax.dynamic_update_index_in_dim(
+        received, lax.dynamic_index_in_dim(pieces, me, 0, keepdims=False), me, 0
+    )
+    for shift in range(1, devices):
+        outgoing = lax.dynamic_index_in_dim(pieces, (me + shift) % devices, 0, keepdims=False)
+        block = lax.ppermute(outgoing, axis, [(i, (i + shift) % devices) for i in range(devices)])
+        received = lax.dynamic_update_index_in_dim(received, block, (me + devices - shift) % devices, 0)
+    return received
 
 
 def sum_over_ctx(value):

time: 155 us -> 162 us (1.045)
  waiting for transfers between devices: 46.5 us -> 78.3 us
  blocking collectives: 21.8 us -> 0 us
  starting transfers between devices: 32 us -> 24.9 us
  local copies, waits for them, and re-layouts: 11.4 us -> 16.8 us
  matrix products: 21.9 us -> 19.2 us
    ppermute x0 -> x9, waiting for transfers between devices: none -> 42.3 us  [ring_all_to_all(): lax.ppermute(outgoing, axis, [(i, (i + shift) % devices) for i in range(d...]
    all_to_all x1 -> x0, blocking collectives: 21.8 us -> none  [rows_of_block(): own_half = lax.all_to_all(pieces, 'fsdp', 0, 0)]
    all_to_all x2 -> x0, starting transfers between devices: 13 us -> none  [reduce_partial(): lax.all_to_all(partial.astype(jnp.float16), 'fsdp', 0, 0)]
    ppermute x0 -> x9, starting transfers between devices: none -> 10.7 us  [ring_all_to_all(): lax.ppermute(outgoing, axis, [(i, (i + shift) % devices) for i in range(d...]
    all_to_all x2 -> x0, waiting for transfers between devices: 5.8 us -> none  [reduce_partial(): lax.all_to_all(partial.astype(jnp.float16), 'fsdp', 0, 0)]
    ppermute x3, starting transfers between devices: 5.15 us -> 1.42 us  [ring_gather(): lax.ppermute(value, axis, [(i, (i + shift) % devices) for i in range(devi...]
    ppermute x1, waiting for transfers between devices: 7.74 us -> 4.4 us  [rows_of_block(): other_half = lax.ppermute(own_half, 'seq', [(0, 1), (1, 0)])]
    dot_general x2, matrix products: 9.88 us -> 7.09 us  [on_device(): jnp.dot(flat, quant, preferred_element_type=jnp.float32)]
  transfers between devices with their start and end apart: 13 -> 20, of which waited for: 8 -> 13; matrix products, arithmetic and copies ran while one was open for 22% -> 24% of each run, Pallas kernels for 0% -> 0%
where the time goes in v15:
time: 162 us; the launch traced here: 161 us
  waiting for transfers between devices  78.3 us (48%)
  starting transfers between devices  24.9 us (15%)
  other arithmetic  20.6 us (13%)
  matrix products  19.2 us (12%)
  local copies, waits for them, and re-layouts  16.8 us (10%)
    ppermute x9, waiting for transfers between devices, ring_all_to_all(): lax.ppermute(outgoing, axis, [(i, (i + shift) % devices) for i in range(d...  42.3 us
    ppermute x3, waiting for transfers between devices, ring_gather(): lax.ppermute(value, axis, [(i, (i + shift) % devices) for i in range(devi...  29.9 us
    dot_general x1, matrix products, on_device(): lax.dot_general(inputs, d_all, (((0,), (0,)), ((), ())), preferred_elemen...  12.1 us
    ppermute x4, starting transfers between devices, from_behind(): return lax.ppermute(value, axis, pairs)  10.8 us
    ppermute x9, starting transfers between devices, ring_all_to_all(): lax.ppermute(outgoing, axis, [(i, (i + shift) % devices) for i in range(d...  10.7 us
    convert_element_type x1, other arithmetic, on_device(): quant = soft_clip(values, clip_upper, clip_lower).astype(jnp.bfloat16)  8.81 us
    dot_general x2, matrix products, on_device(): jnp.dot(flat, quant, preferred_element_type=jnp.float32)  7.09 us
    reduce_max x1, other arithmetic, clip_bounds(): jnp.max(jnp.abs(blocks.astype(jnp.bfloat16)), axis=1).astype(jnp.float32)  5.73 us
  transfers between devices with their start and end apart: 20, of which 13 were waited for; matrix products, arithmetic and copies ran while one was open for 24% of the time, Pallas kernels for 0%

profile of v15, /device:TPU:9, one launch (start us, length us, event | category | flops | bytes accessed | tf_op | source)
XLA Modules:
  0.0 160.9 jit_solution(10752598048365559630)
XLA Ops:
  1.8 1.3 collective-permute-start
  3.1 1.4 slice_bitcast_fusion
  4.5 3.5 %collective-permute-start.14 = (bf16[6,2048]{1,0:T(8,128)(2,1)}, bf16[6,2048]{1,0:T(8,128)(2,1)}, u32[]{:S(2)}, u32[]{:S(2)}) collective-permute-start(bf16[6,2048]{1,0:T(8,128)(2,1)} %slice_bitcast_fusion), channel_id=1, source_target_pairs={{1,0},{3,2},{5,4},{7,6},{9,8},{11,10},{13,12},{15,14},{17,16},{19,... | collective-permute-start | bytes 73736 | tf_op jit(solution)/shard_map/ppermute | solution.py:13
  7.9 5.7 %abs_reduce_fusion = bf16[16,2048]{1,0:T(8,128)(2,1)S(1)} fusion(bf16[2048,2048]{1,0:T(8,128)(2,1)} %param.8), kind=kLoop, calls=%fused_computation.15 | loop fusion | flops 16744448 | bytes 8454144 | tf_op jit(solution)/shard_map/reduce_max | solution.py:20
  14.1 8.8 %fusion.3 = bf16[2048,2048]{1,0:T(8,128)(2,1)} fusion(bf16[2048,2048]{1,0:T(8,128)(2,1)} %param.8, f32[16,2048]{1,0:T(8,128)S(1)} %get-tuple-element.12, f32[16,2048]{1,0:T(8,128)S(1)} %get-tuple-element.13, f32[16,2048]{1,0:T(8,128)S(1)} %get-tuple-element.30), kind=kLoop, calls=%fused_computation.5 | loop fusion | flops 25165824 | bytes 17170432 | tf_op jit(solution)/shard_map/convert_element_type | solution.py:133
  23.2 1.4 maximum_select_fusion
  24.6 1.7 %constant_dynamic-slice_fusion = (bf16[48,1,2048]{2,1,0:T(2,128)(2,1)S(1)}, bf16[48,1,2048]{2,1,0:T(2,128)(2,1)S(1)}, bf16[48,1,2048]{2,1,0:T(2,128)(2,1)S(1)}, bf16[48,1,2048]{2,1,0:T(2,128)(2,1)S(1)}) fusion(bf16[48,4,2048]{2,1,0:T(4,128)(2,1)S(1)} %maximum_select_fusion, s32[]{:T(128)S(6)} %select_n.135, s32[]{:T(128)S(6)} %select_n.137, ...), kind=kLoop, calls=%fused_computation.95 | loop fusion | bytes 1572880 | tf_op jit(solution)/shard_map/dynamic-slice.5
  26.4 1.3 collective-permute-start.1
  29.1 1.5 collective-permute-start.3
  30.9 9.9 %collective-permute-done.1 = bf16[48,2048]{1,0:T(8,128)(2,1)S(1)} collective-permute-done((bf16[48,2048]{1,0:T(8,128)(2,1)S(1)}, bf16[48,2048]{1,0:T(8,128)(2,1)S(1)}, u32[]{:S(2)}, u32[]{:S(2)}) %collective-permute-start.1) | collective-permute-done | bytes 196640 | tf_op jit(solution)/shard_map/ppermute | solution.py:114
  40.8 3.7 %collective-permute-done.2 = bf16[48,2048]{1,0:T(8,128)(2,1)S(1)} collective-permute-done((bf16[48,2048]{1,0:T(8,128)(2,1)S(1)}, bf16[48,2048]{1,0:T(8,128)(2,1)S(1)}, u32[]{:S(2)}, u32[]{:S(2)}) %collective-permute-start.2) | collective-permute-done | bytes 196640 | tf_op jit(solution)/shard_map/ppermute | solution.py:114
  44.5 1.6 %collective-permute-done.3 = bf16[48,2048]{1,0:T(8,128)(2,1)S(1)} collective-permute-done((bf16[48,2048]{1,0:T(8,128)(2,1)S(1)}, bf16[48,2048]{1,0:T(8,128)(2,1)S(1)}, u32[]{:S(2)}, u32[]{:S(2)}) %collective-permute-start.3) | collective-permute-done | bytes 196640 | tf_op jit(solution)/shard_map/ppermute | solution.py:114
  46.1 1.9 %fusion.30 = (f16[4,48,2048]{2,1,0:T(8,128)(2,1)S(1)}, f32[4,48,2048]{2,1,0:T(8,128)S(1)}) fusion(bf16[4,48,2048]{2,1,0:T(8,128)(2,1)S(1)} %bitcast_dynamic-update-slice_fusion.11, bf16[2048,2048]{1,0:T(8,128)(2,1)S(1)} %copy-done), kind=kOutput, calls=%fused_computation.104 | convolution fusion | flops 1611005952 | bytes 11534336 | tf_op jit(solution)/shard_map/dot_general | solution.py:141
  49.1 1.4 slice_bitcast_fusion.1
  50.4 2.9 %collective-permute-start.5 = (bf16[6,2048]{1,0:T(8,128)(2,1)}, bf16[6,2048]{1,0:T(8,128)(2,1)}, u32[]{:S(2)}, u32[]{:S(2)}) collective-permute-start(bf16[6,2048]{1,0:T(8,128)(2,1)} %slice_bitcast_fusion.1), channel_id=1, source_target_pairs={{1,0},{3,2},{5,4},{7,6},{9,8},{11,10},{13,12},{15,14},{17,16},{19,... | collective-permute-start | bytes 73736 | tf_op jit(solution)/shard_map/ppermute | solution.py:13
  54.4 1.3 reshape.67
  56.8 1.7 %collective-permute-start.8 = (f16[48,2048]{1,0:T(8,128)(2,1)}, f16[48,2048]{1,0:T(8,128)(2,1)S(1)}, u32[]{:S(2)}, u32[]{:S(2)}) collective-permute-start(f16[48,2048]{1,0:T(8,128)(2,1)} %get-tuple-element.14), channel_id=1, source_target_pairs={{0,12},{4,0},{8,4},{12,8},{1,13},{5,1},{9,5},{13,9},{2,14},{6,2},{... | collective-permute-start | bytes 589832 | tf_op jit(solution)/shard_map/ppermute | solution.py:114
  59.5 10.3 %collective-permute-done.7 = f16[48,2048]{1,0:T(8,128)(2,1)S(1)} collective-permute-done((f16[48,2048]{1,0:T(8,128)(2,1)}, f16[48,2048]{1,0:T(8,128)(2,1)S(1)}, u32[]{:S(2)}, u32[]{:S(2)}) %collective-permute-start.7) | collective-permute-done | bytes 196640 | tf_op jit(solution)/shard_map/ppermute | solution.py:114
  69.8 4.4 %collective-permute-done.4 = bf16[4,48,2048]{2,1,0:T(8,128)(2,1)S(1)} collective-permute-done((bf16[4,48,2048]{2,1,0:T(8,128)(2,1)S(1)}, bf16[4,48,2048]{2,1,0:T(8,128)(2,1)S(1)}, u32[]{:S(2)}, u32[]{:S(2)}) %collective-permute-start.4) | collective-permute-done | bytes 786464 | tf_op jit(solution)/shard_map/ppermute | solution.py:81
  74.2 5.2 %fusion.29 = (f16[4,48,2048]{2,1,0:T(8,128)(2,1)S(1)}, f32[4,48,2048]{2,1,0:T(8,128)S(1)}) fusion(bf16[4,48,2048]{2,1,0:T(8,128)(2,1)S(1)} %collective-permute-done.4, bf16[2048,2048]{1,0:T(8,128)(2,1)} %fusion.3), kind=kOutput, calls=%fused_computation.103 | convolution fusion | flops 1611005952 | bytes 11534336 | tf_op jit(solution)/shard_map/dot_general | solution.py:141
  79.7 1.4 collective-permute-start.9
  81.2 2.5 %collective-permute-start.10 = (f16[48,2048]{1,0:T(8,128)(2,1)S(1)}, f16[48,2048]{1,0:T(8,128)(2,1)S(1)}, u32[]{:S(2)}, u32[]{:S(2)}) collective-permute-start(f16[48,2048]{1,0:T(8,128)(2,1)S(1)} %get-tuple-element.19), channel_id=1, source_target_pairs={{0,8},{4,12},{8,0},{12,4},{1,9},{5,13},{9,1},{13,5},{2,10},{6,14},... | collective-permute-start | bytes 589832 | tf_op jit(solution)/shard_map/ppermute | solution.py:114
  83.7 3.1 %collective-permute-done.9 = f16[48,2048]{1,0:T(8,128)(2,1)S(1)} collective-permute-done((f16[48,2048]{1,0:T(8,128)(2,1)S(1)}, f16[48,2048]{1,0:T(8,128)(2,1)S(1)}, u32[]{:S(2)}, u32[]{:S(2)}) %collective-permute-start.9) | collective-permute-done | bytes 196640 | tf_op jit(solution)/shard_map/ppermute | solution.py:114
  86.8 11.3 %collective-permute-done.10 = f16[48,2048]{1,0:T(8,128)(2,1)S(1)} collective-permute-done((f16[48,2048]{1,0:T(8,128)(2,1)S(1)}, f16[48,2048]{1,0:T(8,128)(2,1)S(1)}, u32[]{:S(2)}, u32[]{:S(2)}) %collective-permute-start.10) | collective-permute-done | bytes 196640 | tf_op jit(solution)/shard_map/ppermute | solution.py:114
  98.2 2.4 %collective-permute-done.11 = f16[48,2048]{1,0:T(8,128)(2,1)S(1)} collective-permute-done((f16[48,2048]{1,0:T(8,128)(2,1)S(1)}, f16[48,2048]{1,0:T(8,128)(2,1)S(1)}, u32[]{:S(2)}, u32[]{:S(2)}) %collective-permute-start.11) | collective-permute-done | bytes 196640 | tf_op jit(solution)/shard_map/ppermute | solution.py:114
  101.3 1.4 collective-permute-start.12
  102.7 3.0 %collective-permute-start.13 = (bf16[6,2048]{1,0:T(8,128)(2,1)S(1)}, bf16[6,2048]{1,0:T(8,128)(2,1)S(1)}, u32[]{:S(2)}, u32[]{:S(2)}) collective-permute-start(bf16[6,2048]{1,0:T(8,128)(2,1)S(1)} %get-tuple-element.29), channel_id=1, source_target_pairs={{1,0},{3,2},{5,4},{7,6},{9,8},{11,10},{13,12},{15,14},{17,16},{19,... | collective-permute-start | bytes 73736 | tf_op jit(solution)/shard_map/ppermute | solution.py:13
  106.8 1.6 %convert_multiply_fusion = f32[102,2048]{1,0:T(8,128)S(1)} fusion(f32[108,2048]{1,0:T(8,128)S(1)} %maximum_convert_fusion, bf16[6,2048]{1,0:T(8,128)(2,1)} %collective-permute-done.5, bf16[96,2048]{1,0:T(8,128)(2,1)S(1)} %bitcast.121, bf16[6,2048]{1,0:T(8,128)(2,1)} %collective-permute-done.14, bf16[96,2048]{1,0:T(8,128)(2,1)S(1)} %bitcast.122, ...), kind=kLoop, calls=%fused_computation.18 | loop fusion | flops 5222400 | bytes 7577600 | tf_op jit(solution)/shard_map/mul | solution.py:164
  110.5 1.6 %copy.12 = bf16[2048,384]{1,0:T(8,128)(2,1)} copy(bf16[2048,384]{0,1:T(8,128)(2,1)S(1)} %bitcast.118) | data formatting | bytes 3145728 | tf_op jit(solution)/shard_map/dot_general | solution.py:171
  113.5 6.2 %collective-permute-done.15 = bf16[96,2048]{1,0:T(8,128)(2,1)S(1)} collective-permute-done((bf16[96,2048]{1,0:T(8,128)(2,1)S(1)}, bf16[96,2048]{1,0:T(8,128)(2,1)S(1)}, u32[]{:S(2)}, u32[]{:S(2)}) %collective-permute-start.15) | collective-permute-done | bytes 393248 | tf_op jit(solution)/shard_map/ppermute | solution.py:100
  120.5 22.6 %collective-permute-done.16 = bf16[96,2048]{1,0:T(8,128)(2,1)S(1)} collective-permute-done((bf16[96,2048]{1,0:T(8,128)(2,1)S(1)}, bf16[96,2048]{1,0:T(8,128)(2,1)S(1)}, u32[]{:S(2)}, u32[]{:S(2)}) %collective-permute-start.16) | collective-permute-done | bytes 393248 | tf_op jit(solution)/shard_map/ppermute | solution.py:100
  145.8 12.1 %multiply_reduce_fusion = (f32[16,2048]{1,0:T(8,128)S(1)}, f32[16,2048]{1,0:T(8,128)S(1)}) fusion(bf16[2048,2048]{1,0:T(8,128)(2,1)} %param.8, f32[16,2048]{1,0:T(8,128)S(1)} %get-tuple-element.12, f32[16,2048]{1,0:T(8,128)S(1)} %get-tuple-element.30, bf16[16,128,384]{2,1,0:T(8,128)(2,1)S(1)} %bitcast.119, bf16[384,2048,1]{1,0,2:T(8,128)(2,1)} %bitcast.120), kind=kOutput, calls=%fused_computation.6 | convolution fusion | flops 3275685888 | bytes 12058624 | tf_op jit(solution)/shard_map/dot_general | solution.py:171
  (82 shorter events, 19.6 us)
Async XLA Ops:
  1.8 21.1 %collective-permute-start = (bf16[48,4096]{1,0:T(8,128)(2,1)S(1)}, bf16[48,4096]{1,0:T(8,128)(2,1)S(1)}, u32[]{:S(2)}, u32[]{:S(2)}) collective-permute-start(bf16[48,4096]{1,0:T(8,128)(2,1)S(1)} %get-tuple-element.27), channel_id=1, source_target_pairs={{0,2},{2,0},{1,3},{3,1},{4,6},{6,4},{5,7},{7,5},{8,10},{10,8},{9,1... | collective-permute-start | bytes 1179656 | tf_op jit(solution)/shard_map/ppermute | solution.py:74
  4.5 102.3 %collective-permute-start.14 = (bf16[6,2048]{1,0:T(8,128)(2,1)}, bf16[6,2048]{1,0:T(8,128)(2,1)}, u32[]{:S(2)}, u32[]{:S(2)}) collective-permute-start(bf16[6,2048]{1,0:T(8,128)(2,1)} %slice_bitcast_fusion), channel_id=1, source_target_pairs={{1,0},{3,2},{5,4},{7,6},{9,8},{11,10},{13,12},{15,14},{17,16},{19,... | collective-permute-start | bytes 73736 | tf_op jit(solution)/shard_map/ppermute | solution.py:13
  7.9 6.0 %copy-start.3 = (f32[16,2048]{1,0:T(8,128)S(1)}, f32[16,2048]{1,0:T(8,128)}, u32[]{:S(2)}) copy-start(f32[16,2048]{1,0:T(8,128)} %param.10) | copy-start | bytes 393220
  7.9 6.0 %copy-start.5 = (f32[16,2048]{1,0:T(8,128)S(1)}, f32[16,2048]{1,0:T(8,128)}, u32[]{:S(2)}) copy-start(f32[16,2048]{1,0:T(8,128)} %param.9) | copy-start | bytes 393220
  23.2 22.9 %copy-start = (bf16[2048,2048]{1,0:T(8,128)(2,1)S(1)}, bf16[2048,2048]{1,0:T(8,128)(2,1)}, u32[]{:S(2)}) copy-start(bf16[2048,2048]{1,0:T(8,128)(2,1)} %fusion.3) | copy-start | bytes 25165828
  26.4 14.3 %collective-permute-start.1 = (bf16[48,2048]{1,0:T(8,128)(2,1)S(1)}, bf16[48,2048]{1,0:T(8,128)(2,1)S(1)}, u32[]{:S(2)}, u32[]{:S(2)}) collective-permute-start(bf16[48,2048]{1,0:T(8,128)(2,1)S(1)} %bitcast.126), channel_id=1, source_target_pairs={{0,4},{4,8},{8,12},{12,0},{1,5},{5,9},{9,13},{13,1},{2,6},{6,10},{... | collective-permute-start | bytes 589832 | tf_op jit(solution)/shard_map/ppermute | solution.py:114
  27.9 16.5 %collective-permute-start.2 = (bf16[48,2048]{1,0:T(8,128)(2,1)S(1)}, bf16[48,2048]{1,0:T(8,128)(2,1)S(1)}, u32[]{:S(2)}, u32[]{:S(2)}) collective-permute-start(bf16[48,2048]{1,0:T(8,128)(2,1)S(1)} %bitcast.125), channel_id=1, source_target_pairs={{0,8},{4,12},{8,0},{12,4},{1,9},{5,13},{9,1},{13,5},{2,10},{6,14},... | collective-permute-start | bytes 589832 | tf_op jit(solution)/shard_map/ppermute | solution.py:114
  29.1 17.0 %collective-permute-start.3 = (bf16[48,2048]{1,0:T(8,128)(2,1)S(1)}, bf16[48,2048]{1,0:T(8,128)(2,1)S(1)}, u32[]{:S(2)}, u32[]{:S(2)}) collective-permute-start(bf16[48,2048]{1,0:T(8,128)(2,1)S(1)} %bitcast.124), channel_id=1, source_target_pairs={{0,12},{4,0},{8,4},{12,8},{1,13},{5,1},{9,5},{13,9},{2,14},{6,2},{... | collective-permute-start | bytes 589832 | tf_op jit(solution)/shard_map/ppermute | solution.py:114
  48.1 5.3 %copy-start.9 = (f32[128,7]{0,1:T(8,128)S(1)}, f32[128,7]{0,1:T(8,128)}, u32[]{:S(2)}) copy-start(f32[128,7]{0,1:T(8,128)} %param.11) | copy-start | bytes 10756
  49.1 7.8 %collective-permute-start.6 = (f16[48,2048]{1,0:T(8,128)(2,1)}, f16[48,2048]{1,0:T(8,128)(2,1)}, u32[]{:S(2)}, u32[]{:S(2)}) collective-permute-start(f16[48,2048]{1,0:T(8,128)(2,1)} %get-tuple-element.16), channel_id=1, source_target_pairs={{0,4},{4,8},{8,12},{12,0},{1,5},{5,9},{9,13},{13,1},{2,6},{6,10},{... | collective-permute-start | bytes 589832 | tf_op jit(solution)/shard_map/ppermute | solution.py:114
  50.4 56.3 %collective-permute-start.5 = (bf16[6,2048]{1,0:T(8,128)(2,1)}, bf16[6,2048]{1,0:T(8,128)(2,1)}, u32[]{:S(2)}, u32[]{:S(2)}) collective-permute-start(bf16[6,2048]{1,0:T(8,128)(2,1)} %slice_bitcast_fusion.1), channel_id=1, source_target_pairs={{1,0},{3,2},{5,4},{7,6},{9,8},{11,10},{13,12},{15,14},{17,16},{19,... | collective-permute-start | bytes 73736 | tf_op jit(solution)/shard_map/ppermute | solution.py:13
  55.7 18.6 %collective-permute-start.4 = (bf16[4,48,2048]{2,1,0:T(8,128)(2,1)S(1)}, bf16[4,48,2048]{2,1,0:T(8,128)(2,1)S(1)}, u32[]{:S(2)}, u32[]{:S(2)}) collective-permute-start(bf16[4,48,2048]{2,1,0:T(8,128)(2,1)S(1)} %bitcast_dynamic-update-slice_fusion.11), channel_id=1, source_target_pairs={{0,2},{2,0},{1,3},{3,1},{4,6},{6,4},{5,7},{7,5},{8,10},{10,8},{9,1... | collective-permute-start | bytes 2359304 | tf_op jit(solution)/shard_map/ppermute | solution.py:81
  55.8 14.0 %collective-permute-start.7 = (f16[48,2048]{1,0:T(8,128)(2,1)}, f16[48,2048]{1,0:T(8,128)(2,1)S(1)}, u32[]{:S(2)}, u32[]{:S(2)}) collective-permute-start(f16[48,2048]{1,0:T(8,128)(2,1)} %get-tuple-element.15), channel_id=1, source_target_pairs={{0,8},{4,12},{8,0},{12,4},{1,9},{5,13},{9,1},{13,5},{2,10},{6,14},... | collective-permute-start | bytes 589832 | tf_op jit(solution)/shard_map/ppermute | solution.py:114
  56.8 24.3 %collective-permute-start.8 = (f16[48,2048]{1,0:T(8,128)(2,1)}, f16[48,2048]{1,0:T(8,128)(2,1)S(1)}, u32[]{:S(2)}, u32[]{:S(2)}) collective-permute-start(f16[48,2048]{1,0:T(8,128)(2,1)} %get-tuple-element.14), channel_id=1, source_target_pairs={{0,12},{4,0},{8,4},{12,8},{1,13},{5,1},{9,5},{13,9},{2,14},{6,2},{... | collective-permute-start | bytes 589832 | tf_op jit(solution)/shard_map/ppermute | solution.py:114
  79.7 7.1 %collective-permute-start.9 = (f16[48,2048]{1,0:T(8,128)(2,1)S(1)}, f16[48,2048]{1,0:T(8,128)(2,1)S(1)}, u32[]{:S(2)}, u32[]{:S(2)}) collective-permute-start(f16[48,2048]{1,0:T(8,128)(2,1)S(1)} %get-tuple-element.20), channel_id=1, source_target_pairs={{0,4},{4,8},{8,12},{12,0},{1,5},{5,9},{9,13},{13,1},{2,6},{6,10},{... | collective-permute-start | bytes 589832 | tf_op jit(solution)/shard_map/ppermute | solution.py:114
  81.2 17.0 %collective-permute-start.10 = (f16[48,2048]{1,0:T(8,128)(2,1)S(1)}, f16[48,2048]{1,0:T(8,128)(2,1)S(1)}, u32[]{:S(2)}, u32[]{:S(2)}) collective-permute-start(f16[48,2048]{1,0:T(8,128)(2,1)S(1)} %get-tuple-element.19), channel_id=1, source_target_pairs={{0,8},{4,12},{8,0},{12,4},{1,9},{5,13},{9,1},{13,5},{2,10},{6,14},... | collective-permute-start | bytes 589832 | tf_op jit(solution)/shard_map/ppermute | solution.py:114
  83.7 16.9 %collective-permute-start.11 = (f16[48,2048]{1,0:T(8,128)(2,1)S(1)}, f16[48,2048]{1,0:T(8,128)(2,1)S(1)}, u32[]{:S(2)}, u32[]{:S(2)}) collective-permute-start(f16[48,2048]{1,0:T(8,128)(2,1)S(1)} %get-tuple-element.18), channel_id=1, source_target_pairs={{0,12},{4,0},{8,4},{12,8},{1,13},{5,1},{9,5},{13,9},{2,14},{6,2},{... | collective-permute-start | bytes 589832 | tf_op jit(solution)/shard_map/ppermute | solution.py:114
  101.2 5.6 %copy-start.7 = (bf16[1,1,96,2048]{3,2,1,0:T(8,128)(2,1)S(1)}, bf16[1,1,96,2048]{3,2,1,0:T(8,128)(2,1)}, u32[]{:S(2)}) copy-start(bf16[1,1,96,2048]{3,2,1,0:T(8,128)(2,1)} %param.12) | copy-start | bytes 1179652
  101.2 5.6 %copy-start.8 = (bf16[1,1,96,2048]{3,2,1,0:T(8,128)(2,1)S(1)}, bf16[1,1,96,2048]{3,2,1,0:T(8,128)(2,1)}, u32[]{:S(2)}) copy-start(bf16[1,1,96,2048]{3,2,1,0:T(8,128)(2,1)} %param.13) | copy-start | bytes 1179652
  101.3 4.5 %collective-permute-start.12 = (bf16[6,2048]{1,0:T(8,128)(2,1)S(1)}, bf16[6,2048]{1,0:T(8,128)(2,1)S(1)}, u32[]{:S(2)}, u32[]{:S(2)}) collective-permute-start(bf16[6,2048]{1,0:T(8,128)(2,1)S(1)} %get-tuple-element.28), channel_id=1, source_target_pairs={{0,1},{2,3},{4,5},{6,7},{8,9},{10,11},{12,13},{14,15},{16,17},{18,... | collective-permute-start | bytes 73736 | tf_op jit(solution)/shard_map/ppermute | solution.py:13
  102.7 3.9 %collective-permute-start.13 = (bf16[6,2048]{1,0:T(8,128)(2,1)S(1)}, bf16[6,2048]{1,0:T(8,128)(2,1)S(1)}, u32[]{:S(2)}, u32[]{:S(2)}) collective-permute-start(bf16[6,2048]{1,0:T(8,128)(2,1)S(1)} %get-tuple-element.29), channel_id=1, source_target_pairs={{1,0},{3,2},{5,4},{7,6},{9,8},{11,10},{13,12},{15,14},{17,16},{19,... | collective-permute-start | bytes 73736 | tf_op jit(solution)/shard_map/ppermute | solution.py:13
  109.3 1.1 copy-start.2
  109.3 10.4 %collective-permute-start.15 = (bf16[96,2048]{1,0:T(8,128)(2,1)S(1)}, bf16[96,2048]{1,0:T(8,128)(2,1)S(1)}, u32[]{:S(2)}, u32[]{:S(2)}) collective-permute-start(bf16[96,2048]{1,0:T(8,128)(2,1)S(1)} %get-tuple-element.11), channel_id=1, source_target_pairs={{0,4},{4,8},{8,12},{12,0},{1,5},{5,9},{9,13},{13,1},{2,6},{6,10},{... | collective-permute-start | bytes 1179656 | tf_op jit(solution)/shard_map/ppermute | solution.py:100
  112.1 33.6 %copy-start.1 = (bf16[2048,384]{1,0:T(8,128)(2,1)S(1)}, bf16[2048,384]{1,0:T(8,128)(2,1)}, u32[]{:S(2)}) copy-start(bf16[2048,384]{1,0:T(8,128)(2,1)} %copy.12) | copy-start | bytes 4718596
  112.1 31.0 %collective-permute-start.16 = (bf16[96,2048]{1,0:T(8,128)(2,1)S(1)}, bf16[96,2048]{1,0:T(8,128)(2,1)S(1)}, u32[]{:S(2)}, u32[]{:S(2)}) collective-permute-start(bf16[96,2048]{1,0:T(8,128)(2,1)S(1)} %get-tuple-element.11), channel_id=1, source_target_pairs={{0,8},{4,12},{8,0},{12,4},{1,9},{5,13},{9,1},{13,5},{2,10},{6,14},... | collective-permute-start | bytes 1179656 | tf_op jit(solution)/shard_map/ppermute | solution.py:100
  112.8 32.1 %collective-permute-start.17 = (bf16[96,2048]{1,0:T(8,128)(2,1)S(1)}, bf16[96,2048]{1,0:T(8,128)(2,1)S(1)}, u32[]{:S(2)}, u32[]{:S(2)}) collective-permute-start(bf16[96,2048]{1,0:T(8,128)(2,1)S(1)} %get-tuple-element.11), channel_id=1, source_target_pairs={{0,12},{4,0},{8,4},{12,8},{1,13},{5,1},{9,5},{13,9},{2,14},{6,2},{... | collective-permute-start | bytes 1179656 | tf_op jit(solution)/shard_map/ppermute | solution.py:100
  145.8 12.1 %copy-start.4 = (f32[16,2048]{1,0:T(8,128)S(1)}, f32[16,2048]{1,0:T(8,128)}, u32[]{:S(2)}) copy-start(f32[16,2048]{1,0:T(8,128)} %param.10) | copy-start | bytes 393220
  145.8 12.1 %copy-start.6 = (f32[16,2048]{1,0:T(8,128)S(1)}, f32[16,2048]{1,0:T(8,128)}, u32[]{:S(2)}) copy-start(f32[16,2048]{1,0:T(8,128)} %param.9) | copy-start | bytes 393220
  158.0 1.5 collective-permute-start.19
  158.6 1.7 %collective-permute-start.18 = (f32[16,2048]{1,0:T(8,128)S(1)}, f32[16,2048]{1,0:T(8,128)S(1)}, u32[]{:S(2)}, u32[]{:S(2)}) collective-permute-start(f32[16,2048]{1,0:T(8,128)S(1)} %get-tuple-element.32), channel_id=1, source_target_pairs={{0,1},{1,0},{2,3},{3,2},{4,5},{5,4},{6,7},{7,6},{8,9},{9,8},{10,11... | collective-permute-start | bytes 393224 | tf_op jit(solution)/shard_map/ppermute | solution.py:123

commit v16 on v15

--- a/solution.py
+++ b/solution.py
@@ -85,7 +85,7 @@
 
 def reduce_partial(partial, me):
     shards = partial.shape[0]
-    received = ring_all_to_all(partial.astype(jnp.float16), "fsdp").astype(jnp.float32)
+    received = lax.all_to_all(partial.astype(jnp.float16), "fsdp", 0, 0).astype(jnp.float32)
     others = jnp.where((jnp.arange(shards) == me)[:, None, None], 0.0, received)
     own = lax.dynamic_index_in_dim(partial, me, 0, keepdims=False)
     return own + jnp.sum(others, axis=0)

time: 162 us -> 156 us (0.963)
  waiting for transfers between devices: 78.3 us -> 64.9 us
  starting transfers between devices: 24.9 us -> 30.8 us
  local copies, waits for them, and re-layouts: 16.8 us -> 13.8 us
  matrix products: 19.2 us -> 21.9 us
  other arithmetic: 20.6 us -> 23.3 us
    ppermute x9 -> x3, waiting for transfers between devices: 42.3 us -> 15.9 us  [ring_all_to_all(): lax.ppermute(outgoing, axis, [(i, (i + shift) % devices) for i in range(d...]
    all_to_all x0 -> x2, starting transfers between devices: none -> 7.64 us  [reduce_partial(): lax.all_to_all(partial.astype(jnp.float16), 'fsdp', 0, 0)]
    ppermute x1, waiting for transfers between devices: 4.4 us -> 11.6 us  [rows_of_block(): other_half = lax.ppermute(own_half, 'seq', [(0, 1), (1, 0)])]
    ppermute x9 -> x3, starting transfers between devices: 10.7 us -> 3.95 us  [ring_all_to_all(): lax.ppermute(outgoing, axis, [(i, (i + shift) % devices) for i in range(d...]
    all_to_all x0 -> x2, waiting for transfers between devices: none -> 4.4 us  [reduce_partial(): lax.all_to_all(partial.astype(jnp.float16), 'fsdp', 0, 0)]
    ppermute x3, starting transfers between devices: 1.42 us -> 5.15 us  [ring_gather(): lax.ppermute(value, axis, [(i, (i + shift) % devices) for i in range(devi...]
    dot_general x2, matrix products: 7.09 us -> 9.91 us  [on_device(): jnp.dot(flat, quant, preferred_element_type=jnp.float32)]
    dynamic_update_slice x2, other arithmetic: 0.11 us -> 2.16 us  [on_device(): lax.dynamic_update_slice_in_dim(proj, reduce_partial(partial, me), at, 0)]
  transfers between devices with their start and end apart: 20 -> 16, of which waited for: 13 -> 10; matrix products, arithmetic and copies ran while one was open for 24% -> 24% of each run, Pallas kernels for 0% -> 0%
where the time goes in v16:
time: 156 us
  waiting for transfers between devices  64.9 us (42%)
  starting transfers between devices  30.8 us (20%)
  other arithmetic  23.3 us (15%)
  matrix products  21.9 us (14%)
  local copies, waits for them, and re-layouts  13.8 us (9%)
    ppermute x3, waiting for transfers between devices, ring_gather(): lax.ppermute(value, axis, [(i, (i + shift) % devices) for i in range(devi...  31.3 us
    ppermute x3, waiting for transfers between devices, ring_all_to_all(): lax.ppermute(outgoing, axis, [(i, (i + shift) % devices) for i in range(d...  15.9 us
    dot_general x1, matrix products, on_device(): lax.dot_general(inputs, d_all, (((0,), (0,)), ((), ())), preferred_elemen...  12 us
    ppermute x4, starting transfers between devices, from_behind(): return lax.ppermute(value, axis, pairs)  11.9 us
    ppermute x1, waiting for transfers between devices, rows_of_block(): other_half = lax.ppermute(own_half, 'seq', [(0, 1), (1, 0)])  11.6 us
    dot_general x2, matrix products, on_device(): jnp.dot(flat, quant, preferred_element_type=jnp.float32)  9.91 us
    convert_element_type x1, other arithmetic, on_device(): quant = soft_clip(values, clip_upper, clip_lower).astype(jnp.bfloat16)  8.75 us
    all_to_all x2, starting transfers between devices, reduce_partial(): lax.all_to_all(partial.astype(jnp.float16), 'fsdp', 0, 0)  7.64 us
  transfers between devices with their start and end apart: 16, of which 10 were waited for; matrix products, arithmetic and copies ran while one was open for 24% of the time, Pallas kernels for 0%

profile of v16, /device:TPU:9, one launch (start us, length us, event | category | flops | bytes accessed | tf_op | source)
XLA Modules:
  0.0 155.7 jit_solution(3871806803478737142)
XLA Ops:
  0.6 1.2 constant_dynamic-slice_fusion.4
  1.8 1.3 collective-permute-start
  3.1 5.7 %abs_reduce_fusion = bf16[16,2048]{1,0:T(8,128)(2,1)S(1)} fusion(bf16[2048,2048]{1,0:T(8,128)(2,1)} %param.8), kind=kLoop, calls=%fused_computation.15 | loop fusion | flops 16744448 | bytes 8454144 | tf_op jit(solution)/shard_map/reduce_max | solution.py:20
  9.3 8.8 %fusion.3 = bf16[2048,2048]{1,0:T(8,128)(2,1)} fusion(bf16[2048,2048]{1,0:T(8,128)(2,1)} %param.8, f32[16,2048]{1,0:T(8,128)S(1)} %get-tuple-element.12, f32[16,2048]{1,0:T(8,128)S(1)} %get-tuple-element.13, f32[16,2048]{1,0:T(8,128)S(1)} %get-tuple-element.22), kind=kLoop, calls=%fused_computation.5 | loop fusion | flops 25165824 | bytes 17170432 | tf_op jit(solution)/shard_map/convert_element_type | solution.py:133
  18.3 1.4 maximum_select_fusion
  19.7 1.7 %constant_dynamic-slice_fusion = (bf16[48,1,2048]{2,1,0:T(2,128)(2,1)S(1)}, bf16[48,1,2048]{2,1,0:T(2,128)(2,1)S(1)}, bf16[48,1,2048]{2,1,0:T(2,128)(2,1)S(1)}, bf16[48,1,2048]{2,1,0:T(2,128)(2,1)S(1)}) fusion(bf16[48,4,2048]{2,1,0:T(4,128)(2,1)S(1)} %maximum_select_fusion, s32[]{:T(128)S(6)} %select_n.93, s32[]{:T(128)S(6)} %select_n.95, s32[]{:T(128)S(6)} %select_n.91, ...), kind=kLoop, calls=%fused_computation.81 | loop fusion | bytes 1572880 | tf_op jit(solution)/shard_map/dynamic-slice.5
  21.6 1.3 collective-permute-start.1
  24.2 1.5 collective-permute-start.3
  27.1 11.7 %collective-permute-done.2 = bf16[48,2048]{1,0:T(8,128)(2,1)S(1)} collective-permute-done((bf16[48,2048]{1,0:T(8,128)(2,1)S(1)}, bf16[48,2048]{1,0:T(8,128)(2,1)S(1)}, u32[]{:S(2)}, u32[]{:S(2)}) %collective-permute-start.2) | collective-permute-done | bytes 196640 | tf_op jit(solution)/shard_map/ppermute | solution.py:114
  38.8 3.1 %collective-permute-done.3 = bf16[48,2048]{1,0:T(8,128)(2,1)S(1)} collective-permute-done((bf16[48,2048]{1,0:T(8,128)(2,1)S(1)}, bf16[48,2048]{1,0:T(8,128)(2,1)S(1)}, u32[]{:S(2)}, u32[]{:S(2)}) %collective-permute-start.3) | collective-permute-done | bytes 196640 | tf_op jit(solution)/shard_map/ppermute | solution.py:114
  42.3 3.3 %fusion.30 = (f16[4,48,2048]{2,1,0:T(8,128)(2,1)}, f32[4,48,2048]{2,1,0:T(8,128)}) fusion(bf16[4,48,2048]{2,1,0:T(8,128)(2,1)S(1)} %bitcast_dynamic-update-slice_fusion.5, bf16[2048,2048]{1,0:T(8,128)(2,1)S(1)} %copy-done), kind=kOutput, calls=%fused_computation.90 | convolution fusion | flops 1611005952 | bytes 11534336 | tf_op jit(solution)/shard_map/dot_general | solution.py:141
  45.6 3.5 %all-to-all-start = ((f16[4,48,2048]{2,1,0:T(8,128)(2,1)}), f16[4,48,2048]{2,1,0:T(8,128)(2,1)S(1)}, u32[]{:S(2)}, u32[]{:S(2)}) async-start(f16[4,48,2048]{2,1,0:T(8,128)(2,1)} %get-tuple-element.34), calls=%async_computation | async-start | bytes 1572864 | tf_op jit(solution)/shard_map/all_to_all | solution.py:88
  49.1 11.6 %collective-permute-done.4 = bf16[4,48,2048]{2,1,0:T(8,128)(2,1)S(1)} collective-permute-done((bf16[4,48,2048]{2,1,0:T(8,128)(2,1)S(1)}, bf16[4,48,2048]{2,1,0:T(8,128)(2,1)S(1)}, u32[]{:S(2)}, u32[]{:S(2)}) %collective-permute-start.4) | collective-permute-done | bytes 786464 | tf_op jit(solution)/shard_map/ppermute | solution.py:81
  60.6 6.6 %fusion.29 = (f16[4,48,2048]{2,1,0:T(8,128)(2,1)}, f32[4,48,2048]{2,1,0:T(8,128)}) fusion(bf16[4,48,2048]{2,1,0:T(8,128)(2,1)S(1)} %collective-permute-done.4, bf16[2048,2048]{1,0:T(8,128)(2,1)} %fusion.3), kind=kOutput, calls=%fused_computation.89 | convolution fusion | flops 1611005952 | bytes 11534336 | tf_op jit(solution)/shard_map/dot_general | solution.py:141
  67.2 4.2 %all-to-all-start.1 = ((f16[4,48,2048]{2,1,0:T(8,128)(2,1)}), f16[4,48,2048]{2,1,0:T(8,128)(2,1)S(1)}, u32[]{:S(2)}, u32[]{:S(2)}) async-start(f16[4,48,2048]{2,1,0:T(8,128)(2,1)} %get-tuple-element.32), calls=%async_computation.1 | async-start | bytes 1572864 | tf_op jit(solution)/shard_map/all_to_all | solution.py:88
  71.4 1.4 slice_bitcast_fusion.1
  72.8 4.4 %collective-permute-start.5 = (bf16[6,2048]{1,0:T(8,128)(2,1)}, bf16[6,2048]{1,0:T(8,128)(2,1)}, u32[]{:S(2)}, u32[]{:S(2)}) collective-permute-start(bf16[6,2048]{1,0:T(8,128)(2,1)} %slice_bitcast_fusion.1), channel_id=1, source_target_pairs={{1,0},{3,2},{5,4},{7,6},{9,8},{11,10},{13,12},{15,14},{17,16},{19,... | collective-permute-start | bytes 73736 | tf_op jit(solution)/shard_map/ppermute | solution.py:13
  77.2 1.4 slice_bitcast_fusion
  78.5 1.9 %collective-permute-start.8 = (bf16[6,2048]{1,0:T(8,128)(2,1)}, bf16[6,2048]{1,0:T(8,128)(2,1)}, u32[]{:S(2)}, u32[]{:S(2)}) collective-permute-start(bf16[6,2048]{1,0:T(8,128)(2,1)} %slice_bitcast_fusion), channel_id=1, source_target_pairs={{1,0},{3,2},{5,4},{7,6},{9,8},{11,10},{13,12},{15,14},{17,16},{19,... | collective-permute-start | bytes 73736 | tf_op jit(solution)/shard_map/ppermute | solution.py:13
  81.4 1.3 reshape.67
  82.7 4.4 %all-to-all-done.1 = f16[4,48,2048]{2,1,0:T(8,128)(2,1)S(1)} async-done(((f16[4,48,2048]{2,1,0:T(8,128)(2,1)}), f16[4,48,2048]{2,1,0:T(8,128)(2,1)S(1)}, u32[]{:S(2)}, u32[]{:S(2)}) %all-to-all-start.1) | async-done | bytes 786464 | tf_op jit(solution)/shard_map/all_to_all | solution.py:88
  89.8 1.3 collective-permute-start.6
  91.1 4.3 %collective-permute-start.7 = (bf16[6,2048]{1,0:T(8,128)(2,1)S(1)}, bf16[6,2048]{1,0:T(8,128)(2,1)S(1)}, u32[]{:S(2)}, u32[]{:S(2)}) collective-permute-start(bf16[6,2048]{1,0:T(8,128)(2,1)S(1)} %get-tuple-element.21), channel_id=1, source_target_pairs={{1,0},{3,2},{5,4},{7,6},{9,8},{11,10},{13,12},{15,14},{17,16},{19,... | collective-permute-start | bytes 73736 | tf_op jit(solution)/shard_map/ppermute | solution.py:13
  96.4 1.6 %convert_multiply_fusion = f32[102,2048]{1,0:T(8,128)S(1)} fusion(f32[108,2048]{1,0:T(8,128)S(1)} %maximum_convert_fusion, bf16[6,2048]{1,0:T(8,128)(2,1)} %collective-permute-done.5, bf16[96,2048]{1,0:T(8,128)(2,1)S(1)} %bitcast.97, bf16[6,2048]{1,0:T(8,128)(2,1)} %collective-permute-done.8, bf16[96,2048]{1,0:T(8,128)(2,1)S(1)} %bitcast.98, ...), kind=kLoop, calls=%fused_computation.18 | loop fusion | flops 5222400 | bytes 7577600 | tf_op jit(solution)/shard_map/mul | solution.py:164
  98.2 1.4 bitcast_dynamic-update-slice_fusion.3
  99.7 1.2 collective-permute-start.9
  102.1 4.0 %collective-permute-start.10 = (bf16[96,2048]{1,0:T(8,128)(2,1)}, bf16[96,2048]{1,0:T(8,128)(2,1)S(1)}, u32[]{:S(2)}, u32[]{:S(2)}) collective-permute-start(bf16[96,2048]{1,0:T(8,128)(2,1)} %get-tuple-element.11), channel_id=1, source_target_pairs={{0,8},{4,12},{8,0},{12,4},{1,9},{5,13},{9,1},{13,5},{2,10},{6,14},... | collective-permute-start | bytes 1179656 | tf_op jit(solution)/shard_map/ppermute | solution.py:100
  106.1 6.1 %collective-permute-done.9 = bf16[96,2048]{1,0:T(8,128)(2,1)} collective-permute-done((bf16[96,2048]{1,0:T(8,128)(2,1)}, bf16[96,2048]{1,0:T(8,128)(2,1)}, u32[]{:S(2)}, u32[]{:S(2)}) %collective-permute-start.9) | collective-permute-done | bytes 393248 | tf_op jit(solution)/shard_map/ppermute | solution.py:100
  112.2 1.8 %bitcast_dynamic-update-slice_fusion.2 = bf16[4,96,2048]{2,1,0:T(8,128)(2,1)} fusion(bf16[4,96,2048]{2,1,0:T(8,128)(2,1)} %copy-done.1, s32[]{:T(128)S(6)} %select_n.93, bf16[96,2048]{1,0:T(8,128)(2,1)} %collective-permute-done.9), kind=kLoop, calls=%fused_computation.53 | loop fusion | bytes 786436 | tf_op jit(solution)/shard_map/jit(dynamic_update_index_in_dim)/dynamic_update_slice | solution.py:101
  114.0 20.6 %collective-permute-done.10 = bf16[96,2048]{1,0:T(8,128)(2,1)S(1)} collective-permute-done((bf16[96,2048]{1,0:T(8,128)(2,1)}, bf16[96,2048]{1,0:T(8,128)(2,1)S(1)}, u32[]{:S(2)}, u32[]{:S(2)}) %collective-permute-start.10) | collective-permute-done | bytes 393248 | tf_op jit(solution)/shard_map/ppermute | solution.py:100
  135.4 4.5 %collective-permute-done.11 = bf16[96,2048]{1,0:T(8,128)(2,1)S(1)} collective-permute-done((bf16[96,2048]{1,0:T(8,128)(2,1)}, bf16[96,2048]{1,0:T(8,128)(2,1)S(1)}, u32[]{:S(2)}, u32[]{:S(2)}) %collective-permute-start.11) | collective-permute-done | bytes 393248 | tf_op jit(solution)/shard_map/ppermute | solution.py:100
  140.7 12.0 %multiply_reduce_fusion = (f32[16,2048]{1,0:T(8,128)S(1)}, f32[16,2048]{1,0:T(8,128)S(1)}) fusion(bf16[2048,2048]{1,0:T(8,128)(2,1)} %param.8, f32[16,2048]{1,0:T(8,128)S(1)} %get-tuple-element.12, f32[16,2048]{1,0:T(8,128)S(1)} %get-tuple-element.22, bf16[16,128,384]{2,1,0:T(8,128)(2,1)S(1)} %bitcast.95, bf16[384,2048,1]{1,0,2:T(8,128)(2,1)} %bitcast.96), kind=kOutput, calls=%fused_computation.6 | convolution fusion | flops 3275685888 | bytes 12058624 | tf_op jit(solution)/shard_map/dot_general | solution.py:171
  (62 shorter events, 14.3 us)
Async XLA Ops:
  1.8 16.2 %collective-permute-start = (bf16[48,4096]{1,0:T(8,128)(2,1)S(1)}, bf16[48,4096]{1,0:T(8,128)(2,1)S(1)}, u32[]{:S(2)}, u32[]{:S(2)}) collective-permute-start(bf16[48,4096]{1,0:T(8,128)(2,1)S(1)} %get-tuple-element.19), channel_id=1, source_target_pairs={{0,2},{2,0},{1,3},{3,1},{4,6},{6,4},{5,7},{7,5},{8,10},{10,8},{9,1... | collective-permute-start | bytes 1179656 | tf_op jit(solution)/shard_map/ppermute | solution.py:74
  3.1 6.0 %copy-start.2 = (f32[16,2048]{1,0:T(8,128)S(1)}, f32[16,2048]{1,0:T(8,128)}, u32[]{:S(2)}) copy-start(f32[16,2048]{1,0:T(8,128)} %param.10) | copy-start | bytes 393220
  3.1 6.0 %copy-start.4 = (f32[16,2048]{1,0:T(8,128)S(1)}, f32[16,2048]{1,0:T(8,128)}, u32[]{:S(2)}) copy-start(f32[16,2048]{1,0:T(8,128)} %param.9) | copy-start | bytes 393220
  18.3 24.0 %copy-start = (bf16[2048,2048]{1,0:T(8,128)(2,1)S(1)}, bf16[2048,2048]{1,0:T(8,128)(2,1)}, u32[]{:S(2)}) copy-start(bf16[2048,2048]{1,0:T(8,128)(2,1)} %fusion.3) | copy-start | bytes 25165828
  21.6 5.5 %collective-permute-start.1 = (bf16[48,2048]{1,0:T(8,128)(2,1)S(1)}, bf16[48,2048]{1,0:T(8,128)(2,1)S(1)}, u32[]{:S(2)}, u32[]{:S(2)}) collective-permute-start(bf16[48,2048]{1,0:T(8,128)(2,1)S(1)} %bitcast.102), channel_id=1, source_target_pairs={{0,4},{4,8},{8,12},{12,0},{1,5},{5,9},{9,13},{13,1},{2,6},{6,10},{... | collective-permute-start | bytes 589832 | tf_op jit(solution)/shard_map/ppermute | solution.py:114
  23.0 15.8 %collective-permute-start.2 = (bf16[48,2048]{1,0:T(8,128)(2,1)S(1)}, bf16[48,2048]{1,0:T(8,128)(2,1)S(1)}, u32[]{:S(2)}, u32[]{:S(2)}) collective-permute-start(bf16[48,2048]{1,0:T(8,128)(2,1)S(1)} %bitcast.101), channel_id=1, source_target_pairs={{0,8},{4,12},{8,0},{12,4},{1,9},{5,13},{9,1},{13,5},{2,10},{6,14},... | collective-permute-start | bytes 589832 | tf_op jit(solution)/shard_map/ppermute | solution.py:114
  24.2 17.7 %collective-permute-start.3 = (bf16[48,2048]{1,0:T(8,128)(2,1)S(1)}, bf16[48,2048]{1,0:T(8,128)(2,1)S(1)}, u32[]{:S(2)}, u32[]{:S(2)}) collective-permute-start(bf16[48,2048]{1,0:T(8,128)(2,1)S(1)} %bitcast.100), channel_id=1, source_target_pairs={{0,12},{4,0},{8,4},{12,8},{1,13},{5,1},{9,5},{13,9},{2,14},{6,2},{... | collective-permute-start | bytes 589832 | tf_op jit(solution)/shard_map/ppermute | solution.py:114
  41.9 18.7 %collective-permute-start.4 = (bf16[4,48,2048]{2,1,0:T(8,128)(2,1)S(1)}, bf16[4,48,2048]{2,1,0:T(8,128)(2,1)S(1)}, u32[]{:S(2)}, u32[]{:S(2)}) collective-permute-start(bf16[4,48,2048]{2,1,0:T(8,128)(2,1)S(1)} %bitcast_dynamic-update-slice_fusion.5), channel_id=1, source_target_pairs={{0,2},{2,0},{1,3},{3,1},{4,6},{6,4},{5,7},{7,5},{8,10},{10,8},{9,1... | collective-permute-start | bytes 2359304 | tf_op jit(solution)/shard_map/ppermute | solution.py:81
  45.6 21.6 %all-to-all-start = ((f16[4,48,2048]{2,1,0:T(8,128)(2,1)}), f16[4,48,2048]{2,1,0:T(8,128)(2,1)S(1)}, u32[]{:S(2)}, u32[]{:S(2)}) async-start(f16[4,48,2048]{2,1,0:T(8,128)(2,1)} %get-tuple-element.34), calls=%async_computation | async-start | bytes 1572864 | tf_op jit(solution)/shard_map/all_to_all | solution.py:88
  67.2 13.2 %copy-start.8 = (f32[128,7]{0,1:T(8,128)S(1)}, f32[128,7]{0,1:T(8,128)}, u32[]{:S(2)}) copy-start(f32[128,7]{0,1:T(8,128)} %param.11) | copy-start | bytes 10756
  67.2 19.8 %all-to-all-start.1 = ((f16[4,48,2048]{2,1,0:T(8,128)(2,1)}), f16[4,48,2048]{2,1,0:T(8,128)(2,1)S(1)}, u32[]{:S(2)}, u32[]{:S(2)}) async-start(f16[4,48,2048]{2,1,0:T(8,128)(2,1)} %get-tuple-element.32), calls=%async_computation.1 | async-start | bytes 1572864 | tf_op jit(solution)/shard_map/all_to_all | solution.py:88
  72.8 23.6 %collective-permute-start.5 = (bf16[6,2048]{1,0:T(8,128)(2,1)}, bf16[6,2048]{1,0:T(8,128)(2,1)}, u32[]{:S(2)}, u32[]{:S(2)}) collective-permute-start(bf16[6,2048]{1,0:T(8,128)(2,1)} %slice_bitcast_fusion.1), channel_id=1, source_target_pairs={{1,0},{3,2},{5,4},{7,6},{9,8},{11,10},{13,12},{15,14},{17,16},{19,... | collective-permute-start | bytes 73736 | tf_op jit(solution)/shard_map/ppermute | solution.py:13
  78.5 17.8 %collective-permute-start.8 = (bf16[6,2048]{1,0:T(8,128)(2,1)}, bf16[6,2048]{1,0:T(8,128)(2,1)}, u32[]{:S(2)}, u32[]{:S(2)}) collective-permute-start(bf16[6,2048]{1,0:T(8,128)(2,1)} %slice_bitcast_fusion), channel_id=1, source_target_pairs={{1,0},{3,2},{5,4},{7,6},{9,8},{11,10},{13,12},{15,14},{17,16},{19,... | collective-permute-start | bytes 73736 | tf_op jit(solution)/shard_map/ppermute | solution.py:13
  88.6 7.7 %copy-start.6 = (bf16[1,1,96,2048]{3,2,1,0:T(8,128)(2,1)S(1)}, bf16[1,1,96,2048]{3,2,1,0:T(8,128)(2,1)}, u32[]{:S(2)}) copy-start(bf16[1,1,96,2048]{3,2,1,0:T(8,128)(2,1)} %param.12) | copy-start | bytes 1179652
  88.7 7.7 %copy-start.7 = (bf16[1,1,96,2048]{3,2,1,0:T(8,128)(2,1)S(1)}, bf16[1,1,96,2048]{3,2,1,0:T(8,128)(2,1)}, u32[]{:S(2)}) copy-start(bf16[1,1,96,2048]{3,2,1,0:T(8,128)(2,1)} %param.13) | copy-start | bytes 1179652
  89.8 5.7 %collective-permute-start.6 = (bf16[6,2048]{1,0:T(8,128)(2,1)S(1)}, bf16[6,2048]{1,0:T(8,128)(2,1)S(1)}, u32[]{:S(2)}, u32[]{:S(2)}) collective-permute-start(bf16[6,2048]{1,0:T(8,128)(2,1)S(1)} %get-tuple-element.20), channel_id=1, source_target_pairs={{0,1},{2,3},{4,5},{6,7},{8,9},{10,11},{12,13},{14,15},{16,17},{18,... | collective-permute-start | bytes 73736 | tf_op jit(solution)/shard_map/ppermute | solution.py:13
  91.1 5.1 %collective-permute-start.7 = (bf16[6,2048]{1,0:T(8,128)(2,1)S(1)}, bf16[6,2048]{1,0:T(8,128)(2,1)S(1)}, u32[]{:S(2)}, u32[]{:S(2)}) collective-permute-start(bf16[6,2048]{1,0:T(8,128)(2,1)S(1)} %get-tuple-element.21), channel_id=1, source_target_pairs={{1,0},{3,2},{5,4},{7,6},{9,8},{11,10},{13,12},{15,14},{17,16},{19,... | collective-permute-start | bytes 73736 | tf_op jit(solution)/shard_map/ppermute | solution.py:13
  99.7 1.5 copy-start.1
  99.7 12.5 %collective-permute-start.9 = (bf16[96,2048]{1,0:T(8,128)(2,1)}, bf16[96,2048]{1,0:T(8,128)(2,1)}, u32[]{:S(2)}, u32[]{:S(2)}) collective-permute-start(bf16[96,2048]{1,0:T(8,128)(2,1)} %get-tuple-element.11), channel_id=1, source_target_pairs={{0,4},{4,8},{8,12},{12,0},{1,5},{5,9},{9,13},{13,1},{2,6},{6,10},{... | collective-permute-start | bytes 1179656 | tf_op jit(solution)/shard_map/ppermute | solution.py:100
  102.1 32.5 %collective-permute-start.10 = (bf16[96,2048]{1,0:T(8,128)(2,1)}, bf16[96,2048]{1,0:T(8,128)(2,1)S(1)}, u32[]{:S(2)}, u32[]{:S(2)}) collective-permute-start(bf16[96,2048]{1,0:T(8,128)(2,1)} %get-tuple-element.11), channel_id=1, source_target_pairs={{0,8},{4,12},{8,0},{12,4},{1,9},{5,13},{9,1},{13,5},{2,10},{6,14},... | collective-permute-start | bytes 1179656 | tf_op jit(solution)/shard_map/ppermute | solution.py:100
  106.1 33.8 %collective-permute-start.11 = (bf16[96,2048]{1,0:T(8,128)(2,1)}, bf16[96,2048]{1,0:T(8,128)(2,1)S(1)}, u32[]{:S(2)}, u32[]{:S(2)}) collective-permute-start(bf16[96,2048]{1,0:T(8,128)(2,1)} %get-tuple-element.11), channel_id=1, source_target_pairs={{0,12},{4,0},{8,4},{12,8},{1,13},{5,1},{9,5},{13,9},{2,14},{6,2},{... | collective-permute-start | bytes 1179656 | tf_op jit(solution)/shard_map/ppermute | solution.py:100
  140.7 12.0 %copy-start.3 = (f32[16,2048]{1,0:T(8,128)S(1)}, f32[16,2048]{1,0:T(8,128)}, u32[]{:S(2)}) copy-start(f32[16,2048]{1,0:T(8,128)} %param.10) | copy-start | bytes 393220
  140.7 12.0 %copy-start.5 = (f32[16,2048]{1,0:T(8,128)S(1)}, f32[16,2048]{1,0:T(8,128)}, u32[]{:S(2)}) copy-start(f32[16,2048]{1,0:T(8,128)} %param.9) | copy-start | bytes 393220
  152.8 1.5 collective-permute-start.13
  153.4 1.7 %collective-permute-start.12 = (f32[16,2048]{1,0:T(8,128)S(1)}, f32[16,2048]{1,0:T(8,128)S(1)}, u32[]{:S(2)}, u32[]{:S(2)}) collective-permute-start(f32[16,2048]{1,0:T(8,128)S(1)} %get-tuple-element.24), channel_id=1, source_target_pairs={{0,1},{1,0},{2,3},{3,2},{4,5},{5,4},{6,7},{7,6},{8,9},{9,8},{10,11... | collective-permute-start | bytes 393224 | tf_op jit(solution)/shard_map/ppermute | solution.py:123

commit v17 on v14

--- a/solution.py
+++ b/solution.py
@@ -93,20 +93,27 @@
 
 def ring_gather(value, axis):
     devices = lax.axis_size(axis)
-    me = lax.axis_index(axis)
-    gathered = jnp.zeros((devices,) + value.shape, value.dtype)
-    gathered = lax.dynamic_update_index_in_dim(gathered, value, me, 0)
+    blocks = [value]
     for shift in range(1, devices):
-        block = lax.ppermute(value, axis, [(i, (i + shift) % devices) for i in range(devices)])
-        gathered = lax.dynamic_update_index_in_dim(gathered, block, (me + devices - shift) % devices, 0)
-    return gathered
+        blocks.append(lax.ppermute(value, axis, [(i, (i + shift) % devices) for i in range(devices)]))
+    return jnp.stack(blocks)
 
 
-def sum_over_ctx(value):
+def in_shift_order(pieces, axis):
+    devices = lax.axis_size(axis)
+    me = lax.axis_index(axis)
+    return jnp.stack(
+        [lax.dynamic_index_in_dim(pieces, (me + devices - shift) % devices, 0, keepdims=False) for shift in range(devices)]
+    )
+
+
+def sum_over_ctx(first, second):
     devices = lax.axis_size("ctx")
     if devices != 2:
-        return lax.psum(value, "ctx")
-    return value + lax.ppermute(value, "ctx", [(0, 1), (1, 0)])
+        return lax.psum((first, second), "ctx")
+    both = jnp.stack([first, second])
+    total = both + lax.ppermute(both, "ctx", [(0, 1), (1, 0)])
+    return total[0], total[1]
 
 
 def on_device(hidden_in, weight, clip_upper, clip_lower, filters, gate, target):
@@ -154,11 +161,12 @@
     d_proj = d_proj.astype(jnp.bfloat16)
 
     d_all = ring_gather(d_proj, "fsdp").reshape(shards * length, columns)
+    inputs = in_shift_order(mine, "fsdp").reshape(shards * length, rows)
     d_clipped = lax.dot_general(
         inputs, d_all, (((0,), (0,)), ((), ())), preferred_element_type=jnp.float32
     )
     grad_up, grad_low = soft_clip_grads(values, clip_upper, clip_lower, d_clipped)
-    grad_upper, grad_lower = sum_over_ctx(grad_up), sum_over_ctx(grad_low)
+    grad_upper, grad_lower = sum_over_ctx(grad_up, grad_low)
     return (grad_upper, grad_lower)
 
 

time: 155 us -> 164 us (1.058)
  blocking collectives: 21.8 us -> 0 us
  waiting for transfers between devices: 46.5 us -> 60.6 us
  starting transfers between devices: 32 us -> 42.2 us
  other arithmetic: 19.5 us -> 23.7 us
  matrix products: 21.9 us -> 24.6 us
    all_to_all x1 -> x0, blocking collectives: 21.8 us -> none  [rows_of_block(): own_half = lax.all_to_all(pieces, 'fsdp', 0, 0)]
    all_to_all x0 -> x1, waiting for transfers between devices: none -> 10.5 us  [rows_of_block(): own_half = lax.all_to_all(pieces, 'fsdp', 0, 0)]
    all_to_all x2, waiting for transfers between devices: 5.8 us -> 15.6 us  [reduce_partial(): lax.all_to_all(partial.astype(jnp.float16), 'fsdp', 0, 0)]
    ppermute x1, waiting for transfers between devices: 7.74 us -> 0.01 us  [rows_of_block(): other_half = lax.ppermute(own_half, 'seq', [(0, 1), (1, 0)])]
    all_to_all x0 -> x1, starting transfers between devices: none -> 4.76 us  [rows_of_block(): own_half = lax.all_to_all(pieces, 'fsdp', 0, 0)]
    ppermute x4, starting transfers between devices: 11.7 us -> 15.3 us  [from_behind(): return lax.ppermute(value, axis, pairs)]
    dynamic_update_slice x3 -> x0, local copies, waits for them, and re-layouts: 3.33 us -> none  [ring_gather(): lax.dynamic_update_index_in_dim(gathered, block, (me + devices - shift) %...]
    dot_general x2, matrix products: 9.88 us -> 13.2 us  [on_device(): jnp.dot(flat, quant, preferred_element_type=jnp.float32)]
  transfers between devices with their start and end apart: 13 -> 13, of which waited for: 8 -> 7; matrix products, arithmetic and copies ran while one was open for 22% -> 25% of each run, Pallas kernels for 0% -> 0%
where the time goes in v17:
time: 164 us; the launch traced here: 163 us
  waiting for transfers between devices  60.6 us (37%)
  starting transfers between devices  42.2 us (26%)
  matrix products  24.6 us (15%)
  other arithmetic  23.7 us (14%)
  local copies, waits for them, and re-layouts  10.6 us (6%)
    ppermute x3, waiting for transfers between devices, ring_gather(): lax.ppermute(value, axis, [(i, (i + shift) % devices) for i in range(devi...  33.4 us
    all_to_all x2, waiting for transfers between devices, reduce_partial(): lax.all_to_all(partial.astype(jnp.float16), 'fsdp', 0, 0)  15.6 us
    ppermute x4, starting transfers between devices, from_behind(): return lax.ppermute(value, axis, pairs)  15.3 us
    all_to_all x2, starting transfers between devices, reduce_partial(): lax.all_to_all(partial.astype(jnp.float16), 'fsdp', 0, 0)  14.8 us
    dot_general x2, matrix products, on_device(): jnp.dot(flat, quant, preferred_element_type=jnp.float32)  13.2 us
    dot_general x1, matrix products, on_device(): lax.dot_general(inputs, d_all, (((0,), (0,)), ((), ())), preferred_elemen...  11.4 us
    all_to_all x1, waiting for transfers between devices, rows_of_block(): own_half = lax.all_to_all(pieces, 'fsdp', 0, 0)  10.5 us
    convert_element_type x1, other arithmetic, on_device(): quant = soft_clip(values, clip_upper, clip_lower).astype(jnp.bfloat16)  8.94 us
  transfers between devices with their start and end apart: 13, of which 7 were waited for; matrix products, arithmetic and copies ran while one was open for 25% of the time, Pallas kernels for 0%

profile of v17, /device:TPU:9, one launch (start us, length us, event | category | flops | bytes accessed | tf_op | source)
XLA Modules:
  0.0 162.7 jit_solution(9250835955292810429)
XLA Ops:
  0.6 1.2 constant_dynamic-slice_fusion.4
  1.8 1.3 collective-permute-start
  3.1 5.7 %abs_reduce_fusion = bf16[16,2048]{1,0:T(8,128)(2,1)S(1)} fusion(bf16[2048,2048]{1,0:T(8,128)(2,1)} %param.8), kind=kLoop, calls=%fused_computation.15 | loop fusion | flops 16744448 | bytes 8454144 | tf_op jit(solution)/shard_map/reduce_max | solution.py:20
  9.9 8.9 %fusion.3 = bf16[2048,2048]{1,0:T(8,128)(2,1)} fusion(bf16[2048,2048]{1,0:T(8,128)(2,1)} %param.8, f32[16,2048]{1,0:T(8,128)S(1)} %get-tuple-element.10, f32[16,2048]{1,0:T(8,128)S(1)} %get-tuple-element.11, f32[16,2048]{1,0:T(8,128)S(1)} %get-tuple-element.20), kind=kLoop, calls=%fused_computation.5 | loop fusion | flops 25165824 | bytes 17170432 | tf_op jit(solution)/shard_map/convert_element_type | solution.py:126
  18.9 1.1 fusion.23
  20.0 4.8 %all-to-all-start = ((bf16[4,48,2048]{2,1,0:T(8,128)(2,1)}), bf16[4,48,2048]{2,1,0:T(8,128)(2,1)S(1)}, u32[]{:S(2)}, u32[]{:S(2)}) async-start(bf16[4,48,2048]{2,1,0:T(8,128)(2,1)} %fusion.23), calls=%async_computation | async-start | bytes 1572864 | tf_op jit(solution)/shard_map/all_to_all | solution.py:80
  24.7 1.4 slice_bitcast_fusion.3
  26.1 4.0 %collective-permute-start.2 = (bf16[6,2048]{1,0:T(8,128)(2,1)}, bf16[6,2048]{1,0:T(8,128)(2,1)}, u32[]{:S(2)}, u32[]{:S(2)}) collective-permute-start(bf16[6,2048]{1,0:T(8,128)(2,1)} %slice_bitcast_fusion.3), channel_id=1, source_target_pairs={{1,0},{3,2},{5,4},{7,6},{9,8},{11,10},{13,12},{15,14},{17,16},{19,... | collective-permute-start | bytes 73736 | tf_op jit(solution)/shard_map/ppermute | solution.py:13
  30.1 10.5 %all-to-all-done = bf16[4,48,2048]{2,1,0:T(8,128)(2,1)S(1)} async-done(((bf16[4,48,2048]{2,1,0:T(8,128)(2,1)}), bf16[4,48,2048]{2,1,0:T(8,128)(2,1)S(1)}, u32[]{:S(2)}, u32[]{:S(2)}) %all-to-all-start) | async-done | bytes 786464 | tf_op jit(solution)/shard_map/all_to_all | solution.py:80
  40.9 6.6 %fusion.31 = (f16[4,48,2048]{2,1,0:T(8,128)(2,1)}, f32[4,48,2048]{2,1,0:T(8,128)}) fusion(bf16[4,48,2048]{2,1,0:T(8,128)(2,1)S(1)} %all-to-all-done, bf16[2048,2048]{1,0:T(8,128)(2,1)} %fusion.3), kind=kOutput, calls=%fused_computation.87 | convolution fusion | flops 1611005952 | bytes 11534336 | tf_op jit(solution)/shard_map/dot_general | solution.py:134
  47.5 7.3 %all-to-all-start.1 = ((f16[4,48,2048]{2,1,0:T(8,128)(2,1)}), f16[4,48,2048]{2,1,0:T(8,128)(2,1)S(1)}, u32[]{:S(2)}, u32[]{:S(2)}) async-start(f16[4,48,2048]{2,1,0:T(8,128)(2,1)} %get-tuple-element.34), calls=%async_computation.1 | async-start | bytes 1572864 | tf_op jit(solution)/shard_map/all_to_all | solution.py:88
  54.8 1.4 slice_bitcast_fusion.2
  56.2 4.5 %collective-permute-start.5 = (bf16[6,2048]{1,0:T(8,128)(2,1)}, bf16[6,2048]{1,0:T(8,128)(2,1)}, u32[]{:S(2)}, u32[]{:S(2)}) collective-permute-start(bf16[6,2048]{1,0:T(8,128)(2,1)} %slice_bitcast_fusion.2), channel_id=1, source_target_pairs={{1,0},{3,2},{5,4},{7,6},{9,8},{11,10},{13,12},{15,14},{17,16},{19,... | collective-permute-start | bytes 73736 | tf_op jit(solution)/shard_map/ppermute | solution.py:13
  61.7 6.6 %fusion.30 = (f16[4,48,2048]{2,1,0:T(8,128)(2,1)}, f32[4,48,2048]{2,1,0:T(8,128)}) fusion(bf16[4,48,2048]{2,1,0:T(8,128)(2,1)S(1)} %collective-permute-done.1, bf16[2048,2048]{1,0:T(8,128)(2,1)} %fusion.3), kind=kOutput, calls=%fused_computation.86 | convolution fusion | flops 1611005952 | bytes 11534336 | tf_op jit(solution)/shard_map/dot_general | solution.py:134
  68.3 2.0 %all-to-all-done.1 = f16[4,48,2048]{2,1,0:T(8,128)(2,1)S(1)} async-done(((f16[4,48,2048]{2,1,0:T(8,128)(2,1)}), f16[4,48,2048]{2,1,0:T(8,128)(2,1)S(1)}, u32[]{:S(2)}, u32[]{:S(2)}) %all-to-all-start.1) | async-done | bytes 786464 | tf_op jit(solution)/shard_map/all_to_all | solution.py:88
  70.3 7.5 %all-to-all-start.2 = ((f16[4,48,2048]{2,1,0:T(8,128)(2,1)}), f16[4,48,2048]{2,1,0:T(8,128)(2,1)S(1)}, u32[]{:S(2)}, u32[]{:S(2)}) async-start(f16[4,48,2048]{2,1,0:T(8,128)(2,1)} %get-tuple-element.32), calls=%async_computation.2 | async-start | bytes 1572864 | tf_op jit(solution)/shard_map/all_to_all | solution.py:88
  78.9 1.1 constant_dynamic-slice_fusion.3
  80.0 13.6 %all-to-all-done.2 = f16[4,48,2048]{2,1,0:T(8,128)(2,1)S(1)} async-done(((f16[4,48,2048]{2,1,0:T(8,128)(2,1)}), f16[4,48,2048]{2,1,0:T(8,128)(2,1)S(1)}, u32[]{:S(2)}, u32[]{:S(2)}) %all-to-all-start.2) | async-done | bytes 786464 | tf_op jit(solution)/shard_map/all_to_all | solution.py:88
  94.1 1.1 fusion.25
  95.2 1.0 fusion.24
  96.9 1.3 collective-permute-start.3
  98.2 5.5 %collective-permute-start.4 = (bf16[6,2048]{1,0:T(8,128)(2,1)}, bf16[6,2048]{1,0:T(8,128)(2,1)}, u32[]{:S(2)}, u32[]{:S(2)}) collective-permute-start(bf16[6,2048]{1,0:T(8,128)(2,1)} %get-tuple-element.19), channel_id=1, source_target_pairs={{1,0},{3,2},{5,4},{7,6},{9,8},{11,10},{13,12},{15,14},{17,16},{19,... | collective-permute-start | bytes 73736 | tf_op jit(solution)/shard_map/ppermute | solution.py:13
  103.9 0.9 copy.19
  104.8 1.0 maximum_convert_fusion
  106.0 1.8 %convert_multiply_fusion = f32[102,2048]{1,0:T(8,128)S(1)} fusion(f32[108,2048]{1,0:T(8,128)S(1)} %maximum_convert_fusion, bf16[6,2048]{1,0:T(8,128)(2,1)} %collective-permute-done.2, bf16[96,2048]{1,0:T(8,128)(2,1)S(1)} %bitcast.94, bf16[6,2048]{1,0:T(8,128)(2,1)} %collective-permute-done.5, bf16[96,2048]{1,0:T(8,128)(2,1)S(1)} %bitcast.95, ...), kind=kLoop, calls=%fused_computation.20 | loop fusion | flops 5222400 | bytes 7577600 | tf_op jit(solution)/shard_map/mul | solution.py:157
  108.5 1.2 collective-permute-start.6
  109.8 3.9 %collective-permute-start.7 = (bf16[96,2048]{1,0:T(8,128)(2,1)S(1)}, bf16[96,2048]{1,0:T(8,128)(2,1)S(1)}, u32[]{:S(2)}, u32[]{:S(2)}) collective-permute-start(bf16[96,2048]{1,0:T(8,128)(2,1)S(1)} %fusion.17), channel_id=1, source_target_pairs={{0,8},{4,12},{8,0},{12,4},{1,9},{5,13},{9,1},{13,5},{2,10},{6,14},... | collective-permute-start | bytes 1179656 | tf_op jit(solution)/shard_map/ppermute | solution.py:98
  114.3 6.6 %collective-permute-done.6 = bf16[96,2048]{1,0:T(8,128)(2,1)S(1)} collective-permute-done((bf16[96,2048]{1,0:T(8,128)(2,1)S(1)}, bf16[96,2048]{1,0:T(8,128)(2,1)S(1)}, u32[]{:S(2)}, u32[]{:S(2)}) %collective-permute-start.6) | collective-permute-done | bytes 393248 | tf_op jit(solution)/shard_map/ppermute | solution.py:98
  121.0 22.9 %collective-permute-done.7 = bf16[96,2048]{1,0:T(8,128)(2,1)S(1)} collective-permute-done((bf16[96,2048]{1,0:T(8,128)(2,1)S(1)}, bf16[96,2048]{1,0:T(8,128)(2,1)S(1)}, u32[]{:S(2)}, u32[]{:S(2)}) %collective-permute-start.7) | collective-permute-done | bytes 393248 | tf_op jit(solution)/shard_map/ppermute | solution.py:98
  143.9 3.8 %collective-permute-done.8 = bf16[96,2048]{1,0:T(8,128)(2,1)S(1)} collective-permute-done((bf16[96,2048]{1,0:T(8,128)(2,1)S(1)}, bf16[96,2048]{1,0:T(8,128)(2,1)S(1)}, u32[]{:S(2)}, u32[]{:S(2)}) %collective-permute-start.8) | collective-permute-done | bytes 393248 | tf_op jit(solution)/shard_map/ppermute | solution.py:98
  148.7 11.4 %multiply_reduce_fusion.1 = (f32[16,2048]{1,0:T(8,128)S(1)}, f32[16,2048]{1,0:T(8,128)S(1)}) fusion(bf16[2048,2048]{1,0:T(8,128)(2,1)S(1)} %bitcast.89, f32[16,2048]{1,0:T(8,128)S(1)} %copy-done.6, f32[16,2048]{1,0:T(8,128)S(1)} %copy-done.8, bf16[16,128,384]{2,1,0:T(8,128)(2,1)S(1)} %bitcast.91, bf16[384,2048,1]{1,0,2:T(8,128)(2,1)S(1)} %bitcast.92), kind=kOutput, calls=%fused_computation.7 | convolution fusion | flops 3275685888 | bytes 12058624 | tf_op jit(solution)/shard_map/dot_general | solution.py:165
  160.8 1.2 collective-permute-done.9
  (80 shorter events, 8.7 us)
Async XLA Ops:
  1.8 17.1 %collective-permute-start = (bf16[48,4096]{1,0:T(8,128)(2,1)S(1)}, bf16[48,4096]{1,0:T(8,128)(2,1)S(1)}, u32[]{:S(2)}, u32[]{:S(2)}) collective-permute-start(bf16[48,4096]{1,0:T(8,128)(2,1)S(1)} %get-tuple-element.17), channel_id=1, source_target_pairs={{0,2},{2,0},{1,3},{3,1},{4,6},{6,4},{5,7},{7,5},{8,10},{10,8},{9,1... | collective-permute-start | bytes 1179656 | tf_op jit(solution)/shard_map/ppermute | solution.py:74
  8.8 10.1 %copy-start.3 = (bf16[16,2048]{1,0:T(8,128)(2,1)}, bf16[16,2048]{1,0:T(8,128)(2,1)S(1)}, u32[]{:S(2)}) copy-start(bf16[16,2048]{1,0:T(8,128)(2,1)S(1)} %abs_reduce_fusion) | copy-start | bytes 196612
  9.9 9.0 %copy-start.5 = (f32[16,2048]{1,0:T(8,128)}, f32[16,2048]{1,0:T(8,128)S(1)}, u32[]{:S(2)}) copy-start(f32[16,2048]{1,0:T(8,128)S(1)} %get-tuple-element.10) | copy-start | bytes 393220
  9.9 9.0 %copy-start.7 = (f32[16,2048]{1,0:T(8,128)}, f32[16,2048]{1,0:T(8,128)S(1)}, u32[]{:S(2)}) copy-start(f32[16,2048]{1,0:T(8,128)S(1)} %get-tuple-element.20) | copy-start | bytes 393220
  20.0 20.7 %all-to-all-start = ((bf16[4,48,2048]{2,1,0:T(8,128)(2,1)}), bf16[4,48,2048]{2,1,0:T(8,128)(2,1)S(1)}, u32[]{:S(2)}, u32[]{:S(2)}) async-start(bf16[4,48,2048]{2,1,0:T(8,128)(2,1)} %fusion.23), calls=%async_computation | async-start | bytes 1572864 | tf_op jit(solution)/shard_map/all_to_all | solution.py:80
  26.1 79.7 %collective-permute-start.2 = (bf16[6,2048]{1,0:T(8,128)(2,1)}, bf16[6,2048]{1,0:T(8,128)(2,1)}, u32[]{:S(2)}, u32[]{:S(2)}) collective-permute-start(bf16[6,2048]{1,0:T(8,128)(2,1)} %slice_bitcast_fusion.3), channel_id=1, source_target_pairs={{1,0},{3,2},{5,4},{7,6},{9,8},{11,10},{13,12},{15,14},{17,16},{19,... | collective-permute-start | bytes 73736 | tf_op jit(solution)/shard_map/ppermute | solution.py:13
  40.6 21.1 %collective-permute-start.1 = (bf16[4,48,2048]{2,1,0:T(8,128)(2,1)S(1)}, bf16[4,48,2048]{2,1,0:T(8,128)(2,1)S(1)}, u32[]{:S(2)}, u32[]{:S(2)}) collective-permute-start(bf16[4,48,2048]{2,1,0:T(8,128)(2,1)S(1)} %all-to-all-done), channel_id=1, source_target_pairs={{0,2},{2,0},{1,3},{3,1},{4,6},{6,4},{5,7},{7,5},{8,10},{10,8},{9,1... | collective-permute-start | bytes 2359304 | tf_op jit(solution)/shard_map/ppermute | solution.py:81
  47.5 13.2 %copy-start.20 = (f32[128,7]{0,1:T(8,128)S(1)}, f32[128,7]{0,1:T(8,128)}, u32[]{:S(2)}) copy-start(f32[128,7]{0,1:T(8,128)} %param.11) | copy-start | bytes 10756
  47.5 22.8 %all-to-all-start.1 = ((f16[4,48,2048]{2,1,0:T(8,128)(2,1)}), f16[4,48,2048]{2,1,0:T(8,128)(2,1)S(1)}, u32[]{:S(2)}, u32[]{:S(2)}) async-start(f16[4,48,2048]{2,1,0:T(8,128)(2,1)} %get-tuple-element.34), calls=%async_computation.1 | async-start | bytes 1572864 | tf_op jit(solution)/shard_map/all_to_all | solution.py:88
  56.2 49.7 %collective-permute-start.5 = (bf16[6,2048]{1,0:T(8,128)(2,1)}, bf16[6,2048]{1,0:T(8,128)(2,1)}, u32[]{:S(2)}, u32[]{:S(2)}) collective-permute-start(bf16[6,2048]{1,0:T(8,128)(2,1)} %slice_bitcast_fusion.2), channel_id=1, source_target_pairs={{1,0},{3,2},{5,4},{7,6},{9,8},{11,10},{13,12},{15,14},{17,16},{19,... | collective-permute-start | bytes 73736 | tf_op jit(solution)/shard_map/ppermute | solution.py:13
  70.3 23.2 %all-to-all-start.2 = ((f16[4,48,2048]{2,1,0:T(8,128)(2,1)}), f16[4,48,2048]{2,1,0:T(8,128)(2,1)S(1)}, u32[]{:S(2)}, u32[]{:S(2)}) async-start(f16[4,48,2048]{2,1,0:T(8,128)(2,1)} %get-tuple-element.32), calls=%async_computation.2 | async-start | bytes 1572864 | tf_op jit(solution)/shard_map/all_to_all | solution.py:88
  78.9 14.7 %copy-start.21 = (pred[4]{0:T(512)(128)(4,1)S(1)}, pred[4]{0:T(512)(128)(4,1)}, u32[]{:S(2)}) copy-start(pred[4]{0:T(512)(128)(4,1)} %iota_compare_fusion) | copy-start | bytes 16
  94.0 9.7 %copy-start = (bf16[1,96,2048]{2,1,0:T(8,128)(2,1)S(1)}, bf16[1,96,2048]{2,1,0:T(8,128)(2,1)}, u32[]{:S(2)}) copy-start(bf16[1,96,2048]{2,1,0:T(8,128)(2,1)} %get-tuple-element.13) | copy-start | bytes 1179652
  94.0 9.7 %copy-start.1 = (bf16[1,96,2048]{2,1,0:T(8,128)(2,1)S(1)}, bf16[1,96,2048]{2,1,0:T(8,128)(2,1)}, u32[]{:S(2)}) copy-start(bf16[1,96,2048]{2,1,0:T(8,128)(2,1)} %get-tuple-element.14) | copy-start | bytes 1179652
  94.1 9.7 %copy-start.2 = (bf16[1,96,2048]{2,1,0:T(8,128)(2,1)S(1)}, bf16[1,96,2048]{2,1,0:T(8,128)(2,1)}, u32[]{:S(2)}) copy-start(bf16[1,96,2048]{2,1,0:T(8,128)(2,1)} %get-tuple-element.15) | copy-start | bytes 1179652
  96.9 7.9 %collective-permute-start.3 = (bf16[6,2048]{1,0:T(8,128)(2,1)}, bf16[6,2048]{1,0:T(8,128)(2,1)}, u32[]{:S(2)}, u32[]{:S(2)}) collective-permute-start(bf16[6,2048]{1,0:T(8,128)(2,1)} %get-tuple-element.18), channel_id=1, source_target_pairs={{0,1},{2,3},{4,5},{6,7},{8,9},{10,11},{12,13},{14,15},{16,17},{18,... | collective-permute-start | bytes 73736 | tf_op jit(solution)/shard_map/ppermute | solution.py:13
  98.2 6.6 %collective-permute-start.4 = (bf16[6,2048]{1,0:T(8,128)(2,1)}, bf16[6,2048]{1,0:T(8,128)(2,1)}, u32[]{:S(2)}, u32[]{:S(2)}) collective-permute-start(bf16[6,2048]{1,0:T(8,128)(2,1)} %get-tuple-element.19), channel_id=1, source_target_pairs={{1,0},{3,2},{5,4},{7,6},{9,8},{11,10},{13,12},{15,14},{17,16},{19,... | collective-permute-start | bytes 73736 | tf_op jit(solution)/shard_map/ppermute | solution.py:13
  104.8 1.1 copy-start.14
  105.9 1.9 %copy-start.15 = (f32[1,2048]{1,0:T(1,128)S(1)}, f32[1,2048]{1,0:T(1,128)}, u32[]{:S(2)}) copy-start(f32[1,2048]{1,0:T(1,128)} %get-tuple-element.27) | copy-start | bytes 24580
  105.9 1.9 %copy-start.16 = (f32[1,2048]{1,0:T(1,128)S(1)}, f32[1,2048]{1,0:T(1,128)}, u32[]{:S(2)}) copy-start(f32[1,2048]{1,0:T(1,128)} %get-tuple-element.28) | copy-start | bytes 24580
  105.9 1.9 %copy-start.17 = (f32[1,2048]{1,0:T(1,128)S(1)}, f32[1,2048]{1,0:T(1,128)}, u32[]{:S(2)}) copy-start(f32[1,2048]{1,0:T(1,128)} %get-tuple-element.29) | copy-start | bytes 24580
  106.0 1.9 %copy-start.18 = (f32[1,2048]{1,0:T(1,128)S(1)}, f32[1,2048]{1,0:T(1,128)}, u32[]{:S(2)}) copy-start(f32[1,2048]{1,0:T(1,128)} %get-tuple-element.30) | copy-start | bytes 24580
  106.0 1.9 %copy-start.19 = (f32[1,2048]{1,0:T(1,128)S(1)}, f32[1,2048]{1,0:T(1,128)}, u32[]{:S(2)}) copy-start(f32[1,2048]{1,0:T(1,128)} %get-tuple-element.31) | copy-start | bytes 24580
  106.0 41.9 %slice-start = ((s8[8388608]{0:T(1024)(128)(4,1)}), s8[4194304]{0:T(1024)(128)(4,1)S(1)}, s32[]{:S(2)}) async-start(s8[8388608]{0:T(1024)(128)(4,1)} %bitcast.88), calls=%async_computation.3 | async-start | bytes 8388608
  107.9 40.1 %slice-start.1 = ((s8[8388608]{0:T(1024)(128)(4,1)}), s8[4194304]{0:T(1024)(128)(4,1)S(1)}, s32[]{:S(2)}) async-start(s8[8388608]{0:T(1024)(128)(4,1)} %bitcast.88), calls=%async_computation.4 | async-start | bytes 8388608
  108.5 12.4 %collective-permute-start.6 = (bf16[96,2048]{1,0:T(8,128)(2,1)S(1)}, bf16[96,2048]{1,0:T(8,128)(2,1)S(1)}, u32[]{:S(2)}, u32[]{:S(2)}) collective-permute-start(bf16[96,2048]{1,0:T(8,128)(2,1)S(1)} %fusion.17), channel_id=1, source_target_pairs={{0,4},{4,8},{8,12},{12,0},{1,5},{5,9},{9,13},{13,1},{2,6},{6,10},{... | collective-permute-start | bytes 1179656 | tf_op jit(solution)/shard_map/ppermute | solution.py:98
  109.8 34.1 %collective-permute-start.7 = (bf16[96,2048]{1,0:T(8,128)(2,1)S(1)}, bf16[96,2048]{1,0:T(8,128)(2,1)S(1)}, u32[]{:S(2)}, u32[]{:S(2)}) collective-permute-start(bf16[96,2048]{1,0:T(8,128)(2,1)S(1)} %fusion.17), channel_id=1, source_target_pairs={{0,8},{4,12},{8,0},{12,4},{1,9},{5,13},{9,1},{13,5},{2,10},{6,14},... | collective-permute-start | bytes 1179656 | tf_op jit(solution)/shard_map/ppermute | solution.py:98
  113.7 34.0 %collective-permute-start.8 = (bf16[96,2048]{1,0:T(8,128)(2,1)S(1)}, bf16[96,2048]{1,0:T(8,128)(2,1)S(1)}, u32[]{:S(2)}, u32[]{:S(2)}) collective-permute-start(bf16[96,2048]{1,0:T(8,128)(2,1)S(1)} %fusion.17), channel_id=1, source_target_pairs={{0,12},{4,0},{8,4},{12,8},{1,13},{5,1},{9,5},{13,9},{2,14},{6,2},{... | collective-permute-start | bytes 1179656 | tf_op jit(solution)/shard_map/ppermute | solution.py:98
  148.7 11.4 %copy-start.4 = (bf16[16,2048]{1,0:T(8,128)(2,1)S(1)}, bf16[16,2048]{1,0:T(8,128)(2,1)}, u32[]{:S(2)}) copy-start(bf16[16,2048]{1,0:T(8,128)(2,1)} %copy-done.3) | copy-start | bytes 196612
  148.7 11.4 %copy-start.10 = (f32[16,2048]{1,0:T(8,128)S(1)}, f32[16,2048]{1,0:T(8,128)}, u32[]{:S(2)}) copy-start(f32[16,2048]{1,0:T(8,128)} %param.10) | copy-start | bytes 393220
  148.7 11.4 %copy-start.12 = (f32[16,2048]{1,0:T(8,128)S(1)}, f32[16,2048]{1,0:T(8,128)}, u32[]{:S(2)}) copy-start(f32[16,2048]{1,0:T(8,128)} %param.9) | copy-start | bytes 393220
  160.2 1.8 %collective-permute-start.9 = (f32[2,16,2048]{2,1,0:T(8,128)S(1)}, f32[2,16,2048]{2,1,0:T(8,128)S(1)}, u32[]{:S(2)}, u32[]{:S(2)}) collective-permute-start(f32[2,16,2048]{2,1,0:T(8,128)S(1)} %pad_maximum_fusion.2), channel_id=1, source_target_pairs={{0,1},{1,0},{2,3},{3,2},{4,5},{5,4},{6,7},{7,6},{8,9},{9,8},{10,11... | collective-permute-start | bytes 786440 | tf_op jit(solution)/shard_map/ppermute | solution.py:115
  (5 other events, 4.8 us)

commit v18 on v14

--- a/solution.py
+++ b/solution.py
@@ -102,11 +102,13 @@
     return gathered
 
 
-def sum_over_ctx(value):
+def sum_over_ctx(first, second):
     devices = lax.axis_size("ctx")
     if devices != 2:
-        return lax.psum(value, "ctx")
-    return value + lax.ppermute(value, "ctx", [(0, 1), (1, 0)])
+        return lax.psum((first, second), "ctx")
+    both = jnp.stack([first, second])
+    total = both + lax.ppermute(both, "ctx", [(0, 1), (1, 0)])
+    return total[0], total[1]
 
 
 def on_device(hidden_in, weight, clip_upper, clip_lower, filters, gate, target):
@@ -158,7 +160,7 @@
         inputs, d_all, (((0,), (0,)), ((), ())), preferred_element_type=jnp.float32
     )
     grad_up, grad_low = soft_clip_grads(values, clip_upper, clip_lower, d_clipped)
-    grad_upper, grad_lower = sum_over_ctx(grad_up), sum_over_ctx(grad_low)
+    grad_upper, grad_lower = sum_over_ctx(grad_up, grad_low)
     return (grad_upper, grad_lower)
 
 

time: 155 us -> 155 us (level)
  transfers between devices with their start and end apart: 13 -> 12, of which waited for: 8 -> 8; matrix products, arithmetic and copies ran while one was open for 22% -> 22% of each run, Pallas kernels for 0% -> 0%
where the time goes in v18:
time: 155 us; the launch traced here: 154 us
  waiting for transfers between devices  46.7 us (30%)
  starting transfers between devices  31.9 us (21%)
  matrix products  21.9 us (14%)
  blocking collectives  21.8 us (14%)
  other arithmetic  18.2 us (12%)
  local copies, waits for them, and re-layouts  12.2 us (8%)
    ppermute x3, waiting for transfers between devices, ring_gather(): lax.ppermute(value, axis, [(i, (i + shift) % devices) for i in range(devi...  31.3 us
    all_to_all x1, blocking collectives, rows_of_block(): own_half = lax.all_to_all(pieces, 'fsdp', 0, 0)  21.8 us
    all_to_all x2, starting transfers between devices, reduce_partial(): lax.all_to_all(partial.astype(jnp.float16), 'fsdp', 0, 0)  13 us
    dot_general x1, matrix products, on_device(): lax.dot_general(inputs, d_all, (((0,), (0,)), ((), ())), preferred_elemen...  12.1 us
    ppermute x4, starting transfers between devices, from_behind(): return lax.ppermute(value, axis, pairs)  11.7 us
    dot_general x2, matrix products, on_device(): jnp.dot(flat, quant, preferred_element_type=jnp.float32)  9.88 us
    ppermute x1, waiting for transfers between devices, rows_of_block(): other_half = lax.ppermute(own_half, 'seq', [(0, 1), (1, 0)])  7.74 us
    convert_element_type x1, other arithmetic, on_device(): quant = soft_clip(values, clip_upper, clip_lower).astype(jnp.bfloat16)  6.03 us
  transfers between devices with their start and end apart: 12, of which 8 were waited for; matrix products, arithmetic and copies ran while one was open for 22% of the time, Pallas kernels for 0%

profile of v18, /device:TPU:9, one launch (start us, length us, event | category | flops | bytes accessed | tf_op | source)
XLA Modules:
  0.0 153.8 jit_solution(11075376543931958104)
XLA Ops:
  0.7 1.2 constant_dynamic-slice_fusion
  1.9 1.3 collective-permute-start
  3.2 5.7 %abs_reduce_fusion = bf16[16,2048]{1,0:T(8,128)(2,1)S(1)} fusion(bf16[2048,2048]{1,0:T(8,128)(2,1)} %param.8), kind=kLoop, calls=%fused_computation.15 | loop fusion | flops 16744448 | bytes 8454144 | tf_op jit(solution)/shard_map/reduce_max | solution.py:20
  9.4 6.0 %fusion.3 = bf16[2048,2048]{1,0:T(8,128)(2,1)S(1)} fusion(bf16[2048,2048]{1,0:T(8,128)(2,1)} %param.8, f32[16,2048]{1,0:T(8,128)S(1)} %get-tuple-element.12, f32[16,2048]{1,0:T(8,128)S(1)} %get-tuple-element.13, f32[16,2048]{1,0:T(8,128)S(1)} %get-tuple-element.18), kind=kLoop, calls=%fused_computation.5 | loop fusion | flops 25165824 | bytes 17170432 | tf_op jit(solution)/shard_map/convert_element_type | solution.py:121
  15.6 21.8 %all_to_all.15 = bf16[4,48,2048]{2,1,0:T(8,128)(2,1)S(1)} all-to-all(bf16[4,48,2048]{2,1,0:T(8,128)(2,1)S(1)} %fusion.23), channel_id=1, replica_groups=mesh['parts'=2,'fsdp'=4,'seq'=2,'ctx'=2] {'fsdp'}, dimensions={0} | all-to-all | bytes 1572864 | tf_op jit(solution)/shard_map/all_to_all | solution.py:80
  37.7 3.3 %fusion.32 = (f16[4,48,2048]{2,1,0:T(8,128)(2,1)}, f32[4,48,2048]{2,1,0:T(8,128)}) fusion(bf16[4,48,2048]{2,1,0:T(8,128)(2,1)S(1)} %all_to_all.15, bf16[2048,2048]{1,0:T(8,128)(2,1)S(1)} %fusion.3), kind=kOutput, calls=%fused_computation.85 | convolution fusion | flops 1611005952 | bytes 11534336 | tf_op jit(solution)/shard_map/dot_general | solution.py:129
  41.1 5.5 %all-to-all-start.1 = ((f16[4,48,2048]{2,1,0:T(8,128)(2,1)}), f16[4,48,2048]{2,1,0:T(8,128)(2,1)S(1)}, u32[]{:S(2)}, u32[]{:S(2)}) async-start(f16[4,48,2048]{2,1,0:T(8,128)(2,1)} %get-tuple-element.32), calls=%async_computation.1 | async-start | bytes 1572864 | tf_op jit(solution)/shard_map/all_to_all | solution.py:88
  46.5 7.7 %collective-permute-done.1 = bf16[4,48,2048]{2,1,0:T(8,128)(2,1)S(1)} collective-permute-done((bf16[4,48,2048]{2,1,0:T(8,128)(2,1)S(1)}, bf16[4,48,2048]{2,1,0:T(8,128)(2,1)S(1)}, u32[]{:S(2)}, u32[]{:S(2)}) %collective-permute-start.1) | collective-permute-done | bytes 786464 | tf_op jit(solution)/shard_map/ppermute | solution.py:81
  54.3 6.6 %fusion.31 = (f16[4,48,2048]{2,1,0:T(8,128)(2,1)}, f32[4,48,2048]{2,1,0:T(8,128)}) fusion(bf16[4,48,2048]{2,1,0:T(8,128)(2,1)S(1)} %collective-permute-done.1, bf16[2048,2048]{1,0:T(8,128)(2,1)} %copy-done), kind=kOutput, calls=%fused_computation.84 | convolution fusion | flops 1611005952 | bytes 11534336 | tf_op jit(solution)/shard_map/dot_general | solution.py:129
  60.8 1.2 all-to-all-done.1
  62.1 7.5 %all-to-all-start.2 = ((f16[4,48,2048]{2,1,0:T(8,128)(2,1)}), f16[4,48,2048]{2,1,0:T(8,128)(2,1)S(1)}, u32[]{:S(2)}, u32[]{:S(2)}) async-start(f16[4,48,2048]{2,1,0:T(8,128)(2,1)} %get-tuple-element.30), calls=%async_computation.2 | async-start | bytes 1572864 | tf_op jit(solution)/shard_map/all_to_all | solution.py:88
  69.6 1.4 slice_bitcast_fusion.3
  71.0 4.2 %collective-permute-start.2 = (bf16[6,2048]{1,0:T(8,128)(2,1)}, bf16[6,2048]{1,0:T(8,128)(2,1)}, u32[]{:S(2)}, u32[]{:S(2)}) collective-permute-start(bf16[6,2048]{1,0:T(8,128)(2,1)} %slice_bitcast_fusion.3), channel_id=1, source_target_pairs={{1,0},{3,2},{5,4},{7,6},{9,8},{11,10},{13,12},{15,14},{17,16},{19,... | collective-permute-start | bytes 73736 | tf_op jit(solution)/shard_map/ppermute | solution.py:13
  75.2 1.4 slice_bitcast_fusion.2
  76.6 1.9 %collective-permute-start.5 = (bf16[6,2048]{1,0:T(8,128)(2,1)}, bf16[6,2048]{1,0:T(8,128)(2,1)}, u32[]{:S(2)}, u32[]{:S(2)}) collective-permute-start(bf16[6,2048]{1,0:T(8,128)(2,1)} %slice_bitcast_fusion.2), channel_id=1, source_target_pairs={{1,0},{3,2},{5,4},{7,6},{9,8},{11,10},{13,12},{15,14},{17,16},{19,... | collective-permute-start | bytes 73736 | tf_op jit(solution)/shard_map/ppermute | solution.py:13
  78.5 1.0 broadcast_in_dim.41
  79.4 1.3 reshape.60
  80.7 4.6 %all-to-all-done.2 = f16[4,48,2048]{2,1,0:T(8,128)(2,1)S(1)} async-done(((f16[4,48,2048]{2,1,0:T(8,128)(2,1)}), f16[4,48,2048]{2,1,0:T(8,128)(2,1)S(1)}, u32[]{:S(2)}, u32[]{:S(2)}) %all-to-all-start.2) | async-done | bytes 786464 | tf_op jit(solution)/shard_map/all_to_all | solution.py:88
  85.8 1.0 fusion.25
  86.9 1.0 fusion.24
  87.9 1.3 collective-permute-start.3
  89.2 4.3 %collective-permute-start.4 = (bf16[6,2048]{1,0:T(8,128)(2,1)S(1)}, bf16[6,2048]{1,0:T(8,128)(2,1)S(1)}, u32[]{:S(2)}, u32[]{:S(2)}) collective-permute-start(bf16[6,2048]{1,0:T(8,128)(2,1)S(1)} %get-tuple-element.17), channel_id=1, source_target_pairs={{1,0},{3,2},{5,4},{7,6},{9,8},{11,10},{13,12},{15,14},{17,16},{19,... | collective-permute-start | bytes 73736 | tf_op jit(solution)/shard_map/ppermute | solution.py:13
  94.5 2.0 %convert_multiply_fusion = f32[102,2048]{1,0:T(8,128)S(1)} fusion(f32[108,2048]{1,0:T(8,128)S(1)} %maximum_convert_fusion, bf16[6,2048]{1,0:T(8,128)(2,1)} %collective-permute-done.2, bf16[96,2048]{1,0:T(8,128)(2,1)} %bitcast.95, bf16[6,2048]{1,0:T(8,128)(2,1)} %collective-permute-done.5, bf16[96,2048]{1,0:T(8,128)(2,1)} %bitcast.96, f32[2048]{0:T(1024)S(1)} %bitcast.101, ...), kind=kLoop, calls=%fused_computation.18 | loop fusion | flops 5222400 | bytes 7577600 | tf_op jit(solution)/shard_map/mul | solution.py:152
  96.7 1.4 bitcast_dynamic-update-slice_fusion.3
  98.1 1.2 collective-permute-start.6
  100.6 4.0 %collective-permute-start.7 = (bf16[96,2048]{1,0:T(8,128)(2,1)}, bf16[96,2048]{1,0:T(8,128)(2,1)S(1)}, u32[]{:S(2)}, u32[]{:S(2)}) collective-permute-start(bf16[96,2048]{1,0:T(8,128)(2,1)} %get-tuple-element.11), channel_id=1, source_target_pairs={{0,8},{4,12},{8,0},{12,4},{1,9},{5,13},{9,1},{13,5},{2,10},{6,14},... | collective-permute-start | bytes 1179656 | tf_op jit(solution)/shard_map/ppermute | solution.py:100
  104.5 6.1 %collective-permute-done.6 = bf16[96,2048]{1,0:T(8,128)(2,1)} collective-permute-done((bf16[96,2048]{1,0:T(8,128)(2,1)}, bf16[96,2048]{1,0:T(8,128)(2,1)}, u32[]{:S(2)}, u32[]{:S(2)}) %collective-permute-start.6) | collective-permute-done | bytes 393248 | tf_op jit(solution)/shard_map/ppermute | solution.py:100
  110.7 1.8 %bitcast_dynamic-update-slice_fusion.2 = bf16[4,96,2048]{2,1,0:T(8,128)(2,1)} fusion(bf16[4,96,2048]{2,1,0:T(8,128)(2,1)} %copy-done.1, s32[]{:T(128)S(6)} %select_n.72, bf16[96,2048]{1,0:T(8,128)(2,1)} %collective-permute-done.6), kind=kLoop, calls=%fused_computation.55 | loop fusion | bytes 786436 | tf_op jit(solution)/shard_map/jit(dynamic_update_index_in_dim)/dynamic_update_slice | solution.py:101
  112.4 20.6 %collective-permute-done.7 = bf16[96,2048]{1,0:T(8,128)(2,1)S(1)} collective-permute-done((bf16[96,2048]{1,0:T(8,128)(2,1)}, bf16[96,2048]{1,0:T(8,128)(2,1)S(1)}, u32[]{:S(2)}, u32[]{:S(2)}) %collective-permute-start.7) | collective-permute-done | bytes 393248 | tf_op jit(solution)/shard_map/ppermute | solution.py:100
  133.8 4.5 %collective-permute-done.8 = bf16[96,2048]{1,0:T(8,128)(2,1)S(1)} collective-permute-done((bf16[96,2048]{1,0:T(8,128)(2,1)}, bf16[96,2048]{1,0:T(8,128)(2,1)S(1)}, u32[]{:S(2)}, u32[]{:S(2)}) %collective-permute-start.8) | collective-permute-done | bytes 393248 | tf_op jit(solution)/shard_map/ppermute | solution.py:100
  139.1 12.1 %multiply_reduce_fusion.1 = (f32[16,2048]{1,0:T(8,128)S(1)}, f32[16,2048]{1,0:T(8,128)S(1)}) fusion(bf16[2048,2048]{1,0:T(8,128)(2,1)} %param.8, f32[16,2048]{1,0:T(8,128)S(1)} %get-tuple-element.12, f32[16,2048]{1,0:T(8,128)S(1)} %get-tuple-element.18, bf16[16,128,384]{2,1,0:T(8,128)(2,1)S(1)} %bitcast.92, bf16[384,2048,1]{1,0,2:T(8,128)(2,1)} %bitcast.93), kind=kOutput, calls=%fused_computation.7 | convolution fusion | flops 3275685888 | bytes 12058624 | tf_op jit(solution)/shard_map/dot_general | solution.py:159
  151.9 1.2 collective-permute-done.9
  (44 shorter events, 6.7 us)
Async XLA Ops:
  0.6 8.6 %copy-start.2 = (f32[16,2048]{1,0:T(8,128)S(1)}, f32[16,2048]{1,0:T(8,128)}, u32[]{:S(2)}) copy-start(f32[16,2048]{1,0:T(8,128)} %param.10) | copy-start | bytes 393220
  0.6 8.6 %copy-start.4 = (f32[16,2048]{1,0:T(8,128)S(1)}, f32[16,2048]{1,0:T(8,128)}, u32[]{:S(2)}) copy-start(f32[16,2048]{1,0:T(8,128)} %param.9) | copy-start | bytes 393220
  1.9 13.6 %collective-permute-start = (bf16[48,4096]{1,0:T(8,128)(2,1)S(1)}, bf16[48,4096]{1,0:T(8,128)(2,1)S(1)}, u32[]{:S(2)}, u32[]{:S(2)}) collective-permute-start(bf16[48,4096]{1,0:T(8,128)(2,1)S(1)} %get-tuple-element.15), channel_id=1, source_target_pairs={{0,2},{2,0},{1,3},{3,1},{4,6},{6,4},{5,7},{7,5},{8,10},{10,8},{9,1... | collective-permute-start | bytes 1179656 | tf_op jit(solution)/shard_map/ppermute | solution.py:74
  15.5 22.3 %copy-start = (bf16[2048,2048]{1,0:T(8,128)(2,1)}, bf16[2048,2048]{1,0:T(8,128)(2,1)S(1)}, u32[]{:S(2)}) copy-start(bf16[2048,2048]{1,0:T(8,128)(2,1)S(1)} %fusion.3) | copy-start | bytes 25165828
  37.5 16.8 %collective-permute-start.1 = (bf16[4,48,2048]{2,1,0:T(8,128)(2,1)S(1)}, bf16[4,48,2048]{2,1,0:T(8,128)(2,1)S(1)}, u32[]{:S(2)}, u32[]{:S(2)}) collective-permute-start(bf16[4,48,2048]{2,1,0:T(8,128)(2,1)S(1)} %all_to_all.15), channel_id=1, source_target_pairs={{0,2},{2,0},{1,3},{3,1},{4,6},{6,4},{5,7},{7,5},{8,10},{10,8},{9,1... | collective-permute-start | bytes 2359304 | tf_op jit(solution)/shard_map/ppermute | solution.py:81
  41.1 37.4 %copy-start.6 = (f32[128,7]{0,1:T(8,128)S(1)}, f32[128,7]{0,1:T(8,128)}, u32[]{:S(2)}) copy-start(f32[128,7]{0,1:T(8,128)} %param.11) | copy-start | bytes 10756
  41.1 21.0 %all-to-all-start.1 = ((f16[4,48,2048]{2,1,0:T(8,128)(2,1)}), f16[4,48,2048]{2,1,0:T(8,128)(2,1)S(1)}, u32[]{:S(2)}, u32[]{:S(2)}) async-start(f16[4,48,2048]{2,1,0:T(8,128)(2,1)} %get-tuple-element.32), calls=%async_computation.1 | async-start | bytes 1572864 | tf_op jit(solution)/shard_map/all_to_all | solution.py:88
  62.1 23.2 %all-to-all-start.2 = ((f16[4,48,2048]{2,1,0:T(8,128)(2,1)}), f16[4,48,2048]{2,1,0:T(8,128)(2,1)S(1)}, u32[]{:S(2)}, u32[]{:S(2)}) async-start(f16[4,48,2048]{2,1,0:T(8,128)(2,1)} %get-tuple-element.30), calls=%async_computation.2 | async-start | bytes 1572864 | tf_op jit(solution)/shard_map/all_to_all | solution.py:88
  71.0 23.5 %collective-permute-start.2 = (bf16[6,2048]{1,0:T(8,128)(2,1)}, bf16[6,2048]{1,0:T(8,128)(2,1)}, u32[]{:S(2)}, u32[]{:S(2)}) collective-permute-start(bf16[6,2048]{1,0:T(8,128)(2,1)} %slice_bitcast_fusion.3), channel_id=1, source_target_pairs={{1,0},{3,2},{5,4},{7,6},{9,8},{11,10},{13,12},{15,14},{17,16},{19,... | collective-permute-start | bytes 73736 | tf_op jit(solution)/shard_map/ppermute | solution.py:13
  76.6 17.9 %collective-permute-start.5 = (bf16[6,2048]{1,0:T(8,128)(2,1)}, bf16[6,2048]{1,0:T(8,128)(2,1)}, u32[]{:S(2)}, u32[]{:S(2)}) collective-permute-start(bf16[6,2048]{1,0:T(8,128)(2,1)} %slice_bitcast_fusion.2), channel_id=1, source_target_pairs={{1,0},{3,2},{5,4},{7,6},{9,8},{11,10},{13,12},{15,14},{17,16},{19,... | collective-permute-start | bytes 73736 | tf_op jit(solution)/shard_map/ppermute | solution.py:13
  87.9 5.7 %collective-permute-start.3 = (bf16[6,2048]{1,0:T(8,128)(2,1)S(1)}, bf16[6,2048]{1,0:T(8,128)(2,1)S(1)}, u32[]{:S(2)}, u32[]{:S(2)}) collective-permute-start(bf16[6,2048]{1,0:T(8,128)(2,1)S(1)} %get-tuple-element.16), channel_id=1, source_target_pairs={{0,1},{2,3},{4,5},{6,7},{8,9},{10,11},{12,13},{14,15},{16,17},{18,... | collective-permute-start | bytes 73736 | tf_op jit(solution)/shard_map/ppermute | solution.py:13
  89.2 5.1 %collective-permute-start.4 = (bf16[6,2048]{1,0:T(8,128)(2,1)S(1)}, bf16[6,2048]{1,0:T(8,128)(2,1)S(1)}, u32[]{:S(2)}, u32[]{:S(2)}) collective-permute-start(bf16[6,2048]{1,0:T(8,128)(2,1)S(1)} %get-tuple-element.17), channel_id=1, source_target_pairs={{1,0},{3,2},{5,4},{7,6},{9,8},{11,10},{13,12},{15,14},{17,16},{19,... | collective-permute-start | bytes 73736 | tf_op jit(solution)/shard_map/ppermute | solution.py:13
  98.1 1.5 copy-start.1
  98.1 12.5 %collective-permute-start.6 = (bf16[96,2048]{1,0:T(8,128)(2,1)}, bf16[96,2048]{1,0:T(8,128)(2,1)}, u32[]{:S(2)}, u32[]{:S(2)}) collective-permute-start(bf16[96,2048]{1,0:T(8,128)(2,1)} %get-tuple-element.11), channel_id=1, source_target_pairs={{0,4},{4,8},{8,12},{12,0},{1,5},{5,9},{9,13},{13,1},{2,6},{6,10},{... | collective-permute-start | bytes 1179656 | tf_op jit(solution)/shard_map/ppermute | solution.py:100
  100.6 32.5 %collective-permute-start.7 = (bf16[96,2048]{1,0:T(8,128)(2,1)}, bf16[96,2048]{1,0:T(8,128)(2,1)S(1)}, u32[]{:S(2)}, u32[]{:S(2)}) collective-permute-start(bf16[96,2048]{1,0:T(8,128)(2,1)} %get-tuple-element.11), channel_id=1, source_target_pairs={{0,8},{4,12},{8,0},{12,4},{1,9},{5,13},{9,1},{13,5},{2,10},{6,14},... | collective-permute-start | bytes 1179656 | tf_op jit(solution)/shard_map/ppermute | solution.py:100
  104.5 33.8 %collective-permute-start.8 = (bf16[96,2048]{1,0:T(8,128)(2,1)}, bf16[96,2048]{1,0:T(8,128)(2,1)S(1)}, u32[]{:S(2)}, u32[]{:S(2)}) collective-permute-start(bf16[96,2048]{1,0:T(8,128)(2,1)} %get-tuple-element.11), channel_id=1, source_target_pairs={{0,12},{4,0},{8,4},{12,8},{1,13},{5,1},{9,5},{13,9},{2,14},{6,2},{... | collective-permute-start | bytes 1179656 | tf_op jit(solution)/shard_map/ppermute | solution.py:100
  139.1 12.1 %copy-start.3 = (f32[16,2048]{1,0:T(8,128)S(1)}, f32[16,2048]{1,0:T(8,128)}, u32[]{:S(2)}) copy-start(f32[16,2048]{1,0:T(8,128)} %param.10) | copy-start | bytes 393220
  139.1 12.1 %copy-start.5 = (f32[16,2048]{1,0:T(8,128)S(1)}, f32[16,2048]{1,0:T(8,128)}, u32[]{:S(2)}) copy-start(f32[16,2048]{1,0:T(8,128)} %param.9) | copy-start | bytes 393220
  151.4 1.7 %collective-permute-start.9 = (f32[2,16,2048]{2,1,0:T(8,128)S(1)}, f32[2,16,2048]{2,1,0:T(8,128)S(1)}, u32[]{:S(2)}, u32[]{:S(2)}) collective-permute-start(f32[2,16,2048]{2,1,0:T(8,128)S(1)} %pad_maximum_fusion), channel_id=1, source_target_pairs={{0,1},{1,0},{2,3},{3,2},{4,5},{5,4},{6,7},{7,6},{8,9},{9,8},{10,11... | collective-permute-start | bytes 786440 | tf_op jit(solution)/shard_map/ppermute | solution.py:110

commit v19 on v18

--- a/solution.py
+++ b/solution.py
@@ -94,8 +94,7 @@
 def ring_gather(value, axis):
     devices = lax.axis_size(axis)
     me = lax.axis_index(axis)
-    gathered = jnp.zeros((devices,) + value.shape, value.dtype)
-    gathered = lax.dynamic_update_index_in_dim(gathered, value, me, 0)
+    gathered = jnp.broadcast_to(value[None], (devices,) + value.shape)
     for shift in range(1, devices):
         block = lax.ppermute(value, axis, [(i, (i + shift) % devices) for i in range(devices)])
         gathered = lax.dynamic_update_index_in_dim(gathered, block, (me + devices - shift) % devices, 0)

time: 155 us -> 154 us (level)
    dynamic_update_slice x3, local copies, waits for them, and re-layouts: 3.33 us -> 1.1 us  [ring_gather(): lax.dynamic_update_index_in_dim(gathered, block, (me + devices - shift) %...]
  transfers between devices with their start and end apart: 12 -> 12, of which waited for: 8 -> 7; matrix products, arithmetic and copies ran while one was open for 22% -> 22% of each run, Pallas kernels for 0% -> 0%
where the time goes in v19:
time: 154 us
  waiting for transfers between devices  47.2 us (31%)
  starting transfers between devices  31.9 us (21%)
  matrix products  22.9 us (15%)
  blocking collectives  21.8 us (14%)
  other arithmetic  17.5 us (11%)
  local copies, waits for them, and re-layouts  11.2 us (7%)
    ppermute x3, waiting for transfers between devices, ring_gather(): lax.ppermute(value, axis, [(i, (i + shift) % devices) for i in range(devi...  32.4 us
    all_to_all x1, blocking collectives, rows_of_block(): own_half = lax.all_to_all(pieces, 'fsdp', 0, 0)  21.8 us
    all_to_all x2, starting transfers between devices, reduce_partial(): lax.all_to_all(partial.astype(jnp.float16), 'fsdp', 0, 0)  13 us
    dot_general x1, matrix products, on_device(): lax.dot_general(inputs, d_all, (((0,), (0,)), ((), ())), preferred_elemen...  13 us
    ppermute x4, starting transfers between devices, from_behind(): return lax.ppermute(value, axis, pairs)  11.7 us
    dot_general x2, matrix products, on_device(): jnp.dot(flat, quant, preferred_element_type=jnp.float32)  9.89 us
    ppermute x1, waiting for transfers between devices, rows_of_block(): other_half = lax.ppermute(own_half, 'seq', [(0, 1), (1, 0)])  7.74 us
    convert_element_type x1, other arithmetic, on_device(): quant = soft_clip(values, clip_upper, clip_lower).astype(jnp.bfloat16)  6.12 us
  transfers between devices with their start and end apart: 12, of which 7 were waited for; matrix products, arithmetic and copies ran while one was open for 22% of the time, Pallas kernels for 0%

profile of v19, /device:TPU:9, one launch (start us, length us, event | category | flops | bytes accessed | tf_op | source)
XLA Modules:
  0.0 153.6 jit_solution(3612966024952562806)
XLA Ops:
  0.7 1.2 constant_dynamic-slice_fusion
  1.9 1.3 collective-permute-start
  3.2 5.7 %abs_reduce_fusion = bf16[16,2048]{1,0:T(8,128)(2,1)S(1)} fusion(bf16[2048,2048]{1,0:T(8,128)(2,1)} %param.8), kind=kLoop, calls=%fused_computation.15 | loop fusion | flops 16744448 | bytes 8454144 | tf_op jit(solution)/shard_map/reduce_max | solution.py:20
  9.4 6.1 %fusion.3 = bf16[2048,2048]{1,0:T(8,128)(2,1)S(1)} fusion(bf16[2048,2048]{1,0:T(8,128)(2,1)} %param.8, f32[16,2048]{1,0:T(8,128)S(1)} %get-tuple-element.10, f32[16,2048]{1,0:T(8,128)S(1)} %get-tuple-element.11, f32[16,2048]{1,0:T(8,128)S(1)} %get-tuple-element.16), kind=kLoop, calls=%fused_computation.5 | loop fusion | flops 25165824 | bytes 17170432 | tf_op jit(solution)/shard_map/convert_element_type | solution.py:120
  15.8 21.8 %all_to_all.15 = bf16[4,48,2048]{2,1,0:T(8,128)(2,1)S(1)} all-to-all(bf16[4,48,2048]{2,1,0:T(8,128)(2,1)S(1)} %fusion.23), channel_id=1, replica_groups=mesh['parts'=2,'fsdp'=4,'seq'=2,'ctx'=2] {'fsdp'}, dimensions={0} | all-to-all | bytes 1572864 | tf_op jit(solution)/shard_map/all_to_all | solution.py:80
  37.9 3.3 %fusion.31 = (f16[4,48,2048]{2,1,0:T(8,128)(2,1)}, f32[4,48,2048]{2,1,0:T(8,128)}) fusion(bf16[4,48,2048]{2,1,0:T(8,128)(2,1)S(1)} %all_to_all.15, bf16[2048,2048]{1,0:T(8,128)(2,1)S(1)} %fusion.3), kind=kOutput, calls=%fused_computation.84 | convolution fusion | flops 1611005952 | bytes 11534336 | tf_op jit(solution)/shard_map/dot_general | solution.py:128
  41.2 5.5 %all-to-all-start.1 = ((f16[4,48,2048]{2,1,0:T(8,128)(2,1)}), f16[4,48,2048]{2,1,0:T(8,128)(2,1)S(1)}, u32[]{:S(2)}, u32[]{:S(2)}) async-start(f16[4,48,2048]{2,1,0:T(8,128)(2,1)} %get-tuple-element.30), calls=%async_computation.1 | async-start | bytes 1572864 | tf_op jit(solution)/shard_map/all_to_all | solution.py:88
  46.7 7.7 %collective-permute-done.1 = bf16[4,48,2048]{2,1,0:T(8,128)(2,1)S(1)} collective-permute-done((bf16[4,48,2048]{2,1,0:T(8,128)(2,1)S(1)}, bf16[4,48,2048]{2,1,0:T(8,128)(2,1)S(1)}, u32[]{:S(2)}, u32[]{:S(2)}) %collective-permute-start.1) | collective-permute-done | bytes 786464 | tf_op jit(solution)/shard_map/ppermute | solution.py:81
  54.4 6.6 %fusion.30 = (f16[4,48,2048]{2,1,0:T(8,128)(2,1)}, f32[4,48,2048]{2,1,0:T(8,128)}) fusion(bf16[4,48,2048]{2,1,0:T(8,128)(2,1)S(1)} %collective-permute-done.1, bf16[2048,2048]{1,0:T(8,128)(2,1)} %copy-done), kind=kOutput, calls=%fused_computation.83 | convolution fusion | flops 1611005952 | bytes 11534336 | tf_op jit(solution)/shard_map/dot_general | solution.py:128
  61.0 1.2 all-to-all-done.1
  62.2 7.5 %all-to-all-start.2 = ((f16[4,48,2048]{2,1,0:T(8,128)(2,1)}), f16[4,48,2048]{2,1,0:T(8,128)(2,1)S(1)}, u32[]{:S(2)}, u32[]{:S(2)}) async-start(f16[4,48,2048]{2,1,0:T(8,128)(2,1)} %get-tuple-element.28), calls=%async_computation.2 | async-start | bytes 1572864 | tf_op jit(solution)/shard_map/all_to_all | solution.py:88
  70.4 4.2 %collective-permute-start.2 = (bf16[6,2048]{1,0:T(8,128)(2,1)}, bf16[6,2048]{1,0:T(8,128)(2,1)}, u32[]{:S(2)}, u32[]{:S(2)}) collective-permute-start(bf16[6,2048]{1,0:T(8,128)(2,1)} %slice_bitcast_fusion.3), channel_id=1, source_target_pairs={{1,0},{3,2},{5,4},{7,6},{9,8},{11,10},{13,12},{15,14},{17,16},{19,... | collective-permute-start | bytes 73736 | tf_op jit(solution)/shard_map/ppermute | solution.py:13
  74.6 1.4 slice_bitcast_fusion.2
  76.0 1.9 %collective-permute-start.5 = (bf16[6,2048]{1,0:T(8,128)(2,1)}, bf16[6,2048]{1,0:T(8,128)(2,1)}, u32[]{:S(2)}, u32[]{:S(2)}) collective-permute-start(bf16[6,2048]{1,0:T(8,128)(2,1)} %slice_bitcast_fusion.2), channel_id=1, source_target_pairs={{1,0},{3,2},{5,4},{7,6},{9,8},{11,10},{13,12},{15,14},{17,16},{19,... | collective-permute-start | bytes 73736 | tf_op jit(solution)/shard_map/ppermute | solution.py:13
  77.9 1.0 broadcast_in_dim.48
  78.8 1.9 %reshape.61 = f32[2048,7]{0,1:T(8,128)} reshape(f32[128,16,7]{1,0,2:T(8,128)} %broadcast_in_dim.48) | data formatting | bytes 114688 | tf_op jit(solution)/shard_map/reshape | solution.py:134
  80.7 4.7 %all-to-all-done.2 = f16[4,48,2048]{2,1,0:T(8,128)(2,1)S(1)} async-done(((f16[4,48,2048]{2,1,0:T(8,128)(2,1)}), f16[4,48,2048]{2,1,0:T(8,128)(2,1)S(1)}, u32[]{:S(2)}, u32[]{:S(2)}) %all-to-all-start.2) | async-done | bytes 786464 | tf_op jit(solution)/shard_map/all_to_all | solution.py:88
  86.0 1.0 fusion.25
  87.0 1.0 fusion.24
  88.1 1.3 collective-permute-start.3
  89.4 4.3 %collective-permute-start.4 = (bf16[6,2048]{1,0:T(8,128)(2,1)S(1)}, bf16[6,2048]{1,0:T(8,128)(2,1)S(1)}, u32[]{:S(2)}, u32[]{:S(2)}) collective-permute-start(bf16[6,2048]{1,0:T(8,128)(2,1)S(1)} %get-tuple-element.15), channel_id=1, source_target_pairs={{1,0},{3,2},{5,4},{7,6},{9,8},{11,10},{13,12},{15,14},{17,16},{19,... | collective-permute-start | bytes 73736 | tf_op jit(solution)/shard_map/ppermute | solution.py:13
  93.7 1.4 fusion.29
  95.3 1.9 %convert_multiply_fusion = f32[102,2048]{1,0:T(8,128)S(1)} fusion(f32[108,2048]{1,0:T(8,128)S(1)} %maximum_convert_fusion, bf16[6,2048]{1,0:T(8,128)(2,1)} %collective-permute-done.2, bf16[96,2048]{1,0:T(8,128)(2,1)S(1)} %bitcast.93, bf16[6,2048]{1,0:T(8,128)(2,1)} %collective-permute-done.5, bf16[96,2048]{1,0:T(8,128)(2,1)} %bitcast.94, ...), kind=kLoop, calls=%fused_computation.18 | loop fusion | flops 5222400 | bytes 7577600 | tf_op jit(solution)/shard_map/mul | solution.py:151
  97.9 1.2 collective-permute-start.6
  99.5 0.9 copy.20
  100.3 4.0 %collective-permute-start.7 = (bf16[96,2048]{1,0:T(8,128)(2,1)S(1)}, bf16[96,2048]{1,0:T(8,128)(2,1)S(1)}, u32[]{:S(2)}, u32[]{:S(2)}) collective-permute-start(bf16[96,2048]{1,0:T(8,128)(2,1)S(1)} %fusion.17), channel_id=1, source_target_pairs={{0,8},{4,12},{8,0},{12,4},{1,9},{5,13},{9,1},{13,5},{2,10},{6,14},... | collective-permute-start | bytes 1179656 | tf_op jit(solution)/shard_map/ppermute | solution.py:99
  104.3 6.2 %collective-permute-done.6 = bf16[96,2048]{1,0:T(8,128)(2,1)} collective-permute-done((bf16[96,2048]{1,0:T(8,128)(2,1)S(1)}, bf16[96,2048]{1,0:T(8,128)(2,1)}, u32[]{:S(2)}, u32[]{:S(2)}) %collective-permute-start.6) | collective-permute-done | bytes 393248 | tf_op jit(solution)/shard_map/ppermute | solution.py:99
  110.7 1.0 bitcast_dynamic-update-slice_fusion.2
  111.7 21.5 %collective-permute-done.7 = bf16[96,2048]{1,0:T(8,128)(2,1)S(1)} collective-permute-done((bf16[96,2048]{1,0:T(8,128)(2,1)S(1)}, bf16[96,2048]{1,0:T(8,128)(2,1)S(1)}, u32[]{:S(2)}, u32[]{:S(2)}) %collective-permute-start.7) | collective-permute-done | bytes 393248 | tf_op jit(solution)/shard_map/ppermute | solution.py:99
  133.3 4.7 %collective-permute-done.8 = bf16[96,2048]{1,0:T(8,128)(2,1)S(1)} collective-permute-done((bf16[96,2048]{1,0:T(8,128)(2,1)S(1)}, bf16[96,2048]{1,0:T(8,128)(2,1)S(1)}, u32[]{:S(2)}, u32[]{:S(2)}) %collective-permute-start.8) | collective-permute-done | bytes 393248 | tf_op jit(solution)/shard_map/ppermute | solution.py:99
  138.1 13.0 %multiply_reduce_fusion.1 = (f32[16,2048]{1,0:T(8,128)S(1)}, f32[16,2048]{1,0:T(8,128)S(1)}) fusion(bf16[2048,2048]{1,0:T(8,128)(2,1)} %param.8, f32[16,2048]{1,0:T(8,128)} %copy-done.3, f32[16,2048]{1,0:T(8,128)} %copy-done.4, bf16[16,128,384]{2,1,0:T(8,128)(2,1)S(1)} %bitcast.90, bf16[384,2048,1]{1,0,2:T(8,128)(2,1)S(1)} %bitcast.92), kind=kOutput, calls=%fused_computation.7 | convolution fusion | flops 3275685888 | bytes 12058624 | tf_op jit(solution)/shard_map/dot_general | solution.py:158
  151.7 1.2 collective-permute-done.9
  (52 shorter events, 4.8 us)
Async XLA Ops:
  0.6 8.7 %copy-start.5 = (f32[16,2048]{1,0:T(8,128)S(1)}, f32[16,2048]{1,0:T(8,128)}, u32[]{:S(2)}) copy-start(f32[16,2048]{1,0:T(8,128)} %param.10) | copy-start | bytes 393220
  0.6 8.7 %copy-start.7 = (f32[16,2048]{1,0:T(8,128)S(1)}, f32[16,2048]{1,0:T(8,128)}, u32[]{:S(2)}) copy-start(f32[16,2048]{1,0:T(8,128)} %param.9) | copy-start | bytes 393220
  1.9 13.7 %collective-permute-start = (bf16[48,4096]{1,0:T(8,128)(2,1)S(1)}, bf16[48,4096]{1,0:T(8,128)(2,1)S(1)}, u32[]{:S(2)}, u32[]{:S(2)}) collective-permute-start(bf16[48,4096]{1,0:T(8,128)(2,1)S(1)} %get-tuple-element.13), channel_id=1, source_target_pairs={{0,2},{2,0},{1,3},{3,1},{4,6},{6,4},{5,7},{7,5},{8,10},{10,8},{9,1... | collective-permute-start | bytes 1179656 | tf_op jit(solution)/shard_map/ppermute | solution.py:74
  8.9 6.7 %copy-start.1 = (bf16[16,2048]{1,0:T(8,128)(2,1)}, bf16[16,2048]{1,0:T(8,128)(2,1)S(1)}, u32[]{:S(2)}) copy-start(bf16[16,2048]{1,0:T(8,128)(2,1)S(1)} %abs_reduce_fusion) | copy-start | bytes 196612
  9.4 6.2 %copy-start.3 = (f32[16,2048]{1,0:T(8,128)}, f32[16,2048]{1,0:T(8,128)S(1)}, u32[]{:S(2)}) copy-start(f32[16,2048]{1,0:T(8,128)S(1)} %get-tuple-element.10) | copy-start | bytes 393220
  9.4 6.2 %copy-start.4 = (f32[16,2048]{1,0:T(8,128)}, f32[16,2048]{1,0:T(8,128)S(1)}, u32[]{:S(2)}) copy-start(f32[16,2048]{1,0:T(8,128)S(1)} %get-tuple-element.16) | copy-start | bytes 393220
  15.6 22.3 %copy-start = (bf16[2048,2048]{1,0:T(8,128)(2,1)}, bf16[2048,2048]{1,0:T(8,128)(2,1)S(1)}, u32[]{:S(2)}) copy-start(bf16[2048,2048]{1,0:T(8,128)(2,1)S(1)} %fusion.3) | copy-start | bytes 25165828
  37.6 16.8 %collective-permute-start.1 = (bf16[4,48,2048]{2,1,0:T(8,128)(2,1)S(1)}, bf16[4,48,2048]{2,1,0:T(8,128)(2,1)S(1)}, u32[]{:S(2)}, u32[]{:S(2)}) collective-permute-start(bf16[4,48,2048]{2,1,0:T(8,128)(2,1)S(1)} %all_to_all.15), channel_id=1, source_target_pairs={{0,2},{2,0},{1,3},{3,1},{4,6},{6,4},{5,7},{7,5},{8,10},{10,8},{9,1... | collective-permute-start | bytes 2359304 | tf_op jit(solution)/shard_map/ppermute | solution.py:81
  41.2 28.5 %copy-start.9 = (bf16[1,1,96,2048]{3,2,1,0:T(8,128)(2,1)S(1)}, bf16[1,1,96,2048]{3,2,1,0:T(8,128)(2,1)}, u32[]{:S(2)}) copy-start(bf16[1,1,96,2048]{3,2,1,0:T(8,128)(2,1)} %param.12) | copy-start | bytes 1179652
  41.2 36.7 %copy-start.10 = (f32[128,7]{0,1:T(8,128)S(1)}, f32[128,7]{0,1:T(8,128)}, u32[]{:S(2)}) copy-start(f32[128,7]{0,1:T(8,128)} %param.11) | copy-start | bytes 10756
  41.2 21.0 %all-to-all-start.1 = ((f16[4,48,2048]{2,1,0:T(8,128)(2,1)}), f16[4,48,2048]{2,1,0:T(8,128)(2,1)S(1)}, u32[]{:S(2)}, u32[]{:S(2)}) async-start(f16[4,48,2048]{2,1,0:T(8,128)(2,1)} %get-tuple-element.30), calls=%async_computation.1 | async-start | bytes 1572864 | tf_op jit(solution)/shard_map/all_to_all | solution.py:88
  62.2 23.2 %all-to-all-start.2 = ((f16[4,48,2048]{2,1,0:T(8,128)(2,1)}), f16[4,48,2048]{2,1,0:T(8,128)(2,1)S(1)}, u32[]{:S(2)}, u32[]{:S(2)}) async-start(f16[4,48,2048]{2,1,0:T(8,128)(2,1)} %get-tuple-element.28), calls=%async_computation.2 | async-start | bytes 1572864 | tf_op jit(solution)/shard_map/all_to_all | solution.py:88
  70.4 24.9 %collective-permute-start.2 = (bf16[6,2048]{1,0:T(8,128)(2,1)}, bf16[6,2048]{1,0:T(8,128)(2,1)}, u32[]{:S(2)}, u32[]{:S(2)}) collective-permute-start(bf16[6,2048]{1,0:T(8,128)(2,1)} %slice_bitcast_fusion.3), channel_id=1, source_target_pairs={{1,0},{3,2},{5,4},{7,6},{9,8},{11,10},{13,12},{15,14},{17,16},{19,... | collective-permute-start | bytes 73736 | tf_op jit(solution)/shard_map/ppermute | solution.py:13
  76.0 19.3 %collective-permute-start.5 = (bf16[6,2048]{1,0:T(8,128)(2,1)}, bf16[6,2048]{1,0:T(8,128)(2,1)}, u32[]{:S(2)}, u32[]{:S(2)}) collective-permute-start(bf16[6,2048]{1,0:T(8,128)(2,1)} %slice_bitcast_fusion.2), channel_id=1, source_target_pairs={{1,0},{3,2},{5,4},{7,6},{9,8},{11,10},{13,12},{15,14},{17,16},{19,... | collective-permute-start | bytes 73736 | tf_op jit(solution)/shard_map/ppermute | solution.py:13
  88.1 7.1 %collective-permute-start.3 = (bf16[6,2048]{1,0:T(8,128)(2,1)S(1)}, bf16[6,2048]{1,0:T(8,128)(2,1)S(1)}, u32[]{:S(2)}, u32[]{:S(2)}) collective-permute-start(bf16[6,2048]{1,0:T(8,128)(2,1)S(1)} %get-tuple-element.14), channel_id=1, source_target_pairs={{0,1},{2,3},{4,5},{6,7},{8,9},{10,11},{12,13},{14,15},{16,17},{18,... | collective-permute-start | bytes 73736 | tf_op jit(solution)/shard_map/ppermute | solution.py:13
  89.4 5.8 %collective-permute-start.4 = (bf16[6,2048]{1,0:T(8,128)(2,1)S(1)}, bf16[6,2048]{1,0:T(8,128)(2,1)S(1)}, u32[]{:S(2)}, u32[]{:S(2)}) collective-permute-start(bf16[6,2048]{1,0:T(8,128)(2,1)S(1)} %get-tuple-element.15), channel_id=1, source_target_pairs={{1,0},{3,2},{5,4},{7,6},{9,8},{11,10},{13,12},{15,14},{17,16},{19,... | collective-permute-start | bytes 73736 | tf_op jit(solution)/shard_map/ppermute | solution.py:13
  97.9 12.6 %collective-permute-start.6 = (bf16[96,2048]{1,0:T(8,128)(2,1)S(1)}, bf16[96,2048]{1,0:T(8,128)(2,1)}, u32[]{:S(2)}, u32[]{:S(2)}) collective-permute-start(bf16[96,2048]{1,0:T(8,128)(2,1)S(1)} %fusion.17), channel_id=1, source_target_pairs={{0,4},{4,8},{8,12},{12,0},{1,5},{5,9},{9,13},{13,1},{2,6},{6,10},{... | collective-permute-start | bytes 1179656 | tf_op jit(solution)/shard_map/ppermute | solution.py:99
  100.3 32.9 %collective-permute-start.7 = (bf16[96,2048]{1,0:T(8,128)(2,1)S(1)}, bf16[96,2048]{1,0:T(8,128)(2,1)S(1)}, u32[]{:S(2)}, u32[]{:S(2)}) collective-permute-start(bf16[96,2048]{1,0:T(8,128)(2,1)S(1)} %fusion.17), channel_id=1, source_target_pairs={{0,8},{4,12},{8,0},{12,4},{1,9},{5,13},{9,1},{13,5},{2,10},{6,14},... | collective-permute-start | bytes 1179656 | tf_op jit(solution)/shard_map/ppermute | solution.py:99
  104.3 33.7 %collective-permute-start.8 = (bf16[96,2048]{1,0:T(8,128)(2,1)S(1)}, bf16[96,2048]{1,0:T(8,128)(2,1)S(1)}, u32[]{:S(2)}, u32[]{:S(2)}) collective-permute-start(bf16[96,2048]{1,0:T(8,128)(2,1)S(1)} %fusion.17), channel_id=1, source_target_pairs={{0,12},{4,0},{8,4},{12,8},{1,13},{5,1},{9,5},{13,9},{2,14},{6,2},{... | collective-permute-start | bytes 1179656 | tf_op jit(solution)/shard_map/ppermute | solution.py:99
  138.0 13.0 %copy-start.2 = (bf16[16,2048]{1,0:T(8,128)(2,1)S(1)}, bf16[16,2048]{1,0:T(8,128)(2,1)}, u32[]{:S(2)}) copy-start(bf16[16,2048]{1,0:T(8,128)(2,1)} %copy-done.1) | copy-start | bytes 196612
  138.0 13.0 %copy-start.6 = (f32[16,2048]{1,0:T(8,128)S(1)}, f32[16,2048]{1,0:T(8,128)}, u32[]{:S(2)}) copy-start(f32[16,2048]{1,0:T(8,128)} %param.10) | copy-start | bytes 393220
  138.1 13.0 %copy-start.8 = (f32[16,2048]{1,0:T(8,128)S(1)}, f32[16,2048]{1,0:T(8,128)}, u32[]{:S(2)}) copy-start(f32[16,2048]{1,0:T(8,128)} %param.9) | copy-start | bytes 393220
  151.2 1.6 %collective-permute-start.9 = (f32[2,16,2048]{2,1,0:T(8,128)S(1)}, f32[2,16,2048]{2,1,0:T(8,128)S(1)}, u32[]{:S(2)}, u32[]{:S(2)}) collective-permute-start(f32[2,16,2048]{2,1,0:T(8,128)S(1)} %pad_maximum_fusion), channel_id=1, source_target_pairs={{0,1},{1,0},{2,3},{3,2},{4,5},{5,4},{6,7},{7,6},{8,9},{9,8},{10,11... | collective-permute-start | bytes 786440 | tf_op jit(solution)/shard_map/ppermute | solution.py:109

commit v20 on v19

--- a/solution.py
+++ b/solution.py
@@ -120,14 +120,19 @@
     quant = soft_clip(values, clip_upper, clip_lower).astype(jnp.bfloat16)
     pieces, quant = rows_of_block(local_rows, shards, rows, quant)
     me = lax.axis_index("fsdp")
-    proj = jnp.zeros((length, columns), jnp.float32)
-    mine = jnp.zeros((shards, length, rows), local_rows.dtype)
-    for piece, at in pieces:
+    sums = []
+    for piece, _ in pieces:
         count = piece.shape[1]
         flat = piece.reshape(shards * count, rows)
         partial = jnp.dot(flat, quant, preferred_element_type=jnp.float32).reshape(shards, count, columns)
-        proj = lax.dynamic_update_slice_in_dim(proj, reduce_partial(partial, me), at, 0)
-        mine = lax.dynamic_update_slice_in_dim(mine, piece, at, 1)
+        sums.append(reduce_partial(partial, me))
+    if len(pieces) == 1:
+        proj, mine = sums[0], pieces[0][0]
+    else:
+        first = pieces[0][1] == 0
+        proj = jnp.where(first, jnp.concatenate(sums, axis=0), jnp.concatenate(sums[::-1], axis=0))
+        halves = [piece for piece, _ in pieces]
+        mine = jnp.where(first, jnp.concatenate(halves, axis=1), jnp.concatenate(halves[::-1], axis=1))
     proj = proj.astype(jnp.bfloat16)
     inputs = mine.reshape(shards * length, rows)
 

time: 154 us -> 153 us (level)
  local copies, waits for them, and re-layouts: 11.2 us -> 9.39 us
    dynamic_update_slice x2 -> x0, other arithmetic: 2.09 us -> none  [on_device(): lax.dynamic_update_slice_in_dim(proj, reduce_partial(partial, me), at, 0)]
  transfers between devices with their start and end apart: 12 -> 12, of which waited for: 7 -> 8; matrix products, arithmetic and copies ran while one was open for 22% -> 21% of each run, Pallas kernels for 0% -> 0%
where the time goes in v20:
time: 153 us; the launch traced here: 152 us
  waiting for transfers between devices  47.7 us (31%)
  starting transfers between devices  32 us (21%)
  matrix products  22.8 us (15%)
  blocking collectives  21.8 us (14%)
  other arithmetic  17 us (11%)
  local copies, waits for them, and re-layouts  9.39 us (6%)
    ppermute x3, waiting for transfers between devices, ring_gather(): lax.ppermute(value, axis, [(i, (i + shift) % devices) for i in range(devi...  32.1 us
    all_to_all x1, blocking collectives, rows_of_block(): own_half = lax.all_to_all(pieces, 'fsdp', 0, 0)  21.8 us
    dot_general x1, matrix products, on_device(): lax.dot_general(inputs, d_all, (((0,), (0,)), ((), ())), preferred_elemen...  12.9 us
    all_to_all x2, starting transfers between devices, reduce_partial(): lax.all_to_all(partial.astype(jnp.float16), 'fsdp', 0, 0)  12.9 us
    ppermute x4, starting transfers between devices, from_behind(): return lax.ppermute(value, axis, pairs)  11.7 us
    dot_general x2, matrix products, on_device(): jnp.dot(flat, quant, preferred_element_type=jnp.float32)  9.92 us
    ppermute x1, waiting for transfers between devices, rows_of_block(): other_half = lax.ppermute(own_half, 'seq', [(0, 1), (1, 0)])  7.87 us
    convert_element_type x1, other arithmetic, on_device(): quant = soft_clip(values, clip_upper, clip_lower).astype(jnp.bfloat16)  6.15 us
  transfers between devices with their start and end apart: 12, of which 8 were waited for; matrix products, arithmetic and copies ran while one was open for 21% of the time, Pallas kernels for 0%

profile of v20, /device:TPU:9, one launch (start us, length us, event | category | flops | bytes accessed | tf_op | source)
XLA Modules:
  0.0 151.8 jit_solution(12297316349269407368)
XLA Ops:
  0.6 1.2 constant_dynamic-slice_fusion
  1.8 1.3 collective-permute-start
  3.1 5.7 %abs_reduce_fusion = bf16[16,2048]{1,0:T(8,128)(2,1)S(1)} fusion(bf16[2048,2048]{1,0:T(8,128)(2,1)} %param.8), kind=kLoop, calls=%fused_computation.15 | loop fusion | flops 16744448 | bytes 8454144 | tf_op jit(solution)/shard_map/reduce_max | solution.py:20
  9.4 6.2 %fusion.3 = bf16[2048,2048]{1,0:T(8,128)(2,1)S(1)} fusion(bf16[2048,2048]{1,0:T(8,128)(2,1)} %param.8, f32[16,2048]{1,0:T(8,128)S(1)} %get-tuple-element.10, f32[16,2048]{1,0:T(8,128)S(1)} %get-tuple-element.11, f32[16,2048]{1,0:T(8,128)S(1)} %get-tuple-element.16), kind=kLoop, calls=%fused_computation.5 | loop fusion | flops 25165824 | bytes 17170432 | tf_op jit(solution)/shard_map/convert_element_type | solution.py:120
  15.8 21.8 %all_to_all.15 = bf16[4,48,2048]{2,1,0:T(8,128)(2,1)S(1)} all-to-all(bf16[4,48,2048]{2,1,0:T(8,128)(2,1)S(1)} %fusion.23), channel_id=1, replica_groups=mesh['parts'=2,'fsdp'=4,'seq'=2,'ctx'=2] {'fsdp'}, dimensions={0} | all-to-all | bytes 1572864 | tf_op jit(solution)/shard_map/all_to_all | solution.py:80
  37.9 3.3 %fusion.29 = (f16[4,48,2048]{2,1,0:T(8,128)(2,1)}, f32[4,48,2048]{2,1,0:T(8,128)}) fusion(bf16[4,48,2048]{2,1,0:T(8,128)(2,1)S(1)} %all_to_all.15, bf16[2048,2048]{1,0:T(8,128)(2,1)S(1)} %fusion.3), kind=kOutput, calls=%fused_computation.82 | convolution fusion | flops 1611005952 | bytes 11534336 | tf_op jit(solution)/shard_map/dot_general | solution.py:127
  41.2 5.3 %all-to-all-start.1 = ((f16[4,48,2048]{2,1,0:T(8,128)(2,1)}), f16[4,48,2048]{2,1,0:T(8,128)(2,1)S(1)}, u32[]{:S(2)}, u32[]{:S(2)}) async-start(f16[4,48,2048]{2,1,0:T(8,128)(2,1)} %get-tuple-element.28), calls=%async_computation.1 | async-start | bytes 1572864 | tf_op jit(solution)/shard_map/all_to_all | solution.py:88
  46.5 7.9 %collective-permute-done.1 = bf16[4,48,2048]{2,1,0:T(8,128)(2,1)S(1)} collective-permute-done((bf16[4,48,2048]{2,1,0:T(8,128)(2,1)S(1)}, bf16[4,48,2048]{2,1,0:T(8,128)(2,1)S(1)}, u32[]{:S(2)}, u32[]{:S(2)}) %collective-permute-start.1) | collective-permute-done | bytes 786464 | tf_op jit(solution)/shard_map/ppermute | solution.py:81
  54.4 6.6 %fusion.30 = (f16[4,48,2048]{2,1,0:T(8,128)(2,1)}, f32[4,48,2048]{2,1,0:T(8,128)}) fusion(bf16[4,48,2048]{2,1,0:T(8,128)(2,1)S(1)} %collective-permute-done.1, bf16[2048,2048]{1,0:T(8,128)(2,1)} %copy-done), kind=kOutput, calls=%fused_computation.83 | convolution fusion | flops 1611005952 | bytes 11534336 | tf_op jit(solution)/shard_map/dot_general | solution.py:127
  61.0 1.1 all-to-all-done.1
  62.1 7.5 %all-to-all-start.2 = ((f16[4,48,2048]{2,1,0:T(8,128)(2,1)}), f16[4,48,2048]{2,1,0:T(8,128)(2,1)S(1)}, u32[]{:S(2)}, u32[]{:S(2)}) async-start(f16[4,48,2048]{2,1,0:T(8,128)(2,1)} %get-tuple-element.30), calls=%async_computation.2 | async-start | bytes 1572864 | tf_op jit(solution)/shard_map/all_to_all | solution.py:88
  70.2 4.2 %collective-permute-start.2 = (bf16[6,2048]{1,0:T(8,128)(2,1)}, bf16[6,2048]{1,0:T(8,128)(2,1)}, u32[]{:S(2)}, u32[]{:S(2)}) collective-permute-start(bf16[6,2048]{1,0:T(8,128)(2,1)} %slice_bitcast_fusion.3), channel_id=1, source_target_pairs={{1,0},{3,2},{5,4},{7,6},{9,8},{11,10},{13,12},{15,14},{17,16},{19,... | collective-permute-start | bytes 73736 | tf_op jit(solution)/shard_map/ppermute | solution.py:13
  74.5 1.4 slice_bitcast_fusion.2
  75.8 1.9 %collective-permute-start.5 = (bf16[6,2048]{1,0:T(8,128)(2,1)}, bf16[6,2048]{1,0:T(8,128)(2,1)}, u32[]{:S(2)}, u32[]{:S(2)}) collective-permute-start(bf16[6,2048]{1,0:T(8,128)(2,1)} %slice_bitcast_fusion.2), channel_id=1, source_target_pairs={{1,0},{3,2},{5,4},{7,6},{9,8},{11,10},{13,12},{15,14},{17,16},{19,... | collective-permute-start | bytes 73736 | tf_op jit(solution)/shard_map/ppermute | solution.py:13
  77.7 1.0 broadcast_in_dim.41
  78.7 1.9 %reshape.62 = f32[2048,7]{0,1:T(8,128)} reshape(f32[128,16,7]{1,0,2:T(8,128)} %broadcast_in_dim.41) | data formatting | bytes 114688 | tf_op jit(solution)/shard_map/reshape | solution.py:139
  80.6 4.7 %all-to-all-done.2 = f16[4,48,2048]{2,1,0:T(8,128)(2,1)S(1)} async-done(((f16[4,48,2048]{2,1,0:T(8,128)(2,1)}), f16[4,48,2048]{2,1,0:T(8,128)(2,1)S(1)}, u32[]{:S(2)}, u32[]{:S(2)}) %all-to-all-start.2) | async-done | bytes 786464 | tf_op jit(solution)/shard_map/all_to_all | solution.py:88
  85.8 1.2 bitcast_add_fusion.1
  87.1 1.3 collective-permute-start.3
  88.4 4.3 %collective-permute-start.4 = (bf16[6,2048]{1,0:T(8,128)(2,1)S(1)}, bf16[6,2048]{1,0:T(8,128)(2,1)S(1)}, u32[]{:S(2)}, u32[]{:S(2)}) collective-permute-start(bf16[6,2048]{1,0:T(8,128)(2,1)S(1)} %get-tuple-element.15), channel_id=1, source_target_pairs={{1,0},{3,2},{5,4},{7,6},{9,8},{11,10},{13,12},{15,14},{17,16},{19,... | collective-permute-start | bytes 73736 | tf_op jit(solution)/shard_map/ppermute | solution.py:13
  92.8 0.8 collective-permute-done.4
  93.7 1.6 %convert_multiply_fusion = f32[102,2048]{1,0:T(8,128)S(1)} fusion(f32[108,2048]{1,0:T(8,128)S(1)} %maximum_convert_fusion, bf16[6,2048]{1,0:T(8,128)(2,1)} %collective-permute-done.2, bf16[96,2048]{1,0:T(8,128)(2,1)S(1)} %bitcast.89, bf16[6,2048]{1,0:T(8,128)(2,1)} %collective-permute-done.5, bf16[96,2048]{1,0:T(8,128)(2,1)S(1)} %bitcast.90, ...), kind=kLoop, calls=%fused_computation.19 | loop fusion | flops 5222400 | bytes 7577600 | tf_op jit(solution)/shard_map/mul | solution.py:156
  96.0 1.4 collective-permute-start.6
  98.0 0.9 copy.20
  98.9 4.0 %collective-permute-start.7 = (bf16[96,2048]{1,0:T(8,128)(2,1)S(1)}, bf16[96,2048]{1,0:T(8,128)(2,1)S(1)}, u32[]{:S(2)}, u32[]{:S(2)}) collective-permute-start(bf16[96,2048]{1,0:T(8,128)(2,1)S(1)} %fusion.17), channel_id=1, source_target_pairs={{0,8},{4,12},{8,0},{12,4},{1,9},{5,13},{9,1},{13,5},{2,10},{6,14},... | collective-permute-start | bytes 1179656 | tf_op jit(solution)/shard_map/ppermute | solution.py:99
  102.9 5.7 %collective-permute-done.6 = bf16[96,2048]{1,0:T(8,128)(2,1)} collective-permute-done((bf16[96,2048]{1,0:T(8,128)(2,1)S(1)}, bf16[96,2048]{1,0:T(8,128)(2,1)}, u32[]{:S(2)}, u32[]{:S(2)}) %collective-permute-start.6) | collective-permute-done | bytes 393248 | tf_op jit(solution)/shard_map/ppermute | solution.py:99
  108.7 1.0 bitcast_dynamic-update-slice_fusion.2
  109.8 21.1 %collective-permute-done.7 = bf16[96,2048]{1,0:T(8,128)(2,1)S(1)} collective-permute-done((bf16[96,2048]{1,0:T(8,128)(2,1)S(1)}, bf16[96,2048]{1,0:T(8,128)(2,1)S(1)}, u32[]{:S(2)}, u32[]{:S(2)}) %collective-permute-start.7) | collective-permute-done | bytes 393248 | tf_op jit(solution)/shard_map/ppermute | solution.py:99
  130.9 5.3 %collective-permute-done.8 = bf16[96,2048]{1,0:T(8,128)(2,1)S(1)} collective-permute-done((bf16[96,2048]{1,0:T(8,128)(2,1)S(1)}, bf16[96,2048]{1,0:T(8,128)(2,1)S(1)}, u32[]{:S(2)}, u32[]{:S(2)}) %collective-permute-start.8) | collective-permute-done | bytes 393248 | tf_op jit(solution)/shard_map/ppermute | solution.py:99
  136.3 12.9 %multiply_reduce_fusion.1 = (f32[16,2048]{1,0:T(8,128)S(1)}, f32[16,2048]{1,0:T(8,128)S(1)}) fusion(bf16[2048,2048]{1,0:T(8,128)(2,1)} %param.8, f32[16,2048]{1,0:T(8,128)S(1)} %copy-done.4, f32[16,2048]{1,0:T(8,128)S(1)} %copy-done.6, bf16[16,128,384]{2,1,0:T(8,128)(2,1)S(1)} %bitcast.86, bf16[384,2048,1]{1,0,2:T(8,128)(2,1)S(1)} %bitcast.88), kind=kOutput, calls=%fused_computation.7 | convolution fusion | flops 3275685888 | bytes 12058624 | tf_op jit(solution)/shard_map/dot_general | solution.py:163
  149.9 1.2 collective-permute-done.9
  151.1 0.7 slice_bitcast_fusion
  (57 shorter events, 4.5 us)
Async XLA Ops:
  1.8 7.4 %copy-start.7 = (f32[16,2048]{1,0:T(8,128)S(1)}, f32[16,2048]{1,0:T(8,128)}, u32[]{:S(2)}) copy-start(f32[16,2048]{1,0:T(8,128)} %param.10) | copy-start | bytes 393220
  1.8 7.4 %copy-start.9 = (f32[16,2048]{1,0:T(8,128)S(1)}, f32[16,2048]{1,0:T(8,128)}, u32[]{:S(2)}) copy-start(f32[16,2048]{1,0:T(8,128)} %param.9) | copy-start | bytes 393220
  1.8 13.8 %collective-permute-start = (bf16[48,4096]{1,0:T(8,128)(2,1)S(1)}, bf16[48,4096]{1,0:T(8,128)(2,1)S(1)}, u32[]{:S(2)}, u32[]{:S(2)}) collective-permute-start(bf16[48,4096]{1,0:T(8,128)(2,1)S(1)} %get-tuple-element.13), channel_id=1, source_target_pairs={{0,2},{2,0},{1,3},{3,1},{4,6},{6,4},{5,7},{7,5},{8,10},{10,8},{9,1... | collective-permute-start | bytes 1179656 | tf_op jit(solution)/shard_map/ppermute | solution.py:74
  8.8 6.7 %copy-start.1 = (bf16[16,2048]{1,0:T(8,128)(2,1)}, bf16[16,2048]{1,0:T(8,128)(2,1)S(1)}, u32[]{:S(2)}) copy-start(bf16[16,2048]{1,0:T(8,128)(2,1)S(1)} %abs_reduce_fusion) | copy-start | bytes 196612
  9.4 6.2 %copy-start.3 = (f32[16,2048]{1,0:T(8,128)}, f32[16,2048]{1,0:T(8,128)S(1)}, u32[]{:S(2)}) copy-start(f32[16,2048]{1,0:T(8,128)S(1)} %get-tuple-element.10) | copy-start | bytes 393220
  9.4 6.2 %copy-start.5 = (f32[16,2048]{1,0:T(8,128)}, f32[16,2048]{1,0:T(8,128)S(1)}, u32[]{:S(2)}) copy-start(f32[16,2048]{1,0:T(8,128)S(1)} %get-tuple-element.16) | copy-start | bytes 393220
  15.6 25.6 %copy-start = (bf16[2048,2048]{1,0:T(8,128)(2,1)}, bf16[2048,2048]{1,0:T(8,128)(2,1)S(1)}, u32[]{:S(2)}) copy-start(bf16[2048,2048]{1,0:T(8,128)(2,1)S(1)} %fusion.3) | copy-start | bytes 25165828
  37.6 16.8 %collective-permute-start.1 = (bf16[4,48,2048]{2,1,0:T(8,128)(2,1)S(1)}, bf16[4,48,2048]{2,1,0:T(8,128)(2,1)S(1)}, u32[]{:S(2)}, u32[]{:S(2)}) collective-permute-start(bf16[4,48,2048]{2,1,0:T(8,128)(2,1)S(1)} %all_to_all.15), channel_id=1, source_target_pairs={{0,2},{2,0},{1,3},{3,1},{4,6},{6,4},{5,7},{7,5},{8,10},{10,8},{9,1... | collective-permute-start | bytes 2359304 | tf_op jit(solution)/shard_map/ppermute | solution.py:81
  41.2 20.9 %all-to-all-start.1 = ((f16[4,48,2048]{2,1,0:T(8,128)(2,1)}), f16[4,48,2048]{2,1,0:T(8,128)(2,1)S(1)}, u32[]{:S(2)}, u32[]{:S(2)}) async-start(f16[4,48,2048]{2,1,0:T(8,128)(2,1)} %get-tuple-element.28), calls=%async_computation.1 | async-start | bytes 1572864 | tf_op jit(solution)/shard_map/all_to_all | solution.py:88
  46.5 23.1 %copy-start.11 = (bf16[1,1,96,2048]{3,2,1,0:T(8,128)(2,1)S(1)}, bf16[1,1,96,2048]{3,2,1,0:T(8,128)(2,1)}, u32[]{:S(2)}) copy-start(bf16[1,1,96,2048]{3,2,1,0:T(8,128)(2,1)} %param.12) | copy-start | bytes 1179652
  46.5 31.2 %copy-start.14 = (f32[128,7]{0,1:T(8,128)S(1)}, f32[128,7]{0,1:T(8,128)}, u32[]{:S(2)}) copy-start(f32[128,7]{0,1:T(8,128)} %param.11) | copy-start | bytes 10756
  62.1 23.2 %all-to-all-start.2 = ((f16[4,48,2048]{2,1,0:T(8,128)(2,1)}), f16[4,48,2048]{2,1,0:T(8,128)(2,1)S(1)}, u32[]{:S(2)}, u32[]{:S(2)}) async-start(f16[4,48,2048]{2,1,0:T(8,128)(2,1)} %get-tuple-element.30), calls=%async_computation.2 | async-start | bytes 1572864 | tf_op jit(solution)/shard_map/all_to_all | solution.py:88
  70.2 23.4 %collective-permute-start.2 = (bf16[6,2048]{1,0:T(8,128)(2,1)}, bf16[6,2048]{1,0:T(8,128)(2,1)}, u32[]{:S(2)}, u32[]{:S(2)}) collective-permute-start(bf16[6,2048]{1,0:T(8,128)(2,1)} %slice_bitcast_fusion.3), channel_id=1, source_target_pairs={{1,0},{3,2},{5,4},{7,6},{9,8},{11,10},{13,12},{15,14},{17,16},{19,... | collective-permute-start | bytes 73736 | tf_op jit(solution)/shard_map/ppermute | solution.py:13
  75.8 17.8 %collective-permute-start.5 = (bf16[6,2048]{1,0:T(8,128)(2,1)}, bf16[6,2048]{1,0:T(8,128)(2,1)}, u32[]{:S(2)}, u32[]{:S(2)}) collective-permute-start(bf16[6,2048]{1,0:T(8,128)(2,1)} %slice_bitcast_fusion.2), channel_id=1, source_target_pairs={{1,0},{3,2},{5,4},{7,6},{9,8},{11,10},{13,12},{15,14},{17,16},{19,... | collective-permute-start | bytes 73736 | tf_op jit(solution)/shard_map/ppermute | solution.py:13
  85.3 7.4 %copy-start.13 = (f32[2048,7]{0,1:T(8,128)S(1)}, f32[2048,7]{0,1:T(8,128)}, u32[]{:S(2)}) copy-start(f32[2048,7]{0,1:T(8,128)} %reshape.62) | copy-start | bytes 172036
  85.3 8.4 %copy-start.12 = (bf16[1,1,96,2048]{3,2,1,0:T(8,128)(2,1)S(1)}, bf16[1,1,96,2048]{3,2,1,0:T(8,128)(2,1)}, u32[]{:S(2)}) copy-start(bf16[1,1,96,2048]{3,2,1,0:T(8,128)(2,1)} %param.13) | copy-start | bytes 1179652
  87.1 5.7 %collective-permute-start.3 = (bf16[6,2048]{1,0:T(8,128)(2,1)S(1)}, bf16[6,2048]{1,0:T(8,128)(2,1)S(1)}, u32[]{:S(2)}, u32[]{:S(2)}) collective-permute-start(bf16[6,2048]{1,0:T(8,128)(2,1)S(1)} %get-tuple-element.14), channel_id=1, source_target_pairs={{0,1},{2,3},{4,5},{6,7},{8,9},{10,11},{12,13},{14,15},{16,17},{18,... | collective-permute-start | bytes 73736 | tf_op jit(solution)/shard_map/ppermute | solution.py:13
  88.4 5.1 %collective-permute-start.4 = (bf16[6,2048]{1,0:T(8,128)(2,1)S(1)}, bf16[6,2048]{1,0:T(8,128)(2,1)S(1)}, u32[]{:S(2)}, u32[]{:S(2)}) collective-permute-start(bf16[6,2048]{1,0:T(8,128)(2,1)S(1)} %get-tuple-element.15), channel_id=1, source_target_pairs={{1,0},{3,2},{5,4},{7,6},{9,8},{11,10},{13,12},{15,14},{17,16},{19,... | collective-permute-start | bytes 73736 | tf_op jit(solution)/shard_map/ppermute | solution.py:13
  96.0 12.5 %collective-permute-start.6 = (bf16[96,2048]{1,0:T(8,128)(2,1)S(1)}, bf16[96,2048]{1,0:T(8,128)(2,1)}, u32[]{:S(2)}, u32[]{:S(2)}) collective-permute-start(bf16[96,2048]{1,0:T(8,128)(2,1)S(1)} %fusion.17), channel_id=1, source_target_pairs={{0,4},{4,8},{8,12},{12,0},{1,5},{5,9},{9,13},{13,1},{2,6},{6,10},{... | collective-permute-start | bytes 1179656 | tf_op jit(solution)/shard_map/ppermute | solution.py:99
  98.9 37.4 %copy-start.4 = (f32[16,2048]{1,0:T(8,128)S(1)}, f32[16,2048]{1,0:T(8,128)}, u32[]{:S(2)}) copy-start(f32[16,2048]{1,0:T(8,128)} %copy-done.3) | copy-start | bytes 393220
  98.9 37.4 %copy-start.6 = (f32[16,2048]{1,0:T(8,128)S(1)}, f32[16,2048]{1,0:T(8,128)}, u32[]{:S(2)}) copy-start(f32[16,2048]{1,0:T(8,128)} %copy-done.5) | copy-start | bytes 393220
  98.9 31.9 %collective-permute-start.7 = (bf16[96,2048]{1,0:T(8,128)(2,1)S(1)}, bf16[96,2048]{1,0:T(8,128)(2,1)S(1)}, u32[]{:S(2)}, u32[]{:S(2)}) collective-permute-start(bf16[96,2048]{1,0:T(8,128)(2,1)S(1)} %fusion.17), channel_id=1, source_target_pairs={{0,8},{4,12},{8,0},{12,4},{1,9},{5,13},{9,1},{13,5},{2,10},{6,14},... | collective-permute-start | bytes 1179656 | tf_op jit(solution)/shard_map/ppermute | solution.py:99
  102.9 33.4 %collective-permute-start.8 = (bf16[96,2048]{1,0:T(8,128)(2,1)S(1)}, bf16[96,2048]{1,0:T(8,128)(2,1)S(1)}, u32[]{:S(2)}, u32[]{:S(2)}) collective-permute-start(bf16[96,2048]{1,0:T(8,128)(2,1)S(1)} %fusion.17), channel_id=1, source_target_pairs={{0,12},{4,0},{8,4},{12,8},{1,13},{5,1},{9,5},{13,9},{2,14},{6,2},{... | collective-permute-start | bytes 1179656 | tf_op jit(solution)/shard_map/ppermute | solution.py:99
  136.3 12.9 %copy-start.2 = (bf16[16,2048]{1,0:T(8,128)(2,1)S(1)}, bf16[16,2048]{1,0:T(8,128)(2,1)}, u32[]{:S(2)}) copy-start(bf16[16,2048]{1,0:T(8,128)(2,1)} %copy-done.1) | copy-start | bytes 196612
  136.3 12.9 %copy-start.8 = (f32[16,2048]{1,0:T(8,128)S(1)}, f32[16,2048]{1,0:T(8,128)}, u32[]{:S(2)}) copy-start(f32[16,2048]{1,0:T(8,128)} %param.10) | copy-start | bytes 393220
  136.3 12.9 %copy-start.10 = (f32[16,2048]{1,0:T(8,128)S(1)}, f32[16,2048]{1,0:T(8,128)}, u32[]{:S(2)}) copy-start(f32[16,2048]{1,0:T(8,128)} %param.9) | copy-start | bytes 393220
  149.4 1.7 %collective-permute-start.9 = (f32[2,16,2048]{2,1,0:T(8,128)S(1)}, f32[2,16,2048]{2,1,0:T(8,128)S(1)}, u32[]{:S(2)}, u32[]{:S(2)}) collective-permute-start(f32[2,16,2048]{2,1,0:T(8,128)S(1)} %pad_maximum_fusion), channel_id=1, source_target_pairs={{0,1},{1,0},{2,3},{3,2},{4,5},{5,4},{6,7},{7,6},{8,9},{9,8},{10,11... | collective-permute-start | bytes 786440 | tf_op jit(solution)/shard_map/ppermute | solution.py:109

commit v21 on v20

--- a/solution.py
+++ b/solution.py
@@ -69,8 +69,9 @@
         return [(lax.all_to_all(pieces, "fsdp", 0, 0), 0)], quant
     half = length // 2
     first = lax.axis_index("seq") == 0
-    wanted_by_other = lax.dynamic_slice_in_dim(local_rows, jnp.where(first, half, 0), half, 0)
-    kept = lax.dynamic_slice_in_dim(local_rows, jnp.where(first, 0, half), half, 0)
+    lower, upper = local_rows[:half], local_rows[half:]
+    wanted_by_other = jnp.where(first, upper, lower)
+    kept = jnp.where(first, lower, upper)
     other = lax.ppermute(wanted_by_other, "seq", [(0, 1), (1, 0)])
     other, quant = lax.optimization_barrier((other, quant))
     features = jnp.where(

time: 153 us -> 153 us (level)
  no operation moved by 1% of the time
where the time goes in v21:
time: 153 us; the launch traced here: 152 us
  waiting for transfers between devices  47.7 us (31%)
  starting transfers between devices  32 us (21%)
  matrix products  22.8 us (15%)
  blocking collectives  21.8 us (14%)
  other arithmetic  18.2 us (12%)
  local copies, waits for them, and re-layouts  8.22 us (5%)
    ppermute x3, waiting for transfers between devices, ring_gather(): lax.ppermute(value, axis, [(i, (i + shift) % devices) for i in range(devi...  32.1 us
    all_to_all x1, blocking collectives, rows_of_block(): own_half = lax.all_to_all(pieces, 'fsdp', 0, 0)  21.8 us
    dot_general x1, matrix products, on_device(): lax.dot_general(inputs, d_all, (((0,), (0,)), ((), ())), preferred_elemen...  12.9 us
    all_to_all x2, starting transfers between devices, reduce_partial(): lax.all_to_all(partial.astype(jnp.float16), 'fsdp', 0, 0)  12.9 us
    ppermute x4, starting transfers between devices, from_behind(): return lax.ppermute(value, axis, pairs)  11.7 us
    dot_general x2, matrix products, on_device(): jnp.dot(flat, quant, preferred_element_type=jnp.float32)  9.92 us
    ppermute x1, waiting for transfers between devices, rows_of_block(): other_half = lax.ppermute(own_half, 'seq', [(0, 1), (1, 0)])  7.86 us
    convert_element_type x1, other arithmetic, on_device(): quant = soft_clip(values, clip_upper, clip_lower).astype(jnp.bfloat16)  6.15 us
  transfers between devices with their start and end apart: 12, of which 8 were waited for; matrix products, arithmetic and copies ran while one was open for 21% of the time, Pallas kernels for 0%

profile of v21, /device:TPU:9, one launch (start us, length us, event | category | flops | bytes accessed | tf_op | source)
XLA Modules:
  0.0 151.8 jit_solution(5120152353258020865)
XLA Ops:
  0.6 1.2 broadcast_select_fusion
  1.8 1.3 collective-permute-start
  3.1 5.7 %abs_reduce_fusion = bf16[16,2048]{1,0:T(8,128)(2,1)S(1)} fusion(bf16[2048,2048]{1,0:T(8,128)(2,1)} %param.8), kind=kLoop, calls=%fused_computation.15 | loop fusion | flops 16744448 | bytes 8454144 | tf_op jit(solution)/shard_map/reduce_max | solution.py:20
  9.4 6.2 %fusion.3 = bf16[2048,2048]{1,0:T(8,128)(2,1)S(1)} fusion(bf16[2048,2048]{1,0:T(8,128)(2,1)} %param.8, f32[16,2048]{1,0:T(8,128)S(1)} %get-tuple-element.10, f32[16,2048]{1,0:T(8,128)S(1)} %get-tuple-element.11, f32[16,2048]{1,0:T(8,128)S(1)} %get-tuple-element.16), kind=kLoop, calls=%fused_computation.5 | loop fusion | flops 25165824 | bytes 17170432 | tf_op jit(solution)/shard_map/convert_element_type | solution.py:121
  15.8 21.8 %all_to_all.15 = bf16[4,48,2048]{2,1,0:T(8,128)(2,1)S(1)} all-to-all(bf16[4,48,2048]{2,1,0:T(8,128)(2,1)S(1)} %fusion.23), channel_id=1, replica_groups=mesh['parts'=2,'fsdp'=4,'seq'=2,'ctx'=2] {'fsdp'}, dimensions={0} | all-to-all | bytes 1572864 | tf_op jit(solution)/shard_map/all_to_all | solution.py:81
  37.9 3.3 %fusion.29 = (f16[4,48,2048]{2,1,0:T(8,128)(2,1)}, f32[4,48,2048]{2,1,0:T(8,128)}) fusion(bf16[4,48,2048]{2,1,0:T(8,128)(2,1)S(1)} %all_to_all.15, bf16[2048,2048]{1,0:T(8,128)(2,1)S(1)} %fusion.3), kind=kOutput, calls=%fused_computation.82 | convolution fusion | flops 1611005952 | bytes 11534336 | tf_op jit(solution)/shard_map/dot_general | solution.py:128
  41.2 5.3 %all-to-all-start.1 = ((f16[4,48,2048]{2,1,0:T(8,128)(2,1)}), f16[4,48,2048]{2,1,0:T(8,128)(2,1)S(1)}, u32[]{:S(2)}, u32[]{:S(2)}) async-start(f16[4,48,2048]{2,1,0:T(8,128)(2,1)} %get-tuple-element.28), calls=%async_computation.1 | async-start | bytes 1572864 | tf_op jit(solution)/shard_map/all_to_all | solution.py:89
  46.5 7.9 %collective-permute-done.1 = bf16[4,48,2048]{2,1,0:T(8,128)(2,1)S(1)} collective-permute-done((bf16[4,48,2048]{2,1,0:T(8,128)(2,1)S(1)}, bf16[4,48,2048]{2,1,0:T(8,128)(2,1)S(1)}, u32[]{:S(2)}, u32[]{:S(2)}) %collective-permute-start.1) | collective-permute-done | bytes 786464 | tf_op jit(solution)/shard_map/ppermute | solution.py:82
  54.4 6.6 %fusion.30 = (f16[4,48,2048]{2,1,0:T(8,128)(2,1)}, f32[4,48,2048]{2,1,0:T(8,128)}) fusion(bf16[4,48,2048]{2,1,0:T(8,128)(2,1)S(1)} %collective-permute-done.1, bf16[2048,2048]{1,0:T(8,128)(2,1)} %copy-done), kind=kOutput, calls=%fused_computation.83 | convolution fusion | flops 1611005952 | bytes 11534336 | tf_op jit(solution)/shard_map/dot_general | solution.py:128
  61.0 1.1 all-to-all-done.1
  62.1 7.5 %all-to-all-start.2 = ((f16[4,48,2048]{2,1,0:T(8,128)(2,1)}), f16[4,48,2048]{2,1,0:T(8,128)(2,1)S(1)}, u32[]{:S(2)}, u32[]{:S(2)}) async-start(f16[4,48,2048]{2,1,0:T(8,128)(2,1)} %get-tuple-element.30), calls=%async_computation.2 | async-start | bytes 1572864 | tf_op jit(solution)/shard_map/all_to_all | solution.py:89
  70.2 4.2 %collective-permute-start.2 = (bf16[6,2048]{1,0:T(8,128)(2,1)}, bf16[6,2048]{1,0:T(8,128)(2,1)}, u32[]{:S(2)}, u32[]{:S(2)}) collective-permute-start(bf16[6,2048]{1,0:T(8,128)(2,1)} %slice_bitcast_fusion.3), channel_id=1, source_target_pairs={{1,0},{3,2},{5,4},{7,6},{9,8},{11,10},{13,12},{15,14},{17,16},{19,... | collective-permute-start | bytes 73736 | tf_op jit(solution)/shard_map/ppermute | solution.py:13
  74.5 1.4 slice_bitcast_fusion.2
  75.8 1.9 %collective-permute-start.5 = (bf16[6,2048]{1,0:T(8,128)(2,1)}, bf16[6,2048]{1,0:T(8,128)(2,1)}, u32[]{:S(2)}, u32[]{:S(2)}) collective-permute-start(bf16[6,2048]{1,0:T(8,128)(2,1)} %slice_bitcast_fusion.2), channel_id=1, source_target_pairs={{1,0},{3,2},{5,4},{7,6},{9,8},{11,10},{13,12},{15,14},{17,16},{19,... | collective-permute-start | bytes 73736 | tf_op jit(solution)/shard_map/ppermute | solution.py:13
  77.7 1.0 broadcast_in_dim.41
  78.7 1.9 %reshape.66 = f32[2048,7]{0,1:T(8,128)} reshape(f32[128,16,7]{1,0,2:T(8,128)} %broadcast_in_dim.41) | data formatting | bytes 114688 | tf_op jit(solution)/shard_map/reshape | solution.py:140
  80.6 4.7 %all-to-all-done.2 = f16[4,48,2048]{2,1,0:T(8,128)(2,1)S(1)} async-done(((f16[4,48,2048]{2,1,0:T(8,128)(2,1)}), f16[4,48,2048]{2,1,0:T(8,128)(2,1)S(1)}, u32[]{:S(2)}, u32[]{:S(2)}) %all-to-all-start.2) | async-done | bytes 786464 | tf_op jit(solution)/shard_map/all_to_all | solution.py:89
  85.8 1.2 bitcast_add_fusion.1
  87.1 1.3 collective-permute-start.3
  88.4 4.3 %collective-permute-start.4 = (bf16[6,2048]{1,0:T(8,128)(2,1)S(1)}, bf16[6,2048]{1,0:T(8,128)(2,1)S(1)}, u32[]{:S(2)}, u32[]{:S(2)}) collective-permute-start(bf16[6,2048]{1,0:T(8,128)(2,1)S(1)} %get-tuple-element.15), channel_id=1, source_target_pairs={{1,0},{3,2},{5,4},{7,6},{9,8},{11,10},{13,12},{15,14},{17,16},{19,... | collective-permute-start | bytes 73736 | tf_op jit(solution)/shard_map/ppermute | solution.py:13
  92.8 0.8 collective-permute-done.4
  93.7 1.6 %convert_multiply_fusion = f32[102,2048]{1,0:T(8,128)S(1)} fusion(f32[108,2048]{1,0:T(8,128)S(1)} %maximum_convert_fusion, bf16[6,2048]{1,0:T(8,128)(2,1)} %collective-permute-done.2, bf16[96,2048]{1,0:T(8,128)(2,1)S(1)} %bitcast.89, bf16[6,2048]{1,0:T(8,128)(2,1)} %collective-permute-done.5, bf16[96,2048]{1,0:T(8,128)(2,1)S(1)} %bitcast.90, ...), kind=kLoop, calls=%fused_computation.19 | loop fusion | flops 5222400 | bytes 7577600 | tf_op jit(solution)/shard_map/mul | solution.py:157
  96.0 1.4 collective-permute-start.6
  98.0 0.9 copy.20
  98.9 4.0 %collective-permute-start.7 = (bf16[96,2048]{1,0:T(8,128)(2,1)S(1)}, bf16[96,2048]{1,0:T(8,128)(2,1)S(1)}, u32[]{:S(2)}, u32[]{:S(2)}) collective-permute-start(bf16[96,2048]{1,0:T(8,128)(2,1)S(1)} %fusion.17), channel_id=1, source_target_pairs={{0,8},{4,12},{8,0},{12,4},{1,9},{5,13},{9,1},{13,5},{2,10},{6,14},... | collective-permute-start | bytes 1179656 | tf_op jit(solution)/shard_map/ppermute | solution.py:100
  102.9 5.7 %collective-permute-done.6 = bf16[96,2048]{1,0:T(8,128)(2,1)} collective-permute-done((bf16[96,2048]{1,0:T(8,128)(2,1)S(1)}, bf16[96,2048]{1,0:T(8,128)(2,1)}, u32[]{:S(2)}, u32[]{:S(2)}) %collective-permute-start.6) | collective-permute-done | bytes 393248 | tf_op jit(solution)/shard_map/ppermute | solution.py:100
  108.7 1.0 bitcast_dynamic-update-slice_fusion.2
  109.8 21.1 %collective-permute-done.7 = bf16[96,2048]{1,0:T(8,128)(2,1)S(1)} collective-permute-done((bf16[96,2048]{1,0:T(8,128)(2,1)S(1)}, bf16[96,2048]{1,0:T(8,128)(2,1)S(1)}, u32[]{:S(2)}, u32[]{:S(2)}) %collective-permute-start.7) | collective-permute-done | bytes 393248 | tf_op jit(solution)/shard_map/ppermute | solution.py:100
  130.9 5.3 %collective-permute-done.8 = bf16[96,2048]{1,0:T(8,128)(2,1)S(1)} collective-permute-done((bf16[96,2048]{1,0:T(8,128)(2,1)S(1)}, bf16[96,2048]{1,0:T(8,128)(2,1)S(1)}, u32[]{:S(2)}, u32[]{:S(2)}) %collective-permute-start.8) | collective-permute-done | bytes 393248 | tf_op jit(solution)/shard_map/ppermute | solution.py:100
  136.3 12.9 %multiply_reduce_fusion.1 = (f32[16,2048]{1,0:T(8,128)S(1)}, f32[16,2048]{1,0:T(8,128)S(1)}) fusion(bf16[2048,2048]{1,0:T(8,128)(2,1)} %param.8, f32[16,2048]{1,0:T(8,128)S(1)} %copy-done.4, f32[16,2048]{1,0:T(8,128)S(1)} %copy-done.6, bf16[16,128,384]{2,1,0:T(8,128)(2,1)S(1)} %bitcast.86, bf16[384,2048,1]{1,0,2:T(8,128)(2,1)S(1)} %bitcast.88), kind=kOutput, calls=%fused_computation.7 | convolution fusion | flops 3275685888 | bytes 12058624 | tf_op jit(solution)/shard_map/dot_general | solution.py:164
  149.9 1.2 collective-permute-done.9
  151.1 0.7 slice_bitcast_fusion
  (57 shorter events, 4.5 us)
Async XLA Ops:
  1.8 7.4 %copy-start.7 = (f32[16,2048]{1,0:T(8,128)S(1)}, f32[16,2048]{1,0:T(8,128)}, u32[]{:S(2)}) copy-start(f32[16,2048]{1,0:T(8,128)} %param.10) | copy-start | bytes 393220
  1.8 7.4 %copy-start.9 = (f32[16,2048]{1,0:T(8,128)S(1)}, f32[16,2048]{1,0:T(8,128)}, u32[]{:S(2)}) copy-start(f32[16,2048]{1,0:T(8,128)} %param.9) | copy-start | bytes 393220
  1.8 13.8 %collective-permute-start = (bf16[48,4096]{1,0:T(8,128)(2,1)S(1)}, bf16[48,4096]{1,0:T(8,128)(2,1)S(1)}, u32[]{:S(2)}, u32[]{:S(2)}) collective-permute-start(bf16[48,4096]{1,0:T(8,128)(2,1)S(1)} %get-tuple-element.13), channel_id=1, source_target_pairs={{0,2},{2,0},{1,3},{3,1},{4,6},{6,4},{5,7},{7,5},{8,10},{10,8},{9,1... | collective-permute-start | bytes 1179656 | tf_op jit(solution)/shard_map/ppermute | solution.py:75
  8.8 6.7 %copy-start.1 = (bf16[16,2048]{1,0:T(8,128)(2,1)}, bf16[16,2048]{1,0:T(8,128)(2,1)S(1)}, u32[]{:S(2)}) copy-start(bf16[16,2048]{1,0:T(8,128)(2,1)S(1)} %abs_reduce_fusion) | copy-start | bytes 196612
  9.4 6.2 %copy-start.3 = (f32[16,2048]{1,0:T(8,128)}, f32[16,2048]{1,0:T(8,128)S(1)}, u32[]{:S(2)}) copy-start(f32[16,2048]{1,0:T(8,128)S(1)} %get-tuple-element.10) | copy-start | bytes 393220
  9.4 6.2 %copy-start.5 = (f32[16,2048]{1,0:T(8,128)}, f32[16,2048]{1,0:T(8,128)S(1)}, u32[]{:S(2)}) copy-start(f32[16,2048]{1,0:T(8,128)S(1)} %get-tuple-element.16) | copy-start | bytes 393220
  15.6 25.6 %copy-start = (bf16[2048,2048]{1,0:T(8,128)(2,1)}, bf16[2048,2048]{1,0:T(8,128)(2,1)S(1)}, u32[]{:S(2)}) copy-start(bf16[2048,2048]{1,0:T(8,128)(2,1)S(1)} %fusion.3) | copy-start | bytes 25165828
  37.6 16.8 %collective-permute-start.1 = (bf16[4,48,2048]{2,1,0:T(8,128)(2,1)S(1)}, bf16[4,48,2048]{2,1,0:T(8,128)(2,1)S(1)}, u32[]{:S(2)}, u32[]{:S(2)}) collective-permute-start(bf16[4,48,2048]{2,1,0:T(8,128)(2,1)S(1)} %all_to_all.15), channel_id=1, source_target_pairs={{0,2},{2,0},{1,3},{3,1},{4,6},{6,4},{5,7},{7,5},{8,10},{10,8},{9,1... | collective-permute-start | bytes 2359304 | tf_op jit(solution)/shard_map/ppermute | solution.py:82
  41.2 20.9 %all-to-all-start.1 = ((f16[4,48,2048]{2,1,0:T(8,128)(2,1)}), f16[4,48,2048]{2,1,0:T(8,128)(2,1)S(1)}, u32[]{:S(2)}, u32[]{:S(2)}) async-start(f16[4,48,2048]{2,1,0:T(8,128)(2,1)} %get-tuple-element.28), calls=%async_computation.1 | async-start | bytes 1572864 | tf_op jit(solution)/shard_map/all_to_all | solution.py:89
  46.5 23.1 %copy-start.11 = (bf16[1,1,96,2048]{3,2,1,0:T(8,128)(2,1)S(1)}, bf16[1,1,96,2048]{3,2,1,0:T(8,128)(2,1)}, u32[]{:S(2)}) copy-start(bf16[1,1,96,2048]{3,2,1,0:T(8,128)(2,1)} %param.12) | copy-start | bytes 1179652
  46.5 31.2 %copy-start.14 = (f32[128,7]{0,1:T(8,128)S(1)}, f32[128,7]{0,1:T(8,128)}, u32[]{:S(2)}) copy-start(f32[128,7]{0,1:T(8,128)} %param.11) | copy-start | bytes 10756
  62.1 23.2 %all-to-all-start.2 = ((f16[4,48,2048]{2,1,0:T(8,128)(2,1)}), f16[4,48,2048]{2,1,0:T(8,128)(2,1)S(1)}, u32[]{:S(2)}, u32[]{:S(2)}) async-start(f16[4,48,2048]{2,1,0:T(8,128)(2,1)} %get-tuple-element.30), calls=%async_computation.2 | async-start | bytes 1572864 | tf_op jit(solution)/shard_map/all_to_all | solution.py:89
  70.2 23.4 %collective-permute-start.2 = (bf16[6,2048]{1,0:T(8,128)(2,1)}, bf16[6,2048]{1,0:T(8,128)(2,1)}, u32[]{:S(2)}, u32[]{:S(2)}) collective-permute-start(bf16[6,2048]{1,0:T(8,128)(2,1)} %slice_bitcast_fusion.3), channel_id=1, source_target_pairs={{1,0},{3,2},{5,4},{7,6},{9,8},{11,10},{13,12},{15,14},{17,16},{19,... | collective-permute-start | bytes 73736 | tf_op jit(solution)/shard_map/ppermute | solution.py:13
  75.8 17.8 %collective-permute-start.5 = (bf16[6,2048]{1,0:T(8,128)(2,1)}, bf16[6,2048]{1,0:T(8,128)(2,1)}, u32[]{:S(2)}, u32[]{:S(2)}) collective-permute-start(bf16[6,2048]{1,0:T(8,128)(2,1)} %slice_bitcast_fusion.2), channel_id=1, source_target_pairs={{1,0},{3,2},{5,4},{7,6},{9,8},{11,10},{13,12},{15,14},{17,16},{19,... | collective-permute-start | bytes 73736 | tf_op jit(solution)/shard_map/ppermute | solution.py:13
  85.3 7.4 %copy-start.13 = (f32[2048,7]{0,1:T(8,128)S(1)}, f32[2048,7]{0,1:T(8,128)}, u32[]{:S(2)}) copy-start(f32[2048,7]{0,1:T(8,128)} %reshape.66) | copy-start | bytes 172036
  85.3 8.4 %copy-start.12 = (bf16[1,1,96,2048]{3,2,1,0:T(8,128)(2,1)S(1)}, bf16[1,1,96,2048]{3,2,1,0:T(8,128)(2,1)}, u32[]{:S(2)}) copy-start(bf16[1,1,96,2048]{3,2,1,0:T(8,128)(2,1)} %param.13) | copy-start | bytes 1179652
  87.1 5.7 %collective-permute-start.3 = (bf16[6,2048]{1,0:T(8,128)(2,1)S(1)}, bf16[6,2048]{1,0:T(8,128)(2,1)S(1)}, u32[]{:S(2)}, u32[]{:S(2)}) collective-permute-start(bf16[6,2048]{1,0:T(8,128)(2,1)S(1)} %get-tuple-element.14), channel_id=1, source_target_pairs={{0,1},{2,3},{4,5},{6,7},{8,9},{10,11},{12,13},{14,15},{16,17},{18,... | collective-permute-start | bytes 73736 | tf_op jit(solution)/shard_map/ppermute | solution.py:13
  88.4 5.1 %collective-permute-start.4 = (bf16[6,2048]{1,0:T(8,128)(2,1)S(1)}, bf16[6,2048]{1,0:T(8,128)(2,1)S(1)}, u32[]{:S(2)}, u32[]{:S(2)}) collective-permute-start(bf16[6,2048]{1,0:T(8,128)(2,1)S(1)} %get-tuple-element.15), channel_id=1, source_target_pairs={{1,0},{3,2},{5,4},{7,6},{9,8},{11,10},{13,12},{15,14},{17,16},{19,... | collective-permute-start | bytes 73736 | tf_op jit(solution)/shard_map/ppermute | solution.py:13
  96.0 12.5 %collective-permute-start.6 = (bf16[96,2048]{1,0:T(8,128)(2,1)S(1)}, bf16[96,2048]{1,0:T(8,128)(2,1)}, u32[]{:S(2)}, u32[]{:S(2)}) collective-permute-start(bf16[96,2048]{1,0:T(8,128)(2,1)S(1)} %fusion.17), channel_id=1, source_target_pairs={{0,4},{4,8},{8,12},{12,0},{1,5},{5,9},{9,13},{13,1},{2,6},{6,10},{... | collective-permute-start | bytes 1179656 | tf_op jit(solution)/shard_map/ppermute | solution.py:100
  98.9 37.4 %copy-start.4 = (f32[16,2048]{1,0:T(8,128)S(1)}, f32[16,2048]{1,0:T(8,128)}, u32[]{:S(2)}) copy-start(f32[16,2048]{1,0:T(8,128)} %copy-done.3) | copy-start | bytes 393220
  98.9 37.4 %copy-start.6 = (f32[16,2048]{1,0:T(8,128)S(1)}, f32[16,2048]{1,0:T(8,128)}, u32[]{:S(2)}) copy-start(f32[16,2048]{1,0:T(8,128)} %copy-done.5) | copy-start | bytes 393220
  98.9 31.9 %collective-permute-start.7 = (bf16[96,2048]{1,0:T(8,128)(2,1)S(1)}, bf16[96,2048]{1,0:T(8,128)(2,1)S(1)}, u32[]{:S(2)}, u32[]{:S(2)}) collective-permute-start(bf16[96,2048]{1,0:T(8,128)(2,1)S(1)} %fusion.17), channel_id=1, source_target_pairs={{0,8},{4,12},{8,0},{12,4},{1,9},{5,13},{9,1},{13,5},{2,10},{6,14},... | collective-permute-start | bytes 1179656 | tf_op jit(solution)/shard_map/ppermute | solution.py:100
  102.9 33.4 %collective-permute-start.8 = (bf16[96,2048]{1,0:T(8,128)(2,1)S(1)}, bf16[96,2048]{1,0:T(8,128)(2,1)S(1)}, u32[]{:S(2)}, u32[]{:S(2)}) collective-permute-start(bf16[96,2048]{1,0:T(8,128)(2,1)S(1)} %fusion.17), channel_id=1, source_target_pairs={{0,12},{4,0},{8,4},{12,8},{1,13},{5,1},{9,5},{13,9},{2,14},{6,2},{... | collective-permute-start | bytes 1179656 | tf_op jit(solution)/shard_map/ppermute | solution.py:100
  136.3 12.9 %copy-start.2 = (bf16[16,2048]{1,0:T(8,128)(2,1)S(1)}, bf16[16,2048]{1,0:T(8,128)(2,1)}, u32[]{:S(2)}) copy-start(bf16[16,2048]{1,0:T(8,128)(2,1)} %copy-done.1) | copy-start | bytes 196612
  136.3 12.9 %copy-start.8 = (f32[16,2048]{1,0:T(8,128)S(1)}, f32[16,2048]{1,0:T(8,128)}, u32[]{:S(2)}) copy-start(f32[16,2048]{1,0:T(8,128)} %param.10) | copy-start | bytes 393220
  136.3 12.9 %copy-start.10 = (f32[16,2048]{1,0:T(8,128)S(1)}, f32[16,2048]{1,0:T(8,128)}, u32[]{:S(2)}) copy-start(f32[16,2048]{1,0:T(8,128)} %param.9) | copy-start | bytes 393220
  149.4 1.7 %collective-permute-start.9 = (f32[2,16,2048]{2,1,0:T(8,128)S(1)}, f32[2,16,2048]{2,1,0:T(8,128)S(1)}, u32[]{:S(2)}, u32[]{:S(2)}) collective-permute-start(f32[2,16,2048]{2,1,0:T(8,128)S(1)} %pad_maximum_fusion), channel_id=1, source_target_pairs={{0,1},{1,0},{2,3},{3,2},{4,5},{5,4},{6,7},{7,6},{8,9},{9,8},{10,11... | collective-permute-start | bytes 786440 | tf_op jit(solution)/shard_map/ppermute | solution.py:110

commit v22 on v21

--- a/solution.py
+++ b/solution.py
@@ -71,11 +71,10 @@
     first = lax.axis_index("seq") == 0
     lower, upper = local_rows[:half], local_rows[half:]
     wanted_by_other = jnp.where(first, upper, lower)
-    kept = jnp.where(first, lower, upper)
     other = lax.ppermute(wanted_by_other, "seq", [(0, 1), (1, 0)])
     other, quant = lax.optimization_barrier((other, quant))
     features = jnp.where(
-        first, jnp.concatenate([kept, other], axis=1), jnp.concatenate([other, kept], axis=1)
+        first, jnp.concatenate([lower, other], axis=1), jnp.concatenate([other, upper], axis=1)
     )
     pieces = features.reshape(half, shards, rows).transpose(1, 0, 2)
     own_half = lax.all_to_all(pieces, "fsdp", 0, 0)

time: 153 us -> 153 us (level)
  no operation moved by 1% of the time
where the time goes in v22:
time: 153 us; the launch traced here: 152 us
  waiting for transfers between devices  47.7 us (31%)
  starting transfers between devices  32 us (21%)
  matrix products  22.8 us (15%)
  blocking collectives  21.8 us (14%)
  other arithmetic  18.2 us (12%)
  local copies, waits for them, and re-layouts  8.77 us (6%)
    ppermute x3, waiting for transfers between devices, ring_gather(): lax.ppermute(value, axis, [(i, (i + shift) % devices) for i in range(devi...  32.1 us
    all_to_all x1, blocking collectives, rows_of_block(): own_half = lax.all_to_all(pieces, 'fsdp', 0, 0)  21.8 us
    dot_general x1, matrix products, on_device(): lax.dot_general(inputs, d_all, (((0,), (0,)), ((), ())), preferred_elemen...  12.9 us
    all_to_all x2, starting transfers between devices, reduce_partial(): lax.all_to_all(partial.astype(jnp.float16), 'fsdp', 0, 0)  12.9 us
    ppermute x4, starting transfers between devices, from_behind(): return lax.ppermute(value, axis, pairs)  11.7 us
    dot_general x2, matrix products, on_device(): jnp.dot(flat, quant, preferred_element_type=jnp.float32)  9.92 us
    ppermute x1, waiting for transfers between devices, rows_of_block(): other_half = lax.ppermute(own_half, 'seq', [(0, 1), (1, 0)])  7.86 us
    convert_element_type x1, other arithmetic, on_device(): quant = soft_clip(values, clip_upper, clip_lower).astype(jnp.bfloat16)  6.12 us
  transfers between devices with their start and end apart: 12, of which 8 were waited for; matrix products, arithmetic and copies ran while one was open for 21% of the time, Pallas kernels for 0%

profile of v22, /device:TPU:9, one launch (start us, length us, event | category | flops | bytes accessed | tf_op | source)
XLA Modules:
  0.0 152.4 jit_solution(13826518462992203055)
XLA Ops:
  0.6 1.2 fusion.27
  1.8 1.3 collective-permute-start
  3.1 5.7 %abs_reduce_fusion = bf16[16,2048]{1,0:T(8,128)(2,1)S(1)} fusion(bf16[2048,2048]{1,0:T(8,128)(2,1)} %param.8), kind=kLoop, calls=%fused_computation.15 | loop fusion | flops 16744448 | bytes 8454144 | tf_op jit(solution)/shard_map/reduce_max | solution.py:20
  9.9 6.1 %fusion.3 = bf16[2048,2048]{1,0:T(8,128)(2,1)S(1)} fusion(bf16[2048,2048]{1,0:T(8,128)(2,1)} %param.8, f32[16,2048]{1,0:T(8,128)S(1)} %get-tuple-element.10, f32[16,2048]{1,0:T(8,128)S(1)} %get-tuple-element.11, f32[16,2048]{1,0:T(8,128)S(1)} %get-tuple-element.17), kind=kLoop, calls=%fused_computation.5 | loop fusion | flops 25165824 | bytes 17170432 | tf_op jit(solution)/shard_map/convert_element_type | solution.py:120
  16.3 21.8 %all_to_all.15 = bf16[4,48,2048]{2,1,0:T(8,128)(2,1)S(1)} all-to-all(bf16[4,48,2048]{2,1,0:T(8,128)(2,1)S(1)} %fusion.23), channel_id=1, replica_groups=mesh['parts'=2,'fsdp'=4,'seq'=2,'ctx'=2] {'fsdp'}, dimensions={0} | all-to-all | bytes 1572864 | tf_op jit(solution)/shard_map/all_to_all | solution.py:80
  38.4 3.3 %fusion.30 = (f16[4,48,2048]{2,1,0:T(8,128)(2,1)}, f32[4,48,2048]{2,1,0:T(8,128)}) fusion(bf16[4,48,2048]{2,1,0:T(8,128)(2,1)S(1)} %all_to_all.15, bf16[2048,2048]{1,0:T(8,128)(2,1)S(1)} %fusion.3), kind=kOutput, calls=%fused_computation.82 | convolution fusion | flops 1611005952 | bytes 11534336 | tf_op jit(solution)/shard_map/dot_general | solution.py:127
  41.7 5.3 %all-to-all-start.1 = ((f16[4,48,2048]{2,1,0:T(8,128)(2,1)}), f16[4,48,2048]{2,1,0:T(8,128)(2,1)S(1)}, u32[]{:S(2)}, u32[]{:S(2)}) async-start(f16[4,48,2048]{2,1,0:T(8,128)(2,1)} %get-tuple-element.29), calls=%async_computation.1 | async-start | bytes 1572864 | tf_op jit(solution)/shard_map/all_to_all | solution.py:88
  47.1 7.9 %collective-permute-done.1 = bf16[4,48,2048]{2,1,0:T(8,128)(2,1)S(1)} collective-permute-done((bf16[4,48,2048]{2,1,0:T(8,128)(2,1)S(1)}, bf16[4,48,2048]{2,1,0:T(8,128)(2,1)S(1)}, u32[]{:S(2)}, u32[]{:S(2)}) %collective-permute-start.1) | collective-permute-done | bytes 786464 | tf_op jit(solution)/shard_map/ppermute | solution.py:81
  54.9 6.6 %fusion.31 = (f16[4,48,2048]{2,1,0:T(8,128)(2,1)}, f32[4,48,2048]{2,1,0:T(8,128)}) fusion(bf16[4,48,2048]{2,1,0:T(8,128)(2,1)S(1)} %collective-permute-done.1, bf16[2048,2048]{1,0:T(8,128)(2,1)} %copy-done), kind=kOutput, calls=%fused_computation.83 | convolution fusion | flops 1611005952 | bytes 11534336 | tf_op jit(solution)/shard_map/dot_general | solution.py:127
  61.5 1.1 all-to-all-done.1
  62.6 7.5 %all-to-all-start.2 = ((f16[4,48,2048]{2,1,0:T(8,128)(2,1)}), f16[4,48,2048]{2,1,0:T(8,128)(2,1)S(1)}, u32[]{:S(2)}, u32[]{:S(2)}) async-start(f16[4,48,2048]{2,1,0:T(8,128)(2,1)} %get-tuple-element.31), calls=%async_computation.2 | async-start | bytes 1572864 | tf_op jit(solution)/shard_map/all_to_all | solution.py:88
  70.7 4.2 %collective-permute-start.2 = (bf16[6,2048]{1,0:T(8,128)(2,1)}, bf16[6,2048]{1,0:T(8,128)(2,1)}, u32[]{:S(2)}, u32[]{:S(2)}) collective-permute-start(bf16[6,2048]{1,0:T(8,128)(2,1)} %slice_bitcast_fusion.3), channel_id=1, source_target_pairs={{1,0},{3,2},{5,4},{7,6},{9,8},{11,10},{13,12},{15,14},{17,16},{19,... | collective-permute-start | bytes 73736 | tf_op jit(solution)/shard_map/ppermute | solution.py:13
  75.0 1.4 slice_bitcast_fusion.2
  76.3 1.9 %collective-permute-start.5 = (bf16[6,2048]{1,0:T(8,128)(2,1)}, bf16[6,2048]{1,0:T(8,128)(2,1)}, u32[]{:S(2)}, u32[]{:S(2)}) collective-permute-start(bf16[6,2048]{1,0:T(8,128)(2,1)} %slice_bitcast_fusion.2), channel_id=1, source_target_pairs={{1,0},{3,2},{5,4},{7,6},{9,8},{11,10},{13,12},{15,14},{17,16},{19,... | collective-permute-start | bytes 73736 | tf_op jit(solution)/shard_map/ppermute | solution.py:13
  78.2 1.0 broadcast_in_dim.41
  79.2 1.9 %reshape.64 = f32[2048,7]{0,1:T(8,128)} reshape(f32[128,16,7]{1,0,2:T(8,128)} %broadcast_in_dim.41) | data formatting | bytes 114688 | tf_op jit(solution)/shard_map/reshape | solution.py:139
  81.1 4.7 %all-to-all-done.2 = f16[4,48,2048]{2,1,0:T(8,128)(2,1)S(1)} async-done(((f16[4,48,2048]{2,1,0:T(8,128)(2,1)}), f16[4,48,2048]{2,1,0:T(8,128)(2,1)S(1)}, u32[]{:S(2)}, u32[]{:S(2)}) %all-to-all-start.2) | async-done | bytes 786464 | tf_op jit(solution)/shard_map/all_to_all | solution.py:88
  86.3 1.2 bitcast_add_fusion.1
  87.6 1.3 collective-permute-start.3
  88.9 4.3 %collective-permute-start.4 = (bf16[6,2048]{1,0:T(8,128)(2,1)S(1)}, bf16[6,2048]{1,0:T(8,128)(2,1)S(1)}, u32[]{:S(2)}, u32[]{:S(2)}) collective-permute-start(bf16[6,2048]{1,0:T(8,128)(2,1)S(1)} %get-tuple-element.16), channel_id=1, source_target_pairs={{1,0},{3,2},{5,4},{7,6},{9,8},{11,10},{13,12},{15,14},{17,16},{19,... | collective-permute-start | bytes 73736 | tf_op jit(solution)/shard_map/ppermute | solution.py:13
  93.3 0.8 collective-permute-done.4
  94.2 1.6 %convert_multiply_fusion = f32[102,2048]{1,0:T(8,128)S(1)} fusion(f32[108,2048]{1,0:T(8,128)S(1)} %maximum_convert_fusion, bf16[6,2048]{1,0:T(8,128)(2,1)} %collective-permute-done.2, bf16[96,2048]{1,0:T(8,128)(2,1)S(1)} %bitcast.91, bf16[6,2048]{1,0:T(8,128)(2,1)} %collective-permute-done.5, bf16[96,2048]{1,0:T(8,128)(2,1)S(1)} %bitcast.92, ...), kind=kLoop, calls=%fused_computation.19 | loop fusion | flops 5222400 | bytes 7577600 | tf_op jit(solution)/shard_map/mul | solution.py:156
  96.5 1.4 collective-permute-start.6
  98.5 0.9 copy.20
  99.4 4.0 %collective-permute-start.7 = (bf16[96,2048]{1,0:T(8,128)(2,1)S(1)}, bf16[96,2048]{1,0:T(8,128)(2,1)S(1)}, u32[]{:S(2)}, u32[]{:S(2)}) collective-permute-start(bf16[96,2048]{1,0:T(8,128)(2,1)S(1)} %fusion.17), channel_id=1, source_target_pairs={{0,8},{4,12},{8,0},{12,4},{1,9},{5,13},{9,1},{13,5},{2,10},{6,14},... | collective-permute-start | bytes 1179656 | tf_op jit(solution)/shard_map/ppermute | solution.py:99
  103.4 5.7 %collective-permute-done.6 = bf16[96,2048]{1,0:T(8,128)(2,1)} collective-permute-done((bf16[96,2048]{1,0:T(8,128)(2,1)S(1)}, bf16[96,2048]{1,0:T(8,128)(2,1)}, u32[]{:S(2)}, u32[]{:S(2)}) %collective-permute-start.6) | collective-permute-done | bytes 393248 | tf_op jit(solution)/shard_map/ppermute | solution.py:99
  109.2 1.0 bitcast_dynamic-update-slice_fusion.2
  110.3 21.1 %collective-permute-done.7 = bf16[96,2048]{1,0:T(8,128)(2,1)S(1)} collective-permute-done((bf16[96,2048]{1,0:T(8,128)(2,1)S(1)}, bf16[96,2048]{1,0:T(8,128)(2,1)S(1)}, u32[]{:S(2)}, u32[]{:S(2)}) %collective-permute-start.7) | collective-permute-done | bytes 393248 | tf_op jit(solution)/shard_map/ppermute | solution.py:99
  131.4 5.3 %collective-permute-done.8 = bf16[96,2048]{1,0:T(8,128)(2,1)S(1)} collective-permute-done((bf16[96,2048]{1,0:T(8,128)(2,1)S(1)}, bf16[96,2048]{1,0:T(8,128)(2,1)S(1)}, u32[]{:S(2)}, u32[]{:S(2)}) %collective-permute-start.8) | collective-permute-done | bytes 393248 | tf_op jit(solution)/shard_map/ppermute | solution.py:99
  136.8 12.9 %multiply_reduce_fusion.1 = (f32[16,2048]{1,0:T(8,128)S(1)}, f32[16,2048]{1,0:T(8,128)S(1)}) fusion(bf16[2048,2048]{1,0:T(8,128)(2,1)} %param.8, f32[16,2048]{1,0:T(8,128)S(1)} %copy-done.4, f32[16,2048]{1,0:T(8,128)S(1)} %copy-done.6, bf16[16,128,384]{2,1,0:T(8,128)(2,1)S(1)} %bitcast.88, bf16[384,2048,1]{1,0,2:T(8,128)(2,1)S(1)} %bitcast.90), kind=kOutput, calls=%fused_computation.7 | convolution fusion | flops 3275685888 | bytes 12058624 | tf_op jit(solution)/shard_map/dot_general | solution.py:163
  150.5 1.2 collective-permute-done.9
  151.7 0.7 slice_bitcast_fusion
  (59 shorter events, 5.1 us)
Async XLA Ops:
  1.8 14.3 %collective-permute-start = (bf16[48,4096]{1,0:T(8,128)(2,1)S(1)}, bf16[48,4096]{1,0:T(8,128)(2,1)S(1)}, u32[]{:S(2)}, u32[]{:S(2)}) collective-permute-start(bf16[48,4096]{1,0:T(8,128)(2,1)S(1)} %get-tuple-element.13), channel_id=1, source_target_pairs={{0,2},{2,0},{1,3},{3,1},{4,6},{6,4},{5,7},{7,5},{8,10},{10,8},{9,1... | collective-permute-start | bytes 1179656 | tf_op jit(solution)/shard_map/ppermute | solution.py:74
  8.8 7.3 %copy-start.1 = (bf16[16,2048]{1,0:T(8,128)(2,1)}, bf16[16,2048]{1,0:T(8,128)(2,1)S(1)}, u32[]{:S(2)}) copy-start(bf16[16,2048]{1,0:T(8,128)(2,1)S(1)} %abs_reduce_fusion) | copy-start | bytes 196612
  8.8 0.9 copy-start.7
  8.8 1.0 copy-start.9
  9.9 6.2 %copy-start.3 = (f32[16,2048]{1,0:T(8,128)}, f32[16,2048]{1,0:T(8,128)S(1)}, u32[]{:S(2)}) copy-start(f32[16,2048]{1,0:T(8,128)S(1)} %get-tuple-element.10) | copy-start | bytes 393220
  9.9 6.2 %copy-start.5 = (f32[16,2048]{1,0:T(8,128)}, f32[16,2048]{1,0:T(8,128)S(1)}, u32[]{:S(2)}) copy-start(f32[16,2048]{1,0:T(8,128)S(1)} %get-tuple-element.17) | copy-start | bytes 393220
  16.1 25.6 %copy-start = (bf16[2048,2048]{1,0:T(8,128)(2,1)}, bf16[2048,2048]{1,0:T(8,128)(2,1)S(1)}, u32[]{:S(2)}) copy-start(bf16[2048,2048]{1,0:T(8,128)(2,1)S(1)} %fusion.3) | copy-start | bytes 25165828
  38.1 16.8 %collective-permute-start.1 = (bf16[4,48,2048]{2,1,0:T(8,128)(2,1)S(1)}, bf16[4,48,2048]{2,1,0:T(8,128)(2,1)S(1)}, u32[]{:S(2)}, u32[]{:S(2)}) collective-permute-start(bf16[4,48,2048]{2,1,0:T(8,128)(2,1)S(1)} %all_to_all.15), channel_id=1, source_target_pairs={{0,2},{2,0},{1,3},{3,1},{4,6},{6,4},{5,7},{7,5},{8,10},{10,8},{9,1... | collective-permute-start | bytes 2359304 | tf_op jit(solution)/shard_map/ppermute | solution.py:81
  41.7 20.9 %all-to-all-start.1 = ((f16[4,48,2048]{2,1,0:T(8,128)(2,1)}), f16[4,48,2048]{2,1,0:T(8,128)(2,1)S(1)}, u32[]{:S(2)}, u32[]{:S(2)}) async-start(f16[4,48,2048]{2,1,0:T(8,128)(2,1)} %get-tuple-element.29), calls=%async_computation.1 | async-start | bytes 1572864 | tf_op jit(solution)/shard_map/all_to_all | solution.py:88
  47.1 23.1 %copy-start.11 = (bf16[1,1,96,2048]{3,2,1,0:T(8,128)(2,1)S(1)}, bf16[1,1,96,2048]{3,2,1,0:T(8,128)(2,1)}, u32[]{:S(2)}) copy-start(bf16[1,1,96,2048]{3,2,1,0:T(8,128)(2,1)} %param.12) | copy-start | bytes 1179652
  47.1 31.2 %copy-start.14 = (f32[128,7]{0,1:T(8,128)S(1)}, f32[128,7]{0,1:T(8,128)}, u32[]{:S(2)}) copy-start(f32[128,7]{0,1:T(8,128)} %param.11) | copy-start | bytes 10756
  62.6 23.2 %all-to-all-start.2 = ((f16[4,48,2048]{2,1,0:T(8,128)(2,1)}), f16[4,48,2048]{2,1,0:T(8,128)(2,1)S(1)}, u32[]{:S(2)}, u32[]{:S(2)}) async-start(f16[4,48,2048]{2,1,0:T(8,128)(2,1)} %get-tuple-element.31), calls=%async_computation.2 | async-start | bytes 1572864 | tf_op jit(solution)/shard_map/all_to_all | solution.py:88
  70.7 23.4 %collective-permute-start.2 = (bf16[6,2048]{1,0:T(8,128)(2,1)}, bf16[6,2048]{1,0:T(8,128)(2,1)}, u32[]{:S(2)}, u32[]{:S(2)}) collective-permute-start(bf16[6,2048]{1,0:T(8,128)(2,1)} %slice_bitcast_fusion.3), channel_id=1, source_target_pairs={{1,0},{3,2},{5,4},{7,6},{9,8},{11,10},{13,12},{15,14},{17,16},{19,... | collective-permute-start | bytes 73736 | tf_op jit(solution)/shard_map/ppermute | solution.py:13
  76.3 17.8 %collective-permute-start.5 = (bf16[6,2048]{1,0:T(8,128)(2,1)}, bf16[6,2048]{1,0:T(8,128)(2,1)}, u32[]{:S(2)}, u32[]{:S(2)}) collective-permute-start(bf16[6,2048]{1,0:T(8,128)(2,1)} %slice_bitcast_fusion.2), channel_id=1, source_target_pairs={{1,0},{3,2},{5,4},{7,6},{9,8},{11,10},{13,12},{15,14},{17,16},{19,... | collective-permute-start | bytes 73736 | tf_op jit(solution)/shard_map/ppermute | solution.py:13
  85.8 7.4 %copy-start.13 = (f32[2048,7]{0,1:T(8,128)S(1)}, f32[2048,7]{0,1:T(8,128)}, u32[]{:S(2)}) copy-start(f32[2048,7]{0,1:T(8,128)} %reshape.64) | copy-start | bytes 172036
  85.8 8.4 %copy-start.12 = (bf16[1,1,96,2048]{3,2,1,0:T(8,128)(2,1)S(1)}, bf16[1,1,96,2048]{3,2,1,0:T(8,128)(2,1)}, u32[]{:S(2)}) copy-start(bf16[1,1,96,2048]{3,2,1,0:T(8,128)(2,1)} %param.13) | copy-start | bytes 1179652
  87.6 5.7 %collective-permute-start.3 = (bf16[6,2048]{1,0:T(8,128)(2,1)S(1)}, bf16[6,2048]{1,0:T(8,128)(2,1)S(1)}, u32[]{:S(2)}, u32[]{:S(2)}) collective-permute-start(bf16[6,2048]{1,0:T(8,128)(2,1)S(1)} %get-tuple-element.15), channel_id=1, source_target_pairs={{0,1},{2,3},{4,5},{6,7},{8,9},{10,11},{12,13},{14,15},{16,17},{18,... | collective-permute-start | bytes 73736 | tf_op jit(solution)/shard_map/ppermute | solution.py:13
  88.9 5.1 %collective-permute-start.4 = (bf16[6,2048]{1,0:T(8,128)(2,1)S(1)}, bf16[6,2048]{1,0:T(8,128)(2,1)S(1)}, u32[]{:S(2)}, u32[]{:S(2)}) collective-permute-start(bf16[6,2048]{1,0:T(8,128)(2,1)S(1)} %get-tuple-element.16), channel_id=1, source_target_pairs={{1,0},{3,2},{5,4},{7,6},{9,8},{11,10},{13,12},{15,14},{17,16},{19,... | collective-permute-start | bytes 73736 | tf_op jit(solution)/shard_map/ppermute | solution.py:13
  96.5 12.5 %collective-permute-start.6 = (bf16[96,2048]{1,0:T(8,128)(2,1)S(1)}, bf16[96,2048]{1,0:T(8,128)(2,1)}, u32[]{:S(2)}, u32[]{:S(2)}) collective-permute-start(bf16[96,2048]{1,0:T(8,128)(2,1)S(1)} %fusion.17), channel_id=1, source_target_pairs={{0,4},{4,8},{8,12},{12,0},{1,5},{5,9},{9,13},{13,1},{2,6},{6,10},{... | collective-permute-start | bytes 1179656 | tf_op jit(solution)/shard_map/ppermute | solution.py:99
  99.4 37.4 %copy-start.4 = (f32[16,2048]{1,0:T(8,128)S(1)}, f32[16,2048]{1,0:T(8,128)}, u32[]{:S(2)}) copy-start(f32[16,2048]{1,0:T(8,128)} %copy-done.3) | copy-start | bytes 393220
  99.4 37.4 %copy-start.6 = (f32[16,2048]{1,0:T(8,128)S(1)}, f32[16,2048]{1,0:T(8,128)}, u32[]{:S(2)}) copy-start(f32[16,2048]{1,0:T(8,128)} %copy-done.5) | copy-start | bytes 393220
  99.4 31.9 %collective-permute-start.7 = (bf16[96,2048]{1,0:T(8,128)(2,1)S(1)}, bf16[96,2048]{1,0:T(8,128)(2,1)S(1)}, u32[]{:S(2)}, u32[]{:S(2)}) collective-permute-start(bf16[96,2048]{1,0:T(8,128)(2,1)S(1)} %fusion.17), channel_id=1, source_target_pairs={{0,8},{4,12},{8,0},{12,4},{1,9},{5,13},{9,1},{13,5},{2,10},{6,14},... | collective-permute-start | bytes 1179656 | tf_op jit(solution)/shard_map/ppermute | solution.py:99
  103.4 33.4 %collective-permute-start.8 = (bf16[96,2048]{1,0:T(8,128)(2,1)S(1)}, bf16[96,2048]{1,0:T(8,128)(2,1)S(1)}, u32[]{:S(2)}, u32[]{:S(2)}) collective-permute-start(bf16[96,2048]{1,0:T(8,128)(2,1)S(1)} %fusion.17), channel_id=1, source_target_pairs={{0,12},{4,0},{8,4},{12,8},{1,13},{5,1},{9,5},{13,9},{2,14},{6,2},{... | collective-permute-start | bytes 1179656 | tf_op jit(solution)/shard_map/ppermute | solution.py:99
  136.8 12.9 %copy-start.2 = (bf16[16,2048]{1,0:T(8,128)(2,1)S(1)}, bf16[16,2048]{1,0:T(8,128)(2,1)}, u32[]{:S(2)}) copy-start(bf16[16,2048]{1,0:T(8,128)(2,1)} %copy-done.1) | copy-start | bytes 196612
  136.8 12.9 %copy-start.8 = (f32[16,2048]{1,0:T(8,128)S(1)}, f32[16,2048]{1,0:T(8,128)}, u32[]{:S(2)}) copy-start(f32[16,2048]{1,0:T(8,128)} %param.10) | copy-start | bytes 393220
  136.8 12.9 %copy-start.10 = (f32[16,2048]{1,0:T(8,128)S(1)}, f32[16,2048]{1,0:T(8,128)}, u32[]{:S(2)}) copy-start(f32[16,2048]{1,0:T(8,128)} %param.9) | copy-start | bytes 393220
  149.9 1.7 %collective-permute-start.9 = (f32[2,16,2048]{2,1,0:T(8,128)S(1)}, f32[2,16,2048]{2,1,0:T(8,128)S(1)}, u32[]{:S(2)}, u32[]{:S(2)}) collective-permute-start(f32[2,16,2048]{2,1,0:T(8,128)S(1)} %pad_maximum_fusion), channel_id=1, source_target_pairs={{0,1},{1,0},{2,3},{3,2},{4,5},{5,4},{6,7},{7,6},{8,9},{9,8},{10,11... | collective-permute-start | bytes 786440 | tf_op jit(solution)/shard_map/ppermute | solution.py:109

commit v23 on v21

--- a/solution.py
+++ b/solution.py
@@ -86,8 +86,8 @@
 
 def reduce_partial(partial, me):
     shards = partial.shape[0]
-    received = lax.all_to_all(partial.astype(jnp.float16), "fsdp", 0, 0).astype(jnp.float32)
-    others = jnp.where((jnp.arange(shards) == me)[:, None, None], 0.0, received)
+    received = lax.all_to_all(partial.astype(jnp.float16), "fsdp", 0, 0)
+    others = jnp.where((jnp.arange(shards) == me)[:, None, None], 0.0, received).astype(jnp.float32)
     own = lax.dynamic_index_in_dim(partial, me, 0, keepdims=False)
     return own + jnp.sum(others, axis=0)
 

time: 153 us -> 153 us (level)
  transfers between devices with their start and end apart: 12 -> 12, of which waited for: 8 -> 7; matrix products, arithmetic and copies ran while one was open for 21% -> 22% of each run, Pallas kernels for 0% -> 0%
where the time goes in v23:
time: 153 us
  waiting for transfers between devices  47 us (31%)
  starting transfers between devices  32.1 us (21%)
  matrix products  22.9 us (15%)
  blocking collectives  21.8 us (14%)
  other arithmetic  18.5 us (12%)
  local copies, waits for them, and re-layouts  9.37 us (6%)
    ppermute x3, waiting for transfers between devices, ring_gather(): lax.ppermute(value, axis, [(i, (i + shift) % devices) for i in range(devi...  32.1 us
    all_to_all x1, blocking collectives, rows_of_block(): own_half = lax.all_to_all(pieces, 'fsdp', 0, 0)  21.8 us
    all_to_all x2, starting transfers between devices, reduce_partial(): received = lax.all_to_all(partial.astype(jnp.float16), 'fsdp', 0, 0)  13 us
    dot_general x1, matrix products, on_device(): lax.dot_general(inputs, d_all, (((0,), (0,)), ((), ())), preferred_elemen...  13 us
    ppermute x4, starting transfers between devices, from_behind(): return lax.ppermute(value, axis, pairs)  11.7 us
    dot_general x2, matrix products, on_device(): jnp.dot(flat, quant, preferred_element_type=jnp.float32)  9.9 us
    ppermute x1, waiting for transfers between devices, rows_of_block(): other_half = lax.ppermute(own_half, 'seq', [(0, 1), (1, 0)])  7.73 us
    convert_element_type x1, other arithmetic, on_device(): quant = soft_clip(values, clip_upper, clip_lower).astype(jnp.bfloat16)  6.15 us
  transfers between devices with their start and end apart: 12, of which 7 were waited for; matrix products, arithmetic and copies ran while one was open for 22% of the time, Pallas kernels for 0%

profile of v23, /device:TPU:9, one launch (start us, length us, event | category | flops | bytes accessed | tf_op | source)
XLA Modules:
  0.0 152.7 jit_solution(710444928309977432)
XLA Ops:
  0.7 1.2 broadcast_select_fusion
  1.9 1.3 collective-permute-start
  3.2 5.7 %abs_reduce_fusion = bf16[16,2048]{1,0:T(8,128)(2,1)S(1)} fusion(bf16[2048,2048]{1,0:T(8,128)(2,1)} %param.8), kind=kLoop, calls=%fused_computation.15 | loop fusion | flops 16744448 | bytes 8454144 | tf_op jit(solution)/shard_map/reduce_max | solution.py:20
  9.4 6.2 %fusion.3 = bf16[2048,2048]{1,0:T(8,128)(2,1)S(1)} fusion(bf16[2048,2048]{1,0:T(8,128)(2,1)} %param.8, f32[16,2048]{1,0:T(8,128)S(1)} %get-tuple-element.10, f32[16,2048]{1,0:T(8,128)S(1)} %get-tuple-element.11, f32[16,2048]{1,0:T(8,128)S(1)} %get-tuple-element.16), kind=kLoop, calls=%fused_computation.5 | loop fusion | flops 25165824 | bytes 17170432 | tf_op jit(solution)/shard_map/convert_element_type | solution.py:121
  15.8 21.8 %all_to_all.15 = bf16[4,48,2048]{2,1,0:T(8,128)(2,1)S(1)} all-to-all(bf16[4,48,2048]{2,1,0:T(8,128)(2,1)S(1)} %fusion.23), channel_id=1, replica_groups=mesh['parts'=2,'fsdp'=4,'seq'=2,'ctx'=2] {'fsdp'}, dimensions={0} | all-to-all | bytes 1572864 | tf_op jit(solution)/shard_map/all_to_all | solution.py:81
  37.9 3.3 %fusion.29 = (f16[4,48,2048]{2,1,0:T(8,128)(2,1)}, f32[4,48,2048]{2,1,0:T(8,128)}) fusion(bf16[4,48,2048]{2,1,0:T(8,128)(2,1)S(1)} %all_to_all.15, bf16[2048,2048]{1,0:T(8,128)(2,1)S(1)} %fusion.3), kind=kOutput, calls=%fused_computation.82 | convolution fusion | flops 1611005952 | bytes 11534336 | tf_op jit(solution)/shard_map/dot_general | solution.py:128
  41.2 5.5 %all-to-all-start.1 = ((f16[4,48,2048]{2,1,0:T(8,128)(2,1)}), f16[4,48,2048]{2,1,0:T(8,128)(2,1)S(1)}, u32[]{:S(2)}, u32[]{:S(2)}) async-start(f16[4,48,2048]{2,1,0:T(8,128)(2,1)} %get-tuple-element.28), calls=%async_computation.1 | async-start | bytes 1572864 | tf_op jit(solution)/shard_map/all_to_all | solution.py:89
  46.7 7.7 %collective-permute-done.1 = bf16[4,48,2048]{2,1,0:T(8,128)(2,1)S(1)} collective-permute-done((bf16[4,48,2048]{2,1,0:T(8,128)(2,1)S(1)}, bf16[4,48,2048]{2,1,0:T(8,128)(2,1)S(1)}, u32[]{:S(2)}, u32[]{:S(2)}) %collective-permute-start.1) | collective-permute-done | bytes 786464 | tf_op jit(solution)/shard_map/ppermute | solution.py:82
  54.5 6.6 %fusion.30 = (f16[4,48,2048]{2,1,0:T(8,128)(2,1)}, f32[4,48,2048]{2,1,0:T(8,128)}) fusion(bf16[4,48,2048]{2,1,0:T(8,128)(2,1)S(1)} %collective-permute-done.1, bf16[2048,2048]{1,0:T(8,128)(2,1)} %copy-done), kind=kOutput, calls=%fused_computation.83 | convolution fusion | flops 1611005952 | bytes 11534336 | tf_op jit(solution)/shard_map/dot_general | solution.py:128
  61.0 1.2 all-to-all-done.1
  62.2 7.5 %all-to-all-start.2 = ((f16[4,48,2048]{2,1,0:T(8,128)(2,1)}), f16[4,48,2048]{2,1,0:T(8,128)(2,1)S(1)}, u32[]{:S(2)}, u32[]{:S(2)}) async-start(f16[4,48,2048]{2,1,0:T(8,128)(2,1)} %get-tuple-element.30), calls=%async_computation.2 | async-start | bytes 1572864 | tf_op jit(solution)/shard_map/all_to_all | solution.py:89
  70.4 4.2 %collective-permute-start.2 = (bf16[6,2048]{1,0:T(8,128)(2,1)}, bf16[6,2048]{1,0:T(8,128)(2,1)}, u32[]{:S(2)}, u32[]{:S(2)}) collective-permute-start(bf16[6,2048]{1,0:T(8,128)(2,1)} %slice_bitcast_fusion.3), channel_id=1, source_target_pairs={{1,0},{3,2},{5,4},{7,6},{9,8},{11,10},{13,12},{15,14},{17,16},{19,... | collective-permute-start | bytes 73736 | tf_op jit(solution)/shard_map/ppermute | solution.py:13
  74.6 1.4 slice_bitcast_fusion.2
  76.0 1.9 %collective-permute-start.5 = (bf16[6,2048]{1,0:T(8,128)(2,1)}, bf16[6,2048]{1,0:T(8,128)(2,1)}, u32[]{:S(2)}, u32[]{:S(2)}) collective-permute-start(bf16[6,2048]{1,0:T(8,128)(2,1)} %slice_bitcast_fusion.2), channel_id=1, source_target_pairs={{1,0},{3,2},{5,4},{7,6},{9,8},{11,10},{13,12},{15,14},{17,16},{19,... | collective-permute-start | bytes 73736 | tf_op jit(solution)/shard_map/ppermute | solution.py:13
  77.9 1.0 broadcast_in_dim.41
  78.8 1.9 %reshape.66 = f32[2048,7]{0,1:T(8,128)} reshape(f32[128,16,7]{1,0,2:T(8,128)} %broadcast_in_dim.41) | data formatting | bytes 114688 | tf_op jit(solution)/shard_map/reshape | solution.py:140
  80.7 4.7 %all-to-all-done.2 = f16[4,48,2048]{2,1,0:T(8,128)(2,1)S(1)} async-done(((f16[4,48,2048]{2,1,0:T(8,128)(2,1)}), f16[4,48,2048]{2,1,0:T(8,128)(2,1)S(1)}, u32[]{:S(2)}, u32[]{:S(2)}) %all-to-all-start.2) | async-done | bytes 786464 | tf_op jit(solution)/shard_map/all_to_all | solution.py:89
  86.0 1.2 bitcast_add_fusion.1
  87.3 1.3 collective-permute-start.3
  88.6 4.3 %collective-permute-start.4 = (bf16[6,2048]{1,0:T(8,128)(2,1)S(1)}, bf16[6,2048]{1,0:T(8,128)(2,1)S(1)}, u32[]{:S(2)}, u32[]{:S(2)}) collective-permute-start(bf16[6,2048]{1,0:T(8,128)(2,1)S(1)} %get-tuple-element.15), channel_id=1, source_target_pairs={{1,0},{3,2},{5,4},{7,6},{9,8},{11,10},{13,12},{15,14},{17,16},{19,... | collective-permute-start | bytes 73736 | tf_op jit(solution)/shard_map/ppermute | solution.py:13
  92.9 1.2 fusion.28
  94.3 1.9 %convert_multiply_fusion = f32[102,2048]{1,0:T(8,128)S(1)} fusion(f32[108,2048]{1,0:T(8,128)S(1)} %maximum_convert_fusion, bf16[6,2048]{1,0:T(8,128)(2,1)} %collective-permute-done.2, bf16[96,2048]{1,0:T(8,128)(2,1)S(1)} %bitcast.89, bf16[6,2048]{1,0:T(8,128)(2,1)} %collective-permute-done.5, bf16[96,2048]{1,0:T(8,128)(2,1)} %bitcast.90, ...), kind=kLoop, calls=%fused_computation.19 | loop fusion | flops 5222400 | bytes 7577600 | tf_op jit(solution)/shard_map/mul | solution.py:157
  96.8 1.4 collective-permute-start.6
  98.8 0.9 copy.20
  99.7 4.0 %collective-permute-start.7 = (bf16[96,2048]{1,0:T(8,128)(2,1)S(1)}, bf16[96,2048]{1,0:T(8,128)(2,1)S(1)}, u32[]{:S(2)}, u32[]{:S(2)}) collective-permute-start(bf16[96,2048]{1,0:T(8,128)(2,1)S(1)} %fusion.17), channel_id=1, source_target_pairs={{0,8},{4,12},{8,0},{12,4},{1,9},{5,13},{9,1},{13,5},{2,10},{6,14},... | collective-permute-start | bytes 1179656 | tf_op jit(solution)/shard_map/ppermute | solution.py:100
  103.7 6.0 %collective-permute-done.6 = bf16[96,2048]{1,0:T(8,128)(2,1)} collective-permute-done((bf16[96,2048]{1,0:T(8,128)(2,1)S(1)}, bf16[96,2048]{1,0:T(8,128)(2,1)}, u32[]{:S(2)}, u32[]{:S(2)}) %collective-permute-start.6) | collective-permute-done | bytes 393248 | tf_op jit(solution)/shard_map/ppermute | solution.py:100
  109.9 1.0 bitcast_dynamic-update-slice_fusion.2
  110.9 21.3 %collective-permute-done.7 = bf16[96,2048]{1,0:T(8,128)(2,1)S(1)} collective-permute-done((bf16[96,2048]{1,0:T(8,128)(2,1)S(1)}, bf16[96,2048]{1,0:T(8,128)(2,1)S(1)}, u32[]{:S(2)}, u32[]{:S(2)}) %collective-permute-start.7) | collective-permute-done | bytes 393248 | tf_op jit(solution)/shard_map/ppermute | solution.py:100
  132.2 4.9 %collective-permute-done.8 = bf16[96,2048]{1,0:T(8,128)(2,1)S(1)} collective-permute-done((bf16[96,2048]{1,0:T(8,128)(2,1)S(1)}, bf16[96,2048]{1,0:T(8,128)(2,1)S(1)}, u32[]{:S(2)}, u32[]{:S(2)}) %collective-permute-start.8) | collective-permute-done | bytes 393248 | tf_op jit(solution)/shard_map/ppermute | solution.py:100
  137.2 13.0 %multiply_reduce_fusion.1 = (f32[16,2048]{1,0:T(8,128)S(1)}, f32[16,2048]{1,0:T(8,128)S(1)}) fusion(bf16[2048,2048]{1,0:T(8,128)(2,1)} %param.8, f32[16,2048]{1,0:T(8,128)} %copy-done.3, f32[16,2048]{1,0:T(8,128)} %copy-done.4, bf16[16,128,384]{2,1,0:T(8,128)(2,1)S(1)} %bitcast.86, bf16[384,2048,1]{1,0,2:T(8,128)(2,1)S(1)} %bitcast.88), kind=kOutput, calls=%fused_computation.7 | convolution fusion | flops 3275685888 | bytes 12058624 | tf_op jit(solution)/shard_map/dot_general | solution.py:164
  150.8 1.2 collective-permute-done.9
  152.0 0.7 slice_bitcast_fusion
  (49 shorter events, 4.4 us)
Async XLA Ops:
  0.6 8.6 %copy-start.5 = (f32[16,2048]{1,0:T(8,128)S(1)}, f32[16,2048]{1,0:T(8,128)}, u32[]{:S(2)}) copy-start(f32[16,2048]{1,0:T(8,128)} %param.10) | copy-start | bytes 393220
  0.6 8.6 %copy-start.7 = (f32[16,2048]{1,0:T(8,128)S(1)}, f32[16,2048]{1,0:T(8,128)}, u32[]{:S(2)}) copy-start(f32[16,2048]{1,0:T(8,128)} %param.9) | copy-start | bytes 393220
  1.9 13.8 %collective-permute-start = (bf16[48,4096]{1,0:T(8,128)(2,1)S(1)}, bf16[48,4096]{1,0:T(8,128)(2,1)S(1)}, u32[]{:S(2)}, u32[]{:S(2)}) collective-permute-start(bf16[48,4096]{1,0:T(8,128)(2,1)S(1)} %get-tuple-element.13), channel_id=1, source_target_pairs={{0,2},{2,0},{1,3},{3,1},{4,6},{6,4},{5,7},{7,5},{8,10},{10,8},{9,1... | collective-permute-start | bytes 1179656 | tf_op jit(solution)/shard_map/ppermute | solution.py:75
  8.8 6.7 %copy-start.1 = (bf16[16,2048]{1,0:T(8,128)(2,1)}, bf16[16,2048]{1,0:T(8,128)(2,1)S(1)}, u32[]{:S(2)}) copy-start(bf16[16,2048]{1,0:T(8,128)(2,1)S(1)} %abs_reduce_fusion) | copy-start | bytes 196612
  9.4 6.2 %copy-start.3 = (f32[16,2048]{1,0:T(8,128)}, f32[16,2048]{1,0:T(8,128)S(1)}, u32[]{:S(2)}) copy-start(f32[16,2048]{1,0:T(8,128)S(1)} %get-tuple-element.10) | copy-start | bytes 393220
  9.4 6.2 %copy-start.4 = (f32[16,2048]{1,0:T(8,128)}, f32[16,2048]{1,0:T(8,128)S(1)}, u32[]{:S(2)}) copy-start(f32[16,2048]{1,0:T(8,128)S(1)} %get-tuple-element.16) | copy-start | bytes 393220
  15.6 22.3 %copy-start = (bf16[2048,2048]{1,0:T(8,128)(2,1)}, bf16[2048,2048]{1,0:T(8,128)(2,1)S(1)}, u32[]{:S(2)}) copy-start(bf16[2048,2048]{1,0:T(8,128)(2,1)S(1)} %fusion.3) | copy-start | bytes 25165828
  37.7 16.8 %collective-permute-start.1 = (bf16[4,48,2048]{2,1,0:T(8,128)(2,1)S(1)}, bf16[4,48,2048]{2,1,0:T(8,128)(2,1)S(1)}, u32[]{:S(2)}, u32[]{:S(2)}) collective-permute-start(bf16[4,48,2048]{2,1,0:T(8,128)(2,1)S(1)} %all_to_all.15), channel_id=1, source_target_pairs={{0,2},{2,0},{1,3},{3,1},{4,6},{6,4},{5,7},{7,5},{8,10},{10,8},{9,1... | collective-permute-start | bytes 2359304 | tf_op jit(solution)/shard_map/ppermute | solution.py:82
  41.2 28.5 %copy-start.9 = (bf16[1,1,96,2048]{3,2,1,0:T(8,128)(2,1)S(1)}, bf16[1,1,96,2048]{3,2,1,0:T(8,128)(2,1)}, u32[]{:S(2)}) copy-start(bf16[1,1,96,2048]{3,2,1,0:T(8,128)(2,1)} %param.12) | copy-start | bytes 1179652
  41.2 36.6 %copy-start.10 = (f32[128,7]{0,1:T(8,128)S(1)}, f32[128,7]{0,1:T(8,128)}, u32[]{:S(2)}) copy-start(f32[128,7]{0,1:T(8,128)} %param.11) | copy-start | bytes 10756
  41.2 21.0 %all-to-all-start.1 = ((f16[4,48,2048]{2,1,0:T(8,128)(2,1)}), f16[4,48,2048]{2,1,0:T(8,128)(2,1)S(1)}, u32[]{:S(2)}, u32[]{:S(2)}) async-start(f16[4,48,2048]{2,1,0:T(8,128)(2,1)} %get-tuple-element.28), calls=%async_computation.1 | async-start | bytes 1572864 | tf_op jit(solution)/shard_map/all_to_all | solution.py:89
  62.2 23.2 %all-to-all-start.2 = ((f16[4,48,2048]{2,1,0:T(8,128)(2,1)}), f16[4,48,2048]{2,1,0:T(8,128)(2,1)S(1)}, u32[]{:S(2)}, u32[]{:S(2)}) async-start(f16[4,48,2048]{2,1,0:T(8,128)(2,1)} %get-tuple-element.30), calls=%async_computation.2 | async-start | bytes 1572864 | tf_op jit(solution)/shard_map/all_to_all | solution.py:89
  70.4 23.9 %collective-permute-start.2 = (bf16[6,2048]{1,0:T(8,128)(2,1)}, bf16[6,2048]{1,0:T(8,128)(2,1)}, u32[]{:S(2)}, u32[]{:S(2)}) collective-permute-start(bf16[6,2048]{1,0:T(8,128)(2,1)} %slice_bitcast_fusion.3), channel_id=1, source_target_pairs={{1,0},{3,2},{5,4},{7,6},{9,8},{11,10},{13,12},{15,14},{17,16},{19,... | collective-permute-start | bytes 73736 | tf_op jit(solution)/shard_map/ppermute | solution.py:13
  76.0 18.3 %collective-permute-start.5 = (bf16[6,2048]{1,0:T(8,128)(2,1)}, bf16[6,2048]{1,0:T(8,128)(2,1)}, u32[]{:S(2)}, u32[]{:S(2)}) collective-permute-start(bf16[6,2048]{1,0:T(8,128)(2,1)} %slice_bitcast_fusion.2), channel_id=1, source_target_pairs={{1,0},{3,2},{5,4},{7,6},{9,8},{11,10},{13,12},{15,14},{17,16},{19,... | collective-permute-start | bytes 73736 | tf_op jit(solution)/shard_map/ppermute | solution.py:13
  87.3 6.8 %collective-permute-start.3 = (bf16[6,2048]{1,0:T(8,128)(2,1)S(1)}, bf16[6,2048]{1,0:T(8,128)(2,1)S(1)}, u32[]{:S(2)}, u32[]{:S(2)}) collective-permute-start(bf16[6,2048]{1,0:T(8,128)(2,1)S(1)} %get-tuple-element.14), channel_id=1, source_target_pairs={{0,1},{2,3},{4,5},{6,7},{8,9},{10,11},{12,13},{14,15},{16,17},{18,... | collective-permute-start | bytes 73736 | tf_op jit(solution)/shard_map/ppermute | solution.py:13
  88.6 5.5 %collective-permute-start.4 = (bf16[6,2048]{1,0:T(8,128)(2,1)S(1)}, bf16[6,2048]{1,0:T(8,128)(2,1)S(1)}, u32[]{:S(2)}, u32[]{:S(2)}) collective-permute-start(bf16[6,2048]{1,0:T(8,128)(2,1)S(1)} %get-tuple-element.15), channel_id=1, source_target_pairs={{1,0},{3,2},{5,4},{7,6},{9,8},{11,10},{13,12},{15,14},{17,16},{19,... | collective-permute-start | bytes 73736 | tf_op jit(solution)/shard_map/ppermute | solution.py:13
  96.8 12.9 %collective-permute-start.6 = (bf16[96,2048]{1,0:T(8,128)(2,1)S(1)}, bf16[96,2048]{1,0:T(8,128)(2,1)}, u32[]{:S(2)}, u32[]{:S(2)}) collective-permute-start(bf16[96,2048]{1,0:T(8,128)(2,1)S(1)} %fusion.17), channel_id=1, source_target_pairs={{0,4},{4,8},{8,12},{12,0},{1,5},{5,9},{9,13},{13,1},{2,6},{6,10},{... | collective-permute-start | bytes 1179656 | tf_op jit(solution)/shard_map/ppermute | solution.py:100
  99.7 32.5 %collective-permute-start.7 = (bf16[96,2048]{1,0:T(8,128)(2,1)S(1)}, bf16[96,2048]{1,0:T(8,128)(2,1)S(1)}, u32[]{:S(2)}, u32[]{:S(2)}) collective-permute-start(bf16[96,2048]{1,0:T(8,128)(2,1)S(1)} %fusion.17), channel_id=1, source_target_pairs={{0,8},{4,12},{8,0},{12,4},{1,9},{5,13},{9,1},{13,5},{2,10},{6,14},... | collective-permute-start | bytes 1179656 | tf_op jit(solution)/shard_map/ppermute | solution.py:100
  103.7 33.4 %collective-permute-start.8 = (bf16[96,2048]{1,0:T(8,128)(2,1)S(1)}, bf16[96,2048]{1,0:T(8,128)(2,1)S(1)}, u32[]{:S(2)}, u32[]{:S(2)}) collective-permute-start(bf16[96,2048]{1,0:T(8,128)(2,1)S(1)} %fusion.17), channel_id=1, source_target_pairs={{0,12},{4,0},{8,4},{12,8},{1,13},{5,1},{9,5},{13,9},{2,14},{6,2},{... | collective-permute-start | bytes 1179656 | tf_op jit(solution)/shard_map/ppermute | solution.py:100
  137.1 13.0 %copy-start.2 = (bf16[16,2048]{1,0:T(8,128)(2,1)S(1)}, bf16[16,2048]{1,0:T(8,128)(2,1)}, u32[]{:S(2)}) copy-start(bf16[16,2048]{1,0:T(8,128)(2,1)} %copy-done.1) | copy-start | bytes 196612
  137.1 13.0 %copy-start.6 = (f32[16,2048]{1,0:T(8,128)S(1)}, f32[16,2048]{1,0:T(8,128)}, u32[]{:S(2)}) copy-start(f32[16,2048]{1,0:T(8,128)} %param.10) | copy-start | bytes 393220
  137.2 13.0 %copy-start.8 = (f32[16,2048]{1,0:T(8,128)S(1)}, f32[16,2048]{1,0:T(8,128)}, u32[]{:S(2)}) copy-start(f32[16,2048]{1,0:T(8,128)} %param.9) | copy-start | bytes 393220
  150.3 1.7 %collective-permute-start.9 = (f32[2,16,2048]{2,1,0:T(8,128)S(1)}, f32[2,16,2048]{2,1,0:T(8,128)S(1)}, u32[]{:S(2)}, u32[]{:S(2)}) collective-permute-start(f32[2,16,2048]{2,1,0:T(8,128)S(1)} %pad_maximum_fusion), channel_id=1, source_target_pairs={{0,1},{1,0},{2,3},{3,2},{4,5},{5,4},{6,7},{7,6},{8,9},{9,8},{10,11... | collective-permute-start | bytes 786440 | tf_op jit(solution)/shard_map/ppermute | solution.py:110

commit v24 on v21

--- a/solution.py
+++ b/solution.py
@@ -140,11 +140,10 @@
     taps = jnp.repeat(filters, CGROUP, axis=0).T
     pad = FILT - 1
     previous = from_behind(proj[length - pad :], "ctx", 1)
-    upcoming = from_behind(proj[:pad], "ctx", -1)
     gates_in = gate.reshape(length, columns)
     wanted_in = target.reshape(length, columns)
-    gates_next = from_behind(gates_in[:pad], "ctx", -1)
-    wanted_next = from_behind(wanted_in[:pad], "ctx", -1)
+    ahead = from_behind(jnp.stack([proj[:pad], gates_in[:pad].astype(proj.dtype), wanted_in[:pad].astype(proj.dtype)]), "ctx", -1)
+    upcoming, gates_next, wanted_next = ahead[0], ahead[1], ahead[2]
     padded = jnp.concatenate([previous, proj, upcoming], axis=0).astype(jnp.float32)
     extent = length + pad
     conv = jnp.zeros((extent, columns), jnp.float32)

time: 153 us -> 153 us (level)
  waiting for transfers between devices: 47.7 us -> 55.4 us
  starting transfers between devices: 32 us -> 25.9 us
    all_to_all x2, waiting for transfers between devices: 5.79 us -> 12.5 us  [reduce_partial(): lax.all_to_all(partial.astype(jnp.float16), 'fsdp', 0, 0)]
    ppermute x4 -> x2, starting transfers between devices: 11.7 us -> 5.59 us  [from_behind(): return lax.ppermute(value, axis, pairs)]
    slice x2 -> x0, local copies, waits for them, and re-layouts: 1.97 us -> none  [the longest x1 1.37 us: on_device(): wanted_next = from_behind(wanted_in[:pad], 'ctx', -1)]
  transfers between devices with their start and end apart: 12 -> 10, of which waited for: 8 -> 8; matrix products, arithmetic and copies ran while one was open for 21% -> 19% of each run, Pallas kernels for 0% -> 0%
where the time goes in v24:
time: 153 us; the launch traced here: 152 us
  waiting for transfers between devices  55.4 us (36%)
  starting transfers between devices  25.9 us (17%)
  matrix products  22.8 us (15%)
  blocking collectives  21.8 us (14%)
  other arithmetic  17.4 us (11%)
  local copies, waits for them, and re-layouts  7.66 us (5%)
    ppermute x3, waiting for transfers between devices, ring_gather(): lax.ppermute(value, axis, [(i, (i + shift) % devices) for i in range(devi...  32.1 us
    all_to_all x1, blocking collectives, rows_of_block(): own_half = lax.all_to_all(pieces, 'fsdp', 0, 0)  21.8 us
    dot_general x1, matrix products, on_device(): lax.dot_general(inputs, d_all, (((0,), (0,)), ((), ())), preferred_elemen...  12.9 us
    all_to_all x2, starting transfers between devices, reduce_partial(): lax.all_to_all(partial.astype(jnp.float16), 'fsdp', 0, 0)  12.9 us
    all_to_all x2, waiting for transfers between devices, reduce_partial(): lax.all_to_all(partial.astype(jnp.float16), 'fsdp', 0, 0)  12.5 us
    dot_general x2, matrix products, on_device(): jnp.dot(flat, quant, preferred_element_type=jnp.float32)  9.9 us
    ppermute x1, waiting for transfers between devices, rows_of_block(): other_half = lax.ppermute(own_half, 'seq', [(0, 1), (1, 0)])  7.87 us
    convert_element_type x1, other arithmetic, on_device(): quant = soft_clip(values, clip_upper, clip_lower).astype(jnp.bfloat16)  6.15 us
  transfers between devices with their start and end apart: 10, of which 8 were waited for; matrix products, arithmetic and copies ran while one was open for 19% of the time, Pallas kernels for 0%

profile of v24, /device:TPU:9, one launch (start us, length us, event | category | flops | bytes accessed | tf_op | source)
XLA Modules:
  0.0 152.1 jit_solution(3583549192431110482)
XLA Ops:
  0.6 1.2 broadcast_select_fusion
  1.8 1.3 collective-permute-start
  3.1 5.7 %abs_reduce_fusion = bf16[16,2048]{1,0:T(8,128)(2,1)S(1)} fusion(bf16[2048,2048]{1,0:T(8,128)(2,1)} %param.8), kind=kLoop, calls=%fused_computation.15 | loop fusion | flops 16744448 | bytes 8454144 | tf_op jit(solution)/shard_map/reduce_max | solution.py:20
  9.4 6.2 %fusion.3 = bf16[2048,2048]{1,0:T(8,128)(2,1)S(1)} fusion(bf16[2048,2048]{1,0:T(8,128)(2,1)} %param.8, f32[16,2048]{1,0:T(8,128)S(1)} %get-tuple-element.10, f32[16,2048]{1,0:T(8,128)S(1)} %get-tuple-element.11, f32[16,2048]{1,0:T(8,128)S(1)} %get-tuple-element.16), kind=kLoop, calls=%fused_computation.5 | loop fusion | flops 25165824 | bytes 17170432 | tf_op jit(solution)/shard_map/convert_element_type | solution.py:121
  15.8 21.8 %all_to_all.15 = bf16[4,48,2048]{2,1,0:T(8,128)(2,1)S(1)} all-to-all(bf16[4,48,2048]{2,1,0:T(8,128)(2,1)S(1)} %fusion.23), channel_id=1, replica_groups=mesh['parts'=2,'fsdp'=4,'seq'=2,'ctx'=2] {'fsdp'}, dimensions={0} | all-to-all | bytes 1572864 | tf_op jit(solution)/shard_map/all_to_all | solution.py:81
  37.9 3.3 %fusion.29 = (f16[4,48,2048]{2,1,0:T(8,128)(2,1)}, f32[4,48,2048]{2,1,0:T(8,128)}) fusion(bf16[4,48,2048]{2,1,0:T(8,128)(2,1)S(1)} %all_to_all.15, bf16[2048,2048]{1,0:T(8,128)(2,1)S(1)} %fusion.3), kind=kOutput, calls=%fused_computation.87 | convolution fusion | flops 1611005952 | bytes 11534336 | tf_op jit(solution)/shard_map/dot_general | solution.py:128
  41.2 5.3 %all-to-all-start.1 = ((f16[4,48,2048]{2,1,0:T(8,128)(2,1)}), f16[4,48,2048]{2,1,0:T(8,128)(2,1)S(1)}, u32[]{:S(2)}, u32[]{:S(2)}) async-start(f16[4,48,2048]{2,1,0:T(8,128)(2,1)} %get-tuple-element.31), calls=%async_computation.1 | async-start | bytes 1572864 | tf_op jit(solution)/shard_map/all_to_all | solution.py:89
  46.5 7.9 %collective-permute-done.1 = bf16[4,48,2048]{2,1,0:T(8,128)(2,1)S(1)} collective-permute-done((bf16[4,48,2048]{2,1,0:T(8,128)(2,1)S(1)}, bf16[4,48,2048]{2,1,0:T(8,128)(2,1)S(1)}, u32[]{:S(2)}, u32[]{:S(2)}) %collective-permute-start.1) | collective-permute-done | bytes 786464 | tf_op jit(solution)/shard_map/ppermute | solution.py:82
  54.4 6.6 %fusion.30 = (f16[4,48,2048]{2,1,0:T(8,128)(2,1)}, f32[4,48,2048]{2,1,0:T(8,128)}) fusion(bf16[4,48,2048]{2,1,0:T(8,128)(2,1)S(1)} %collective-permute-done.1, bf16[2048,2048]{1,0:T(8,128)(2,1)} %copy-done), kind=kOutput, calls=%fused_computation.88 | convolution fusion | flops 1611005952 | bytes 11534336 | tf_op jit(solution)/shard_map/dot_general | solution.py:128
  61.0 1.1 all-to-all-done.1
  62.1 7.5 %all-to-all-start.2 = ((f16[4,48,2048]{2,1,0:T(8,128)(2,1)}), f16[4,48,2048]{2,1,0:T(8,128)(2,1)S(1)}, u32[]{:S(2)}, u32[]{:S(2)}) async-start(f16[4,48,2048]{2,1,0:T(8,128)(2,1)} %get-tuple-element.33), calls=%async_computation.2 | async-start | bytes 1572864 | tf_op jit(solution)/shard_map/all_to_all | solution.py:89
  69.6 1.0 broadcast_in_dim.41
  70.6 1.9 %reshape.68 = f32[2048,7]{0,1:T(8,128)} reshape(f32[128,16,7]{1,0,2:T(8,128)} %broadcast_in_dim.41) | data formatting | bytes 114688 | tf_op jit(solution)/shard_map/reshape | solution.py:140
  72.5 1.4 slice_bitcast_fusion.6
  73.8 11.4 %all-to-all-done.2 = f16[4,48,2048]{2,1,0:T(8,128)(2,1)S(1)} async-done(((f16[4,48,2048]{2,1,0:T(8,128)(2,1)}), f16[4,48,2048]{2,1,0:T(8,128)(2,1)S(1)}, u32[]{:S(2)}, u32[]{:S(2)}) %all-to-all-start.2) | async-done | bytes 786464 | tf_op jit(solution)/shard_map/all_to_all | solution.py:89
  85.8 1.2 bitcast_add_fusion.1
  87.1 4.3 %collective-permute-start.2 = (bf16[3,6,2048]{2,1,0:T(8,128)(2,1)S(1)}, bf16[3,6,2048]{2,1,0:T(8,128)(2,1)S(1)}, u32[]{:S(2)}, u32[]{:S(2)}) collective-permute-start(bf16[3,6,2048]{2,1,0:T(8,128)(2,1)S(1)} %pad_maximum_fusion.1), channel_id=1, source_target_pairs={{1,0},{3,2},{5,4},{7,6},{9,8},{11,10},{13,12},{15,14},{17,16},{19,... | collective-permute-start | bytes 221192 | tf_op jit(solution)/shard_map/ppermute | solution.py:13
  91.5 1.3 collective-permute-start.3
  92.8 1.8 %collective-permute-done.3 = bf16[6,2048]{1,0:T(8,128)(2,1)S(1)} collective-permute-done((bf16[6,2048]{1,0:T(8,128)(2,1)S(1)}, bf16[6,2048]{1,0:T(8,128)(2,1)S(1)}, u32[]{:S(2)}, u32[]{:S(2)}) %collective-permute-start.3) | collective-permute-done | bytes 24608 | tf_op jit(solution)/shard_map/ppermute | solution.py:13
  94.7 0.9 convert_multiply_fusion
  95.6 0.7 fusion.17
  96.3 1.4 collective-permute-start.4
  97.7 0.6 maximum_select_fusion
  98.3 0.9 copy.20
  99.2 4.0 %collective-permute-start.5 = (bf16[96,2048]{1,0:T(8,128)(2,1)S(1)}, bf16[96,2048]{1,0:T(8,128)(2,1)S(1)}, u32[]{:S(2)}, u32[]{:S(2)}) collective-permute-start(bf16[96,2048]{1,0:T(8,128)(2,1)S(1)} %fusion.17), channel_id=1, source_target_pairs={{0,8},{4,12},{8,0},{12,4},{1,9},{5,13},{9,1},{13,5},{2,10},{6,14},... | collective-permute-start | bytes 1179656 | tf_op jit(solution)/shard_map/ppermute | solution.py:100
  103.2 5.8 %collective-permute-done.4 = bf16[96,2048]{1,0:T(8,128)(2,1)} collective-permute-done((bf16[96,2048]{1,0:T(8,128)(2,1)S(1)}, bf16[96,2048]{1,0:T(8,128)(2,1)}, u32[]{:S(2)}, u32[]{:S(2)}) %collective-permute-start.4) | collective-permute-done | bytes 393248 | tf_op jit(solution)/shard_map/ppermute | solution.py:100
  109.1 1.0 bitcast_dynamic-update-slice_fusion.2
  110.2 21.2 %collective-permute-done.5 = bf16[96,2048]{1,0:T(8,128)(2,1)S(1)} collective-permute-done((bf16[96,2048]{1,0:T(8,128)(2,1)S(1)}, bf16[96,2048]{1,0:T(8,128)(2,1)S(1)}, u32[]{:S(2)}, u32[]{:S(2)}) %collective-permute-start.5) | collective-permute-done | bytes 393248 | tf_op jit(solution)/shard_map/ppermute | solution.py:100
  131.4 5.1 %collective-permute-done.6 = bf16[96,2048]{1,0:T(8,128)(2,1)S(1)} collective-permute-done((bf16[96,2048]{1,0:T(8,128)(2,1)S(1)}, bf16[96,2048]{1,0:T(8,128)(2,1)S(1)}, u32[]{:S(2)}, u32[]{:S(2)}) %collective-permute-start.6) | collective-permute-done | bytes 393248 | tf_op jit(solution)/shard_map/ppermute | solution.py:100
  136.6 12.9 %multiply_reduce_fusion.1 = (f32[16,2048]{1,0:T(8,128)S(1)}, f32[16,2048]{1,0:T(8,128)S(1)}) fusion(bf16[2048,2048]{1,0:T(8,128)(2,1)} %param.8, f32[16,2048]{1,0:T(8,128)S(1)} %copy-done.4, f32[16,2048]{1,0:T(8,128)S(1)} %copy-done.6, bf16[16,128,384]{2,1,0:T(8,128)(2,1)S(1)} %bitcast.94, bf16[384,2048,1]{1,0,2:T(8,128)(2,1)S(1)} %bitcast.96), kind=kOutput, calls=%fused_computation.7 | convolution fusion | flops 3275685888 | bytes 12058624 | tf_op jit(solution)/shard_map/dot_general | solution.py:163
  150.2 1.2 collective-permute-done.7
  151.4 0.7 slice_bitcast_fusion
  (58 shorter events, 2.7 us)
Async XLA Ops:
  1.8 7.4 %copy-start.7 = (f32[16,2048]{1,0:T(8,128)S(1)}, f32[16,2048]{1,0:T(8,128)}, u32[]{:S(2)}) copy-start(f32[16,2048]{1,0:T(8,128)} %param.10) | copy-start | bytes 393220
  1.8 7.4 %copy-start.9 = (f32[16,2048]{1,0:T(8,128)S(1)}, f32[16,2048]{1,0:T(8,128)}, u32[]{:S(2)}) copy-start(f32[16,2048]{1,0:T(8,128)} %param.9) | copy-start | bytes 393220
  1.8 13.8 %collective-permute-start = (bf16[48,4096]{1,0:T(8,128)(2,1)S(1)}, bf16[48,4096]{1,0:T(8,128)(2,1)S(1)}, u32[]{:S(2)}, u32[]{:S(2)}) collective-permute-start(bf16[48,4096]{1,0:T(8,128)(2,1)S(1)} %get-tuple-element.13), channel_id=1, source_target_pairs={{0,2},{2,0},{1,3},{3,1},{4,6},{6,4},{5,7},{7,5},{8,10},{10,8},{9,1... | collective-permute-start | bytes 1179656 | tf_op jit(solution)/shard_map/ppermute | solution.py:75
  8.8 6.7 %copy-start.1 = (bf16[16,2048]{1,0:T(8,128)(2,1)}, bf16[16,2048]{1,0:T(8,128)(2,1)S(1)}, u32[]{:S(2)}) copy-start(bf16[16,2048]{1,0:T(8,128)(2,1)S(1)} %abs_reduce_fusion) | copy-start | bytes 196612
  9.4 6.2 %copy-start.3 = (f32[16,2048]{1,0:T(8,128)}, f32[16,2048]{1,0:T(8,128)S(1)}, u32[]{:S(2)}) copy-start(f32[16,2048]{1,0:T(8,128)S(1)} %get-tuple-element.10) | copy-start | bytes 393220
  9.4 6.2 %copy-start.5 = (f32[16,2048]{1,0:T(8,128)}, f32[16,2048]{1,0:T(8,128)S(1)}, u32[]{:S(2)}) copy-start(f32[16,2048]{1,0:T(8,128)S(1)} %get-tuple-element.16) | copy-start | bytes 393220
  15.6 25.6 %copy-start = (bf16[2048,2048]{1,0:T(8,128)(2,1)}, bf16[2048,2048]{1,0:T(8,128)(2,1)S(1)}, u32[]{:S(2)}) copy-start(bf16[2048,2048]{1,0:T(8,128)(2,1)S(1)} %fusion.3) | copy-start | bytes 25165828
  37.6 16.8 %collective-permute-start.1 = (bf16[4,48,2048]{2,1,0:T(8,128)(2,1)S(1)}, bf16[4,48,2048]{2,1,0:T(8,128)(2,1)S(1)}, u32[]{:S(2)}, u32[]{:S(2)}) collective-permute-start(bf16[4,48,2048]{2,1,0:T(8,128)(2,1)S(1)} %all_to_all.15), channel_id=1, source_target_pairs={{0,2},{2,0},{1,3},{3,1},{4,6},{6,4},{5,7},{7,5},{8,10},{10,8},{9,1... | collective-permute-start | bytes 2359304 | tf_op jit(solution)/shard_map/ppermute | solution.py:82
  41.2 20.9 %all-to-all-start.1 = ((f16[4,48,2048]{2,1,0:T(8,128)(2,1)}), f16[4,48,2048]{2,1,0:T(8,128)(2,1)S(1)}, u32[]{:S(2)}, u32[]{:S(2)}) async-start(f16[4,48,2048]{2,1,0:T(8,128)(2,1)} %get-tuple-element.31), calls=%async_computation.1 | async-start | bytes 1572864 | tf_op jit(solution)/shard_map/all_to_all | solution.py:89
  46.5 23.1 %copy-start.16 = (f32[128,7]{0,1:T(8,128)S(1)}, f32[128,7]{0,1:T(8,128)}, u32[]{:S(2)}) copy-start(f32[128,7]{0,1:T(8,128)} %param.11) | copy-start | bytes 10756
  46.5 25.9 %copy-start.11 = (bf16[1,1,96,2048]{3,2,1,0:T(8,128)(2,1)S(1)}, bf16[1,1,96,2048]{3,2,1,0:T(8,128)(2,1)}, u32[]{:S(2)}) copy-start(bf16[1,1,96,2048]{3,2,1,0:T(8,128)(2,1)} %param.13) | copy-start | bytes 1179652
  62.1 23.2 %all-to-all-start.2 = ((f16[4,48,2048]{2,1,0:T(8,128)(2,1)}), f16[4,48,2048]{2,1,0:T(8,128)(2,1)S(1)}, u32[]{:S(2)}, u32[]{:S(2)}) async-start(f16[4,48,2048]{2,1,0:T(8,128)(2,1)} %get-tuple-element.33), calls=%async_computation.2 | async-start | bytes 1572864 | tf_op jit(solution)/shard_map/all_to_all | solution.py:89
  85.3 1.8 %copy-start.14 = (bf16[1,6,2048]{2,1,0:T(8,128)(2,1)S(1)}, bf16[1,6,2048]{2,1,0:T(8,128)(2,1)}, u32[]{:S(2)}) copy-start(bf16[1,6,2048]{2,1,0:T(8,128)(2,1)} %get-tuple-element.37) | copy-start | bytes 73732
  85.3 1.8 %copy-start.15 = (bf16[1,6,2048]{2,1,0:T(8,128)(2,1)S(1)}, bf16[1,6,2048]{2,1,0:T(8,128)(2,1)}, u32[]{:S(2)}) copy-start(bf16[1,6,2048]{2,1,0:T(8,128)(2,1)} %get-tuple-element.38) | copy-start | bytes 73732
  85.3 6.2 %copy-start.13 = (f32[2048,7]{0,1:T(8,128)S(1)}, f32[2048,7]{0,1:T(8,128)}, u32[]{:S(2)}) copy-start(f32[2048,7]{0,1:T(8,128)} %reshape.68) | copy-start | bytes 172036
  85.3 9.4 %copy-start.12 = (bf16[1,1,96,2048]{3,2,1,0:T(8,128)(2,1)S(1)}, bf16[1,1,96,2048]{3,2,1,0:T(8,128)(2,1)}, u32[]{:S(2)}) copy-start(bf16[1,1,96,2048]{3,2,1,0:T(8,128)(2,1)} %param.12) | copy-start | bytes 1179652
  87.1 5.7 %collective-permute-start.2 = (bf16[3,6,2048]{2,1,0:T(8,128)(2,1)S(1)}, bf16[3,6,2048]{2,1,0:T(8,128)(2,1)S(1)}, u32[]{:S(2)}, u32[]{:S(2)}) collective-permute-start(bf16[3,6,2048]{2,1,0:T(8,128)(2,1)S(1)} %pad_maximum_fusion.1), channel_id=1, source_target_pairs={{1,0},{3,2},{5,4},{7,6},{9,8},{11,10},{13,12},{15,14},{17,16},{19,... | collective-permute-start | bytes 221192 | tf_op jit(solution)/shard_map/ppermute | solution.py:13
  91.5 3.1 %collective-permute-start.3 = (bf16[6,2048]{1,0:T(8,128)(2,1)S(1)}, bf16[6,2048]{1,0:T(8,128)(2,1)S(1)}, u32[]{:S(2)}, u32[]{:S(2)}) collective-permute-start(bf16[6,2048]{1,0:T(8,128)(2,1)S(1)} %get-tuple-element.14), channel_id=1, source_target_pairs={{0,1},{2,3},{4,5},{6,7},{8,9},{10,11},{12,13},{14,15},{16,17},{18,... | collective-permute-start | bytes 73736 | tf_op jit(solution)/shard_map/ppermute | solution.py:13
  96.3 12.7 %collective-permute-start.4 = (bf16[96,2048]{1,0:T(8,128)(2,1)S(1)}, bf16[96,2048]{1,0:T(8,128)(2,1)}, u32[]{:S(2)}, u32[]{:S(2)}) collective-permute-start(bf16[96,2048]{1,0:T(8,128)(2,1)S(1)} %fusion.17), channel_id=1, source_target_pairs={{0,4},{4,8},{8,12},{12,0},{1,5},{5,9},{9,13},{13,1},{2,6},{6,10},{... | collective-permute-start | bytes 1179656 | tf_op jit(solution)/shard_map/ppermute | solution.py:100
  99.2 37.4 %copy-start.4 = (f32[16,2048]{1,0:T(8,128)S(1)}, f32[16,2048]{1,0:T(8,128)}, u32[]{:S(2)}) copy-start(f32[16,2048]{1,0:T(8,128)} %copy-done.3) | copy-start | bytes 393220
  99.2 37.4 %copy-start.6 = (f32[16,2048]{1,0:T(8,128)S(1)}, f32[16,2048]{1,0:T(8,128)}, u32[]{:S(2)}) copy-start(f32[16,2048]{1,0:T(8,128)} %copy-done.5) | copy-start | bytes 393220
  99.2 32.1 %collective-permute-start.5 = (bf16[96,2048]{1,0:T(8,128)(2,1)S(1)}, bf16[96,2048]{1,0:T(8,128)(2,1)S(1)}, u32[]{:S(2)}, u32[]{:S(2)}) collective-permute-start(bf16[96,2048]{1,0:T(8,128)(2,1)S(1)} %fusion.17), channel_id=1, source_target_pairs={{0,8},{4,12},{8,0},{12,4},{1,9},{5,13},{9,1},{13,5},{2,10},{6,14},... | collective-permute-start | bytes 1179656 | tf_op jit(solution)/shard_map/ppermute | solution.py:100
  103.2 33.4 %collective-permute-start.6 = (bf16[96,2048]{1,0:T(8,128)(2,1)S(1)}, bf16[96,2048]{1,0:T(8,128)(2,1)S(1)}, u32[]{:S(2)}, u32[]{:S(2)}) collective-permute-start(bf16[96,2048]{1,0:T(8,128)(2,1)S(1)} %fusion.17), channel_id=1, source_target_pairs={{0,12},{4,0},{8,4},{12,8},{1,13},{5,1},{9,5},{13,9},{2,14},{6,2},{... | collective-permute-start | bytes 1179656 | tf_op jit(solution)/shard_map/ppermute | solution.py:100
  136.6 12.9 %copy-start.2 = (bf16[16,2048]{1,0:T(8,128)(2,1)S(1)}, bf16[16,2048]{1,0:T(8,128)(2,1)}, u32[]{:S(2)}) copy-start(bf16[16,2048]{1,0:T(8,128)(2,1)} %copy-done.1) | copy-start | bytes 196612
  136.6 12.9 %copy-start.8 = (f32[16,2048]{1,0:T(8,128)S(1)}, f32[16,2048]{1,0:T(8,128)}, u32[]{:S(2)}) copy-start(f32[16,2048]{1,0:T(8,128)} %param.10) | copy-start | bytes 393220
  136.6 12.9 %copy-start.10 = (f32[16,2048]{1,0:T(8,128)S(1)}, f32[16,2048]{1,0:T(8,128)}, u32[]{:S(2)}) copy-start(f32[16,2048]{1,0:T(8,128)} %param.9) | copy-start | bytes 393220
  149.7 1.7 %collective-permute-start.7 = (f32[2,16,2048]{2,1,0:T(8,128)S(1)}, f32[2,16,2048]{2,1,0:T(8,128)S(1)}, u32[]{:S(2)}, u32[]{:S(2)}) collective-permute-start(f32[2,16,2048]{2,1,0:T(8,128)S(1)} %pad_maximum_fusion), channel_id=1, source_target_pairs={{0,1},{1,0},{2,3},{3,2},{4,5},{5,4},{6,7},{7,6},{8,9},{9,8},{10,11... | collective-permute-start | bytes 786440 | tf_op jit(solution)/shard_map/ppermute | solution.py:110
